TPU v7x, 32 devices: a whole 2x2x4 slice. The times are simulated.
32 devices in a mesh: clips: 2 (over y), rows: 4 (over z), tm: 2 (over x), chan: 2 (over core).
Axes of the slice: x: 2, y: 2, z: 4, core: 2. Of those that a mesh axis runs over, the one named last changes fastest.
Arguments:
- latent: bfloat16 [8, 4, 64, 512], P(('clips', 'tm'), 'rows', None, 'chan'), parts along dimension 0, may hold values from -24 to 24, as said below
- norm1_gain: float32 [512], P('chan'), may hold values from 0.5 to 1.5
- norm1_bias: float32 [512], P('chan'), may hold values from -1.2 to 1.2
- conv_weight: bfloat16 [13824, 512], P('rows', 'chan'), may hold values from -0.0546875 to 0.0546875
- conv_bias: float32 [512], P('chan'), may hold values from -1.2 to 1.2
- norm2_gain: float32 [512], P('chan'), may hold values from 0.5 to 1.5
- norm2_bias: float32 [512], P('chan'), may hold values from -1.2 to 1.2
- w_query: bfloat16 [512, 512], replicated, may hold values from -2 to 2
- b_query: float32 [512], replicated, may hold values from -1.2 to 1.2
- w_key: bfloat16 [512, 512], replicated, may hold values from -3 to 3
- w_value: bfloat16 [512, 512], replicated, may hold values from -0.25 to 0.25
- b_value: float32 [512], replicated, may hold values from -1.2 to 1.2
- w_out: bfloat16 [512, 512], replicated, may hold values from -0.25 to 0.25
- b_out: float32 [512], replicated, may hold values from -1.2 to 1.2
Outputs:
- decoded: bfloat16 [8, 4, 64, 512], P(('clips', 'tm'), 'rows', None, 'chan'), parts along dimension 0
There are 2 independent parts, one for each index of `clips`. A program takes and returns all parts, laid end to end along the dimension named above; an argument that names none is the same for every part. Nothing has to cross between parts.
Inputs may be any that keep to these rules, and one draw needn't show every extreme that they name: `latent`: activations of order one.
All inputs are finite; a program needn't handle non-finite values.
Results may differ from a plain program's by a relative error of at most 0.012.
The roundings to bfloat16 on the way count: a program that leaves them out, or rounds other values in their place, can miss the bound.
Values may be sent and summed in bfloat16 or wider, within the bound.
No kernel may reach another device: no remote copies, remote signals or barrier semaphores. Data moves between devices by JAX's collectives and lax.ppermute only.
A program may use at most 64 MiB of HBM per device.

v0:
```python
import jax
import jax.numpy as jnp
from jax import lax
from jax.sharding import PartitionSpec as P

C = 512
GROUPS = 32


EPSILON = 1e-06


def passed_along(value, axis, steps):
    count = lax.axis_size(axis)
    leading, last = (max(0, -steps), min(count, count - steps))
    return lax.ppermute(value, axis, [(source, source + steps) for source in range(leading, last)])


def with_halo(cells, sides, width):
    for axis, dim in sides:
        count = lax.axis_size(axis)
        ends = count - 1
        head = lax.slice_in_dim(cells, 0, width, axis=dim)
        tail = lax.slice_in_dim(cells, cells.shape[dim] - width, cells.shape[dim], axis=dim)
        cells = jnp.concatenate(
            [
                lax.ppermute(tail, axis, [(i, (i + 1) % count) for i in range(ends)]),
                cells,
                lax.ppermute(head, axis, [((i + 1) % count, i) for i in range(ends)]),
            ],
            axis=dim,
        )
    return cells


def group_view(values, group_size):
    full_shape = values.shape
    return values.astype(jnp.float32).reshape(
        full_shape[:-1] + (full_shape[-1] // group_size, group_size)
    )


def clip_normalize(latent, group_size):
    grouped = group_view(latent, group_size)
    cell_count = (
        grouped.shape[0]
        * grouped.shape[1]
        * grouped.shape[2]
        * group_size
        * lax.axis_size("rows")
        * lax.axis_size("tm")
    )
    group_mean = lax.psum(jnp.sum(grouped, axis=(0, 1, 2, 4)), ("rows", "tm")) / cell_count
    centered = grouped - group_mean[:, None]
    group_var = (
        lax.psum(jnp.sum(centered * centered, axis=(0, 1, 2, 4)), ("rows", "tm")) / cell_count
    )
    centered = grouped - group_mean[:, None]
    return (centered * lax.rsqrt(group_var + EPSILON)[:, None]).reshape(latent.shape)


def frame_normalize(middle, group_size):
    grouped = group_view(middle, group_size)
    cell_count = grouped.shape[1] * grouped.shape[2] * group_size * lax.axis_size("rows")
    group_mean = lax.psum(jnp.sum(grouped, axis=(1, 2, 4)), "rows") / cell_count
    centered = grouped - group_mean[:, None, None, :, None]
    group_var = lax.psum(jnp.sum(centered * centered, axis=(1, 2, 4)), "rows") / cell_count
    centered = grouped - group_mean[:, None, None, :, None]
    return (centered * lax.rsqrt(group_var + EPSILON)[:, None, None, :, None]).reshape(middle.shape)


def softmax_update(running, queries, key_block, value_block, score_scale):
    row_peak, weight_sum, accumulated = running
    scores = (
        jnp.einsum("fqc,fkc->fqk", queries, key_block, preferred_element_type=jnp.float32)
        * score_scale
    )
    new_peak = jnp.max(scores, axis=2)
    factor = jnp.exp(row_peak - new_peak)
    weights = jnp.exp(scores - new_peak[:, :, None])
    weight_sum = weight_sum * factor + jnp.sum(weights, axis=2)
    accumulated = accumulated * factor[:, :, None] + jnp.einsum(
        "fqk,fkc->fqc",
        weights.astype(jnp.bfloat16),
        value_block,
        preferred_element_type=jnp.float32,
    )
    return (new_peak, weight_sum, accumulated)


def local(
    latent,
    norm1_gain,
    norm1_bias,
    conv_weight,
    conv_bias,
    norm2_gain,
    norm2_bias,
    w_query,
    b_query,
    w_key,
    w_value,
    b_value,
    w_out,
    b_out,
):
    frames, rows_here, columns, channels = latent.shape
    group_size = C // GROUPS
    activated = jax.nn.silu(clip_normalize(latent, group_size) * norm1_gain + norm1_bias).astype(
        jnp.bfloat16
    )
    all_channels = lax.all_gather(activated, "chan", axis=3, tiled=True)
    carried = passed_along(all_channels, "tm", 1)
    carried = jnp.where(
        lax.axis_index("tm") == 0, jnp.broadcast_to(all_channels[:1], carried.shape), carried
    )
    timed = jnp.concatenate([carried, all_channels], axis=0)
    rimmed = with_halo(timed, (("rows", 1),), 1)
    row_place = lax.axis_index("rows")
    upper_rim = jnp.where(row_place == 0, rimmed[:, 1:2], rimmed[:, :1])
    lower_rim = jnp.where(row_place == lax.axis_size("rows") - 1, rimmed[:, -2:-1], rimmed[:, -1:])
    rimmed = jnp.concatenate([upper_rim, rimmed[:, 1:-1], lower_rim], axis=1)
    padded = jnp.concatenate([rimmed[:, :, :1], rimmed, rimmed[:, :, -1:]], axis=2)
    windows = []
    for frame_step in range(3):
        for row_step in range(3):
            for column_step in range(3):
                windows.append(
                    padded[
                        frame_step : frame_step + frames,
                        row_step : row_step + rows_here,
                        column_step : column_step + columns,
                    ].reshape(-1, C)
                )
    patches = jnp.concatenate(windows, axis=1)
    convolved = jnp.dot(
        patches,
        lax.all_gather(conv_weight, "rows", axis=0, tiled=True),
        preferred_element_type=jnp.float32,
    )
    middle = (latent.astype(jnp.float32) + (convolved + conv_bias).reshape(latent.shape)).astype(
        jnp.bfloat16
    )
    normed = (frame_normalize(middle, group_size) * norm2_gain + norm2_bias).astype(jnp.bfloat16)
    swapped = lax.all_to_all(normed, "chan", split_axis=0, concat_axis=3, tiled=True)
    frame_count = swapped.shape[0]
    local_tokens = rows_here * columns
    flattened = swapped.reshape(-1, C)
    queries = (
        (jnp.dot(flattened, w_query, preferred_element_type=jnp.float32) + b_query)
        .astype(jnp.bfloat16)
        .reshape(frame_count, local_tokens, C)
    )
    score_scale = C ** (-0.5)
    initial = (
        jnp.full((frame_count, local_tokens), -jnp.inf, jnp.float32),
        jnp.zeros((frame_count, local_tokens), jnp.float32),
        jnp.zeros((frame_count, local_tokens, C), jnp.float32),
    )
    feature_rows = swapped.reshape(frame_count, local_tokens, C)
    shard_flat = lax.all_gather(feature_rows, "rows", axis=1, tiled=True).reshape(-1, C)
    key_block = (
        jnp.dot(shard_flat, w_key, preferred_element_type=jnp.float32)
        .astype(jnp.bfloat16)
        .reshape(frame_count, -1, C)
    )
    value_block = (
        (jnp.dot(shard_flat, w_value, preferred_element_type=jnp.float32) + b_value)
        .astype(jnp.bfloat16)
        .reshape(frame_count, -1, C)
    )
    row_peak, weight_sum, accumulated = softmax_update(
        initial, queries, key_block, value_block, score_scale
    )
    attended = (accumulated / weight_sum[:, :, None]).astype(jnp.bfloat16)
    branch = (
        (jnp.dot(attended.reshape(-1, C), w_out, preferred_element_type=jnp.float32) + b_out)
        .astype(jnp.bfloat16)
        .reshape(frame_count, rows_here, columns, C)
    )
    returned = lax.all_to_all(branch, "chan", split_axis=3, concat_axis=0, tiled=True)
    return (middle.astype(jnp.float32) + returned.astype(jnp.float32)).astype(jnp.bfloat16)


def solution(mesh):
    in_specs = (
        P(("clips", "tm"), "rows", None, "chan"),
        P("chan"),
        P("chan"),
        P("rows", "chan"),
        P("chan"),
        P("chan"),
        P("chan"),
        P(),
        P(),
        P(),
        P(),
        P(),
        P(),
        P(),
    )
    out_specs = P(("clips", "tm"), "rows", None, "chan")
    return jax.shard_map(local, mesh=mesh, in_specs=in_specs, out_specs=out_specs, check_vma=False)
```

profile of v0, /device:TPU:0, one launch (start us, length us, event | category | flops | bytes accessed | tf_op | source)
XLA Modules:
  0.0 204.5 jit_solution(6646806189756094243)
XLA Ops:
  6.5 0.7 all-gather.2.cloned.1.call-update
  7.3 0.9 convert_reduce_fusion.1
  8.2 0.1 reduce_sum.59
  8.3 23.4 %psum.28 = f32[16]{0:T(128)S(1)} all-reduce(f32[16]{0:T(128)S(1)} %reduce_sum.59), channel_id=1, replica_groups=mesh['clips'=2,'rows'=4,'tm'=2,'chan'=2] {'rows','tm'}, use_global_device_ids=true, to_apply=%region_2.0 | all-reduce | flops 16 | bytes 128 | tf_op jit(solution)/shard_map/psum | solution.py:53
  31.9 0.9 fusion.39
  32.9 0.1 reduce_sum.62
  33.0 17.6 %psum.29 = f32[16]{0:T(128)S(1)} all-reduce(f32[16]{0:T(128)S(1)} %reduce_sum.62), channel_id=1, replica_groups=mesh['clips'=2,'rows'=4,'tm'=2,'chan'=2] {'rows','tm'}, use_global_device_ids=true, to_apply=%region_5.6 | all-reduce | flops 16 | bytes 128 | tf_op jit(solution)/shard_map/psum | solution.py:56
  50.8 0.9 fusion.47
  51.7 1.9 all_gather.9
  53.6 3.9 %collective-permute-start = (bf16[2,1,64,512]{3,2,1,0:T(8,128)(2,1)S(1)}, bf16[2,1,64,512]{3,2,1,0:T(8,128)(2,1)S(1)}, u32[]{:S(2)}, u32[]{:S(2)}) collective-permute-start(bf16[2,1,64,512]{3,2,1,0:T(8,128)(2,1)S(1)} %all_gather.9), channel_id=1, source_target_pairs={{0,2},{1,3},{4,6},{5,7},{8,10},{9,11},{12,14},{13,15},{16,18},{17,... | collective-permute-start | bytes 393224 | tf_op jit(solution)/shard_map/ppermute | solution.py:16
  57.5 3.0 %collective-permute-done = bf16[2,1,64,512]{3,2,1,0:T(8,128)(2,1)S(1)} collective-permute-done((bf16[2,1,64,512]{3,2,1,0:T(8,128)(2,1)S(1)}, bf16[2,1,64,512]{3,2,1,0:T(8,128)(2,1)S(1)}, u32[]{:S(2)}, u32[]{:S(2)}) %collective-permute-start) | collective-permute-done | bytes 131104 | tf_op jit(solution)/shard_map/ppermute | solution.py:16
  60.6 2.1 %collective-permute-start.1 = (bf16[4,1,64,512]{3,2,1,0:T(8,128)(2,1)S(1)}, bf16[4,1,64,512]{3,2,1,0:T(8,128)(2,1)S(1)}, u32[]{:S(2)}, u32[]{:S(2)}) collective-permute-start(bf16[4,1,64,512]{3,2,1,0:T(8,128)(2,1)S(1)} %pad_maximum_fusion.6), channel_id=1, source_target_pairs={{0,4},{4,8},{8,12},{1,5},{5,9},{9,13},{2,6},{6,10},{10,14},{3,7},{... | collective-permute-start | bytes 786440 | tf_op jit(solution)/shard_map/ppermute | solution.py:27
  62.7 1.3 collective-permute-start.2
  64.1 10.4 %collective-permute-done.1 = bf16[4,1,64,512]{3,2,1,0:T(8,128)(2,1)S(1)} collective-permute-done((bf16[4,1,64,512]{3,2,1,0:T(8,128)(2,1)S(1)}, bf16[4,1,64,512]{3,2,1,0:T(8,128)(2,1)S(1)}, u32[]{:S(2)}, u32[]{:S(2)}) %collective-permute-start.1) | collective-permute-done | bytes 262176 | tf_op jit(solution)/shard_map/ppermute | solution.py:27
  74.4 9.7 %collective-permute-done.2 = bf16[4,1,64,512]{3,2,1,0:T(8,128)(2,1)S(1)} collective-permute-done((bf16[4,1,64,512]{3,2,1,0:T(8,128)(2,1)S(1)}, bf16[4,1,64,512]{3,2,1,0:T(8,128)(2,1)S(1)}, u32[]{:S(2)}, u32[]{:S(2)}) %collective-permute-start.2) | collective-permute-done | bytes 262176 | tf_op jit(solution)/shard_map/ppermute | solution.py:29
  84.2 0.4 fusion.19
  84.6 0.3 fusion.57
  85.0 0.7 constant_dynamic-update-slice_fusion.26
  85.8 0.7 constant_dynamic-update-slice_fusion.25
  86.5 0.7 constant_dynamic-update-slice_fusion.24
  87.2 0.7 constant_dynamic-update-slice_fusion.23
  87.9 0.7 constant_dynamic-update-slice_fusion.22
  88.6 0.7 constant_dynamic-update-slice_fusion.21
  89.2 0.7 constant_dynamic-update-slice_fusion.20
  89.9 0.7 constant_dynamic-update-slice_fusion.19
  90.6 0.7 constant_dynamic-update-slice_fusion.18
  91.3 0.7 constant_dynamic-update-slice_fusion.17
  92.0 0.7 constant_dynamic-update-slice_fusion.16
  92.7 0.7 constant_dynamic-update-slice_fusion.15
  93.3 0.7 constant_dynamic-update-slice_fusion.14
  94.0 0.7 constant_dynamic-update-slice_fusion.13
  94.7 0.7 constant_dynamic-update-slice_fusion.12
  95.4 0.7 constant_dynamic-update-slice_fusion.11
  96.0 0.7 constant_dynamic-update-slice_fusion.10
  96.7 0.7 constant_dynamic-update-slice_fusion.9
  97.4 0.7 constant_dynamic-update-slice_fusion.8
  98.1 0.7 constant_dynamic-update-slice_fusion.7
  98.8 0.7 constant_dynamic-update-slice_fusion.6
  99.5 0.7 constant_dynamic-update-slice_fusion.5
  100.2 0.7 constant_dynamic-update-slice_fusion.4
  100.9 0.7 constant_dynamic-update-slice_fusion.3
  101.6 0.7 constant_dynamic-update-slice_fusion.2
  102.2 0.7 constant_dynamic-update-slice_fusion.1
  102.9 0.7 constant_dynamic-update-slice_fusion
  103.6 42.1 %all-gather.2.cloned.1.call-done = bf16[13824,256]{1,0:T(8,128)(2,1)} async-done(((bf16[3456,256]{1,0:T(8,128)(2,1)}), bf16[13824,256]{1,0:T(8,128)(2,1)}) %all-gather.2.cloned.1.call-update) | async-done | bytes 7077904 | tf_op jit(solution)/shard_map/all_gather | solution.py:138
  145.7 5.2 %convert_reduce_fusion = (f32[2,256]{1,0:T(2,128)S(1)}, bf16[2,1,64,256]{3,2,1,0:T(8,128)(2,1)S(1)}) fusion(bf16[2,1,64,256]{3,2,1,0:T(8,128)(2,1)S(1)} %copy-done.1, f32[256]{0:T(256)S(1)} %copy-done.5, bf16[13824,256]{1,0:T(8,128)(2,1)} %all-gather.2.cloned.1.call-done, bf16[128,13824]{1,0:T(8,128)(2,1)} %constant_dynamic-update-slice_fusion), kind=kOutput, calls=%fused_computation.49 | convolution fusion | flops 906165760 | bytes 10750976 | tf_op jit(solution)/shard_map/dot_general | solution.py:136
  151.1 8.7 %psum.30 = f32[2,16]{1,0:T(2,128)S(1)} all-reduce(f32[2,16]{1,0:T(2,128)S(1)} %reduce_sum.81), channel_id=1, replica_groups=mesh['clips'=2,'rows'=4,'tm'=2,'chan'=2] {'rows'}, use_global_device_ids=true, to_apply=%region_8.9 | all-reduce | flops 32 | bytes 256 | tf_op jit(solution)/shard_map/psum | solution.py:65
  160.1 10.1 %psum.31 = f32[2,16]{1,0:T(2,128)S(1)} all-reduce(f32[2,16]{1,0:T(2,128)S(1)} %reduce_sum.84), channel_id=1, replica_groups=mesh['clips'=2,'rows'=4,'tm'=2,'chan'=2] {'rows'}, use_global_device_ids=true, to_apply=%region_11.12 | all-reduce | flops 32 | bytes 256 | tf_op jit(solution)/shard_map/psum | solution.py:67
  170.4 3.8 %all_to_all.24 = bf16[2,1,64,256]{3,2,1,0:T(8,128)(2,1)S(1)} all-to-all(bf16[2,1,64,256]{3,2,1,0:T(8,128)(2,1)S(1)} %fusion.38), channel_id=1, replica_groups=mesh['clips'=2,'rows'=4,'tm'=2,'chan'=2] {'chan'}, dimensions={0} | all-to-all | bytes 131072 | tf_op jit(solution)/shard_map/all_to_all | solution.py:145
  174.3 14.3 %all_gather.11 = bf16[1,256,512]{2,1,0:T(8,128)(2,1)S(1)} all-gather(bf16[1,64,512]{2,1,0:T(8,128)(2,1)S(1)} %reshape.270), channel_id=1, replica_groups=mesh['clips'=2,'rows'=4,'tm'=2,'chan'=2] {'rows'}, dimensions={1}, use_global_device_ids=true | all-gather | bytes 327680 | tf_op jit(solution)/shard_map/all_gather | solution.py:161
  188.7 0.2 fusion.14
  188.9 0.5 fusion.61
  189.4 0.2 fusion.51
  189.7 0.4 fusion.13
  190.1 0.2 fusion.16
  190.3 0.2 copy.29
  190.5 0.5 broadcast.130
  191.0 1.4 reduce.14
  192.5 0.2 reshape.275
  192.6 3.8 %all_to_all.25 = bf16[2,2,8192]{2,1,0:T(2,128)(2,1)S(1)} all-to-all(bf16[2,2,8192]{2,1,0:T(2,128)(2,1)S(1)} %reshape.275), channel_id=1, replica_groups=mesh['clips'=2,'rows'=4,'tm'=2,'chan'=2] {'chan'}, dimensions={0} | all-to-all | bytes 131072 | tf_op jit(solution)/shard_map/all_to_all | solution.py:181
  196.4 0.1 reshape.276
  196.6 0.3 bitcast_convert_fusion
  196.9 0.1 copy.30
  197.0 0.6 fusion.49
  (53 shorter events, 1.6 us)
Async XLA Ops:
  6.5 182.1 %copy-start = (bf16[512,512]{1,0:T(8,128)(2,1)S(1)}, bf16[512,512]{1,0:T(8,128)(2,1)}, u32[]{:S(2)}) copy-start(bf16[512,512]{1,0:T(8,128)(2,1)} %param.21) | copy-start | bytes 1572868
  6.5 139.1 %all-gather.2.cloned.1.call-start = ((), (), s32[]{:S(2)}) async-start(), calls=%async_computation.2 | async-start | bytes 8847360 | tf_op jit(solution)/shard_map/all_gather | solution.py:138
  53.6 6.9 %collective-permute-start = (bf16[2,1,64,512]{3,2,1,0:T(8,128)(2,1)S(1)}, bf16[2,1,64,512]{3,2,1,0:T(8,128)(2,1)S(1)}, u32[]{:S(2)}, u32[]{:S(2)}) collective-permute-start(bf16[2,1,64,512]{3,2,1,0:T(8,128)(2,1)S(1)} %all_gather.9), channel_id=1, source_target_pairs={{0,2},{1,3},{4,6},{5,7},{8,10},{9,11},{12,14},{13,15},{16,18},{17,... | collective-permute-start | bytes 393224 | tf_op jit(solution)/shard_map/ppermute | solution.py:16
  60.6 13.8 %collective-permute-start.1 = (bf16[4,1,64,512]{3,2,1,0:T(8,128)(2,1)S(1)}, bf16[4,1,64,512]{3,2,1,0:T(8,128)(2,1)S(1)}, u32[]{:S(2)}, u32[]{:S(2)}) collective-permute-start(bf16[4,1,64,512]{3,2,1,0:T(8,128)(2,1)S(1)} %pad_maximum_fusion.6), channel_id=1, source_target_pairs={{0,4},{4,8},{8,12},{1,5},{5,9},{9,13},{2,6},{6,10},{10,14},{3,7},{... | collective-permute-start | bytes 786440 | tf_op jit(solution)/shard_map/ppermute | solution.py:27
  62.7 21.4 %collective-permute-start.2 = (bf16[4,1,64,512]{3,2,1,0:T(8,128)(2,1)S(1)}, bf16[4,1,64,512]{3,2,1,0:T(8,128)(2,1)S(1)}, u32[]{:S(2)}, u32[]{:S(2)}) collective-permute-start(bf16[4,1,64,512]{3,2,1,0:T(8,128)(2,1)S(1)} %pad_maximum_fusion.6), channel_id=1, source_target_pairs={{4,0},{8,4},{12,8},{5,1},{9,5},{13,9},{6,2},{10,6},{14,10},{7,3},{... | collective-permute-start | bytes 786440 | tf_op jit(solution)/shard_map/ppermute | solution.py:29
  85.8 59.9 %copy-start.1 = (bf16[2,1,64,256]{3,2,1,0:T(8,128)(2,1)S(1)}, bf16[2,1,64,256]{3,2,1,0:T(8,128)(2,1)}, u32[]{:S(2)}) copy-start(bf16[2,1,64,256]{3,2,1,0:T(8,128)(2,1)} %param.14) | copy-start | bytes 196612
  85.8 59.9 %copy-start.5 = (f32[256]{0:T(256)S(1)}, f32[256]{0:T(256)}, u32[]{:S(2)}) copy-start(f32[256]{0:T(256)} %param.18) | copy-start | bytes 3076
  103.6 66.8 %copy-start.6 = (f32[256]{0:T(256)S(1)}, f32[256]{0:T(256)}, u32[]{:S(2)}) copy-start(f32[256]{0:T(256)} %param.20) | copy-start | bytes 3076
  103.6 66.8 %copy-start.7 = (f32[256]{0:T(256)S(1)}, f32[256]{0:T(256)}, u32[]{:S(2)}) copy-start(f32[256]{0:T(256)} %param.19) | copy-start | bytes 3076
  103.6 85.1 %copy-start.3 = (f32[512]{0:T(512)S(1)}, f32[512]{0:T(512)}, u32[]{:S(2)}) copy-start(f32[512]{0:T(512)} %param.22) | copy-start | bytes 6148
  103.6 85.3 %copy-start.8 = (bf16[512,512]{1,0:T(8,128)(2,1)S(1)}, bf16[512,512]{1,0:T(8,128)(2,1)}, u32[]{:S(2)}) copy-start(bf16[512,512]{1,0:T(8,128)(2,1)} %param.23) | copy-start | bytes 1572868
  103.6 86.1 %copy-start.9 = (bf16[512,512]{1,0:T(8,128)(2,1)S(1)}, bf16[512,512]{1,0:T(8,128)(2,1)}, u32[]{:S(2)}) copy-start(bf16[512,512]{1,0:T(8,128)(2,1)} %param.24) | copy-start | bytes 1572868
  103.6 86.1 %copy-start.10 = (f32[512]{0:T(512)S(1)}, f32[512]{0:T(512)}, u32[]{:S(2)}) copy-start(f32[512]{0:T(512)} %param.25) | copy-start | bytes 6148
  150.9 39.3 %copy-start.2 = (bf16[512,512]{1,0:T(8,128)(2,1)S(1)}, bf16[512,512]{1,0:T(8,128)(2,1)}, u32[]{:S(2)}) copy-start(bf16[512,512]{1,0:T(8,128)(2,1)} %param.26) | copy-start | bytes 1572868
  150.9 39.3 %copy-start.4 = (f32[512]{0:T(512)S(1)}, f32[512]{0:T(512)}, u32[]{:S(2)}) copy-start(f32[512]{0:T(512)} %param.27) | copy-start | bytes 6148
Sparse Core Ops, SparseCore 0:
  8.9 136.6 all-gather.1
where the time goes:
time: 205 us; the launch traced here: 204 us
  blocking collectives  83.6 us (41%)
  waiting for transfers between devices  65.9 us (32%)
  local copies, waits for them, and re-layouts  21.1 us (10%)
  between operations  13.7 us (7%)
  starting transfers between devices  7.29 us (4%)
  matrix products  6.57 us (3%)
  other arithmetic  6.28 us (3%)
    all_gather x1, waiting for transfers between devices, local(): lax.all_gather(conv_weight, 'rows', axis=0, tiled=True)  42.1 us
    psum x1, blocking collectives, clip_normalize(): lax.psum(jnp.sum(grouped, axis=(0, 1, 2, 4)), ('rows', 'tm')) / cell_count  23.4 us
    unnamed x52, local copies, waits for them, and re-layouts  18.7 us
    psum x1, blocking collectives, clip_normalize(): lax.psum(jnp.sum(centered * centered, axis=(0, 1, 2, 4)), ('rows', 'tm'))  17.6 us
    all_gather x1, blocking collectives, local(): lax.all_gather(feature_rows, 'rows', axis=1, tiled=True).reshape(-1, C)  14.3 us
    ppermute x1, waiting for transfers between devices, with_halo(): lax.ppermute(tail, axis, [(i, (i + 1) % count) for i in range(ends)])  10.4 us
    psum x1, blocking collectives, frame_normalize(): lax.psum(jnp.sum(centered * centered, axis=(1, 2, 4)), 'rows') / cell_count  10.1 us
    ppermute x1, waiting for transfers between devices, with_halo(): lax.ppermute(head, axis, [((i + 1) % count, i) for i in range(ends)])  9.72 us
  transfers between devices with their start and end apart: 4, of which 4 were waited for; matrix products, arithmetic and copies ran while one was open for 11% of the time, Pallas kernels for 0%

commit v1 on v0

v1 whole, which is shorter than its diff:
```python
import jax
import jax.numpy as jnp
from jax import lax
from jax.sharding import PartitionSpec as P

C = 512
GROUPS = 32


EPSILON = 1e-06


def group_stats(values, group_size, axes):
    grouped = values.astype(jnp.float32).reshape(
        values.shape[:-1] + (values.shape[-1] // group_size, group_size)
    )
    group_mean = jnp.mean(grouped, axis=axes, keepdims=True)
    centered = grouped - group_mean
    group_var = jnp.mean(centered * centered, axis=axes, keepdims=True)
    return group_mean, group_var


def apply_norm(values, group_mean, group_var, group_size):
    grouped = values.astype(jnp.float32).reshape(
        values.shape[:-1] + (values.shape[-1] // group_size, group_size)
    )
    return ((grouped - group_mean) * lax.rsqrt(group_var + EPSILON)).reshape(values.shape)


def edge_pad(cells, dim, before, after):
    size = cells.shape[dim]
    parts = [lax.slice_in_dim(cells, 0, 1, axis=dim)] * before + [cells]
    parts += [lax.slice_in_dim(cells, size - 1, size, axis=dim)] * after
    return jnp.concatenate(parts, axis=dim)


def local(
    latent,
    norm1_gain,
    norm1_bias,
    conv_weight,
    conv_bias,
    norm2_gain,
    norm2_bias,
    w_query,
    b_query,
    w_key,
    w_value,
    b_value,
    w_out,
    b_out,
):
    frames, rows_here, columns, channels = latent.shape
    group_size = C // GROUPS
    time_count = lax.axis_size("tm")
    row_count = lax.axis_size("rows")
    chan_count = lax.axis_size("chan")
    time_place = lax.axis_index("tm")
    row_place = lax.axis_index("rows")
    chan_place = lax.axis_index("chan")
    all_rows = rows_here * row_count

    gathered = lax.all_gather(latent, ("tm", "rows", "chan"), axis=0, tiled=False)
    gathered = gathered.reshape(
        (time_count, row_count, chan_count, frames, rows_here, columns, channels)
    )
    clip = jnp.transpose(gathered, (0, 3, 1, 4, 5, 2, 6)).reshape(
        (time_count * frames, all_rows, columns, chan_count * channels)
    )

    mean1, var1 = group_stats(clip, group_size, (0, 1, 2, 4))
    frame_index = jnp.clip(
        time_place * frames - 2 + jnp.arange(frames + 2), 0, time_count * frames - 1
    )
    segment = jnp.take(clip, frame_index, axis=0)
    gain1 = lax.all_gather(norm1_gain, "chan", axis=0, tiled=True)
    bias1 = lax.all_gather(norm1_bias, "chan", axis=0, tiled=True)
    activated = jax.nn.silu(apply_norm(segment, mean1, var1, group_size) * gain1 + bias1).astype(
        jnp.bfloat16
    )
    padded = edge_pad(edge_pad(activated, 1, 1, 1), 2, 1, 1)

    block_rows = conv_weight.shape[0]
    start = row_place * block_rows
    first_tap = start // C
    offset = start % C
    span = max(
        (place * block_rows + block_rows - 1) // C - (place * block_rows) // C + 1
        for place in range(row_count)
    )
    out_channels = conv_weight.shape[1]
    placed = lax.dynamic_update_slice(
        jnp.zeros((span * C, out_channels), conv_weight.dtype), conv_weight, (offset, 0)
    )
    windows = []
    for step in range(span):
        tap = jnp.minimum(first_tap + step, (block_rows * row_count) // C - 1)
        windows.append(
            lax.dynamic_slice(
                padded,
                (tap // 9, (tap // 3) % 3, tap % 3, 0),
                (frames, all_rows, columns, C),
            ).reshape(-1, C)
        )
    patches = jnp.concatenate(windows, axis=1)
    partial = jnp.dot(patches, placed, preferred_element_type=jnp.float32)
    convolved = lax.psum(partial, "rows").reshape(frames, all_rows, columns, out_channels)

    own = lax.dynamic_slice(
        clip,
        (time_place * frames, 0, 0, chan_place * out_channels),
        (frames, all_rows, columns, out_channels),
    )
    middle = (own.astype(jnp.float32) + convolved + conv_bias).astype(jnp.bfloat16)

    mean2, var2 = group_stats(middle, group_size, (1, 2, 4))
    normed = (apply_norm(middle, mean2, var2, group_size) * norm2_gain + norm2_bias).astype(
        jnp.bfloat16
    )
    features = lax.all_gather(normed, "chan", axis=3, tiled=True)

    tokens = all_rows * columns
    local_tokens = rows_here * columns
    feature_rows = features.reshape(frames, tokens, C)
    own_rows = lax.dynamic_slice(
        features, (0, row_place * rows_here, 0, 0), (frames, rows_here, columns, C)
    ).reshape(-1, C)
    queries = (
        (jnp.dot(own_rows, w_query, preferred_element_type=jnp.float32) + b_query)
        .astype(jnp.bfloat16)
        .reshape(frames, local_tokens, C)
    )
    flat = feature_rows.reshape(-1, C)
    keys = (
        jnp.dot(flat, w_key, preferred_element_type=jnp.float32)
        .astype(jnp.bfloat16)
        .reshape(frames, tokens, C)
    )
    values = (
        (jnp.dot(flat, w_value, preferred_element_type=jnp.float32) + b_value)
        .astype(jnp.bfloat16)
        .reshape(frames, tokens, C)
    )
    scores = jnp.einsum("fqc,fkc->fqk", queries, keys, preferred_element_type=jnp.float32) * (
        C ** (-0.5)
    )
    row_peak = jnp.max(scores, axis=2, keepdims=True)
    weights = jnp.exp(scores - row_peak)
    weight_sum = jnp.sum(weights, axis=2, keepdims=True)
    attended = (
        jnp.einsum(
            "fqk,fkc->fqc",
            weights.astype(jnp.bfloat16),
            values,
            preferred_element_type=jnp.float32,
        )
        / weight_sum
    ).astype(jnp.bfloat16)
    out_block = lax.dynamic_slice(w_out, (0, chan_place * out_channels), (C, out_channels))
    out_bias = lax.dynamic_slice(b_out, (chan_place * out_channels,), (out_channels,))
    branch = (
        (jnp.dot(attended.reshape(-1, C), out_block, preferred_element_type=jnp.float32) + out_bias)
        .astype(jnp.bfloat16)
        .reshape(frames, rows_here, columns, out_channels)
    )
    own_middle = lax.dynamic_slice(
        middle, (0, row_place * rows_here, 0, 0), (frames, rows_here, columns, out_channels)
    )
    return (own_middle.astype(jnp.float32) + branch.astype(jnp.float32)).astype(jnp.bfloat16)


def solution(mesh):
    in_specs = (
        P(("clips", "tm"), "rows", None, "chan"),
        P("chan"),
        P("chan"),
        P("rows", "chan"),
        P("chan"),
        P("chan"),
        P("chan"),
        P(),
        P(),
        P(),
        P(),
        P(),
        P(),
        P(),
    )
    out_specs = P(("clips", "tm"), "rows", None, "chan")
    return jax.shard_map(local, mesh=mesh, in_specs=in_specs, out_specs=out_specs, check_vma=False)
```

time: 205 us -> 117 us (0.57)
  blocking collectives: 83.6 us -> 6.3 us
  local copies, waits for them, and re-layouts: 21.1 us -> 10.9 us
  waiting for transfers between devices: 65.9 us -> 73.3 us
  starting transfers between devices: 7.29 us -> 0.04 us
    psum x4 -> x0, blocking collectives: 59.8 us -> none  [the longest x1 23.4 us: clip_normalize(): lax.psum(jnp.sum(grouped, axis=(0, 1, 2, 4)), ('rows', 'tm')) / cell_count]
    psum x0 -> x1, waiting for transfers between devices: none -> 37.3 us  [local(): lax.psum(partial, 'rows').reshape(frames, all_rows, columns, out_channels)]
    ppermute x3 -> x0, waiting for transfers between devices: 23.1 us -> none  [the longest x1 10.4 us: with_halo(): lax.ppermute(tail, axis, [(i, (i + 1) % count) for i in range(ends)])]
    unnamed x52 -> x31, local copies, waits for them, and re-layouts: 18.7 us -> 0.6 us
    all_gather x2 -> x3, blocking collectives: 16.2 us -> 6.3 us  [the longest x1 2.18 us: local(): features = lax.all_gather(normed, 'chan', axis=3, tiled=True)]
    all_to_all x2 -> x0, blocking collectives: 7.58 us -> none  [the longest x1 3.79 us: local(): lax.all_to_all(normed, 'chan', split_axis=0, concat_axis=3, tiled=True)]
    ppermute x3 -> x0, starting transfers between devices: 7.29 us -> none  [the longest x1 3.85 us: passed_along(): lax.ppermute(value, axis, [(source, source + steps) for source in range(l...]
    all_gather x1, waiting for transfers between devices: 42.1 us -> 35.3 us  [local(): lax.all_gather(latent, ('tm', 'rows', 'chan'), axis=0, tiled=False)]
  transfers between devices with their start and end apart: 4 -> 2, of which waited for: 4 -> 2; matrix products, arithmetic and copies ran while one was open for 11% -> 3% of each run, Pallas kernels for 0% -> 0%
where the time goes in v1:
time: 117 us
  waiting for transfers between devices  73.3 us (63%)
  between operations  14.4 us (12%)
  local copies, waits for them, and re-layouts  10.9 us (9%)
  blocking collectives  6.3 us (5%)
  other arithmetic  5.99 us (5%)
  matrix products  5.61 us (5%)
    psum x1, waiting for transfers between devices, local(): lax.psum(partial, 'rows').reshape(frames, all_rows, columns, out_channels)  37.3 us
    all_gather x1, waiting for transfers between devices, local(): lax.all_gather(latent, ('tm', 'rows', 'chan'), axis=0, tiled=False)  35.3 us
    dot_general x1, matrix products, local(): partial = jnp.dot(patches, placed, preferred_element_type=jnp.float32)  3.68 us
    reduce_sum x4, other arithmetic, group_stats(): group_mean = jnp.mean(grouped, axis=axes, keepdims=True)  2.84 us
    dynamic_slice x2, local copies, waits for them, and re-layouts, local(): lax.dynamic_slice(padded, (tap // 9, tap // 3 % 3, tap % 3, 0), (frames,...  2.52 us
  transfers between devices with their start and end apart: 2, of which 2 were waited for; matrix products, arithmetic and copies ran while one was open for 3% of the time, Pallas kernels for 0%

profile of v1, /device:TPU:0, one launch (start us, length us, event | category | flops | bytes accessed | tf_op | source)
XLA Modules:
  0.0 116.6 jit_solution(14555595631547143152)
XLA Ops:
  6.5 0.7 all-gather.5.cloned.1.call-update
  7.3 0.0 all-reduce.2.cloned.1.call-start
  8.0 2.1 %all-gather.2 = f32[2,1,256]{2,1,0:T(1,128)S(1)} all-gather(f32[1,1,256]{2,1,0:T(1,128)} %bitcast.64), channel_id=1, replica_groups=mesh['clips'=2,'rows'=4,'tm'=2,'chan'=2] {'chan'}, dimensions={0}, use_global_device_ids=true | all-gather | bytes 3072 | tf_op jit(solution)/shard_map/all_gather | solution.py:77
  10.1 2.0 %all-gather.1 = f32[2,1,256]{2,1,0:T(1,128)S(1)} all-gather(f32[1,1,256]{2,1,0:T(1,128)} %bitcast.65), channel_id=1, replica_groups=mesh['clips'=2,'rows'=4,'tm'=2,'chan'=2] {'chan'}, dimensions={0}, use_global_device_ids=true | all-gather | bytes 3072 | tf_op jit(solution)/shard_map/all_gather | solution.py:76
  12.2 1.5 %broadcast_in_dim.14 = bf16[4096,256]{1,0:T(8,128)(2,1)} broadcast(bf16[]{:T(256)} %constant.179.clone.1), dimensions={} | broadcast | bytes 2097154 | tf_op jit(solution)/shard_map/broadcast_in_dim | solution.py:93
  13.7 1.3 %constant_dynamic-update-slice_fusion.8 = bf16[4096,256]{1,0:T(8,128)(2,1)} fusion(bf16[4096,256]{1,0:T(8,128)(2,1)} %broadcast_in_dim.14, bf16[3456,256]{1,0:T(8,128)(2,1)S(1)} %copy-done.2, s32[]{:T(128)S(6)} %select_n.295), kind=kLoop, calls=%fused_computation.57 | loop fusion | bytes 3538948 | tf_op jit(solution)/shard_map/dynamic_update_slice | solution.py:92
  15.0 35.3 %all-gather.5.cloned.1.call-done = bf16[32,1,64,256]{3,2,1,0:T(8,128)(2,1)} async-done(((bf16[2,1,64,256]{3,2,1,0:T(8,128)(2,1)}), bf16[32,1,64,256]{3,2,1,0:T(8,128)(2,1)}) %all-gather.5.cloned.1.call-update) | async-done | bytes 1048592 | tf_op jit(solution)/shard_map/all_gather | solution.py:63
  50.3 1.5 %convert_reduce_fusion = f32[2,256]{1,0:T(2,128)S(1)} fusion(bf16[2,2,4,1,64,2,256]{6,4,1,5,2,0,3:T(8,128)(2,1)} %bitcast.43), kind=kLoop, calls=%fused_computation.10 | loop fusion | flops 1048064 | bytes 1050624 | tf_op jit(solution)/shard_map/reduce_sum | solution.py:17
  51.8 2.3 %copy.21 = bf16[2,2,4,1,64,2,256]{6,5,4,2,1,0,3:T(2,128)(2,1)S(1)} copy(bf16[2,2,4,1,64,2,256]{6,4,1,5,2,0,3:T(8,128)(2,1)} %bitcast.44) | data formatting | bytes 2097152 | tf_op jit(solution)/shard_map/transpose | solution.py:67
  54.1 0.1 reduce_sum.55
  54.1 0.1 reduce_sum.59
  54.3 0.1 div.83
  54.4 0.1 sub.112
  54.4 0.1 sub.113
  54.5 0.3 fusion.7
  54.8 0.1 reduce_sum.61
  54.9 0.1 reduce_sum.62
  55.0 0.1 mul.75
  55.1 0.1 mul.76
  55.2 0.1 sub.108
  55.3 0.1 sub.109
  55.3 0.7 reshape.146
  56.1 0.6 gather_fusion
  56.7 0.9 multiply_convert_fusion
  57.6 0.7 fusion.11
  58.3 0.4 constant_dynamic-slice_fusion.7
  58.7 0.1 constant_dynamic-update-slice_fusion.7
  58.8 0.1 constant_dynamic-update-slice_fusion.6
  58.9 2.1 %constant_dynamic-slice_fusion.1 = (bf16[2,4,64,512]{3,2,1,0:T(8,128)(2,1)S(1)}, bf16[2,4,64,512]{3,2,1,0:T(8,128)(2,1)S(1)}, bf16[2,4,64,512]{3,2,1,0:T(8,128)(...) fusion(bf16[4,6,66,512]{3,2,1,0:T(8,128)(2,1)S(1)} %fusion.11, ...), kind=kLoop, calls=%fused_computation.58 | loop fusion | bytes 6291528 | tf_op jit(solution)/shard_map/dynamic_slice | solution.py:99
  61.0 0.1 constant_dynamic-update-slice_fusion.5
  61.0 0.1 constant_dynamic-update-slice_fusion.4
  61.1 0.1 constant_dynamic-update-slice_fusion.3
  61.2 0.1 constant_dynamic-update-slice_fusion.2
  61.3 0.1 constant_dynamic-update-slice_fusion.1
  61.3 0.1 constant_dynamic-update-slice_fusion
  61.4 0.0 copy-start.9
  61.4 0.0 copy-start.8
  61.5 0.0 copy-start.7
  61.5 3.7 %fusion.34 = f32[512,256]{1,0:T(8,128)} fusion(bf16[512,4096]{1,0:T(8,128)(2,1)S(1)} %constant_dynamic-update-slice_fusion, bf16[4096,256]{1,0:T(8,128)(2,1)} %constant_dynamic-update-slice_fusion.8), kind=kOutput, calls=%fused_computation.76 | convolution fusion | flops 1073741824 | bytes 6815744 | tf_op jit(solution)/shard_map/dot_general | solution.py:106
  65.1 0.0 all-reduce.2.cloned.1.call-update
  65.2 0.1 dynamic_slice.51
  65.3 37.3 %all-reduce.2.cloned.1.call-done = f32[2,4,64,256]{3,2,1,0:T(8,128)} async-done(((f32[2,4,64,256]{3,2,1,0:T(8,128)}), f32[2,4,64,256]{3,2,1,0:T(8,128)}) %all-reduce.2.cloned.1.call-update) | async-done | bytes 524304 | tf_op jit(solution)/shard_map/psum | solution.py:107
  102.5 1.1 convert_reduce_fusion.1
  103.7 0.1 reduce_sum.80
  103.8 0.1 reduce_sum.81
  103.9 0.1 sub.133
  103.9 0.1 sub.134
  104.0 0.1 fusion.20
  104.1 0.1 reduce_sum.83
  104.2 0.1 reduce_sum.84
  104.3 0.1 mul.84
  104.4 0.1 mul.85
  104.5 0.1 fusion.23
  104.6 2.2 %all_gather.19 = bf16[2,4,64,512]{3,2,1,0:T(8,128)(2,1)S(1)} all-gather(bf16[2,4,64,256]{3,2,1,0:T(8,128)(2,1)S(1)} %fusion.23), channel_id=1, replica_groups=mesh['clips'=2,'rows'=4,'tm'=2,'chan'=2] {'chan'}, dimensions={3}, use_global_device_ids=true | all-gather | bytes 786432 | tf_op jit(solution)/shard_map/all_gather | solution.py:120
  106.8 0.4 convolution_convert_fusion
  107.3 0.0 copy-start.4
  107.3 0.4 fusion.14
  107.7 0.1 copy-done.3
  107.8 0.2 fusion.15
  108.0 0.4 fusion.33
  108.4 0.2 fusion.26
  108.6 0.3 fusion.16
  108.9 0.2 fusion.17
  109.1 0.7 fusion.25
  (29 shorter events, 0.1 us)
Async XLA Ops:
  6.5 100.2 %copy-start = (bf16[512,512]{1,0:T(8,128)(2,1)S(1)}, bf16[512,512]{1,0:T(8,128)(2,1)}, u32[]{:S(2)}) copy-start(bf16[512,512]{1,0:T(8,128)(2,1)} %param.23) | copy-start | bytes 1572868
  6.5 7.1 %copy-start.2 = (bf16[3456,256]{1,0:T(8,128)(2,1)S(1)}, bf16[3456,256]{1,0:T(8,128)(2,1)}, u32[]{:S(2)}) copy-start(bf16[3456,256]{1,0:T(8,128)(2,1)} %param.17) | copy-start | bytes 5308420
  6.5 43.7 %all-gather.5.cloned.1.call-start = ((), (), s32[]{:S(2)}) async-start(), calls=%async_computation.1 | async-start | bytes 1114112 | tf_op jit(solution)/shard_map/all_gather | solution.py:63
  7.3 95.3 %all-reduce.2.cloned.1.call-start = ((), (), s32[]{:S(2)}) async-start(), calls=%async_computation | async-start | bytes 1048576 | tf_op jit(solution)/shard_map/psum | solution.py:107
  50.3 4.3 %copy-start.1 = (bf16[32,1,64,256]{3,2,1,0:T(8,128)(2,1)S(1)}, bf16[32,1,64,256]{3,2,1,0:T(8,128)(2,1)}, u32[]{:S(2)}) copy-start(bf16[32,1,64,256]{3,2,1,0:T(8,128)(2,1)} %all-gather.5.cloned.1.call-done) | copy-start | bytes 3145732
  61.4 3.8 %copy-start.9 = (f32[512]{0:T(512)S(1)}, f32[512]{0:T(512)}, u32[]{:S(2)}) copy-start(f32[512]{0:T(512)} %param.27) | copy-start | bytes 6148
  61.4 41.1 %copy-start.8 = (f32[256]{0:T(256)S(1)}, f32[256]{0:T(256)}, u32[]{:S(2)}) copy-start(f32[256]{0:T(256)} %param.18) | copy-start | bytes 3076
  61.4 43.0 %copy-start.6 = (f32[256]{0:T(256)S(1)}, f32[256]{0:T(256)}, u32[]{:S(2)}) copy-start(f32[256]{0:T(256)} %param.20) | copy-start | bytes 3076
  61.5 43.0 %copy-start.7 = (f32[256]{0:T(256)S(1)}, f32[256]{0:T(256)}, u32[]{:S(2)}) copy-start(f32[256]{0:T(256)} %param.19) | copy-start | bytes 3076
  65.3 42.0 %copy-start.10 = (bf16[512,512]{1,0:T(8,128)(2,1)S(1)}, bf16[512,512]{1,0:T(8,128)(2,1)}, u32[]{:S(2)}) copy-start(bf16[512,512]{1,0:T(8,128)(2,1)} %param.24) | copy-start | bytes 1572868
  65.3 42.0 %copy-start.11 = (f32[512]{0:T(512)S(1)}, f32[512]{0:T(512)}, u32[]{:S(2)}) copy-start(f32[512]{0:T(512)} %param.25) | copy-start | bytes 6148
  106.8 1.0 copy-start.3
  106.8 1.0 copy-start.5
  107.3 1.6 %copy-start.4 = (bf16[512,512]{1,0:T(8,128)(2,1)S(1)}, bf16[512,512]{1,0:T(8,128)(2,1)}, u32[]{:S(2)}) copy-start(bf16[512,512]{1,0:T(8,128)(2,1)} %param.26) | copy-start | bytes 1572868
Sparse Core Ops, SparseCore 0:
  9.6 40.6 all-gather.4
  65.3 37.2 all-reduce.1

commit v2 on v1

--- a/solution.py
+++ b/solution.py
@@ -60,11 +60,12 @@
     chan_place = lax.axis_index("chan")
     all_rows = rows_here * row_count
 
-    gathered = lax.all_gather(latent, ("tm", "rows", "chan"), axis=0, tiled=False)
-    gathered = gathered.reshape(
-        (time_count, row_count, chan_count, frames, rows_here, columns, channels)
+    group = ("rows", "tm", "chan")
+    copies = jnp.broadcast_to(latent[None], (row_count * time_count * chan_count,) + latent.shape)
+    gathered = lax.all_to_all(copies, group, 0, 0, tiled=True).reshape(
+        (row_count, time_count, chan_count, frames, rows_here, columns, channels)
     )
-    clip = jnp.transpose(gathered, (0, 3, 1, 4, 5, 2, 6)).reshape(
+    clip = jnp.transpose(gathered, (1, 3, 0, 4, 5, 2, 6)).reshape(
         (time_count * frames, all_rows, columns, chan_count * channels)
     )
 
@@ -73,8 +74,10 @@
         time_place * frames - 2 + jnp.arange(frames + 2), 0, time_count * frames - 1
     )
     segment = jnp.take(clip, frame_index, axis=0)
-    gain1 = lax.all_gather(norm1_gain, "chan", axis=0, tiled=True)
-    bias1 = lax.all_gather(norm1_bias, "chan", axis=0, tiled=True)
+    scales = lax.all_gather(
+        jnp.stack([norm1_gain, norm1_bias, norm2_gain, norm2_bias]), "chan", axis=1, tiled=True
+    )
+    gain1, bias1, gain2, bias2 = scales[0], scales[1], scales[2], scales[3]
     activated = jax.nn.silu(apply_norm(segment, mean1, var1, group_size) * gain1 + bias1).astype(
         jnp.bfloat16
     )
@@ -104,20 +107,17 @@
         )
     patches = jnp.concatenate(windows, axis=1)
     partial = jnp.dot(patches, placed, preferred_element_type=jnp.float32)
-    convolved = lax.psum(partial, "rows").reshape(frames, all_rows, columns, out_channels)
+    pieces = partial.reshape(frames, row_count, rows_here, columns, out_channels)
+    convolved = jnp.sum(lax.all_to_all(pieces, "rows", 1, 1, tiled=True), axis=1)
+    own_middle = (latent.astype(jnp.float32) + convolved + conv_bias).astype(jnp.bfloat16)
 
-    own = lax.dynamic_slice(
-        clip,
-        (time_place * frames, 0, 0, chan_place * out_channels),
-        (frames, all_rows, columns, out_channels),
+    spread = jnp.broadcast_to(own_middle[None], (row_count * chan_count,) + own_middle.shape)
+    middle = lax.all_to_all(spread, ("rows", "chan"), 0, 0, tiled=True).reshape(
+        (row_count, chan_count, frames, rows_here, columns, out_channels)
     )
-    middle = (own.astype(jnp.float32) + convolved + conv_bias).astype(jnp.bfloat16)
-
+    middle = jnp.transpose(middle, (2, 0, 3, 4, 1, 5)).reshape(frames, all_rows, columns, C)
     mean2, var2 = group_stats(middle, group_size, (1, 2, 4))
-    normed = (apply_norm(middle, mean2, var2, group_size) * norm2_gain + norm2_bias).astype(
-        jnp.bfloat16
-    )
-    features = lax.all_gather(normed, "chan", axis=3, tiled=True)
+    features = (apply_norm(middle, mean2, var2, group_size) * gain2 + bias2).astype(jnp.bfloat16)
 
     tokens = all_rows * columns
     local_tokens = rows_here * columns
@@ -163,9 +163,6 @@
         .astype(jnp.bfloat16)
         .reshape(frames, rows_here, columns, out_channels)
     )
-    own_middle = lax.dynamic_slice(
-        middle, (0, row_place * rows_here, 0, 0), (frames, rows_here, columns, out_channels)
-    )
     return (own_middle.astype(jnp.float32) + branch.astype(jnp.float32)).astype(jnp.bfloat16)
 
 

time: 117 us -> 99.2 us (0.85)
  waiting for transfers between devices: 73.3 us -> 32.5 us
  blocking collectives: 6.3 us -> 22.2 us
  between operations: 14.4 us -> 1.14 us
  starting transfers between devices: 0.04 us -> 11.2 us
  local copies, waits for them, and re-layouts: 10.9 us -> 19.6 us
  other arithmetic: 5.99 us -> 7.22 us
    psum x1 -> x0, waiting for transfers between devices: 37.3 us -> none  [local(): lax.psum(partial, 'rows').reshape(frames, all_rows, columns, out_channels)]
    all_gather x1 -> x0, waiting for transfers between devices: 35.3 us -> none  [local(): lax.all_gather(latent, ('tm', 'rows', 'chan'), axis=0, tiled=False)]
    all_to_all x0 -> x2, waiting for transfers between devices: none -> 32.5 us  [the longest x1 17.5 us: local(): lax.all_to_all(copies, group, 0, 0, tiled=True)]
    all_to_all x0 -> x1, blocking collectives: none -> 20.4 us  [local(): lax.all_to_all(pieces, 'rows', 1, 1, tiled=True)]
    all_to_all x0 -> x2, starting transfers between devices: none -> 11.2 us  [the longest x1 7.5 us: local(): lax.all_to_all(copies, group, 0, 0, tiled=True)]
    all_gather x3 -> x1, blocking collectives: 6.3 us -> 1.8 us  [local(): lax.all_gather(jnp.stack([norm1_gain, norm1_bias, norm2_gain, norm2_bias]...]
    convert_element_type x0 -> x2, local copies, waits for them, and re-layouts: none -> 3.87 us  [apply_norm(): values.astype(jnp.float32)]
    convert_element_type x1 -> x4, other arithmetic: 0.1 us -> 3.58 us  [the longest x2 2.46 us: local(): (apply_norm(middle, mean2, var2, group_size) * gain2 + bias2).astype(jnp....]
where the time goes in v2:
time: 99.2 us; the launch traced here: 98.7 us
  waiting for transfers between devices  32.5 us (33%)
  blocking collectives  22.2 us (22%)
  local copies, waits for them, and re-layouts  19.6 us (20%)
  starting transfers between devices  11.2 us (11%)
  other arithmetic  7.22 us (7%)
  matrix products  4.79 us (5%)
  between operations  1.14 us (1%)
    all_to_all x1, blocking collectives, local(): lax.all_to_all(pieces, 'rows', 1, 1, tiled=True)  20.4 us
    all_to_all x1, waiting for transfers between devices, local(): lax.all_to_all(copies, group, 0, 0, tiled=True)  17.5 us
    all_to_all x1, waiting for transfers between devices, local(): lax.all_to_all(spread, ('rows', 'chan'), 0, 0, tiled=True)  15 us
    all_to_all x1, starting transfers between devices, local(): lax.all_to_all(copies, group, 0, 0, tiled=True)  7.5 us
    convert_element_type x2, local copies, waits for them, and re-layouts, apply_norm(): values.astype(jnp.float32)  3.87 us
    all_to_all x1, starting transfers between devices, local(): lax.all_to_all(spread, ('rows', 'chan'), 0, 0, tiled=True)  3.67 us
    dot_general x1, matrix products, local(): partial = jnp.dot(patches, placed, preferred_element_type=jnp.float32)  2.86 us
    dynamic_slice x2, local copies, waits for them, and re-layouts, local(): lax.dynamic_slice(padded, (tap // 9, tap // 3 % 3, tap % 3, 0), (frames,...  2.52 us
  transfers between devices with their start and end apart: 2, of which 2 were waited for; matrix products, arithmetic and copies ran while one was open for 3% of the time, Pallas kernels for 0%

profile of v2, /device:TPU:0, one launch (start us, length us, event | category | flops | bytes accessed | tf_op | source)
XLA Modules:
  0.0 98.7 jit_solution(9353153959813184006)
XLA Ops:
  0.0 2.0 %broadcast_in_dim.22 = bf16[16,2,1,64,256]{4,3,1,2,0:T(8,128)(2,1)} broadcast(bf16[2,64,256]{2,1,0:T(8,128)(2,1)} %bitcast.103), dimensions={1,3,4} | broadcast | bytes 1114112 | tf_op jit(solution)/shard_map/broadcast_in_dim | solution.py:64
  2.0 7.5 %all-to-all-start = ((bf16[16,2,1,64,256]{4,3,1,2,0:T(8,128)(2,1)}), bf16[16,2,1,64,256]{4,3,1,2,0:T(8,128)(2,1)S(1)}, u32[]{:S(2)}, u32[]{:S(2)}) async-start(bf16[16,2,1,64,256]{4,3,1,2,0:T(8,128)(2,1)} %broadcast_in_dim.22), calls=%async_computation | async-start | bytes 2097152 | tf_op jit(solution)/shard_map/all_to_all | solution.py:65
  10.3 1.8 %all_gather.3 = f32[4,512]{1,0:T(4,128)S(1)} all-gather(f32[4,256]{1,0:T(4,128)S(1)} %pad_maximum_fusion), channel_id=1, replica_groups=mesh['clips'=2,'rows'=4,'tm'=2,'chan'=2] {'chan'}, dimensions={1}, use_global_device_ids=true | all-gather | bytes 12288 | tf_op jit(solution)/shard_map/all_gather | solution.py:77
  12.1 1.5 %broadcast_in_dim.24 = bf16[4096,256]{1,0:T(8,128)(2,1)} broadcast(bf16[]{:T(256)} %constant.177.clone.1), dimensions={} | broadcast | bytes 2097154 | tf_op jit(solution)/shard_map/broadcast_in_dim | solution.py:96
  13.6 1.3 %constant_dynamic-update-slice_fusion.8 = bf16[4096,256]{1,0:T(8,128)(2,1)} fusion(bf16[4096,256]{1,0:T(8,128)(2,1)} %broadcast_in_dim.24, bf16[3456,256]{1,0:T(8,128)(2,1)S(1)} %copy-done.1, s32[]{:T(128)S(6)} %select_n.288), kind=kLoop, calls=%fused_computation.66 | loop fusion | bytes 3538948 | tf_op jit(solution)/shard_map/dynamic_update_slice | solution.py:95
  15.0 17.5 %all-to-all-done = bf16[16,2,1,64,256]{4,3,1,2,0:T(8,128)(2,1)S(1)} async-done(((bf16[16,2,1,64,256]{4,3,1,2,0:T(8,128)(2,1)}), bf16[16,2,1,64,256]{4,3,1,2,0:T(8,128)(2,1)S(1)}, u32[]{:S(2)}, u32[]{:S(2)}) %all-to-all-start) | async-done | bytes 1048608 | tf_op jit(solution)/shard_map/all_to_all | solution.py:65
  32.5 0.2 convert_reduce_fusion
  32.7 2.1 %copy.22 = bf16[2,2,4,1,64,2,256]{6,5,4,2,1,0,3:T(2,128)(2,1)} copy(bf16[2,2,4,1,64,2,256]{6,4,1,5,0,2,3:T(8,128)(2,1)S(1)} %bitcast.83) | data formatting | bytes 2097152 | tf_op jit(solution)/shard_map/transpose | solution.py:68
  34.7 0.1 reduce_sum.67
  34.8 0.1 reduce_sum.68
  34.9 0.1 div.83
  35.0 0.1 sub.123
  35.1 0.1 sub.124
  35.2 0.3 fusion.7
  35.5 0.1 reduce_sum.70
  35.6 0.1 reduce_sum.74
  35.7 0.1 mul.86
  35.8 0.1 mul.87
  35.8 0.1 sub.119
  35.9 0.1 sub.120
  36.0 1.8 %reshape.172 = bf16[4,4,64,512]{3,2,1,0:T(8,128)(2,1)S(1)} reshape(bf16[2,2,4,1,64,2,256]{6,5,4,2,1,0,3:T(2,128)(2,1)} %copy.22) | data formatting | bytes 2097152 | tf_op jit(solution)/shard_map/reshape | solution.py:68
  37.8 0.6 gather_fusion
  38.4 0.9 multiply_convert_fusion
  39.3 0.7 fusion.11
  40.0 0.4 constant_dynamic-slice_fusion.6
  40.5 0.1 constant_dynamic-update-slice_fusion.6
  40.6 2.1 %constant_dynamic-slice_fusion = (bf16[2,4,64,512]{3,2,1,0:T(8,128)(2,1)S(1)}, bf16[2,4,64,512]{3,2,1,0:T(8,128)(2,1)S(1)}, bf16[2,4,64,512]{3,2,1,0:T(8,128)(2,...) fusion(bf16[4,6,66,512]{3,2,1,0:T(8,128)(2,1)S(1)} %fusion.11, ...), kind=kLoop, calls=%fused_computation.67 | loop fusion | bytes 6291528 | tf_op jit(solution)/shard_map/dynamic_slice | solution.py:102
  42.7 0.1 constant_dynamic-update-slice_fusion.5
  42.7 0.1 constant_dynamic-update-slice_fusion.4
  42.8 0.1 constant_dynamic-update-slice_fusion.3
  42.9 0.1 constant_dynamic-update-slice_fusion.2
  43.0 0.1 constant_dynamic-update-slice_fusion.1
  43.0 0.1 constant_dynamic-update-slice_fusion
  43.1 2.9 %fusion.39 = f32[512,256]{1,0:T(8,128)S(1)} fusion(bf16[512,4096]{1,0:T(8,128)(2,1)S(1)} %constant_dynamic-update-slice_fusion, bf16[4096,256]{1,0:T(8,128)(2,1)} %constant_dynamic-update-slice_fusion.8), kind=kOutput, calls=%fused_computation.84 | convolution fusion | flops 1073741824 | bytes 6815744 | tf_op jit(solution)/shard_map/dot_general | solution.py:109
  46.1 20.4 %all_to_all.15 = f32[2,4,1,64,256]{4,3,0,2,1:T(8,128)S(1)} all-to-all(f32[2,4,1,64,256]{4,3,0,2,1:T(8,128)S(1)} %copy.23), channel_id=1, replica_groups=mesh['clips'=2,'rows'=4,'tm'=2,'chan'=2] {'rows'}, dimensions={1} | all-to-all | bytes 1048576 | tf_op jit(solution)/shard_map/all_to_all | solution.py:111
  66.6 0.8 broadcast_in_dim.45
  67.4 3.7 %all-to-all-start.2 = ((bf16[8,2,1,64,256]{4,3,1,2,0:T(8,128)(2,1)}), bf16[8,2,1,64,256]{4,3,1,2,0:T(8,128)(2,1)S(1)}, u32[]{:S(2)}, u32[]{:S(2)}) async-start(bf16[8,2,1,64,256]{4,3,1,2,0:T(8,128)(2,1)} %broadcast_in_dim.45), calls=%async_computation.2 | async-start | bytes 1048576 | tf_op jit(solution)/shard_map/all_to_all | solution.py:115
  71.1 0.1 dynamic_slice.43
  71.2 15.0 %all-to-all-done.2 = bf16[8,2,1,64,256]{4,3,1,2,0:T(8,128)(2,1)S(1)} async-done(((bf16[8,2,1,64,256]{4,3,1,2,0:T(8,128)(2,1)}), bf16[8,2,1,64,256]{4,3,1,2,0:T(8,128)(2,1)S(1)}, u32[]{:S(2)}, u32[]{:S(2)}) %all-to-all-start.2) | async-done | bytes 524320 | tf_op jit(solution)/shard_map/all_to_all | solution.py:115
  86.2 1.1 %convert_bitcast_fusion = f32[2,4,1,64,2,256]{5,3,0,4,1,2:T(8,128)} fusion(bf16[4,2,2,1,64,256]{5,4,2,1,0,3:T(8,128)(2,1)S(1)} %bitcast.86), kind=kLoop, calls=%fused_computation.35 | loop fusion | flops 262144 | bytes 1572864 | tf_op jit(solution)/shard_map/convert_element_type | solution.py:24
  87.3 0.1 fusion.21
  87.4 0.1 reduce_sum.93
  87.5 0.1 reduce_sum.94
  87.6 0.1 sub.144
  87.6 0.1 sub.148
  87.7 0.1 sub.145
  87.8 2.0 %copy.25 = f32[2,4,1,64,2,256]{5,4,3,1,0,2:T(2,128)S(1)} copy(f32[2,4,1,64,2,256]{5,3,0,4,1,2:T(8,128)} %convert_bitcast_fusion) | data formatting | bytes 2097152 | tf_op jit(solution)/shard_map/convert_element_type | solution.py:24
  89.9 1.8 %reshape.187 = f32[2,4,64,512]{3,2,1,0:T(8,128)} reshape(f32[2,4,1,64,2,256]{5,4,3,1,0,2:T(2,128)S(1)} %copy.25) | data formatting | bytes 2097152 | tf_op jit(solution)/shard_map/convert_element_type | solution.py:24
  91.7 1.1 %copy.31 = f32[64,8,2,256]{3,1,2,0:T(8,128)} copy(f32[64,8,2,256]{3,2,1,0:T(2,128)S(1)} %bitcast.85) | data formatting | bytes 2097152
  92.8 0.2 multiply_reduce_fusion
  93.0 0.1 reduce_sum.96
  93.1 0.1 reduce_sum.97
  93.2 0.1 mul.96
  93.2 0.1 mul.97
  93.3 1.4 %fusion.20 = bf16[512,512]{1,0:T(8,128)(2,1)S(1)} fusion(f32[512,512]{1,0:T(8,128)} %bitcast.89, f32[512]{0:T(512)S(1)} %bitcast.108, f32[512]{0:T(512)S(1)} %bitcast.106, f32[2,512]{1,0:T(2,128)S(1)} %mul.97, f32[2,512]{1,0:T(2,128)S(1)} %sub.145), kind=kLoop, calls=%fused_computation.33 | loop fusion | flops 1310720 | bytes 1585152 | tf_op jit(solution)/shard_map/convert_element_type | solution.py:120
  94.8 0.4 convolution_convert_fusion
  95.2 0.4 fusion.14
  95.7 1.1 %fusion.25 = bf16[2,1,64,512]{3,2,1,0:T(8,128)(2,1)S(1)} fusion(f32[2,4,64,512]{3,2,1,0:T(8,128)} %reshape.187, s32[]{:T(128)S(6)} %select_n.289, f32[512]{0:T(512)S(1)} %bitcast.109, f32[512]{0:T(512)S(1)} %bitcast.107, f32[2,512]{1,0:T(2,128)S(1)} %mul.97, f32[2,512]{1,0:T(2,128)S(1)} %sub.145), kind=kLoop, calls=%fused_computation.42 | loop fusion | flops 327680 | bytes 405508 | tf_op jit(solution)/shard_map/convert_element_type | solution.py:120
  96.8 0.2 fusion.15
  97.0 0.4 fusion.38
  97.4 0.2 fusion.30
  97.6 0.3 fusion.16
  97.8 0.2 fusion.17
  98.0 0.6 fusion.27
  (45 shorter events, 0.3 us)
Async XLA Ops:
  0.0 94.7 %copy-start = (bf16[512,512]{1,0:T(8,128)(2,1)S(1)}, bf16[512,512]{1,0:T(8,128)(2,1)}, u32[]{:S(2)}) copy-start(bf16[512,512]{1,0:T(8,128)(2,1)} %param.23) | copy-start | bytes 1572868
  0.0 10.2 %copy-start.7 = (f32[256]{0:T(256)S(1)}, f32[256]{0:T(256)}, u32[]{:S(2)}) copy-start(f32[256]{0:T(256)} %param.20) | copy-start | bytes 3076
  0.0 10.2 %copy-start.8 = (f32[256]{0:T(256)S(1)}, f32[256]{0:T(256)}, u32[]{:S(2)}) copy-start(f32[256]{0:T(256)} %param.19) | copy-start | bytes 3076
  0.0 10.2 %copy-start.9 = (f32[256]{0:T(256)S(1)}, f32[256]{0:T(256)}, u32[]{:S(2)}) copy-start(f32[256]{0:T(256)} %param.16) | copy-start | bytes 3076
  0.0 10.2 %copy-start.10 = (f32[256]{0:T(256)S(1)}, f32[256]{0:T(256)}, u32[]{:S(2)}) copy-start(f32[256]{0:T(256)} %param.15) | copy-start | bytes 3076
  2.0 11.6 %copy-start.1 = (bf16[3456,256]{1,0:T(8,128)(2,1)S(1)}, bf16[3456,256]{1,0:T(8,128)(2,1)}, u32[]{:S(2)}) copy-start(bf16[3456,256]{1,0:T(8,128)(2,1)} %param.17) | copy-start | bytes 5308420
  2.0 30.4 %all-to-all-start = ((bf16[16,2,1,64,256]{4,3,1,2,0:T(8,128)(2,1)}), bf16[16,2,1,64,256]{4,3,1,2,0:T(8,128)(2,1)S(1)}, u32[]{:S(2)}, u32[]{:S(2)}) async-start(bf16[16,2,1,64,256]{4,3,1,2,0:T(8,128)(2,1)} %broadcast_in_dim.22), calls=%async_computation | async-start | bytes 2097152 | tf_op jit(solution)/shard_map/all_to_all | solution.py:65
  46.0 20.5 %copy-start.3 = (bf16[2,1,64,256]{3,2,1,0:T(8,128)(2,1)S(1)}, bf16[2,1,64,256]{3,2,1,0:T(8,128)(2,1)}, u32[]{:S(2)}) copy-start(bf16[2,1,64,256]{3,2,1,0:T(8,128)(2,1)} %param.14) | copy-start | bytes 196612
  46.0 20.5 %copy-start.6 = (f32[256]{0:T(256)S(1)}, f32[256]{0:T(256)}, u32[]{:S(2)}) copy-start(f32[256]{0:T(256)} %param.18) | copy-start | bytes 3076
  46.0 25.1 %copy-start.11 = (f32[512]{0:T(512)S(1)}, f32[512]{0:T(512)}, u32[]{:S(2)}) copy-start(f32[512]{0:T(512)} %param.27) | copy-start | bytes 6148
  67.4 18.8 %all-to-all-start.2 = ((bf16[8,2,1,64,256]{4,3,1,2,0:T(8,128)(2,1)}), bf16[8,2,1,64,256]{4,3,1,2,0:T(8,128)(2,1)S(1)}, u32[]{:S(2)}, u32[]{:S(2)}) async-start(bf16[8,2,1,64,256]{4,3,1,2,0:T(8,128)(2,1)} %broadcast_in_dim.45), calls=%async_computation.2 | async-start | bytes 1048576 | tf_op jit(solution)/shard_map/all_to_all | solution.py:115
  92.8 2.4 %copy-start.12 = (bf16[512,512]{1,0:T(8,128)(2,1)S(1)}, bf16[512,512]{1,0:T(8,128)(2,1)}, u32[]{:S(2)}) copy-start(bf16[512,512]{1,0:T(8,128)(2,1)} %param.24) | copy-start | bytes 1572868
  92.8 2.4 %copy-start.13 = (f32[512]{0:T(512)S(1)}, f32[512]{0:T(512)}, u32[]{:S(2)}) copy-start(f32[512]{0:T(512)} %param.25) | copy-start | bytes 6148
  94.7 2.0 %copy-start.2 = (bf16[512,512]{1,0:T(8,128)(2,1)S(1)}, bf16[512,512]{1,0:T(8,128)(2,1)}, u32[]{:S(2)}) copy-start(bf16[512,512]{1,0:T(8,128)(2,1)} %param.21) | copy-start | bytes 1572868
  94.8 2.0 %copy-start.5 = (f32[512]{0:T(512)S(1)}, f32[512]{0:T(512)}, u32[]{:S(2)}) copy-start(f32[512]{0:T(512)} %param.22) | copy-start | bytes 6148
  95.7 2.2 %copy-start.4 = (bf16[512,512]{1,0:T(8,128)(2,1)S(1)}, bf16[512,512]{1,0:T(8,128)(2,1)}, u32[]{:S(2)}) copy-start(bf16[512,512]{1,0:T(8,128)(2,1)} %param.26) | copy-start | bytes 1572868

commit v3 on v2

--- a/solution.py
+++ b/solution.py
@@ -60,12 +60,13 @@
     chan_place = lax.axis_index("chan")
     all_rows = rows_here * row_count
 
-    group = ("rows", "tm", "chan")
-    copies = jnp.broadcast_to(latent[None], (row_count * time_count * chan_count,) + latent.shape)
-    gathered = lax.all_to_all(copies, group, 0, 0, tiled=True).reshape(
-        (row_count, time_count, chan_count, frames, rows_here, columns, channels)
+    group = ("rows", "tm")
+    copies = jnp.broadcast_to(latent[None], (row_count * time_count,) + latent.shape)
+    gathered = lax.all_to_all(copies, group, 0, 0, tiled=True)
+    gathered = lax.all_gather(gathered, "chan", axis=4, tiled=True).reshape(
+        (row_count, time_count, frames, rows_here, columns, chan_count * channels)
     )
-    clip = jnp.transpose(gathered, (1, 3, 0, 4, 5, 2, 6)).reshape(
+    clip = jnp.transpose(gathered, (1, 2, 0, 3, 4, 5)).reshape(
         (time_count * frames, all_rows, columns, chan_count * channels)
     )
 
@@ -111,11 +112,9 @@
     convolved = jnp.sum(lax.all_to_all(pieces, "rows", 1, 1, tiled=True), axis=1)
     own_middle = (latent.astype(jnp.float32) + convolved + conv_bias).astype(jnp.bfloat16)
 
-    spread = jnp.broadcast_to(own_middle[None], (row_count * chan_count,) + own_middle.shape)
-    middle = lax.all_to_all(spread, ("rows", "chan"), 0, 0, tiled=True).reshape(
-        (row_count, chan_count, frames, rows_here, columns, out_channels)
-    )
-    middle = jnp.transpose(middle, (2, 0, 3, 4, 1, 5)).reshape(frames, all_rows, columns, C)
+    spread = jnp.tile(own_middle, (1, row_count, 1, 1))
+    middle = lax.all_to_all(spread, "rows", 1, 1, tiled=True)
+    middle = lax.all_gather(middle, "chan", axis=3, tiled=True)
     mean2, var2 = group_stats(middle, group_size, (1, 2, 4))
     features = (apply_norm(middle, mean2, var2, group_size) * gain2 + bias2).astype(jnp.bfloat16)
 

time: 99.2 us -> 97.3 us (0.981)
  between operations: 1.14 us -> 14.5 us
  local copies, waits for them, and re-layouts: 19.6 us -> 11 us
  waiting for transfers between devices: 32.5 us -> 25.6 us
  blocking collectives: 22.2 us -> 23.6 us
    all_to_all x2, waiting for transfers between devices: 32.5 us -> 20.2 us  [the longest x1 11.9 us: local(): gathered = lax.all_to_all(copies, group, 0, 0, tiled=True)]
    all_gather x0 -> x1, waiting for transfers between devices: none -> 5.35 us  [local(): lax.all_gather(gathered, 'chan', axis=4, tiled=True)]
    convert_element_type x2 -> x0, local copies, waits for them, and re-layouts: 3.87 us -> none  [apply_norm(): values.astype(jnp.float32)]
    convert_element_type x2 -> x1, other arithmetic: 2.46 us -> 0.19 us  [local(): (apply_norm(middle, mean2, var2, group_size) * gain2 + bias2).astype(jnp....]
    all_gather x0 -> x1, blocking collectives: none -> 2.18 us  [local(): middle = lax.all_gather(middle, 'chan', axis=3, tiled=True)]
    transpose x1 -> x0, local copies, waits for them, and re-layouts: 2.07 us -> none  [local(): jnp.transpose(gathered, (1, 3, 0, 4, 5, 2, 6))]
    reshape x1 -> x0, local copies, waits for them, and re-layouts: 1.76 us -> none  [local(): jnp.transpose(gathered, (1, 3, 0, 4, 5, 2, 6))]
    reduce_sum x4, other arithmetic: 0.48 us -> 1.83 us  [group_stats(): group_mean = jnp.mean(grouped, axis=axes, keepdims=True)]
  transfers between devices with their start and end apart: 2 -> 3, of which waited for: 2 -> 3; matrix products, arithmetic and copies ran while one was open for 3% -> 3% of each run, Pallas kernels for 0% -> 0%
where the time goes in v3:
time: 97.3 us; the launch traced here: 96.8 us
  waiting for transfers between devices  25.6 us (26%)
  blocking collectives  23.6 us (24%)
  between operations  14.5 us (15%)
  local copies, waits for them, and re-layouts  11 us (11%)
  starting transfers between devices  10.8 us (11%)
  other arithmetic  6.49 us (7%)
  matrix products  4.79 us (5%)
    all_to_all x1, blocking collectives, local(): lax.all_to_all(pieces, 'rows', 1, 1, tiled=True)  19.6 us
    all_to_all x1, waiting for transfers between devices, local(): gathered = lax.all_to_all(copies, group, 0, 0, tiled=True)  11.9 us
    all_to_all x1, waiting for transfers between devices, local(): middle = lax.all_to_all(spread, 'rows', 1, 1, tiled=True)  8.34 us
    all_to_all x1, starting transfers between devices, local(): gathered = lax.all_to_all(copies, group, 0, 0, tiled=True)  7.38 us
    all_gather x1, waiting for transfers between devices, local(): lax.all_gather(gathered, 'chan', axis=4, tiled=True)  5.35 us
    all_to_all x1, starting transfers between devices, local(): middle = lax.all_to_all(spread, 'rows', 1, 1, tiled=True)  3.4 us
    dot_general x1, matrix products, local(): partial = jnp.dot(patches, placed, preferred_element_type=jnp.float32)  2.86 us
    dynamic_slice x2, local copies, waits for them, and re-layouts, local(): lax.dynamic_slice(padded, (tap // 9, tap // 3 % 3, tap % 3, 0), (frames,...  2.52 us
  transfers between devices with their start and end apart: 3, of which 3 were waited for; matrix products, arithmetic and copies ran while one was open for 3% of the time, Pallas kernels for 0%

profile of v3, /device:TPU:0, one launch (start us, length us, event | category | flops | bytes accessed | tf_op | source)
XLA Modules:
  0.0 96.8 jit_solution(2986036430098855552)
XLA Ops:
  6.5 1.7 %broadcast_in_dim.18 = bf16[8,2,1,64,256]{4,3,1,2,0:T(8,128)(2,1)} broadcast(bf16[2,64,256]{2,1,0:T(8,128)(2,1)} %bitcast.73), dimensions={1,3,4} | broadcast | bytes 589824 | tf_op jit(solution)/shard_map/broadcast_in_dim | solution.py:64
  8.3 7.4 %all-to-all-start = ((bf16[8,2,1,64,256]{4,3,1,2,0:T(8,128)(2,1)}), bf16[8,2,1,64,256]{4,3,1,2,0:T(8,128)(2,1)S(1)}, u32[]{:S(2)}, u32[]{:S(2)}) async-start(bf16[8,2,1,64,256]{4,3,1,2,0:T(8,128)(2,1)} %broadcast_in_dim.18), calls=%async_computation | async-start | bytes 1048576 | tf_op jit(solution)/shard_map/all_to_all | solution.py:65
  15.7 0.0 all-gather.2.cloned.1.call-start
  16.5 1.8 %all_gather.10 = f32[4,512]{1,0:T(4,128)S(1)} all-gather(f32[4,256]{1,0:T(4,128)S(1)} %pad_maximum_fusion), channel_id=1, replica_groups=mesh['clips'=2,'rows'=4,'tm'=2,'chan'=2] {'chan'}, dimensions={1}, use_global_device_ids=true | all-gather | bytes 12288 | tf_op jit(solution)/shard_map/all_gather | solution.py:78
  18.3 11.9 %all-to-all-done = bf16[8,2,1,64,256]{4,3,1,2,0:T(8,128)(2,1)S(1)} async-done(((bf16[8,2,1,64,256]{4,3,1,2,0:T(8,128)(2,1)}), bf16[8,2,1,64,256]{4,3,1,2,0:T(8,128)(2,1)S(1)}, u32[]{:S(2)}, u32[]{:S(2)}) %all-to-all-start) | async-done | bytes 524320 | tf_op jit(solution)/shard_map/all_to_all | solution.py:65
  30.2 0.8 copy-done.2
  30.9 0.0 all-gather.2.cloned.1.call-update
  31.0 1.5 %broadcast_in_dim.20 = bf16[4096,256]{1,0:T(8,128)(2,1)} broadcast(bf16[]{:T(256)} %constant.177.clone.1), dimensions={} | broadcast | bytes 2097154 | tf_op jit(solution)/shard_map/broadcast_in_dim | solution.py:97
  32.5 1.3 %constant_dynamic-update-slice_fusion.8 = bf16[4096,256]{1,0:T(8,128)(2,1)} fusion(bf16[4096,256]{1,0:T(8,128)(2,1)} %broadcast_in_dim.20, bf16[3456,256]{1,0:T(8,128)(2,1)S(1)} %copy-done.3, s32[]{:T(128)S(6)} %select_n.288), kind=kLoop, calls=%fused_computation.62 | loop fusion | bytes 3538948 | tf_op jit(solution)/shard_map/dynamic_update_slice | solution.py:96
  33.9 5.3 %all-gather.2.cloned.1.call-done = bf16[8,2,1,64,512]{4,3,1,2,0:T(8,128)(2,1)} async-done(((bf16[8,2,1,64,256]{4,3,1,2,0:T(8,128)(2,1)}), bf16[8,2,1,64,512]{4,3,1,2,0:T(8,128)(2,1)}) %all-gather.2.cloned.1.call-update) | async-done | bytes 1048592 | tf_op jit(solution)/shard_map/all_gather | solution.py:66
  39.2 1.5 %convert_reduce_fusion = f32[512]{0:T(512)S(1)} fusion(bf16[2,2,4,1,64,512]{5,4,1,0,2,3:T(8,128)(2,1)} %bitcast.55), kind=kLoop, calls=%fused_computation.10 | loop fusion | flops 1048064 | bytes 1050624 | tf_op jit(solution)/shard_map/reduce_sum | solution.py:17
  40.7 0.1 reduce_sum.67
  40.8 0.1 reduce_sum.68
  40.9 0.1 sub.104
  41.0 0.1 sub.105
  41.1 1.6 %fusion.7 = f32[512]{0:T(512)S(1)} fusion(bf16[2,2,4,1,64,512]{5,4,1,0,2,3:T(8,128)(2,1)} %bitcast.56, f32[512]{0:T(512)S(1)} %sub.105), kind=kLoop, calls=%fused_computation.12 | loop fusion | flops 2096640 | bytes 1052672 | tf_op jit(solution)/shard_map/reduce_sum | solution.py:19
  42.7 0.1 reduce_sum.70
  42.8 0.1 reduce_sum.74
  42.9 0.1 mul.76
  43.0 0.1 mul.77
  43.1 0.6 gather_fusion
  43.7 0.9 multiply_convert_fusion
  44.6 0.7 fusion.11
  45.3 0.4 constant_dynamic-slice_fusion.7
  45.7 0.1 constant_dynamic-update-slice_fusion.7
  45.8 0.1 constant_dynamic-update-slice_fusion.6
  45.9 2.1 %constant_dynamic-slice_fusion.1 = (bf16[2,4,64,512]{3,2,1,0:T(8,128)(2,1)S(1)}, bf16[2,4,64,512]{3,2,1,0:T(8,128)(2,1)S(1)}, bf16[2,4,64,512]{3,2,1,0:T(8,128)(...) fusion(bf16[4,6,66,512]{3,2,1,0:T(8,128)(2,1)S(1)} %fusion.11, ...), kind=kLoop, calls=%fused_computation.63 | loop fusion | bytes 6291528 | tf_op jit(solution)/shard_map/dynamic_slice | solution.py:103
  48.0 0.1 constant_dynamic-update-slice_fusion.5
  48.0 0.1 constant_dynamic-update-slice_fusion.4
  48.1 0.1 constant_dynamic-update-slice_fusion.3
  48.2 0.1 constant_dynamic-update-slice_fusion.2
  48.3 0.1 constant_dynamic-update-slice_fusion.1
  48.4 0.1 constant_dynamic-update-slice_fusion
  48.4 2.9 %fusion.37 = f32[512,256]{1,0:T(8,128)S(1)} fusion(bf16[512,4096]{1,0:T(8,128)(2,1)S(1)} %constant_dynamic-update-slice_fusion, bf16[4096,256]{1,0:T(8,128)(2,1)} %constant_dynamic-update-slice_fusion.8), kind=kOutput, calls=%fused_computation.80 | convolution fusion | flops 1073741824 | bytes 6815744 | tf_op jit(solution)/shard_map/dot_general | solution.py:110
  51.3 0.0 copy-start.5
  51.3 0.0 copy-start.8
  51.3 0.0 copy-start.13
  51.4 19.6 %all_to_all.15 = f32[2,4,1,64,256]{4,3,0,2,1:T(8,128)S(1)} all-to-all(f32[2,4,1,64,256]{4,3,0,2,1:T(8,128)S(1)} %copy.25), channel_id=1, replica_groups=mesh['clips'=2,'rows'=4,'tm'=2,'chan'=2] {'rows'}, dimensions={1} | all-to-all | bytes 1048576 | tf_op jit(solution)/shard_map/all_to_all | solution.py:112
  71.1 0.7 tile.10
  71.8 3.4 %all-to-all-start.2 = ((bf16[2,4,64,256]{3,2,0,1:T(8,128)(2,1)}), bf16[2,4,64,256]{3,2,0,1:T(8,128)(2,1)S(1)}, u32[]{:S(2)}, u32[]{:S(2)}) async-start(bf16[2,4,64,256]{3,2,0,1:T(8,128)(2,1)} %tile.10), calls=%async_computation.2 | async-start | bytes 524288 | tf_op jit(solution)/shard_map/all_to_all | solution.py:116
  75.2 0.1 dynamic_slice.43
  75.3 8.3 %all-to-all-done.2 = bf16[2,4,64,256]{3,2,0,1:T(8,128)(2,1)S(1)} async-done(((bf16[2,4,64,256]{3,2,0,1:T(8,128)(2,1)}), bf16[2,4,64,256]{3,2,0,1:T(8,128)(2,1)S(1)}, u32[]{:S(2)}, u32[]{:S(2)}) %all-to-all-start.2) | async-done | bytes 262176 | tf_op jit(solution)/shard_map/all_to_all | solution.py:116
  83.7 2.2 %all_gather.11 = bf16[2,4,64,512]{3,2,1,0:T(8,128)(2,1)S(1)} all-gather(bf16[2,4,64,256]{3,2,1,0:T(8,128)(2,1)S(1)} %copy.26), channel_id=1, replica_groups=mesh['clips'=2,'rows'=4,'tm'=2,'chan'=2] {'chan'}, dimensions={3}, use_global_device_ids=true | all-gather | bytes 786432 | tf_op jit(solution)/shard_map/all_gather | solution.py:117
  85.9 0.1 convert_reduce_fusion.1
  86.0 0.1 reduce_sum.93
  86.0 0.1 reduce_sum.94
  86.1 0.1 sub.127
  86.2 0.1 sub.128
  86.3 0.2 fusion.20
  86.5 0.1 reduce_sum.96
  86.5 0.1 reduce_sum.97
  86.6 0.1 mul.86
  86.7 0.1 mul.87
  86.8 0.2 fusion.23
  87.1 0.4 convolution_convert_fusion
  87.6 0.0 copy-start.6
  87.6 0.4 fusion.14
  88.0 0.1 copy-done.4
  88.1 0.2 fusion.17
  88.3 0.4 fusion.36
  88.7 0.2 fusion.28
  88.9 0.3 fusion.18
  89.1 0.2 fusion.19
  89.4 0.6 fusion.25
  (41 shorter events, 0.3 us)
Async XLA Ops:
  6.5 80.5 %copy-start = (bf16[512,512]{1,0:T(8,128)(2,1)S(1)}, bf16[512,512]{1,0:T(8,128)(2,1)}, u32[]{:S(2)}) copy-start(bf16[512,512]{1,0:T(8,128)(2,1)} %param.23) | copy-start | bytes 1572868
  6.5 9.9 %copy-start.9 = (f32[256]{0:T(256)S(1)}, f32[256]{0:T(256)}, u32[]{:S(2)}) copy-start(f32[256]{0:T(256)} %param.20) | copy-start | bytes 3076
  6.5 9.9 %copy-start.10 = (f32[256]{0:T(256)S(1)}, f32[256]{0:T(256)}, u32[]{:S(2)}) copy-start(f32[256]{0:T(256)} %param.19) | copy-start | bytes 3076
  6.5 9.9 %copy-start.11 = (f32[256]{0:T(256)S(1)}, f32[256]{0:T(256)}, u32[]{:S(2)}) copy-start(f32[256]{0:T(256)} %param.16) | copy-start | bytes 3076
  6.5 9.9 %copy-start.12 = (f32[256]{0:T(256)S(1)}, f32[256]{0:T(256)}, u32[]{:S(2)}) copy-start(f32[256]{0:T(256)} %param.15) | copy-start | bytes 3076
  8.3 24.2 %copy-start.3 = (bf16[3456,256]{1,0:T(8,128)(2,1)S(1)}, bf16[3456,256]{1,0:T(8,128)(2,1)}, u32[]{:S(2)}) copy-start(bf16[3456,256]{1,0:T(8,128)(2,1)} %param.17) | copy-start | bytes 5308420
  8.3 21.9 %all-to-all-start = ((bf16[8,2,1,64,256]{4,3,1,2,0:T(8,128)(2,1)}), bf16[8,2,1,64,256]{4,3,1,2,0:T(8,128)(2,1)S(1)}, u32[]{:S(2)}, u32[]{:S(2)}) async-start(bf16[8,2,1,64,256]{4,3,1,2,0:T(8,128)(2,1)} %broadcast_in_dim.18), calls=%async_computation | async-start | bytes 1048576 | tf_op jit(solution)/shard_map/all_to_all | solution.py:65
  15.7 23.5 %all-gather.2.cloned.1.call-start = ((), (), s32[]{:S(2)}) async-start(), calls=%async_computation.3 | async-start | bytes 1572864 | tf_op jit(solution)/shard_map/all_gather | solution.py:66
  30.2 0.8 copy-start.2
  39.2 3.8 %copy-start.1 = (bf16[8,2,1,64,512]{4,3,1,2,0:T(8,128)(2,1)S(1)}, bf16[8,2,1,64,512]{4,3,1,2,0:T(8,128)(2,1)}, u32[]{:S(2)}) copy-start(bf16[8,2,1,64,512]{4,3,1,2,0:T(8,128)(2,1)} %all-gather.2.cloned.1.call-done) | copy-start | bytes 3145732
  51.3 19.7 %copy-start.5 = (bf16[2,1,64,256]{3,2,1,0:T(8,128)(2,1)S(1)}, bf16[2,1,64,256]{3,2,1,0:T(8,128)(2,1)}, u32[]{:S(2)}) copy-start(bf16[2,1,64,256]{3,2,1,0:T(8,128)(2,1)} %param.14) | copy-start | bytes 196612
  51.3 19.7 %copy-start.8 = (f32[256]{0:T(256)S(1)}, f32[256]{0:T(256)}, u32[]{:S(2)}) copy-start(f32[256]{0:T(256)} %param.18) | copy-start | bytes 3076
  51.3 23.9 %copy-start.13 = (f32[512]{0:T(512)S(1)}, f32[512]{0:T(512)}, u32[]{:S(2)}) copy-start(f32[512]{0:T(512)} %param.27) | copy-start | bytes 6148
  71.8 11.8 %all-to-all-start.2 = ((bf16[2,4,64,256]{3,2,0,1:T(8,128)(2,1)}), bf16[2,4,64,256]{3,2,0,1:T(8,128)(2,1)S(1)}, u32[]{:S(2)}, u32[]{:S(2)}) async-start(bf16[2,4,64,256]{3,2,0,1:T(8,128)(2,1)} %tile.10), calls=%async_computation.2 | async-start | bytes 524288 | tf_op jit(solution)/shard_map/all_to_all | solution.py:116
  85.9 1.7 %copy-start.14 = (bf16[512,512]{1,0:T(8,128)(2,1)S(1)}, bf16[512,512]{1,0:T(8,128)(2,1)}, u32[]{:S(2)}) copy-start(bf16[512,512]{1,0:T(8,128)(2,1)} %param.24) | copy-start | bytes 1572868
  85.9 1.7 %copy-start.15 = (f32[512]{0:T(512)S(1)}, f32[512]{0:T(512)}, u32[]{:S(2)}) copy-start(f32[512]{0:T(512)} %param.25) | copy-start | bytes 6148
  87.0 1.0 %copy-start.4 = (bf16[512,512]{1,0:T(8,128)(2,1)S(1)}, bf16[512,512]{1,0:T(8,128)(2,1)}, u32[]{:S(2)}) copy-start(bf16[512,512]{1,0:T(8,128)(2,1)} %param.21) | copy-start | bytes 1572868
  87.0 1.0 %copy-start.7 = (f32[512]{0:T(512)S(1)}, f32[512]{0:T(512)}, u32[]{:S(2)}) copy-start(f32[512]{0:T(512)} %param.22) | copy-start | bytes 6148
  87.6 1.6 %copy-start.6 = (bf16[512,512]{1,0:T(8,128)(2,1)S(1)}, bf16[512,512]{1,0:T(8,128)(2,1)}, u32[]{:S(2)}) copy-start(bf16[512,512]{1,0:T(8,128)(2,1)} %param.26) | copy-start | bytes 1572868
Sparse Core Ops, SparseCore 0:
  31.1 8.0 all-gather.1

commit v4 on v3

--- a/solution.py
+++ b/solution.py
@@ -32,6 +32,22 @@
     parts = [lax.slice_in_dim(cells, 0, 1, axis=dim)] * before + [cells]
     parts += [lax.slice_in_dim(cells, size - 1, size, axis=dim)] * after
     return jnp.concatenate(parts, axis=dim)
+
+
+def chan_gather(cells, axis):
+    count = lax.axis_size("chan")
+    place = lax.axis_index("chan")
+    received = [cells] + [
+        lax.ppermute(cells, "chan", [(i, (i + shift) % count) for i in range(count)])
+        for shift in range(1, count)
+    ]
+    blocks = []
+    for position in range(count):
+        chosen = received[0]
+        for shift in range(1, count):
+            chosen = jnp.where((place - position) % count == shift, received[shift], chosen)
+        blocks.append(chosen)
+    return jnp.concatenate(blocks, axis=axis)
 
 
 def local(
@@ -63,7 +79,7 @@
     group = ("rows", "tm")
     copies = jnp.broadcast_to(latent[None], (row_count * time_count,) + latent.shape)
     gathered = lax.all_to_all(copies, group, 0, 0, tiled=True)
-    gathered = lax.all_gather(gathered, "chan", axis=4, tiled=True).reshape(
+    gathered = chan_gather(gathered, 4).reshape(
         (row_count, time_count, frames, rows_here, columns, chan_count * channels)
     )
     clip = jnp.transpose(gathered, (1, 2, 0, 3, 4, 5)).reshape(
@@ -75,9 +91,7 @@
         time_place * frames - 2 + jnp.arange(frames + 2), 0, time_count * frames - 1
     )
     segment = jnp.take(clip, frame_index, axis=0)
-    scales = lax.all_gather(
-        jnp.stack([norm1_gain, norm1_bias, norm2_gain, norm2_bias]), "chan", axis=1, tiled=True
-    )
+    scales = chan_gather(jnp.stack([norm1_gain, norm1_bias, norm2_gain, norm2_bias]), 1)
     gain1, bias1, gain2, bias2 = scales[0], scales[1], scales[2], scales[3]
     activated = jax.nn.silu(apply_norm(segment, mean1, var1, group_size) * gain1 + bias1).astype(
         jnp.bfloat16
@@ -114,7 +128,7 @@
 
     spread = jnp.tile(own_middle, (1, row_count, 1, 1))
     middle = lax.all_to_all(spread, "rows", 1, 1, tiled=True)
-    middle = lax.all_gather(middle, "chan", axis=3, tiled=True)
+    middle = chan_gather(middle, 3)
     mean2, var2 = group_stats(middle, group_size, (1, 2, 4))
     features = (apply_norm(middle, mean2, var2, group_size) * gain2 + bias2).astype(jnp.bfloat16)
 

time: 97.3 us -> 88 us (0.904)
  between operations: 14.5 us -> 1.3 us
  local copies, waits for them, and re-layouts: 11 us -> 23.4 us
  waiting for transfers between devices: 25.6 us -> 13.6 us
  blocking collectives: 23.6 us -> 28.5 us
  starting transfers between devices: 10.8 us -> 7.4 us
  other arithmetic: 6.49 us -> 8.52 us
    all_to_all x0 -> x1, blocking collectives: none -> 11 us  [local(): middle = lax.all_to_all(spread, 'rows', 1, 1, tiled=True)]
    all_to_all x1 -> x0, waiting for transfers between devices: 8.34 us -> none  [local(): middle = lax.all_to_all(spread, 'rows', 1, 1, tiled=True)]
    convert_element_type x0 -> x2, local copies, waits for them, and re-layouts: none -> 6.16 us  [apply_norm(): values.astype(jnp.float32)]
    all_gather x1 -> x0, waiting for transfers between devices: 5.35 us -> none  [local(): lax.all_gather(gathered, 'chan', axis=4, tiled=True)]
    all_gather x2 -> x0, blocking collectives: 3.98 us -> none  [the longest x1 2.18 us: local(): middle = lax.all_gather(middle, 'chan', axis=3, tiled=True)]
    sub x4 -> x6, local copies, waits for them, and re-layouts: 0.33 us -> 4.02 us  [apply_norm(): grouped - group_mean]
    mul x4 -> x6, local copies, waits for them, and re-layouts: 0.33 us -> 4 us  [apply_norm(): (grouped - group_mean) * lax.rsqrt(group_var + EPSILON)]
    all_to_all x1 -> x0, starting transfers between devices: 3.4 us -> none  [local(): middle = lax.all_to_all(spread, 'rows', 1, 1, tiled=True)]
  transfers between devices with their start and end apart: 3 -> 4, of which waited for: 3 -> 3; matrix products, arithmetic and copies ran while one was open for 3% -> 4% of each run, Pallas kernels for 0% -> 0%
where the time goes in v4:
time: 88 us; the launch traced here: 87.5 us
  blocking collectives  28.5 us (32%)
  local copies, waits for them, and re-layouts  23.4 us (27%)
  waiting for transfers between devices  13.6 us (15%)
  other arithmetic  8.52 us (10%)
  starting transfers between devices  7.4 us (8%)
  matrix products  4.84 us (6%)
  between operations  1.3 us (1%)
    all_to_all x1, blocking collectives, local(): lax.all_to_all(pieces, 'rows', 1, 1, tiled=True)  17.5 us
    all_to_all x1, blocking collectives, local(): middle = lax.all_to_all(spread, 'rows', 1, 1, tiled=True)  11 us
    all_to_all x1, waiting for transfers between devices, local(): gathered = lax.all_to_all(copies, group, 0, 0, tiled=True)  10.3 us
    all_to_all x1, starting transfers between devices, local(): gathered = lax.all_to_all(copies, group, 0, 0, tiled=True)  7.25 us
    convert_element_type x2, local copies, waits for them, and re-layouts, apply_norm(): values.astype(jnp.float32)  6.16 us
    sub x6, local copies, waits for them, and re-layouts, apply_norm(): grouped - group_mean  4.02 us
    mul x6, local copies, waits for them, and re-layouts, apply_norm(): (grouped - group_mean) * lax.rsqrt(group_var + EPSILON)  4 us
    ppermute x3, waiting for transfers between devices, chan_gather(): lax.ppermute(cells, 'chan', [(i, (i + shift) % count) for i in range(coun...  3.33 us
  transfers between devices with their start and end apart: 4, of which 3 were waited for; matrix products, arithmetic and copies ran while one was open for 4% of the time, Pallas kernels for 0%

profile of v4, /device:TPU:0, one launch (start us, length us, event | category | flops | bytes accessed | tf_op | source)
XLA Modules:
  0.0 87.5 jit_solution(12645820792107828461)
XLA Ops:
  0.0 1.8 %broadcast_in_dim.18 = bf16[8,2,1,64,256]{4,3,1,2,0:T(8,128)(2,1)} broadcast(bf16[2,64,256]{2,1,0:T(8,128)(2,1)} %bitcast.86), dimensions={1,3,4} | broadcast | bytes 589824 | tf_op jit(solution)/shard_map/broadcast_in_dim | solution.py:80
  1.8 7.3 %all-to-all-start = ((bf16[8,2,1,64,256]{4,3,1,2,0:T(8,128)(2,1)}), bf16[8,2,1,64,256]{4,3,1,2,0:T(8,128)(2,1)S(1)}, u32[]{:S(2)}, u32[]{:S(2)}) async-start(bf16[8,2,1,64,256]{4,3,1,2,0:T(8,128)(2,1)} %broadcast_in_dim.18), calls=%async_computation | async-start | bytes 1048576 | tf_op jit(solution)/shard_map/all_to_all | solution.py:81
  9.1 0.7 pad_maximum_fusion.1
  9.8 0.1 collective-permute-start.1
  10.5 1.5 %broadcast_in_dim.20 = bf16[4096,256]{1,0:T(8,128)(2,1)} broadcast(bf16[]{:T(256)} %constant.197.clone.1), dimensions={} | broadcast | bytes 2097154 | tf_op jit(solution)/shard_map/broadcast_in_dim | solution.py:111
  12.0 1.4 %constant_dynamic-update-slice_fusion.8 = bf16[4096,256]{1,0:T(8,128)(2,1)} fusion(bf16[4096,256]{1,0:T(8,128)(2,1)} %broadcast_in_dim.20, bf16[3456,256]{1,0:T(8,128)(2,1)S(1)} %copy-done.1, s32[]{:T(128)S(6)} %select_n.356), kind=kLoop, calls=%fused_computation.73 | loop fusion | bytes 3538948 | tf_op jit(solution)/shard_map/dynamic_update_slice | solution.py:110
  13.3 10.3 %all-to-all-done = bf16[8,2,1,64,256]{4,3,1,2,0:T(8,128)(2,1)S(1)} async-done(((bf16[8,2,1,64,256]{4,3,1,2,0:T(8,128)(2,1)}), bf16[8,2,1,64,256]{4,3,1,2,0:T(8,128)(2,1)S(1)}, u32[]{:S(2)}, u32[]{:S(2)}) %all-to-all-start) | async-done | bytes 524320 | tf_op jit(solution)/shard_map/all_to_all | solution.py:81
  24.0 1.5 %collective-permute-done = bf16[8,2,1,64,256]{4,3,1,2,0:T(8,128)(2,1)S(1)} collective-permute-done((bf16[8,2,1,64,256]{4,3,1,2,0:T(8,128)(2,1)S(1)}, bf16[8,2,1,64,256]{4,3,1,2,0:T(8,128)(2,1)S(1)}, u32[]{:S(2)}, u32[]{:S(2)}) %collective-permute-start) | collective-permute-done | bytes 524320 | tf_op jit(solution)/shard_map/ppermute | solution.py:41
  25.5 0.1 broadcast_select_fusion.3
  25.6 0.1 pad_maximum_fusion
  25.7 0.2 convert_reduce_fusion
  25.9 0.1 reduce_sum.71
  26.0 0.1 reduce_sum.72
  26.1 0.1 sub.118
  26.2 0.1 sub.119
  26.2 0.4 fusion.7
  26.6 0.1 reduce_sum.74
  26.7 0.1 reduce_sum.75
  26.8 0.1 mul.85
  26.9 0.1 mul.86
  27.0 0.6 gather_fusion
  27.6 0.9 multiply_convert_fusion
  28.5 0.7 fusion.11
  29.2 0.4 constant_dynamic-slice_fusion.6
  29.7 0.1 constant_dynamic-update-slice_fusion.6
  29.8 2.1 %constant_dynamic-slice_fusion = (bf16[2,4,64,512]{3,2,1,0:T(8,128)(2,1)S(1)}, bf16[2,4,64,512]{3,2,1,0:T(8,128)(2,1)S(1)}, bf16[2,4,64,512]{3,2,1,0:T(8,128)(2,...) fusion(bf16[4,6,66,512]{3,2,1,0:T(8,128)(2,1)S(1)} %fusion.11, ...), kind=kLoop, calls=%fused_computation.74 | loop fusion | bytes 6291528 | tf_op jit(solution)/shard_map/dynamic_slice | solution.py:117
  31.9 0.1 constant_dynamic-update-slice_fusion.5
  32.0 0.1 constant_dynamic-update-slice_fusion.4
  32.0 0.1 constant_dynamic-update-slice_fusion.3
  32.1 0.1 constant_dynamic-update-slice_fusion.2
  32.2 0.1 constant_dynamic-update-slice_fusion.1
  32.3 0.1 constant_dynamic-update-slice_fusion
  32.4 2.9 %fusion.38 = f32[512,256]{1,0:T(8,128)S(1)} fusion(bf16[512,4096]{1,0:T(8,128)(2,1)S(1)} %constant_dynamic-update-slice_fusion, bf16[4096,256]{1,0:T(8,128)(2,1)} %constant_dynamic-update-slice_fusion.8), kind=kOutput, calls=%fused_computation.96 | convolution fusion | flops 1073741824 | bytes 6815744 | tf_op jit(solution)/shard_map/dot_general | solution.py:124
  35.3 17.5 %all_to_all.15 = f32[2,4,1,64,256]{4,3,0,2,1:T(8,128)S(1)} all-to-all(f32[2,4,1,64,256]{4,3,0,2,1:T(8,128)S(1)} %copy.49), channel_id=1, replica_groups=mesh['clips'=2,'rows'=4,'tm'=2,'chan'=2] {'rows'}, dimensions={1} | all-to-all | bytes 1048576 | tf_op jit(solution)/shard_map/all_to_all | solution.py:126
  52.9 11.0 %all_to_all.16 = bf16[2,4,64,256]{3,2,0,1:T(8,128)(2,1)S(1)} all-to-all(bf16[2,4,64,256]{3,2,0,1:T(8,128)(2,1)S(1)} %tile.10), channel_id=1, replica_groups=mesh['clips'=2,'rows'=4,'tm'=2,'chan'=2] {'rows'}, dimensions={1} | all-to-all | bytes 524288 | tf_op jit(solution)/shard_map/all_to_all | solution.py:130
  63.9 0.3 copy.50
  64.2 0.1 collective-permute-start.2
  64.3 0.1 dynamic_slice.43
  64.4 1.8 %collective-permute-done.2 = bf16[2,4,64,256]{2,3,1,0:T(8,128)(2,1)S(1)} collective-permute-done((bf16[2,4,64,256]{2,3,1,0:T(8,128)(2,1)S(1)}, bf16[2,4,64,256]{2,3,1,0:T(8,128)(2,1)S(1)}, u32[]{:S(2)}, u32[]{:S(2)}) %collective-permute-start.2) | collective-permute-done | bytes 262176 | tf_op jit(solution)/shard_map/ppermute | solution.py:41
  66.2 0.1 broadcast_select_fusion.1
  66.2 0.5 fusion.22
  66.7 0.3 maximum_convert_fusion
  67.0 0.8 multiply_reduce_fusion
  67.9 0.1 mul.95
  68.0 0.1 mul.96
  68.1 1.1 %mul.97.clone = f32[2,4,64,512]{3,2,1,0:T(8,128)} broadcast(f32[2,512]{1,0:T(2,128)S(1)} %mul.96), dimensions={0,3} | broadcast | bytes 1052672 | tf_op jit(solution)/shard_map/mul | solution.py:27
  69.2 2.6 %copy.58 = f32[512,512]{0,1:T(8,128)} copy(f32[512,512]{1,0:T(8,128)} %bitcast.71) | data formatting | bytes 2097152 | tf_op jit(solution)/shard_map/mul | solution.py:27
  71.7 2.7 %copy.54 = f32[2,4,64,32,16]{2,1,0,4,3:T(4,128)} copy(f32[2,4,64,32,16]{2,4,3,1,0:T(8,128)S(1)} %maximum_convert_fusion) | data formatting | bytes 2097152 | tf_op jit(solution)/shard_map/convert_element_type | solution.py:24
  74.4 3.5 %reshape.172 = f32[512,512]{0,1:T(8,128)} reshape(f32[2,4,64,32,16]{2,1,0,4,3:T(4,128)} %copy.54) | data formatting | bytes 2097152 | tf_op jit(solution)/shard_map/convert_element_type | solution.py:24
  77.9 0.1 sub.141
  78.0 0.1 sub.142
  78.1 1.2 %sub.143.clone = f32[2,4,64,512]{3,2,1,0:T(8,128)} broadcast(f32[2,512]{1,0:T(2,128)S(1)} %sub.142), dimensions={0,3} | broadcast | bytes 1052672 | tf_op jit(solution)/shard_map/sub | solution.py:27
  79.2 2.5 %copy.56 = f32[512,512]{0,1:T(8,128)} copy(f32[512,512]{1,0:T(8,128)} %bitcast.72) | data formatting | bytes 2097152 | tf_op jit(solution)/shard_map/sub | solution.py:27
  81.8 0.5 fusion.21
  82.3 0.1 copy.53
  82.4 2.1 %add_convert_fusion = bf16[512,512]{0,1:T(8,128)(2,1)S(1)} fusion(f32[512,512]{0,1:T(8,128)} %copy.58, f32[512,512]{0,1:T(8,128)} %reshape.172, f32[512,512]{0,1:T(8,128)} %copy.56, f32[512]{0:T(512)S(1)} %bitcast.92, f32[512]{0:T(512)S(1)} %bitcast.90), kind=kLoop, calls=%fused_computation.33 | loop fusion | flops 1310720 | bytes 3674112 | tf_op jit(solution)/shard_map/convert_element_type | solution.py:133
  84.6 0.5 convolution_convert_fusion
  85.1 0.5 fusion.14
  85.6 0.2 fusion.15
  85.8 0.4 fusion.37
  86.2 0.2 fusion.27
  86.4 0.3 fusion.16
  86.7 0.2 fusion.17
  86.9 0.6 fusion.24
  (45 shorter events, 0.4 us)
Async XLA Ops:
  0.0 84.5 %copy-start = (bf16[512,512]{1,0:T(8,128)(2,1)S(1)}, bf16[512,512]{1,0:T(8,128)(2,1)}, u32[]{:S(2)}) copy-start(bf16[512,512]{1,0:T(8,128)(2,1)} %param.23) | copy-start | bytes 1572868
  0.0 12.0 %copy-start.1 = (bf16[3456,256]{1,0:T(8,128)(2,1)S(1)}, bf16[3456,256]{1,0:T(8,128)(2,1)}, u32[]{:S(2)}) copy-start(bf16[3456,256]{1,0:T(8,128)(2,1)} %param.17) | copy-start | bytes 5308420
  1.8 21.7 %all-to-all-start = ((bf16[8,2,1,64,256]{4,3,1,2,0:T(8,128)(2,1)}), bf16[8,2,1,64,256]{4,3,1,2,0:T(8,128)(2,1)S(1)}, u32[]{:S(2)}, u32[]{:S(2)}) async-start(bf16[8,2,1,64,256]{4,3,1,2,0:T(8,128)(2,1)} %broadcast_in_dim.18), calls=%async_computation | async-start | bytes 1048576 | tf_op jit(solution)/shard_map/all_to_all | solution.py:81
  9.8 14.0 %collective-permute-start.1 = (f32[4,256]{1,0:T(4,128)S(1)}, f32[4,256]{1,0:T(4,128)S(1)}, u32[]{:S(2)}, u32[]{:S(2)}) collective-permute-start(f32[4,256]{1,0:T(4,128)S(1)} %pad_maximum_fusion.1), channel_id=1, source_target_pairs={{0,1},{1,0},{2,3},{3,2},{4,5},{5,4},{6,7},{7,6},{8,9},{9,8},{10,11... | collective-permute-start | bytes 12296 | tf_op jit(solution)/shard_map/ppermute | solution.py:41
  12.0 11.9 %copy-start.5 = (f32[256]{0:T(256)S(1)}, f32[256]{0:T(256)}, u32[]{:S(2)}) copy-start(f32[256]{0:T(256)} %param.20) | copy-start | bytes 3076
  12.0 11.9 %copy-start.6 = (f32[256]{0:T(256)S(1)}, f32[256]{0:T(256)}, u32[]{:S(2)}) copy-start(f32[256]{0:T(256)} %param.19) | copy-start | bytes 3076
  12.0 12.0 %copy-start.7 = (f32[256]{0:T(256)S(1)}, f32[256]{0:T(256)}, u32[]{:S(2)}) copy-start(f32[256]{0:T(256)} %param.16) | copy-start | bytes 3076
  12.0 12.0 %copy-start.8 = (f32[256]{0:T(256)S(1)}, f32[256]{0:T(256)}, u32[]{:S(2)}) copy-start(f32[256]{0:T(256)} %param.15) | copy-start | bytes 3076
  23.6 1.9 %collective-permute-start = (bf16[8,2,1,64,256]{4,3,1,2,0:T(8,128)(2,1)S(1)}, bf16[8,2,1,64,256]{4,3,1,2,0:T(8,128)(2,1)S(1)}, u32[]{:S(2)}, u32[]{:S(2)}) collective-permute-start(bf16[8,2,1,64,256]{4,3,1,2,0:T(8,128)(2,1)S(1)} %all-to-all-done), channel_id=1, source_target_pairs={{0,1},{1,0},{2,3},{3,2},{4,5},{5,4},{6,7},{7,6},{8,9},{9,8},{10,11... | collective-permute-start | bytes 1572872 | tf_op jit(solution)/shard_map/ppermute | solution.py:41
  35.2 17.6 %copy-start.3 = (bf16[2,1,64,256]{3,2,1,0:T(8,128)(2,1)S(1)}, bf16[2,1,64,256]{3,2,1,0:T(8,128)(2,1)}, u32[]{:S(2)}) copy-start(bf16[2,1,64,256]{3,2,1,0:T(8,128)(2,1)} %param.14) | copy-start | bytes 196612
  35.2 17.6 %copy-start.10 = (f32[256]{0:T(256)S(1)}, f32[256]{0:T(256)}, u32[]{:S(2)}) copy-start(f32[256]{0:T(256)} %param.18) | copy-start | bytes 3076
  35.2 29.0 %copy-start.11 = (f32[512]{0:T(512)S(1)}, f32[512]{0:T(512)}, u32[]{:S(2)}) copy-start(f32[512]{0:T(512)} %param.27) | copy-start | bytes 6148
  64.2 2.0 %collective-permute-start.2 = (bf16[2,4,64,256]{2,3,1,0:T(8,128)(2,1)S(1)}, bf16[2,4,64,256]{2,3,1,0:T(8,128)(2,1)S(1)}, u32[]{:S(2)}, u32[]{:S(2)}) collective-permute-start(bf16[2,4,64,256]{2,3,1,0:T(8,128)(2,1)S(1)} %copy.50), channel_id=1, source_target_pairs={{0,1},{1,0},{2,3},{3,2},{4,5},{5,4},{6,7},{7,6},{8,9},{9,8},{10,11... | collective-permute-start | bytes 786440 | tf_op jit(solution)/shard_map/ppermute | solution.py:41
  82.4 2.7 %copy-start.12 = (bf16[512,512]{1,0:T(8,128)(2,1)S(1)}, bf16[512,512]{1,0:T(8,128)(2,1)}, u32[]{:S(2)}) copy-start(bf16[512,512]{1,0:T(8,128)(2,1)} %param.24) | copy-start | bytes 1572868
  82.4 2.7 %copy-start.13 = (f32[512]{0:T(512)S(1)}, f32[512]{0:T(512)}, u32[]{:S(2)}) copy-start(f32[512]{0:T(512)} %param.25) | copy-start | bytes 6148
  84.6 1.0 %copy-start.2 = (bf16[512,512]{1,0:T(8,128)(2,1)S(1)}, bf16[512,512]{1,0:T(8,128)(2,1)}, u32[]{:S(2)}) copy-start(bf16[512,512]{1,0:T(8,128)(2,1)} %param.21) | copy-start | bytes 1572868
  84.6 1.0 %copy-start.9 = (f32[512]{0:T(512)S(1)}, f32[512]{0:T(512)}, u32[]{:S(2)}) copy-start(f32[512]{0:T(512)} %param.22) | copy-start | bytes 6148
  85.1 1.6 %copy-start.4 = (bf16[512,512]{1,0:T(8,128)(2,1)S(1)}, bf16[512,512]{1,0:T(8,128)(2,1)}, u32[]{:S(2)}) copy-start(bf16[512,512]{1,0:T(8,128)(2,1)} %param.26) | copy-start | bytes 1572868

commit v5 on v3

--- a/solution.py
+++ b/solution.py
@@ -32,6 +32,28 @@
     parts = [lax.slice_in_dim(cells, 0, 1, axis=dim)] * before + [cells]
     parts += [lax.slice_in_dim(cells, size - 1, size, axis=dim)] * after
     return jnp.concatenate(parts, axis=dim)
+
+
+def chan_halves(cells):
+    count = lax.axis_size("chan")
+    return [cells] + [
+        lax.ppermute(cells, "chan", [(i, (i + shift) % count) for i in range(count)])
+        for shift in range(1, count)
+    ]
+
+
+def half_rows(weight, shift, width):
+    count = lax.axis_size("chan")
+    source = (lax.axis_index("chan") - shift) % count
+    return lax.dynamic_slice_in_dim(weight, source * width, width, axis=0)
+
+
+def split_dot(halves, weight, width):
+    total = None
+    for shift, half in enumerate(halves):
+        term = jnp.dot(half, half_rows(weight, shift, width), preferred_element_type=jnp.float32)
+        total = term if total is None else total + term
+    return total
 
 
 def local(
@@ -60,14 +82,12 @@
     chan_place = lax.axis_index("chan")
     all_rows = rows_here * row_count
 
-    group = ("rows", "tm")
     copies = jnp.broadcast_to(latent[None], (row_count * time_count,) + latent.shape)
-    gathered = lax.all_to_all(copies, group, 0, 0, tiled=True)
-    gathered = lax.all_gather(gathered, "chan", axis=4, tiled=True).reshape(
-        (row_count, time_count, frames, rows_here, columns, chan_count * channels)
+    gathered = lax.all_to_all(copies, ("rows", "tm"), 0, 0, tiled=True).reshape(
+        (row_count, time_count, frames, rows_here, columns, channels)
     )
     clip = jnp.transpose(gathered, (1, 2, 0, 3, 4, 5)).reshape(
-        (time_count * frames, all_rows, columns, chan_count * channels)
+        (time_count * frames, all_rows, columns, channels)
     )
 
     mean1, var1 = group_stats(clip, group_size, (0, 1, 2, 4))
@@ -75,14 +95,11 @@
         time_place * frames - 2 + jnp.arange(frames + 2), 0, time_count * frames - 1
     )
     segment = jnp.take(clip, frame_index, axis=0)
-    scales = lax.all_gather(
-        jnp.stack([norm1_gain, norm1_bias, norm2_gain, norm2_bias]), "chan", axis=1, tiled=True
-    )
-    gain1, bias1, gain2, bias2 = scales[0], scales[1], scales[2], scales[3]
-    activated = jax.nn.silu(apply_norm(segment, mean1, var1, group_size) * gain1 + bias1).astype(
-        jnp.bfloat16
-    )
+    activated = jax.nn.silu(
+        apply_norm(segment, mean1, var1, group_size) * norm1_gain + norm1_bias
+    ).astype(jnp.bfloat16)
     padded = edge_pad(edge_pad(activated, 1, 1, 1), 2, 1, 1)
+    padded_halves = chan_halves(padded)
 
     block_rows = conv_weight.shape[0]
     start = row_place * block_rows
@@ -95,48 +112,56 @@
     out_channels = conv_weight.shape[1]
     placed = lax.dynamic_update_slice(
         jnp.zeros((span * C, out_channels), conv_weight.dtype), conv_weight, (offset, 0)
-    )
-    windows = []
-    for step in range(span):
-        tap = jnp.minimum(first_tap + step, (block_rows * row_count) // C - 1)
-        windows.append(
-            lax.dynamic_slice(
-                padded,
-                (tap // 9, (tap // 3) % 3, tap % 3, 0),
-                (frames, all_rows, columns, C),
-            ).reshape(-1, C)
+    ).reshape(span, chan_count, channels, out_channels)
+    taps = (block_rows * row_count) // C
+    partial = None
+    for shift, half in enumerate(padded_halves):
+        source = (chan_place - shift) % chan_count
+        windows = []
+        for step in range(span):
+            tap = jnp.minimum(first_tap + step, taps - 1)
+            windows.append(
+                lax.dynamic_slice(
+                    half,
+                    (tap // 9, (tap // 3) % 3, tap % 3, 0),
+                    (frames, all_rows, columns, channels),
+                ).reshape(-1, channels)
+            )
+        patches = jnp.concatenate(windows, axis=1)
+        block = lax.dynamic_index_in_dim(placed, source, axis=1, keepdims=False).reshape(
+            span * channels, out_channels
         )
-    patches = jnp.concatenate(windows, axis=1)
-    partial = jnp.dot(patches, placed, preferred_element_type=jnp.float32)
+        term = jnp.dot(patches, block, preferred_element_type=jnp.float32)
+        partial = term if partial is None else partial + term
+
     pieces = partial.reshape(frames, row_count, rows_here, columns, out_channels)
     convolved = jnp.sum(lax.all_to_all(pieces, "rows", 1, 1, tiled=True), axis=1)
     own_middle = (latent.astype(jnp.float32) + convolved + conv_bias).astype(jnp.bfloat16)
 
-    spread = jnp.tile(own_middle, (1, row_count, 1, 1))
-    middle = lax.all_to_all(spread, "rows", 1, 1, tiled=True)
-    middle = lax.all_gather(middle, "chan", axis=3, tiled=True)
+    middle = lax.all_to_all(jnp.tile(own_middle, (1, row_count, 1, 1)), "rows", 1, 1, tiled=True)
     mean2, var2 = group_stats(middle, group_size, (1, 2, 4))
-    features = (apply_norm(middle, mean2, var2, group_size) * gain2 + bias2).astype(jnp.bfloat16)
+    normed = (apply_norm(middle, mean2, var2, group_size) * norm2_gain + norm2_bias).astype(
+        jnp.bfloat16
+    )
+    normed_halves = chan_halves(normed)
 
     tokens = all_rows * columns
     local_tokens = rows_here * columns
-    feature_rows = features.reshape(frames, tokens, C)
-    own_rows = lax.dynamic_slice(
-        features, (0, row_place * rows_here, 0, 0), (frames, rows_here, columns, C)
-    ).reshape(-1, C)
+    own_rows = [
+        lax.dynamic_slice_in_dim(half, row_place * rows_here, rows_here, axis=1).reshape(
+            -1, channels
+        )
+        for half in normed_halves
+    ]
+    flat = [half.reshape(-1, channels) for half in normed_halves]
     queries = (
-        (jnp.dot(own_rows, w_query, preferred_element_type=jnp.float32) + b_query)
+        (split_dot(own_rows, w_query, channels) + b_query)
         .astype(jnp.bfloat16)
         .reshape(frames, local_tokens, C)
     )
-    flat = feature_rows.reshape(-1, C)
-    keys = (
-        jnp.dot(flat, w_key, preferred_element_type=jnp.float32)
-        .astype(jnp.bfloat16)
-        .reshape(frames, tokens, C)
-    )
+    keys = split_dot(flat, w_key, channels).astype(jnp.bfloat16).reshape(frames, tokens, C)
     values = (
-        (jnp.dot(flat, w_value, preferred_element_type=jnp.float32) + b_value)
+        (split_dot(flat, w_value, channels) + b_value)
         .astype(jnp.bfloat16)
         .reshape(frames, tokens, C)
     )

time: 97.3 us -> 70.3 us (0.72)
  between operations: 14.5 us -> 1.38 us
  blocking collectives: 23.6 us -> 18 us
  waiting for transfers between devices: 25.6 us -> 21.5 us
  other arithmetic: 6.49 us -> 2.8 us
    all_gather x1 -> x0, waiting for transfers between devices: 5.35 us -> none  [local(): lax.all_gather(gathered, 'chan', axis=4, tiled=True)]
    all_gather x2 -> x0, blocking collectives: 3.98 us -> none  [the longest x1 2.18 us: local(): middle = lax.all_gather(middle, 'chan', axis=3, tiled=True)]
    dynamic_slice x3 -> x7, local copies, waits for them, and re-layouts: 2.54 us -> 4.87 us  [the longest x4 3.7 us: local(): lax.dynamic_slice(half, (tap // 9, tap // 3 % 3, tap % 3, 0), (frames, al...]
    all_to_all x1, blocking collectives: 19.6 us -> 18 us  [local(): lax.all_to_all(pieces, 'rows', 1, 1, tiled=True)]
    reduce_sum x4, other arithmetic: 1.94 us -> 0.51 us  [group_stats(): group_var = jnp.mean(centered * centered, axis=axes, keepdims=True)]
    reduce_sum x4, other arithmetic: 1.83 us -> 0.42 us  [group_stats(): group_mean = jnp.mean(grouped, axis=axes, keepdims=True)]
    broadcast_in_dim x1, local copies, waits for them, and re-layouts: 1.49 us -> 0.14 us  [local(): jnp.zeros((span * C, out_channels), conv_weight.dtype)]
    dynamic_update_slice x1, local copies, waits for them, and re-layouts: 1.33 us -> 0.21 us  [local(): lax.dynamic_update_slice(jnp.zeros((span * C, out_channels), conv_weight....]
  transfers between devices with their start and end apart: 3 -> 4, of which waited for: 3 -> 3; matrix products, arithmetic and copies ran while one was open for 3% -> 6% of each run, Pallas kernels for 0% -> 0%
where the time goes in v5:
time: 70.3 us; the launch traced here: 69.9 us
  waiting for transfers between devices  21.5 us (31%)
  blocking collectives  18 us (26%)
  local copies, waits for them, and re-layouts  11.7 us (17%)
  starting transfers between devices  10.8 us (15%)
  matrix products  3.82 us (5%)
  other arithmetic  2.8 us (4%)
  between operations  1.38 us (2%)
    all_to_all x1, blocking collectives, local(): lax.all_to_all(pieces, 'rows', 1, 1, tiled=True)  18 us
    all_to_all x1, waiting for transfers between devices, local(): lax.all_to_all(copies, ('rows', 'tm'), 0, 0, tiled=True)  12.2 us
    all_to_all x1, waiting for transfers between devices, local(): lax.all_to_all(jnp.tile(own_middle, (1, row_count, 1, 1)), 'rows', 1, 1,...  8.64 us
    all_to_all x1, starting transfers between devices, local(): lax.all_to_all(copies, ('rows', 'tm'), 0, 0, tiled=True)  7.25 us
    dynamic_slice x4, local copies, waits for them, and re-layouts, local(): lax.dynamic_slice(half, (tap // 9, tap // 3 % 3, tap % 3, 0), (frames, al...  3.7 us
    all_to_all x1, starting transfers between devices, local(): lax.all_to_all(jnp.tile(own_middle, (1, row_count, 1, 1)), 'rows', 1, 1,...  3.4 us
    broadcast_in_dim x1, local copies, waits for them, and re-layouts, local(): jnp.broadcast_to(latent[None], (row_count * time_count,) + latent.shape)  1.86 us
    unnamed x52, local copies, waits for them, and re-layouts  1.71 us
  transfers between devices with their start and end apart: 4, of which 3 were waited for; matrix products, arithmetic and copies ran while one was open for 6% of the time, Pallas kernels for 0%

profile of v5, /device:TPU:0, one launch (start us, length us, event | category | flops | bytes accessed | tf_op | source)
XLA Modules:
  0.0 69.9 jit_solution(12935622177557722812)
XLA Ops:
  0.0 1.9 %broadcast_in_dim.18 = bf16[8,2,1,64,256]{4,3,1,2,0:T(8,128)(2,1)} broadcast(bf16[2,64,256]{2,1,0:T(8,128)(2,1)} %bitcast.94), dimensions={1,3,4} | broadcast | bytes 589824 | tf_op jit(solution)/shard_map/broadcast_in_dim | solution.py:85
  1.9 7.3 %all-to-all-start = ((bf16[8,2,1,64,256]{4,3,1,2,0:T(8,128)(2,1)}), bf16[8,2,1,64,256]{4,3,1,2,0:T(8,128)(2,1)S(1)}, u32[]{:S(2)}, u32[]{:S(2)}) async-start(bf16[8,2,1,64,256]{4,3,1,2,0:T(8,128)(2,1)} %broadcast_in_dim.18), calls=%async_computation | async-start | bytes 1048576 | tf_op jit(solution)/shard_map/all_to_all | solution.py:86
  9.9 0.1 broadcast_in_dim.20
  10.0 0.2 constant_dynamic-update-slice_fusion.16
  10.3 1.1 %constant_dynamic-slice_fusion.2 = (bf16[8,1,256,256]{3,2,1,0:T(8,128)(2,1)S(1)}, bf16[8,1,256,256]{3,2,1,0:T(8,128)(2,1)}) fusion(bf16[8,2,256,256]{3,2,1,0:T(8,128)(2,1)S(1)} %bitcast.61, s32[]{:T(128)S(6)} %select_n.402, s32[]{:T(128)S(6)} %select_n.400), kind=kLoop, calls=%fused_computation.86 | loop fusion | bytes 4194312 | tf_op jit(solution)/shard_map/jit(dynamic_index_in_dim)/dynamic_slice | solution.py:131
  11.4 12.2 %all-to-all-done = bf16[8,2,1,64,256]{4,3,1,2,0:T(8,128)(2,1)S(1)} async-done(((bf16[8,2,1,64,256]{4,3,1,2,0:T(8,128)(2,1)}), bf16[8,2,1,64,256]{4,3,1,2,0:T(8,128)(2,1)S(1)}, u32[]{:S(2)}, u32[]{:S(2)}) %all-to-all-start) | async-done | bytes 524320 | tf_op jit(solution)/shard_map/all_to_all | solution.py:86
  23.6 0.2 convert_reduce_fusion
  23.8 0.1 reduce_sum.67
  23.9 0.1 reduce_sum.68
  24.0 0.1 sub.126
  24.1 0.1 sub.127
  24.2 0.2 fusion.14
  24.4 0.1 reduce_sum.70
  24.5 0.1 reduce_sum.74
  24.6 0.1 mul.82
  24.7 0.1 mul.83
  24.7 0.6 gather_fusion
  25.4 0.5 multiply_convert_fusion
  25.9 0.4 fusion.18
  26.2 0.4 copy.57
  26.7 0.2 constant_dynamic-slice_fusion.18
  26.9 0.1 collective-permute-start
  27.0 1.1 %constant_dynamic-slice_fusion.12 = (bf16[2,4,64,256]{3,2,1,0:T(8,128)(2,1)S(1)}, bf16[2,4,64,256]{3,2,1,0:T(8,128)(2,1)S(1)}, bf16[2,4,64,256]{3,2,1,0:T(8,128)...) fusion(bf16[4,6,66,256]{3,2,1,0:T(8,128)(2,1)S(1)} %fusion.18, ...), kind=kLoop, calls=%fused_computation.97 | loop fusion | bytes 3145800 | tf_op jit(solution)/shard_map/dynamic_slice | solution.py:124
  28.3 1.0 %copy-done.2 = bf16[8,1,256,256]{3,2,1,0:T(8,128)(2,1)S(1)} copy-done((bf16[8,1,256,256]{3,2,1,0:T(8,128)(2,1)S(1)}, bf16[8,1,256,256]{3,2,1,0:T(8,128)(2,1)}, u32[]{:S(2)}) %copy-start.2) | copy-done | bytes 1048600
  29.3 0.7 %fusion.54 = f32[512,256]{1,0:T(8,128)S(1)} fusion(bf16[512,2048]{1,0:T(8,128)(2,1)S(1)} %constant_dynamic-update-slice_fusion, bf16[2048,256]{1,0:T(8,128)(2,1)S(1)} %bitcast.72), kind=kOutput, calls=%fused_computation.116 | convolution fusion | flops 536870912 | bytes 3670016 | tf_op jit(solution)/shard_map/dot_general | solution.py:134
  30.0 0.6 constant_dynamic-slice_fusion.9
  30.7 1.9 %constant_dynamic-slice_fusion.3 = (bf16[2,4,64,256]{3,0,2,1:T(2,128)(2,1)S(1)}, bf16[2,4,64,256]{3,0,2,1:T(2,128)(2,1)S(1)}, bf16[2,4,64,256]{3,0,2,1:T(2,128)(...) fusion(bf16[4,6,66,256]{3,0,2,1:T(4,128)(2,1)S(1)} %collective-, ...), kind=kLoop, calls=%fused_computation.87 | loop fusion | bytes 3145800 | tf_op jit(solution)/shard_map/dynamic_slice | solution.py:124
  33.1 0.7 %convolution_add_fusion.2 = f32[512,256]{1,0:T(8,128)S(1)} fusion(f32[512,256]{1,0:T(8,128)S(1)} %fusion.54, bf16[512,2048]{1,0:T(8,128)(2,1)S(1)} %constant_dynamic-update-slice_fusion.8, bf16[2048,256]{1,0:T(8,128)(2,1)S(1)} %bitcast.71), kind=kOutput, calls=%fused_computation.16 | convolution fusion | flops 537001984 | bytes 4194304 | tf_op jit(solution)/shard_map/dot_general | solution.py:134
  33.8 0.0 copy-start.5
  33.8 0.0 copy-start.9
  33.8 0.0 copy-start.14
  33.8 0.0 copy-start.10
  33.9 0.0 copy-start.4
  33.9 18.0 %all_to_all.15 = f32[2,4,1,64,256]{4,3,0,2,1:T(8,128)S(1)} all-to-all(f32[2,4,1,64,256]{4,3,0,2,1:T(8,128)S(1)} %copy.66), channel_id=1, replica_groups=mesh['clips'=2,'rows'=4,'tm'=2,'chan'=2] {'rows'}, dimensions={1} | all-to-all | bytes 1048576 | tf_op jit(solution)/shard_map/all_to_all | solution.py:138
  52.0 0.7 %tile.10 = bf16[2,4,64,256]{3,2,0,1:T(8,128)(2,1)} broadcast(bf16[2,64,256]{2,1,0:T(8,128)(2,1)S(1)} %bitcast.89), dimensions={0,2,3} | broadcast | bytes 327680 | tf_op jit(solution)/shard_map/tile | solution.py:141
  52.7 3.4 %all-to-all-start.2 = ((bf16[2,4,64,256]{3,2,0,1:T(8,128)(2,1)}), bf16[2,4,64,256]{3,2,0,1:T(8,128)(2,1)S(1)}, u32[]{:S(2)}, u32[]{:S(2)}) async-start(bf16[2,4,64,256]{3,2,0,1:T(8,128)(2,1)} %tile.10), calls=%async_computation.2 | async-start | bytes 524288 | tf_op jit(solution)/shard_map/all_to_all | solution.py:141
  56.1 0.1 dynamic_slice.112
  56.2 8.6 %all-to-all-done.2 = bf16[2,4,64,256]{3,2,0,1:T(8,128)(2,1)S(1)} async-done(((bf16[2,4,64,256]{3,2,0,1:T(8,128)(2,1)}), bf16[2,4,64,256]{3,2,0,1:T(8,128)(2,1)S(1)}, u32[]{:S(2)}, u32[]{:S(2)}) %all-to-all-start.2) | async-done | bytes 262176 | tf_op jit(solution)/shard_map/all_to_all | solution.py:141
  64.8 0.1 convert_reduce_fusion.1
  64.9 0.1 reduce_sum.93
  65.0 0.1 reduce_sum.94
  65.1 0.1 sub.150
  65.1 0.1 sub.151
  65.2 0.1 fusion.23
  65.3 0.1 reduce_sum.96
  65.4 0.1 reduce_sum.97
  65.5 0.1 mul.91
  65.6 0.1 mul.92
  65.7 0.1 fusion.26
  65.8 0.1 collective-permute-start.1
  65.9 0.3 fusion.29
  66.2 0.2 fusion.35
  66.4 0.3 fusion.32
  66.7 0.7 collective-permute-done.1
  67.4 0.3 fusion.7
  67.7 0.0 copy-start.6
  67.7 0.3 fusion.8
  68.0 0.0 copy-done.7
  68.1 0.2 fusion.10
  68.3 0.4 fusion.53
  68.6 0.2 fusion.40
  68.8 0.3 fusion.11
  69.1 0.2 fusion.12
  69.3 0.6 fusion.37
  (61 shorter events, 0.9 us)
Async XLA Ops:
  0.0 66.4 %copy-start = (bf16[512,512]{1,0:T(8,128)(2,1)S(1)}, bf16[512,512]{1,0:T(8,128)(2,1)}, u32[]{:S(2)}) copy-start(bf16[512,512]{1,0:T(8,128)(2,1)} %param.23) | copy-start | bytes 1572868
  0.0 10.0 %copy-start.1 = (bf16[3456,256]{1,0:T(8,128)(2,1)S(1)}, bf16[3456,256]{1,0:T(8,128)(2,1)}, u32[]{:S(2)}) copy-start(bf16[3456,256]{1,0:T(8,128)(2,1)} %param.17) | copy-start | bytes 5308420
  1.9 21.7 %all-to-all-start = ((bf16[8,2,1,64,256]{4,3,1,2,0:T(8,128)(2,1)}), bf16[8,2,1,64,256]{4,3,1,2,0:T(8,128)(2,1)S(1)}, u32[]{:S(2)}, u32[]{:S(2)}) async-start(bf16[8,2,1,64,256]{4,3,1,2,0:T(8,128)(2,1)} %broadcast_in_dim.18), calls=%async_computation | async-start | bytes 1048576 | tf_op jit(solution)/shard_map/all_to_all | solution.py:86
  11.4 13.9 %copy-start.12 = (f32[256]{0:T(256)S(1)}, f32[256]{0:T(256)}, u32[]{:S(2)}) copy-start(f32[256]{0:T(256)} %param.16) | copy-start | bytes 3076
  11.4 14.0 %copy-start.13 = (f32[256]{0:T(256)S(1)}, f32[256]{0:T(256)}, u32[]{:S(2)}) copy-start(f32[256]{0:T(256)} %param.15) | copy-start | bytes 3076
  26.9 3.1 %collective-permute-start = (bf16[4,6,66,256]{3,0,2,1:T(4,128)(2,1)S(1)}, bf16[4,6,66,256]{3,0,2,1:T(4,128)(2,1)S(1)}, u32[]{:S(2)}, u32[]{:S(2)}) collective-permute-start(bf16[4,6,66,256]{3,0,2,1:T(4,128)(2,1)S(1)} %copy.57), channel_id=1, source_target_pairs={{0,1},{1,0},{2,3},{3,2},{4,5},{5,4},{6,7},{7,6},{8,9},{9,8},{10,11... | collective-permute-start | bytes 2433032 | tf_op jit(solution)/shard_map/ppermute | solution.py:40
  28.1 1.2 %copy-start.2 = (bf16[8,1,256,256]{3,2,1,0:T(8,128)(2,1)S(1)}, bf16[8,1,256,256]{3,2,1,0:T(8,128)(2,1)}, u32[]{:S(2)}) copy-start(bf16[8,1,256,256]{3,2,1,0:T(8,128)(2,1)} %get-tuple-element.6) | copy-start | bytes 3145732
  33.8 18.1 %copy-start.5 = (bf16[2,1,64,256]{3,2,1,0:T(8,128)(2,1)S(1)}, bf16[2,1,64,256]{3,2,1,0:T(8,128)(2,1)}, u32[]{:S(2)}) copy-start(bf16[2,1,64,256]{3,2,1,0:T(8,128)(2,1)} %param.14) | copy-start | bytes 196612
  33.8 18.1 %copy-start.9 = (f32[256]{0:T(256)S(1)}, f32[256]{0:T(256)}, u32[]{:S(2)}) copy-start(f32[256]{0:T(256)} %param.18) | copy-start | bytes 3076
  33.8 22.3 %copy-start.14 = (f32[512]{0:T(512)S(1)}, f32[512]{0:T(512)}, u32[]{:S(2)}) copy-start(f32[512]{0:T(512)} %param.27) | copy-start | bytes 6148
  33.8 31.8 %copy-start.10 = (f32[256]{0:T(256)S(1)}, f32[256]{0:T(256)}, u32[]{:S(2)}) copy-start(f32[256]{0:T(256)} %param.20) | copy-start | bytes 3076
  33.8 31.8 %copy-start.11 = (f32[256]{0:T(256)S(1)}, f32[256]{0:T(256)}, u32[]{:S(2)}) copy-start(f32[256]{0:T(256)} %param.19) | copy-start | bytes 3076
  33.9 32.0 %copy-start.4 = (bf16[512,512]{1,0:T(8,128)(2,1)S(1)}, bf16[512,512]{1,0:T(8,128)(2,1)}, u32[]{:S(2)}) copy-start(bf16[512,512]{1,0:T(8,128)(2,1)} %param.24) | copy-start | bytes 1572868
  51.9 14.3 %copy-start.3 = (bf16[512,512]{1,0:T(8,128)(2,1)S(1)}, bf16[512,512]{1,0:T(8,128)(2,1)}, u32[]{:S(2)}) copy-start(bf16[512,512]{1,0:T(8,128)(2,1)} %param.21) | copy-start | bytes 1572868
  52.7 12.2 %all-to-all-start.2 = ((bf16[2,4,64,256]{3,2,0,1:T(8,128)(2,1)}), bf16[2,4,64,256]{3,2,0,1:T(8,128)(2,1)S(1)}, u32[]{:S(2)}, u32[]{:S(2)}) async-start(bf16[2,4,64,256]{3,2,0,1:T(8,128)(2,1)} %tile.10), calls=%async_computation.2 | async-start | bytes 524288 | tf_op jit(solution)/shard_map/all_to_all | solution.py:141
  65.8 1.6 %collective-permute-start.1 = (bf16[2,4,64,256]{3,2,1,0:T(8,128)(2,1)S(1)}, bf16[2,4,64,256]{3,2,1,0:T(8,128)(2,1)S(1)}, u32[]{:S(2)}, u32[]{:S(2)}) collective-permute-start(bf16[2,4,64,256]{3,2,1,0:T(8,128)(2,1)S(1)} %fusion.26), channel_id=1, source_target_pairs={{0,1},{1,0},{2,3},{3,2},{4,5},{5,4},{6,7},{7,6},{8,9},{9,8},{10,11... | collective-permute-start | bytes 786440 | tf_op jit(solution)/shard_map/ppermute | solution.py:40
  66.2 1.5 %copy-start.8 = (f32[512]{0:T(512)S(1)}, f32[512]{0:T(512)}, u32[]{:S(2)}) copy-start(f32[512]{0:T(512)} %param.25) | copy-start | bytes 6148
  67.4 0.7 copy-start.7
  67.7 1.4 %copy-start.6 = (bf16[512,512]{1,0:T(8,128)(2,1)S(1)}, bf16[512,512]{1,0:T(8,128)(2,1)}, u32[]{:S(2)}) copy-start(bf16[512,512]{1,0:T(8,128)(2,1)} %param.26) | copy-start | bytes 1572868

commit v6 on v5

--- a/solution.py
+++ b/solution.py
@@ -117,22 +117,16 @@
     partial = None
     for shift, half in enumerate(padded_halves):
         source = (chan_place - shift) % chan_count
-        windows = []
+        block = lax.dynamic_index_in_dim(placed, source, axis=1, keepdims=False)
         for step in range(span):
             tap = jnp.minimum(first_tap + step, taps - 1)
-            windows.append(
-                lax.dynamic_slice(
-                    half,
-                    (tap // 9, (tap // 3) % 3, tap % 3, 0),
-                    (frames, all_rows, columns, channels),
-                ).reshape(-1, channels)
-            )
-        patches = jnp.concatenate(windows, axis=1)
-        block = lax.dynamic_index_in_dim(placed, source, axis=1, keepdims=False).reshape(
-            span * channels, out_channels
-        )
-        term = jnp.dot(patches, block, preferred_element_type=jnp.float32)
-        partial = term if partial is None else partial + term
+            window = lax.dynamic_slice(
+                half,
+                (tap // 9, (tap // 3) % 3, tap % 3, 0),
+                (frames, all_rows, columns, channels),
+            ).reshape(-1, channels)
+            term = jnp.dot(window, block[step], preferred_element_type=jnp.float32)
+            partial = term if partial is None else partial + term
 
     pieces = partial.reshape(frames, row_count, rows_here, columns, out_channels)
     convolved = jnp.sum(lax.all_to_all(pieces, "rows", 1, 1, tiled=True), axis=1)

time: 70.3 us -> 74.7 us (1.063)
  matrix products: 3.82 us -> 6.26 us
  local copies, waits for them, and re-layouts: 11.7 us -> 13.1 us
  other arithmetic: 2.8 us -> 3.84 us
  between operations: 1.38 us -> 0.57 us
    dot_general x2 -> x16, matrix products: 1.43 us -> 3.86 us  [local(): term = jnp.dot(window, block[step], preferred_element_type=jnp.float32)]
    gather x1, local copies, waits for them, and re-layouts: 0.6 us -> 2.45 us  [local(): segment = jnp.take(clip, frame_index, axis=0)]
    dynamic_update_slice x1, local copies, waits for them, and re-layouts: 0.21 us -> 1.69 us  [local(): lax.dynamic_update_slice(jnp.zeros((span * C, out_channels), conv_weight....]
    unnamed x52 -> x34, local copies, waits for them, and re-layouts: 1.71 us -> 0.32 us
    dynamic_slice x1 -> x0, local copies, waits for them, and re-layouts: 1.14 us -> none  [local(): lax.dynamic_index_in_dim(placed, source, axis=1, keepdims=False)]
    convert_element_type x1, other arithmetic: 0.47 us -> 1.51 us  [local(): activated = jax.nn.silu(apply_norm(segment, mean1, var1, group_size) * no...]
    transpose x1, local copies, waits for them, and re-layouts: 0.04 us -> 0.84 us  [local(): jnp.transpose(gathered, (1, 2, 0, 3, 4, 5))]
  transfers between devices with their start and end apart: 4 -> 4, of which waited for: 3 -> 3; matrix products, arithmetic and copies ran while one was open for 6% -> 8% of each run, Pallas kernels for 0% -> 0%
where the time goes in v6:
time: 74.7 us; the launch traced here: 74.3 us
  waiting for transfers between devices  21.8 us (29%)
  blocking collectives  17.8 us (24%)
  local copies, waits for them, and re-layouts  13.1 us (18%)
  starting transfers between devices  10.9 us (15%)
  matrix products  6.26 us (8%)
  other arithmetic  3.84 us (5%)
    all_to_all x1, blocking collectives, local(): lax.all_to_all(pieces, 'rows', 1, 1, tiled=True)  17.8 us
    all_to_all x1, waiting for transfers between devices, local(): lax.all_to_all(copies, ('rows', 'tm'), 0, 0, tiled=True)  12.6 us
    all_to_all x1, waiting for transfers between devices, local(): lax.all_to_all(jnp.tile(own_middle, (1, row_count, 1, 1)), 'rows', 1, 1,...  8.53 us
    all_to_all x1, starting transfers between devices, local(): lax.all_to_all(copies, ('rows', 'tm'), 0, 0, tiled=True)  7.25 us
    dot_general x16, matrix products, local(): term = jnp.dot(window, block[step], preferred_element_type=jnp.float32)  3.86 us
    dynamic_slice x4, local copies, waits for them, and re-layouts, local(): lax.dynamic_slice(half, (tap // 9, tap // 3 % 3, tap % 3, 0), (frames, al...  3.71 us
    all_to_all x1, starting transfers between devices, local(): lax.all_to_all(jnp.tile(own_middle, (1, row_count, 1, 1)), 'rows', 1, 1,...  3.54 us
    gather x1, local copies, waits for them, and re-layouts, local(): segment = jnp.take(clip, frame_index, axis=0)  2.45 us
  transfers between devices with their start and end apart: 4, of which 3 were waited for; matrix products, arithmetic and copies ran while one was open for 8% of the time, Pallas kernels for 0%

profile of v6, /device:TPU:0, one launch (start us, length us, event | category | flops | bytes accessed | tf_op | source)
XLA Modules:
  0.0 74.3 jit_solution(18016351300718140654)
XLA Ops:
  0.0 1.7 %broadcast_in_dim.18 = bf16[8,2,1,64,256]{4,3,1,2,0:T(8,128)(2,1)} broadcast(bf16[2,64,256]{2,1,0:T(8,128)(2,1)} %bitcast.165), dimensions={1,3,4} | broadcast | bytes 589824 | tf_op jit(solution)/shard_map/broadcast_in_dim | solution.py:85
  1.7 7.3 %all-to-all-start = ((bf16[8,2,1,64,256]{4,3,1,2,0:T(8,128)(2,1)}), bf16[8,2,1,64,256]{4,3,1,2,0:T(8,128)(2,1)S(1)}, u32[]{:S(2)}, u32[]{:S(2)}) async-start(bf16[8,2,1,64,256]{4,3,1,2,0:T(8,128)(2,1)} %broadcast_in_dim.18), calls=%async_computation | async-start | bytes 1048576 | tf_op jit(solution)/shard_map/all_to_all | solution.py:86
  9.0 0.1 broadcast_in_dim.20
  9.2 1.7 %constant_dynamic-update-slice_fusion = bf16[4096,256]{1,0:T(8,128)(2,1)S(1)} fusion(bf16[4096,256]{1,0:T(8,128)(2,1)S(1)} %broadcast_in_dim.20, bf16[3456,256]{1,0:T(8,128)(2,1)} %param.17, s32[]{:T(128)S(6)} %select_n.349), kind=kLoop, calls=%fused_computation.139 | loop fusion | bytes 3538948 | tf_op jit(solution)/shard_map/dynamic_update_slice | solution.py:113
  10.9 12.6 %all-to-all-done = bf16[8,2,1,64,256]{4,3,1,2,0:T(8,128)(2,1)S(1)} async-done(((bf16[8,2,1,64,256]{4,3,1,2,0:T(8,128)(2,1)}), bf16[8,2,1,64,256]{4,3,1,2,0:T(8,128)(2,1)S(1)}, u32[]{:S(2)}, u32[]{:S(2)}) %all-to-all-start) | async-done | bytes 524320 | tf_op jit(solution)/shard_map/all_to_all | solution.py:86
  23.5 0.8 %copy.56 = bf16[2,2,4,1,64,256]{5,4,2,1,0,3:T(8,128)(2,1)} copy(bf16[2,2,4,1,64,256]{5,4,1,0,2,3:T(8,128)(2,1)S(1)} %bitcast.135) | data formatting | bytes 1048576 | tf_op jit(solution)/shard_map/transpose | solution.py:89
  24.3 0.2 convert_reduce_fusion
  24.5 0.1 reduce_sum.67
  24.6 0.1 reduce_sum.68
  24.8 0.1 sub.127
  24.8 0.2 fusion.21
  25.0 0.1 reduce_sum.70
  25.1 0.1 reduce_sum.74
  25.3 0.1 mul.83
  25.4 2.4 %gather_fusion = bf16[4,4,64,256]{3,2,1,0:T(8,128)(2,1)} fusion(bf16[4,4,64,256]{3,2,1,0:T(8,128)(2,1)} %bitcast.141, s32[1024]{0:T(1024)S(1)} %pad_clamp_fusion), kind=kCustom, calls=%fused_computation | custom fusion | bytes 1048592 | tf_op jit(solution)/shard_map/jit(_take)/gather | solution.py:97
  27.9 1.5 %multiply_convert_fusion = bf16[4,4,64,256]{3,2,1,0:T(8,128)(2,1)S(1)} fusion(f32[256]{0:T(256)S(1)} %copy-done.10, f32[256]{0:T(256)S(1)} %copy-done.11, f32[256]{0:T(256)S(1)} %mul.83, f32[256]{0:T(256)S(1)} %sub.127, bf16[4,4,64,256]{3,2,1,0:T(8,128)(2,1)} %gather_fusion, pred[4]{0:T(512)(128)(4,1)S(1)} %compare_and_fusion), kind=kLoop, calls=%fused_computation.41 | loop fusion | flops 2883584 | bytes 1052676 | tf_op jit(solution)/shard_map/convert_element_type | solution.py:100
  29.4 0.4 fusion.25
  29.8 0.4 copy.57
  30.3 0.2 constant_dynamic-slice_fusion.16
  30.5 0.2 fusion.51
  30.7 0.2 convolution_add_fusion.9
  31.0 1.1 %constant_dynamic-slice_fusion.10 = (bf16[2,4,64,256]{3,2,1,0:T(8,128)(2,1)S(1)}, bf16[2,4,64,256]{3,2,1,0:T(8,128)(2,1)S(1)}, bf16[2,4,64,256]{3,2,1,0:T(8,128)...) fusion(bf16[4,6,66,256]{3,2,1,0:T(8,128)(2,1)S(1)} %fusion.25, ...), kind=kLoop, calls=%fused_computation.131 | loop fusion | bytes 3145800 | tf_op jit(solution)/shard_map/dynamic_slice | solution.py:123
  32.0 0.2 convolution_add_fusion.8
  32.3 0.2 convolution_add_fusion.7
  32.5 0.2 convolution_add_fusion.6
  32.8 0.2 convolution_add_fusion.5
  33.0 0.2 convolution_add_fusion.4
  33.2 0.2 convolution_add_fusion.3
  33.5 1.9 %constant_dynamic-slice_fusion.9 = (bf16[2,4,64,256]{3,0,2,1:T(2,128)(2,1)S(1)}, bf16[2,4,64,256]{3,0,2,1:T(2,128)(2,1)S(1)}, bf16[2,4,64,256]{3,0,2,1:T(2,128)(...) fusion(bf16[4,6,66,256]{3,0,2,1:T(4,128)(2,1)S(1)} %collective-, ...), kind=kLoop, calls=%fused_computation.130 | loop fusion | bytes 3145800 | tf_op jit(solution)/shard_map/dynamic_slice | solution.py:123
  35.5 0.2 fusion.49
  35.7 0.2 fusion.48
  36.0 0.2 fusion.47
  36.2 0.2 fusion.46
  36.5 0.2 fusion.45
  36.8 0.6 constant_dynamic-slice_fusion.8
  37.4 0.2 fusion.50
  37.7 0.2 fusion.44
  37.9 0.3 fusion.15
  38.4 17.8 %all_to_all.15 = f32[2,4,1,64,256]{4,3,0,2,1:T(8,128)S(1)} all-to-all(f32[2,4,1,64,256]{4,3,0,2,1:T(8,128)S(1)} %copy.66), channel_id=1, replica_groups=mesh['clips'=2,'rows'=4,'tm'=2,'chan'=2] {'rows'}, dimensions={1} | all-to-all | bytes 1048576 | tf_op jit(solution)/shard_map/all_to_all | solution.py:132
  56.3 0.7 tile.10
  57.0 3.5 %all-to-all-start.2 = ((bf16[2,4,64,256]{3,2,0,1:T(8,128)(2,1)}), bf16[2,4,64,256]{3,2,0,1:T(8,128)(2,1)S(1)}, u32[]{:S(2)}, u32[]{:S(2)}) async-start(bf16[2,4,64,256]{3,2,0,1:T(8,128)(2,1)} %tile.10), calls=%async_computation.2 | async-start | bytes 524288 | tf_op jit(solution)/shard_map/all_to_all | solution.py:135
  60.5 0.1 dynamic_slice.112
  60.6 8.5 %all-to-all-done.2 = bf16[2,4,64,256]{3,2,0,1:T(8,128)(2,1)S(1)} async-done(((bf16[2,4,64,256]{3,2,0,1:T(8,128)(2,1)}), bf16[2,4,64,256]{3,2,0,1:T(8,128)(2,1)S(1)}, u32[]{:S(2)}, u32[]{:S(2)}) %all-to-all-start.2) | async-done | bytes 262176 | tf_op jit(solution)/shard_map/all_to_all | solution.py:135
  69.2 0.1 reduce_sum.93
  69.3 0.1 reduce_sum.94
  69.4 0.1 sub.150
  69.5 0.1 sub.151
  69.5 0.1 fusion.30
  69.6 0.1 reduce_sum.96
  69.7 0.1 reduce_sum.97
  69.9 0.1 mul.92
  70.0 0.1 fusion.33
  70.2 0.3 fusion.39
  70.6 0.2 fusion.42
  70.8 0.3 fusion.36
  71.1 0.6 collective-permute-done.1
  71.7 0.3 fusion.7
  72.0 0.2 fusion.17
  72.3 0.4 fusion.84
  72.6 0.2 fusion.55
  72.8 0.3 fusion.8
  73.1 0.3 fusion.18
  73.4 0.2 fusion.19
  73.6 0.6 fusion.52
  (54 shorter events, 0.9 us)
Async XLA Ops:
  0.0 70.2 %copy-start = (bf16[512,512]{1,0:T(8,128)(2,1)S(1)}, bf16[512,512]{1,0:T(8,128)(2,1)}, u32[]{:S(2)}) copy-start(bf16[512,512]{1,0:T(8,128)(2,1)} %param.23) | copy-start | bytes 1572868
  1.7 21.7 %all-to-all-start = ((bf16[8,2,1,64,256]{4,3,1,2,0:T(8,128)(2,1)}), bf16[8,2,1,64,256]{4,3,1,2,0:T(8,128)(2,1)S(1)}, u32[]{:S(2)}, u32[]{:S(2)}) async-start(bf16[8,2,1,64,256]{4,3,1,2,0:T(8,128)(2,1)} %broadcast_in_dim.18), calls=%async_computation | async-start | bytes 1048576 | tf_op jit(solution)/shard_map/all_to_all | solution.py:86
  10.9 17.0 %copy-start.10 = (f32[256]{0:T(256)S(1)}, f32[256]{0:T(256)}, u32[]{:S(2)}) copy-start(f32[256]{0:T(256)} %param.16) | copy-start | bytes 3076
  10.9 17.0 %copy-start.11 = (f32[256]{0:T(256)S(1)}, f32[256]{0:T(256)}, u32[]{:S(2)}) copy-start(f32[256]{0:T(256)} %param.15) | copy-start | bytes 3076
  30.2 3.3 %collective-permute-start = (bf16[4,6,66,256]{3,0,2,1:T(4,128)(2,1)S(1)}, bf16[4,6,66,256]{3,0,2,1:T(4,128)(2,1)S(1)}, u32[]{:S(2)}, u32[]{:S(2)}) collective-permute-start(bf16[4,6,66,256]{3,0,2,1:T(4,128)(2,1)S(1)} %copy.57), channel_id=1, source_target_pairs={{0,1},{1,0},{2,3},{3,2},{4,5},{5,4},{6,7},{7,6},{8,9},{9,8},{10,11... | collective-permute-start | bytes 2433032 | tf_op jit(solution)/shard_map/ppermute | solution.py:40
  38.3 17.9 %copy-start.3 = (bf16[2,1,64,256]{3,2,1,0:T(8,128)(2,1)S(1)}, bf16[2,1,64,256]{3,2,1,0:T(8,128)(2,1)}, u32[]{:S(2)}) copy-start(bf16[2,1,64,256]{3,2,1,0:T(8,128)(2,1)} %param.14) | copy-start | bytes 196612
  38.3 17.9 %copy-start.7 = (f32[256]{0:T(256)S(1)}, f32[256]{0:T(256)}, u32[]{:S(2)}) copy-start(f32[256]{0:T(256)} %param.18) | copy-start | bytes 3076
  38.3 22.2 %copy-start.12 = (f32[512]{0:T(512)S(1)}, f32[512]{0:T(512)}, u32[]{:S(2)}) copy-start(f32[512]{0:T(512)} %param.27) | copy-start | bytes 6148
  38.3 31.7 %copy-start.8 = (f32[256]{0:T(256)S(1)}, f32[256]{0:T(256)}, u32[]{:S(2)}) copy-start(f32[256]{0:T(256)} %param.20) | copy-start | bytes 3076
  38.3 31.7 %copy-start.9 = (f32[256]{0:T(256)S(1)}, f32[256]{0:T(256)}, u32[]{:S(2)}) copy-start(f32[256]{0:T(256)} %param.19) | copy-start | bytes 3076
  56.2 14.3 %copy-start.1 = (bf16[512,512]{1,0:T(8,128)(2,1)S(1)}, bf16[512,512]{1,0:T(8,128)(2,1)}, u32[]{:S(2)}) copy-start(bf16[512,512]{1,0:T(8,128)(2,1)} %param.21) | copy-start | bytes 1572868
  57.0 13.8 %copy-start.2 = (bf16[512,512]{1,0:T(8,128)(2,1)S(1)}, bf16[512,512]{1,0:T(8,128)(2,1)}, u32[]{:S(2)}) copy-start(bf16[512,512]{1,0:T(8,128)(2,1)} %param.24) | copy-start | bytes 1572868
  57.0 12.2 %all-to-all-start.2 = ((bf16[2,4,64,256]{3,2,0,1:T(8,128)(2,1)}), bf16[2,4,64,256]{3,2,0,1:T(8,128)(2,1)S(1)}, u32[]{:S(2)}, u32[]{:S(2)}) async-start(bf16[2,4,64,256]{3,2,0,1:T(8,128)(2,1)} %tile.10), calls=%async_computation.2 | async-start | bytes 524288 | tf_op jit(solution)/shard_map/all_to_all | solution.py:135
  70.1 1.6 %collective-permute-start.1 = (bf16[2,4,64,256]{3,2,1,0:T(8,128)(2,1)S(1)}, bf16[2,4,64,256]{3,2,1,0:T(8,128)(2,1)S(1)}, u32[]{:S(2)}, u32[]{:S(2)}) collective-permute-start(bf16[2,4,64,256]{3,2,1,0:T(8,128)(2,1)S(1)} %fusion.33), channel_id=1, source_target_pairs={{0,1},{1,0},{2,3},{3,2},{4,5},{5,4},{6,7},{7,6},{8,9},{9,8},{10,11... | collective-permute-start | bytes 786440 | tf_op jit(solution)/shard_map/ppermute | solution.py:40
  70.5 1.5 %copy-start.5 = (f32[512]{0:T(512)S(1)}, f32[512]{0:T(512)}, u32[]{:S(2)}) copy-start(f32[512]{0:T(512)} %param.22) | copy-start | bytes 6148
  71.1 1.8 %copy-start.6 = (f32[512]{0:T(512)S(1)}, f32[512]{0:T(512)}, u32[]{:S(2)}) copy-start(f32[512]{0:T(512)} %param.25) | copy-start | bytes 6148
  72.2 1.1 %copy-start.4 = (bf16[512,512]{1,0:T(8,128)(2,1)S(1)}, bf16[512,512]{1,0:T(8,128)(2,1)}, u32[]{:S(2)}) copy-start(bf16[512,512]{1,0:T(8,128)(2,1)} %param.26) | copy-start | bytes 1572868

commit v7 on v5

--- a/solution.py
+++ b/solution.py
@@ -32,6 +32,32 @@
     parts = [lax.slice_in_dim(cells, 0, 1, axis=dim)] * before + [cells]
     parts += [lax.slice_in_dim(cells, size - 1, size, axis=dim)] * after
     return jnp.concatenate(parts, axis=dim)
+
+
+PERMUTE_GROUP = 8
+
+
+def shifted(cells, axes, sizes, offsets):
+    pairs = []
+    places = [()]
+    for size in sizes:
+        places = [place + (i,) for place in places for i in range(size)]
+    for place in places:
+        target = tuple((p + o) % n for p, o, n in zip(place, offsets, sizes))
+        source_index = 0
+        target_index = 0
+        for p, q, n in zip(place, target, sizes):
+            source_index = source_index * n + p
+            target_index = target_index * n + q
+        pairs.append((source_index, target_index))
+    return lax.ppermute(cells, axes, pairs)
+
+
+def offset_list(sizes):
+    offsets = [()]
+    for size in sizes:
+        offsets = [offset + (i,) for offset in offsets for i in range(size)]
+    return offsets
 
 
 def chan_halves(cells):
@@ -82,13 +108,25 @@
     chan_place = lax.axis_index("chan")
     all_rows = rows_here * row_count
 
-    copies = jnp.broadcast_to(latent[None], (row_count * time_count,) + latent.shape)
-    gathered = lax.all_to_all(copies, ("rows", "tm"), 0, 0, tiled=True).reshape(
-        (row_count, time_count, frames, rows_here, columns, channels)
-    )
-    clip = jnp.transpose(gathered, (1, 2, 0, 3, 4, 5)).reshape(
-        (time_count * frames, all_rows, columns, channels)
-    )
+    if row_count * time_count <= PERMUTE_GROUP:
+        clip = jnp.zeros((time_count * frames, all_rows, columns, channels), latent.dtype)
+        for offset in offset_list((row_count, time_count)):
+            block = latent if offset == (0, 0) else shifted(
+                latent, ("rows", "tm"), (row_count, time_count), offset
+            )
+            source_row = (row_place - offset[0]) % row_count
+            source_time = (time_place - offset[1]) % time_count
+            clip = lax.dynamic_update_slice(
+                clip, block, (source_time * frames, source_row * rows_here, 0, 0)
+            )
+    else:
+        copies = jnp.broadcast_to(latent[None], (row_count * time_count,) + latent.shape)
+        gathered = lax.all_to_all(copies, ("rows", "tm"), 0, 0, tiled=True).reshape(
+            (row_count, time_count, frames, rows_here, columns, channels)
+        )
+        clip = jnp.transpose(gathered, (1, 2, 0, 3, 4, 5)).reshape(
+            (time_count * frames, all_rows, columns, channels)
+        )
 
     mean1, var1 = group_stats(clip, group_size, (0, 1, 2, 4))
     frame_index = jnp.clip(
@@ -135,10 +173,29 @@
         partial = term if partial is None else partial + term
 
     pieces = partial.reshape(frames, row_count, rows_here, columns, out_channels)
-    convolved = jnp.sum(lax.all_to_all(pieces, "rows", 1, 1, tiled=True), axis=1)
+    if row_count <= PERMUTE_GROUP:
+        convolved = lax.dynamic_index_in_dim(pieces, row_place, axis=1, keepdims=False)
+        for shift in range(1, row_count):
+            chunk = lax.dynamic_index_in_dim(
+                pieces, (row_place + shift) % row_count, axis=1, keepdims=False
+            )
+            convolved = convolved + shifted(chunk, ("rows",), (row_count,), (shift,))
+    else:
+        convolved = jnp.sum(lax.all_to_all(pieces, "rows", 1, 1, tiled=True), axis=1)
     own_middle = (latent.astype(jnp.float32) + convolved + conv_bias).astype(jnp.bfloat16)
 
-    middle = lax.all_to_all(jnp.tile(own_middle, (1, row_count, 1, 1)), "rows", 1, 1, tiled=True)
+    if row_count <= PERMUTE_GROUP:
+        middle = jnp.zeros((frames, all_rows, columns, out_channels), own_middle.dtype)
+        for shift in range(row_count):
+            block = own_middle if shift == 0 else shifted(
+                own_middle, ("rows",), (row_count,), (shift,)
+            )
+            source_row = (row_place - shift) % row_count
+            middle = lax.dynamic_update_slice(middle, block, (0, source_row * rows_here, 0, 0))
+    else:
+        middle = lax.all_to_all(
+            jnp.tile(own_middle, (1, row_count, 1, 1)), "rows", 1, 1, tiled=True
+        )
     mean2, var2 = group_stats(middle, group_size, (1, 2, 4))
     normed = (apply_norm(middle, mean2, var2, group_size) * norm2_gain + norm2_bias).astype(
         jnp.bfloat16

time: 70.3 us -> 58.1 us (0.83)
  blocking collectives: 18 us -> 0 us
  starting transfers between devices: 10.8 us -> 20.9 us
  waiting for transfers between devices: 21.5 us -> 19.4 us
  local copies, waits for them, and re-layouts: 11.7 us -> 10.1 us
    all_to_all x2 -> x0, waiting for transfers between devices: 20.8 us -> none  [the longest x1 12.2 us: local(): lax.all_to_all(copies, ('rows', 'tm'), 0, 0, tiled=True)]
    ppermute x0 -> x13, starting transfers between devices: none -> 20.7 us  [shifted(): return lax.ppermute(cells, axes, pairs)]
    ppermute x0 -> x13, waiting for transfers between devices: none -> 18.7 us  [shifted(): return lax.ppermute(cells, axes, pairs)]
    all_to_all x1 -> x0, blocking collectives: 18 us -> none  [local(): lax.all_to_all(pieces, 'rows', 1, 1, tiled=True)]
    all_to_all x2 -> x0, starting transfers between devices: 10.7 us -> none  [the longest x1 7.25 us: local(): lax.all_to_all(copies, ('rows', 'tm'), 0, 0, tiled=True)]
    broadcast_in_dim x1 -> x2, local copies, waits for them, and re-layouts: 1.86 us -> 0.07 us  [the longest x1 0.05 us: local(): jnp.zeros((time_count * frames, all_rows, columns, channels), latent.dtype)]
    dynamic_update_slice x0 -> x11, local copies, waits for them, and re-layouts: none -> 0.95 us  [the longest x8 0.92 us: local(): lax.dynamic_update_slice(clip, block, (source_time * frames, source_row *...]
    another operation x1 -> x0, local copies, waits for them, and re-layouts: 0.71 us -> none  [local(): jnp.tile(own_middle, (1, row_count, 1, 1))]
  transfers between devices with their start and end apart: 4 -> 15, of which waited for: 3 -> 8; matrix products, arithmetic and copies ran while one was open for 6% -> 9% of each run, Pallas kernels for 0% -> 0%
where the time goes in v7:
time: 58.1 us; the launch traced here: 57.8 us
  starting transfers between devices  20.9 us (36%)
  waiting for transfers between devices  19.4 us (33%)
  local copies, waits for them, and re-layouts  10.1 us (17%)
  matrix products  3.82 us (7%)
  other arithmetic  2.79 us (5%)
  between operations  0.91 us (2%)
    ppermute x13, starting transfers between devices, shifted(): return lax.ppermute(cells, axes, pairs)  20.7 us
    ppermute x13, waiting for transfers between devices, shifted(): return lax.ppermute(cells, axes, pairs)  18.7 us
    dynamic_slice x4, local copies, waits for them, and re-layouts, local(): lax.dynamic_slice(half, (tap // 9, tap // 3 % 3, tap % 3, 0), (frames, al...  3.7 us
    unnamed x52, local copies, waits for them, and re-layouts  1.71 us
    dot_general x6, matrix products, split_dot(): jnp.dot(half, half_rows(weight, shift, width), preferred_element_type=jnp...  1.58 us
    dot_general x2, matrix products, local(): term = jnp.dot(patches, block, preferred_element_type=jnp.float32)  1.42 us
  transfers between devices with their start and end apart: 15, of which 8 were waited for; matrix products, arithmetic and copies ran while one was open for 9% of the time, Pallas kernels for 0%

profile of v7, /device:TPU:0, one launch (start us, length us, event | category | flops | bytes accessed | tf_op | source)
XLA Modules:
  0.0 57.8 jit_solution(16840087174295216738)
XLA Ops:
  0.0 2.9 %collective-permute-start = (bf16[2,1,64,256]{3,2,1,0:T(8,128)(2,1)}, bf16[2,1,64,256]{3,2,1,0:T(8,128)(2,1)S(1)}, u32[]{:S(2)}, u32[]{:S(2)}) collective-permute-start(bf16[2,1,64,256]{3,2,1,0:T(8,128)(2,1)} %param.14), channel_id=1, source_target_pairs={{0,2},{2,0},{4,6},{6,4},{8,10},{10,8},{12,14},{14,12},{1,3},{3,1},... | collective-permute-start | bytes 196616 | tf_op jit(solution)/shard_map/ppermute | solution.py:53
  2.9 1.6 %collective-permute-start.1 = (bf16[2,1,64,256]{3,2,1,0:T(8,128)(2,1)}, bf16[2,1,64,256]{3,2,1,0:T(8,128)(2,1)S(1)}, u32[]{:S(2)}, u32[]{:S(2)}) collective-permute-start(bf16[2,1,64,256]{3,2,1,0:T(8,128)(2,1)} %param.14), channel_id=1, source_target_pairs={{0,4},{2,6},{4,8},{6,10},{8,12},{10,14},{12,0},{14,2},{1,5},{3,7},... | collective-permute-start | bytes 196616 | tf_op jit(solution)/shard_map/ppermute | solution.py:53
  4.5 1.5 %collective-permute-start.2 = (bf16[2,1,64,256]{3,2,1,0:T(8,128)(2,1)}, bf16[2,1,64,256]{3,2,1,0:T(8,128)(2,1)S(1)}, u32[]{:S(2)}, u32[]{:S(2)}) collective-permute-start(bf16[2,1,64,256]{3,2,1,0:T(8,128)(2,1)} %param.14), channel_id=1, source_target_pairs={{0,6},{2,4},{4,10},{6,8},{8,14},{10,12},{12,2},{14,0},{1,7},{3,5},... | collective-permute-start | bytes 196616 | tf_op jit(solution)/shard_map/ppermute | solution.py:53
  6.1 1.0 %collective-permute-start.3 = (bf16[2,1,64,256]{3,2,1,0:T(8,128)(2,1)}, bf16[2,1,64,256]{3,2,1,0:T(8,128)(2,1)S(1)}, u32[]{:S(2)}, u32[]{:S(2)}) collective-permute-start(bf16[2,1,64,256]{3,2,1,0:T(8,128)(2,1)} %param.14), channel_id=1, source_target_pairs={{0,8},{2,10},{4,12},{6,14},{8,0},{10,2},{12,4},{14,6},{1,9},{3,11}... | collective-permute-start | bytes 196616 | tf_op jit(solution)/shard_map/ppermute | solution.py:53
  7.1 2.8 %collective-permute-start.4 = (bf16[2,1,64,256]{3,2,1,0:T(8,128)(2,1)}, bf16[2,1,64,256]{3,2,1,0:T(8,128)(2,1)S(1)}, u32[]{:S(2)}, u32[]{:S(2)}) collective-permute-start(bf16[2,1,64,256]{3,2,1,0:T(8,128)(2,1)} %param.14), channel_id=1, source_target_pairs={{0,10},{2,8},{4,14},{6,12},{8,2},{10,0},{12,6},{14,4},{1,11},{3,9}... | collective-permute-start | bytes 196616 | tf_op jit(solution)/shard_map/ppermute | solution.py:53
  10.2 0.9 %constant_dynamic-update-slice_fusion.28 = bf16[4,4,64,256]{3,2,1,0:T(8,128)(2,1)S(1)} fusion(bf16[4,4,64,256]{3,2,1,0:T(8,128)(2,1)S(1)} %broadcast_in_dim.17, bf16[2,1,64,256]{3,2,1,0:T(8,128)(2,1)} %param.14, s32[]{:T(128)S(6)} %select_n.446, s32[]{:T(128)S(6)} %select_n.448), kind=kLoop, calls=%fused_computation.122 | loop fusion | bytes 131080 | tf_op jit(solution)/shard_map/dynamic_update_slice | solution.py:119
  11.1 0.1 broadcast_in_dim.19
  11.2 0.2 constant_dynamic-update-slice_fusion.20
  11.4 1.1 %constant_dynamic-slice_fusion.2 = (bf16[8,1,256,256]{3,2,1,0:T(8,128)(2,1)S(1)}, bf16[8,1,256,256]{3,2,1,0:T(8,128)(2,1)}) fusion(bf16[8,2,256,256]{3,2,1,0:T(8,128)(2,1)S(1)} %bitcast.68, s32[]{:T(128)S(6)} %select_n.521, s32[]{:T(128)S(6)} %select_n.519), kind=kLoop, calls=%fused_computation.96 | loop fusion | bytes 4194312 | tf_op jit(solution)/shard_map/jit(dynamic_index_in_dim)/dynamic_slice | solution.py:169
  12.6 2.3 %collective-permute-start.5 = (bf16[2,1,64,256]{3,2,1,0:T(8,128)(2,1)S(1)}, bf16[2,1,64,256]{3,2,1,0:T(8,128)(2,1)S(1)}, u32[]{:S(2)}, u32[]{:S(2)}) collective-permute-start(bf16[2,1,64,256]{3,2,1,0:T(8,128)(2,1)S(1)} %copy-done.5), channel_id=1, source_target_pairs={{0,12},{2,14},{4,0},{6,2},{8,4},{10,6},{12,8},{14,10},{1,13},{3,15... | collective-permute-start | bytes 196616 | tf_op jit(solution)/shard_map/ppermute | solution.py:53
  14.9 0.3 collective-permute-start.6
  15.3 1.8 %collective-permute-done.4 = bf16[2,1,64,256]{3,2,1,0:T(8,128)(2,1)S(1)} collective-permute-done((bf16[2,1,64,256]{3,2,1,0:T(8,128)(2,1)}, bf16[2,1,64,256]{3,2,1,0:T(8,128)(2,1)S(1)}, u32[]{:S(2)}, u32[]{:S(2)}) %collective-permute-start.4) | collective-permute-done | bytes 65568 | tf_op jit(solution)/shard_map/ppermute | solution.py:53
  17.1 0.4 collective-permute-done.5
  17.5 2.6 %collective-permute-done.6 = bf16[2,1,64,256]{3,2,1,0:T(8,128)(2,1)S(1)} collective-permute-done((bf16[2,1,64,256]{3,2,1,0:T(8,128)(2,1)S(1)}, bf16[2,1,64,256]{3,2,1,0:T(8,128)(2,1)S(1)}, u32[]{:S(2)}, u32[]{:S(2)}) %collective-permute-start.6) | collective-permute-done | bytes 65568 | tf_op jit(solution)/shard_map/ppermute | solution.py:53
  20.1 0.2 convert_reduce_fusion
  20.3 0.1 reduce_sum.55
  20.4 0.1 reduce_sum.59
  20.6 0.1 sub.150
  20.7 0.2 fusion.14
  20.9 0.1 reduce_sum.61
  21.0 0.1 reduce_sum.62
  21.2 0.1 mul.97
  21.2 0.6 %gather_fusion = bf16[4,4,64,256]{3,2,1,0:T(8,128)(2,1)S(1)} fusion(bf16[4,4,64,256]{3,2,1,0:T(8,128)(2,1)S(1)} %constant_dynamic-update-slice_fusion.21, s32[1024]{0:T(1024)S(1)} %pad_clamp_fusion), kind=kCustom, calls=%fused_computation | custom fusion | bytes 1048592 | tf_op jit(solution)/shard_map/jit(_take)/gather | solution.py:135
  21.9 0.5 multiply_convert_fusion
  22.4 0.4 fusion.18
  22.7 0.4 copy.29
  23.2 0.2 constant_dynamic-slice_fusion.18
  23.5 1.1 %constant_dynamic-slice_fusion.12 = (bf16[2,4,64,256]{3,2,1,0:T(8,128)(2,1)S(1)}, bf16[2,4,64,256]{3,2,1,0:T(8,128)(2,1)S(1)}, bf16[2,4,64,256]{3,2,1,0:T(8,128)...) fusion(bf16[4,6,66,256]{3,2,1,0:T(8,128)(2,1)S(1)} %fusion.18, ...), kind=kLoop, calls=%fused_computation.107 | loop fusion | bytes 3145800 | tf_op jit(solution)/shard_map/dynamic_slice | solution.py:162
  24.8 1.0 %copy-done.2 = bf16[8,1,256,256]{3,2,1,0:T(8,128)(2,1)S(1)} copy-done((bf16[8,1,256,256]{3,2,1,0:T(8,128)(2,1)S(1)}, bf16[8,1,256,256]{3,2,1,0:T(8,128)(2,1)}, u32[]{:S(2)}) %copy-start.2) | copy-done | bytes 1048600
  25.8 0.7 %fusion.58 = f32[512,256]{1,0:T(8,128)S(1)} fusion(bf16[512,2048]{1,0:T(8,128)(2,1)S(1)} %constant_dynamic-update-slice_fusion, bf16[2048,256]{1,0:T(8,128)(2,1)S(1)} %bitcast.75), kind=kOutput, calls=%fused_computation.134 | convolution fusion | flops 536870912 | bytes 3670016 | tf_op jit(solution)/shard_map/dot_general | solution.py:172
  26.5 0.6 constant_dynamic-slice_fusion.9
  27.2 1.9 %constant_dynamic-slice_fusion.3 = (bf16[2,4,64,256]{3,0,2,1:T(2,128)(2,1)S(1)}, bf16[2,4,64,256]{3,0,2,1:T(2,128)(2,1)S(1)}, bf16[2,4,64,256]{3,0,2,1:T(2,128)(...) fusion(bf16[4,6,66,256]{3,0,2,1:T(4,128)(2,1)S(1)} %collective-, ...), kind=kLoop, calls=%fused_computation.97 | loop fusion | bytes 3145800 | tf_op jit(solution)/shard_map/dynamic_slice | solution.py:162
  29.6 0.7 %convolution_add_fusion.2 = f32[512,256]{1,0:T(8,128)S(1)} fusion(f32[512,256]{1,0:T(8,128)S(1)} %fusion.58, bf16[512,2048]{1,0:T(8,128)(2,1)S(1)} %constant_dynamic-update-slice_fusion.8, bf16[2048,256]{1,0:T(8,128)(2,1)S(1)} %bitcast.74), kind=kOutput, calls=%fused_computation.16 | convolution fusion | flops 537001984 | bytes 4194304 | tf_op jit(solution)/shard_map/dot_general | solution.py:172
  30.4 2.3 %collective-permute-start.10 = (f32[2,1,64,256]{3,2,1,0:T(8,128)S(1)}, f32[2,1,64,256]{3,2,1,0:T(8,128)S(1)}, u32[]{:S(2)}, u32[]{:S(2)}) collective-permute-start(f32[2,1,64,256]{3,2,1,0:T(8,128)S(1)} %get-tuple-element.26), channel_id=1, source_target_pairs={{0,12},{4,0},{8,4},{12,8},{1,13},{5,1},{9,5},{13,9},{2,14},{6,2},{... | collective-permute-start | bytes 393224 | tf_op jit(solution)/shard_map/ppermute | solution.py:53
  32.7 0.6 %collective-permute-start.8 = (f32[2,1,64,256]{3,2,1,0:T(8,128)S(1)}, f32[2,1,64,256]{3,2,1,0:T(8,128)S(1)}, u32[]{:S(2)}, u32[]{:S(2)}) collective-permute-start(f32[2,1,64,256]{3,2,1,0:T(8,128)S(1)} %get-tuple-element.25), channel_id=1, source_target_pairs={{0,4},{4,8},{8,12},{12,0},{1,5},{5,9},{9,13},{13,1},{2,6},{6,10},{... | collective-permute-start | bytes 393224 | tf_op jit(solution)/shard_map/ppermute | solution.py:53
  33.3 3.3 %collective-permute-done.10 = f32[2,1,64,256]{3,2,1,0:T(8,128)S(1)} collective-permute-done((f32[2,1,64,256]{3,2,1,0:T(8,128)S(1)}, f32[2,1,64,256]{3,2,1,0:T(8,128)S(1)}, u32[]{:S(2)}, u32[]{:S(2)}) %collective-permute-start.10) | collective-permute-done | bytes 131104 | tf_op jit(solution)/shard_map/ppermute | solution.py:53
  36.6 8.2 %collective-permute-done.9 = f32[2,1,64,256]{3,2,1,0:T(8,128)S(1)} collective-permute-done((f32[2,1,64,256]{3,2,1,0:T(8,128)S(1)}, f32[2,1,64,256]{3,2,1,0:T(8,128)S(1)}, u32[]{:S(2)}, u32[]{:S(2)}) %collective-permute-start.9) | collective-permute-done | bytes 131104 | tf_op jit(solution)/shard_map/ppermute | solution.py:53
  44.9 0.4 collective-permute-start.11
  45.4 0.1 dynamic_slice.129
  45.4 2.0 %collective-permute-start.12 = (bf16[2,1,64,256]{3,2,1,0:T(8,128)(2,1)S(1)}, bf16[2,1,64,256]{3,2,1,0:T(8,128)(2,1)S(1)}, u32[]{:S(2)}, u32[]{:S(2)}) collective-permute-start(bf16[2,1,64,256]{3,2,1,0:T(8,128)(2,1)S(1)} %get-tuple-element.6), channel_id=1, source_target_pairs={{0,8},{4,12},{8,0},{12,4},{1,9},{5,13},{9,1},{13,5},{2,10},{6,14},... | collective-permute-start | bytes 196616 | tf_op jit(solution)/shard_map/ppermute | solution.py:53
  47.4 2.9 %collective-permute-start.13 = (bf16[2,1,64,256]{3,2,1,0:T(8,128)(2,1)S(1)}, bf16[2,1,64,256]{3,2,1,0:T(8,128)(2,1)S(1)}, u32[]{:S(2)}, u32[]{:S(2)}) collective-permute-start(bf16[2,1,64,256]{3,2,1,0:T(8,128)(2,1)S(1)} %get-tuple-element.6), channel_id=1, source_target_pairs={{0,12},{4,0},{8,4},{12,8},{1,13},{5,1},{9,5},{13,9},{2,14},{6,2},{... | collective-permute-start | bytes 196616 | tf_op jit(solution)/shard_map/ppermute | solution.py:53
  50.3 1.5 %collective-permute-done.11 = bf16[2,1,64,256]{3,2,1,0:T(8,128)(2,1)S(1)} collective-permute-done((bf16[2,1,64,256]{3,2,1,0:T(8,128)(2,1)S(1)}, bf16[2,1,64,256]{3,2,1,0:T(8,128)(2,1)S(1)}, u32[]{:S(2)}, u32[]{:S(2)}) %collective-permute-start.11) | collective-permute-done | bytes 65568 | tf_op jit(solution)/shard_map/ppermute | solution.py:53
  51.8 0.9 %collective-permute-done.12 = bf16[2,1,64,256]{3,2,1,0:T(8,128)(2,1)S(1)} collective-permute-done((bf16[2,1,64,256]{3,2,1,0:T(8,128)(2,1)S(1)}, bf16[2,1,64,256]{3,2,1,0:T(8,128)(2,1)S(1)}, u32[]{:S(2)}, u32[]{:S(2)}) %collective-permute-start.12) | collective-permute-done | bytes 65568 | tf_op jit(solution)/shard_map/ppermute | solution.py:53
  52.8 0.1 reduce_sum.80
  52.9 0.1 reduce_sum.81
  53.0 0.1 sub.172
  53.0 0.1 sub.173
  53.1 0.1 fusion.23
  53.2 0.1 reduce_sum.83
  53.3 0.1 reduce_sum.84
  53.5 0.1 mul.106
  53.6 0.1 fusion.26
  53.8 0.3 fusion.29
  54.1 0.2 fusion.35
  54.3 0.3 fusion.32
  54.6 0.7 %collective-permute-done.14 = bf16[2,4,64,256]{3,2,1,0:T(8,128)(2,1)S(1)} collective-permute-done((bf16[2,4,64,256]{3,2,1,0:T(8,128)(2,1)S(1)}, bf16[2,4,64,256]{3,2,1,0:T(8,128)(2,1)S(1)}, u32[]{:S(2)}, u32[]{:S(2)}) %collective-permute-start.14) | collective-permute-done | bytes 262176 | tf_op jit(solution)/shard_map/ppermute | solution.py:66
  55.3 0.3 fusion.7
  55.6 0.3 fusion.8
  56.0 0.2 fusion.10
  56.2 0.4 fusion.57
  56.5 0.2 fusion.43
  56.7 0.3 fusion.11
  57.0 0.2 fusion.12
  57.2 0.6 %fusion.37 = bf16[2,1,64,256]{3,2,1,0:T(8,128)(2,1)} fusion(bf16[2,1,64,256]{3,2,1,0:T(8,128)(2,1)S(1)} %bitcast.97, bf16[2,1,64,256]{3,2,1,0:T(8,128)(2,1)S(1)} %get-tuple-element.6), kind=kLoop, calls=%fused_computation.53 | loop fusion | flops 131072 | bytes 196608 | tf_op jit(solution)/shard_map/convert_element_type | solution.py:247
  (91 shorter events, 1.5 us)
Async XLA Ops:
  0.0 54.3 %copy-start = (bf16[512,512]{1,0:T(8,128)(2,1)S(1)}, bf16[512,512]{1,0:T(8,128)(2,1)}, u32[]{:S(2)}) copy-start(bf16[512,512]{1,0:T(8,128)(2,1)} %param.23) | copy-start | bytes 1572868
  0.0 11.2 %copy-start.1 = (bf16[3456,256]{1,0:T(8,128)(2,1)S(1)}, bf16[3456,256]{1,0:T(8,128)(2,1)}, u32[]{:S(2)}) copy-start(bf16[3456,256]{1,0:T(8,128)(2,1)} %param.17) | copy-start | bytes 5308420
  0.0 12.6 %collective-permute-start = (bf16[2,1,64,256]{3,2,1,0:T(8,128)(2,1)}, bf16[2,1,64,256]{3,2,1,0:T(8,128)(2,1)S(1)}, u32[]{:S(2)}, u32[]{:S(2)}) collective-permute-start(bf16[2,1,64,256]{3,2,1,0:T(8,128)(2,1)} %param.14), channel_id=1, source_target_pairs={{0,2},{2,0},{4,6},{6,4},{8,10},{10,8},{12,14},{14,12},{1,3},{3,1},... | collective-permute-start | bytes 196616 | tf_op jit(solution)/shard_map/ppermute | solution.py:53
  2.9 12.0 %collective-permute-start.1 = (bf16[2,1,64,256]{3,2,1,0:T(8,128)(2,1)}, bf16[2,1,64,256]{3,2,1,0:T(8,128)(2,1)S(1)}, u32[]{:S(2)}, u32[]{:S(2)}) collective-permute-start(bf16[2,1,64,256]{3,2,1,0:T(8,128)(2,1)} %param.14), channel_id=1, source_target_pairs={{0,4},{2,6},{4,8},{6,10},{8,12},{10,14},{12,0},{14,2},{1,5},{3,7},... | collective-permute-start | bytes 196616 | tf_op jit(solution)/shard_map/ppermute | solution.py:53
  4.5 10.7 %collective-permute-start.2 = (bf16[2,1,64,256]{3,2,1,0:T(8,128)(2,1)}, bf16[2,1,64,256]{3,2,1,0:T(8,128)(2,1)S(1)}, u32[]{:S(2)}, u32[]{:S(2)}) collective-permute-start(bf16[2,1,64,256]{3,2,1,0:T(8,128)(2,1)} %param.14), channel_id=1, source_target_pairs={{0,6},{2,4},{4,10},{6,8},{8,14},{10,12},{12,2},{14,0},{1,7},{3,5},... | collective-permute-start | bytes 196616 | tf_op jit(solution)/shard_map/ppermute | solution.py:53
  6.1 9.2 %collective-permute-start.3 = (bf16[2,1,64,256]{3,2,1,0:T(8,128)(2,1)}, bf16[2,1,64,256]{3,2,1,0:T(8,128)(2,1)S(1)}, u32[]{:S(2)}, u32[]{:S(2)}) collective-permute-start(bf16[2,1,64,256]{3,2,1,0:T(8,128)(2,1)} %param.14), channel_id=1, source_target_pairs={{0,8},{2,10},{4,12},{6,14},{8,0},{10,2},{12,4},{14,6},{1,9},{3,11}... | collective-permute-start | bytes 196616 | tf_op jit(solution)/shard_map/ppermute | solution.py:53
  7.1 10.0 %collective-permute-start.4 = (bf16[2,1,64,256]{3,2,1,0:T(8,128)(2,1)}, bf16[2,1,64,256]{3,2,1,0:T(8,128)(2,1)S(1)}, u32[]{:S(2)}, u32[]{:S(2)}) collective-permute-start(bf16[2,1,64,256]{3,2,1,0:T(8,128)(2,1)} %param.14), channel_id=1, source_target_pairs={{0,10},{2,8},{4,14},{6,12},{8,2},{10,0},{12,6},{14,4},{1,11},{3,9}... | collective-permute-start | bytes 196616 | tf_op jit(solution)/shard_map/ppermute | solution.py:53
  11.4 1.2 %copy-start.5 = (bf16[2,1,64,256]{3,2,1,0:T(8,128)(2,1)S(1)}, bf16[2,1,64,256]{3,2,1,0:T(8,128)(2,1)}, u32[]{:S(2)}) copy-start(bf16[2,1,64,256]{3,2,1,0:T(8,128)(2,1)} %param.14) | copy-start | bytes 196612
  12.6 9.3 %copy-start.12 = (f32[256]{0:T(256)S(1)}, f32[256]{0:T(256)}, u32[]{:S(2)}) copy-start(f32[256]{0:T(256)} %param.16) | copy-start | bytes 3076
  12.6 9.3 %copy-start.13 = (f32[256]{0:T(256)S(1)}, f32[256]{0:T(256)}, u32[]{:S(2)}) copy-start(f32[256]{0:T(256)} %param.15) | copy-start | bytes 3076
  12.6 4.9 %collective-permute-start.5 = (bf16[2,1,64,256]{3,2,1,0:T(8,128)(2,1)S(1)}, bf16[2,1,64,256]{3,2,1,0:T(8,128)(2,1)S(1)}, u32[]{:S(2)}, u32[]{:S(2)}) collective-permute-start(bf16[2,1,64,256]{3,2,1,0:T(8,128)(2,1)S(1)} %copy-done.5), channel_id=1, source_target_pairs={{0,12},{2,14},{4,0},{6,2},{8,4},{10,6},{12,8},{14,10},{1,13},{3,15... | collective-permute-start | bytes 196616 | tf_op jit(solution)/shard_map/ppermute | solution.py:53
  14.9 5.2 %collective-permute-start.6 = (bf16[2,1,64,256]{3,2,1,0:T(8,128)(2,1)S(1)}, bf16[2,1,64,256]{3,2,1,0:T(8,128)(2,1)S(1)}, u32[]{:S(2)}, u32[]{:S(2)}) collective-permute-start(bf16[2,1,64,256]{3,2,1,0:T(8,128)(2,1)S(1)} %copy-done.5), channel_id=1, source_target_pairs={{0,14},{2,12},{4,2},{6,0},{8,6},{10,4},{12,10},{14,8},{1,15},{3,13... | collective-permute-start | bytes 196616 | tf_op jit(solution)/shard_map/ppermute | solution.py:53
  23.4 3.1 %collective-permute-start.7 = (bf16[4,6,66,256]{3,0,2,1:T(4,128)(2,1)S(1)}, bf16[4,6,66,256]{3,0,2,1:T(4,128)(2,1)S(1)}, u32[]{:S(2)}, u32[]{:S(2)}) collective-permute-start(bf16[4,6,66,256]{3,0,2,1:T(4,128)(2,1)S(1)} %copy.29), channel_id=1, source_target_pairs={{0,1},{1,0},{2,3},{3,2},{4,5},{5,4},{6,7},{7,6},{8,9},{9,8},{10,11... | collective-permute-start | bytes 2433032 | tf_op jit(solution)/shard_map/ppermute | solution.py:66
  24.6 1.2 %copy-start.2 = (bf16[8,1,256,256]{3,2,1,0:T(8,128)(2,1)S(1)}, bf16[8,1,256,256]{3,2,1,0:T(8,128)(2,1)}, u32[]{:S(2)}) copy-start(bf16[8,1,256,256]{3,2,1,0:T(8,128)(2,1)} %get-tuple-element.8) | copy-start | bytes 3145732
  29.6 15.3 %copy-start.9 = (f32[256]{0:T(256)S(1)}, f32[256]{0:T(256)}, u32[]{:S(2)}) copy-start(f32[256]{0:T(256)} %param.18) | copy-start | bytes 3076
  29.6 15.8 %copy-start.14 = (f32[512]{0:T(512)S(1)}, f32[512]{0:T(512)}, u32[]{:S(2)}) copy-start(f32[512]{0:T(512)} %param.27) | copy-start | bytes 6148
  30.3 23.3 %copy-start.10 = (f32[256]{0:T(256)S(1)}, f32[256]{0:T(256)}, u32[]{:S(2)}) copy-start(f32[256]{0:T(256)} %param.20) | copy-start | bytes 3076
  30.3 23.3 %copy-start.11 = (f32[256]{0:T(256)S(1)}, f32[256]{0:T(256)}, u32[]{:S(2)}) copy-start(f32[256]{0:T(256)} %param.19) | copy-start | bytes 3076
  30.3 23.5 %copy-start.4 = (bf16[512,512]{1,0:T(8,128)(2,1)S(1)}, bf16[512,512]{1,0:T(8,128)(2,1)}, u32[]{:S(2)}) copy-start(bf16[512,512]{1,0:T(8,128)(2,1)} %param.24) | copy-start | bytes 1572868
  30.4 6.2 %collective-permute-start.10 = (f32[2,1,64,256]{3,2,1,0:T(8,128)S(1)}, f32[2,1,64,256]{3,2,1,0:T(8,128)S(1)}, u32[]{:S(2)}, u32[]{:S(2)}) collective-permute-start(f32[2,1,64,256]{3,2,1,0:T(8,128)S(1)} %get-tuple-element.26), channel_id=1, source_target_pairs={{0,12},{4,0},{8,4},{12,8},{1,13},{5,1},{9,5},{13,9},{2,14},{6,2},{... | collective-permute-start | bytes 393224 | tf_op jit(solution)/shard_map/ppermute | solution.py:53
  32.7 12.1 %collective-permute-start.9 = (f32[2,1,64,256]{3,2,1,0:T(8,128)S(1)}, f32[2,1,64,256]{3,2,1,0:T(8,128)S(1)}, u32[]{:S(2)}, u32[]{:S(2)}) collective-permute-start(f32[2,1,64,256]{3,2,1,0:T(8,128)S(1)} %get-tuple-element.27), channel_id=1, source_target_pairs={{0,8},{4,12},{8,0},{12,4},{1,9},{5,13},{9,1},{13,5},{2,10},{6,14},... | collective-permute-start | bytes 393224 | tf_op jit(solution)/shard_map/ppermute | solution.py:53
  32.7 12.1 %collective-permute-start.8 = (f32[2,1,64,256]{3,2,1,0:T(8,128)S(1)}, f32[2,1,64,256]{3,2,1,0:T(8,128)S(1)}, u32[]{:S(2)}, u32[]{:S(2)}) collective-permute-start(f32[2,1,64,256]{3,2,1,0:T(8,128)S(1)} %get-tuple-element.25), channel_id=1, source_target_pairs={{0,4},{4,8},{8,12},{12,0},{1,5},{5,9},{9,13},{13,1},{2,6},{6,10},{... | collective-permute-start | bytes 393224 | tf_op jit(solution)/shard_map/ppermute | solution.py:53
  44.9 9.3 %copy-start.3 = (bf16[512,512]{1,0:T(8,128)(2,1)S(1)}, bf16[512,512]{1,0:T(8,128)(2,1)}, u32[]{:S(2)}) copy-start(bf16[512,512]{1,0:T(8,128)(2,1)} %param.21) | copy-start | bytes 1572868
  44.9 6.9 %collective-permute-start.11 = (bf16[2,1,64,256]{3,2,1,0:T(8,128)(2,1)S(1)}, bf16[2,1,64,256]{3,2,1,0:T(8,128)(2,1)S(1)}, u32[]{:S(2)}, u32[]{:S(2)}) collective-permute-start(bf16[2,1,64,256]{3,2,1,0:T(8,128)(2,1)S(1)} %get-tuple-element.6), channel_id=1, source_target_pairs={{0,4},{4,8},{8,12},{12,0},{1,5},{5,9},{9,13},{13,1},{2,6},{6,10},{... | collective-permute-start | bytes 196616 | tf_op jit(solution)/shard_map/ppermute | solution.py:53
  45.4 7.2 %collective-permute-start.12 = (bf16[2,1,64,256]{3,2,1,0:T(8,128)(2,1)S(1)}, bf16[2,1,64,256]{3,2,1,0:T(8,128)(2,1)S(1)}, u32[]{:S(2)}, u32[]{:S(2)}) collective-permute-start(bf16[2,1,64,256]{3,2,1,0:T(8,128)(2,1)S(1)} %get-tuple-element.6), channel_id=1, source_target_pairs={{0,8},{4,12},{8,0},{12,4},{1,9},{5,13},{9,1},{13,5},{2,10},{6,14},... | collective-permute-start | bytes 196616 | tf_op jit(solution)/shard_map/ppermute | solution.py:53
  47.4 5.3 %collective-permute-start.13 = (bf16[2,1,64,256]{3,2,1,0:T(8,128)(2,1)S(1)}, bf16[2,1,64,256]{3,2,1,0:T(8,128)(2,1)S(1)}, u32[]{:S(2)}, u32[]{:S(2)}) collective-permute-start(bf16[2,1,64,256]{3,2,1,0:T(8,128)(2,1)S(1)} %get-tuple-element.6), channel_id=1, source_target_pairs={{0,12},{4,0},{8,4},{12,8},{1,13},{5,1},{9,5},{13,9},{2,14},{6,2},{... | collective-permute-start | bytes 196616 | tf_op jit(solution)/shard_map/ppermute | solution.py:53
  53.7 1.6 %collective-permute-start.14 = (bf16[2,4,64,256]{3,2,1,0:T(8,128)(2,1)S(1)}, bf16[2,4,64,256]{3,2,1,0:T(8,128)(2,1)S(1)}, u32[]{:S(2)}, u32[]{:S(2)}) collective-permute-start(bf16[2,4,64,256]{3,2,1,0:T(8,128)(2,1)S(1)} %fusion.26), channel_id=1, source_target_pairs={{0,1},{1,0},{2,3},{3,2},{4,5},{5,4},{6,7},{7,6},{8,9},{9,8},{10,11... | collective-permute-start | bytes 786440 | tf_op jit(solution)/shard_map/ppermute | solution.py:66
  54.1 1.5 %copy-start.8 = (f32[512]{0:T(512)S(1)}, f32[512]{0:T(512)}, u32[]{:S(2)}) copy-start(f32[512]{0:T(512)} %param.25) | copy-start | bytes 6148
  55.3 0.7 %copy-start.7 = (f32[512]{0:T(512)S(1)}, f32[512]{0:T(512)}, u32[]{:S(2)}) copy-start(f32[512]{0:T(512)} %param.22) | copy-start | bytes 6148
  55.6 1.4 %copy-start.6 = (bf16[512,512]{1,0:T(8,128)(2,1)S(1)}, bf16[512,512]{1,0:T(8,128)(2,1)}, u32[]{:S(2)}) copy-start(bf16[512,512]{1,0:T(8,128)(2,1)} %param.26) | copy-start | bytes 1572868

commit v8 on v7

--- a/solution.py
+++ b/solution.py
@@ -53,11 +53,13 @@
     return lax.ppermute(cells, axes, pairs)
 
 
-def offset_list(sizes):
-    offsets = [()]
-    for size in sizes:
-        offsets = [offset + (i,) for offset in offsets for i in range(size)]
-    return offsets
+def nearest_first(count):
+    order = []
+    for step in range(1, count):
+        for shift in (step, count - step):
+            if 0 < shift < count and shift not in order:
+                order.append(shift)
+    return order
 
 
 def chan_halves(cells):
@@ -109,16 +111,20 @@
     all_rows = rows_here * row_count
 
     if row_count * time_count <= PERMUTE_GROUP:
+        segment_rows = jnp.zeros((frames, all_rows, columns, channels), latent.dtype)
+        for shift in [0] + nearest_first(row_count):
+            block = latent if shift == 0 else shifted(latent, ("rows",), (row_count,), (shift,))
+            source_row = (row_place - shift) % row_count
+            segment_rows = lax.dynamic_update_slice(
+                segment_rows, block, (0, source_row * rows_here, 0, 0)
+            )
         clip = jnp.zeros((time_count * frames, all_rows, columns, channels), latent.dtype)
-        for offset in offset_list((row_count, time_count)):
-            block = latent if offset == (0, 0) else shifted(
-                latent, ("rows", "tm"), (row_count, time_count), offset
-            )
-            source_row = (row_place - offset[0]) % row_count
-            source_time = (time_place - offset[1]) % time_count
-            clip = lax.dynamic_update_slice(
-                clip, block, (source_time * frames, source_row * rows_here, 0, 0)
-            )
+        for shift in [0] + nearest_first(time_count):
+            block = segment_rows if shift == 0 else shifted(
+                segment_rows, ("tm",), (time_count,), (shift,)
+            )
+            source_time = (time_place - shift) % time_count
+            clip = lax.dynamic_update_slice(clip, block, (source_time * frames, 0, 0, 0))
     else:
         copies = jnp.broadcast_to(latent[None], (row_count * time_count,) + latent.shape)
         gathered = lax.all_to_all(copies, ("rows", "tm"), 0, 0, tiled=True).reshape(
@@ -175,7 +181,7 @@
     pieces = partial.reshape(frames, row_count, rows_here, columns, out_channels)
     if row_count <= PERMUTE_GROUP:
         convolved = lax.dynamic_index_in_dim(pieces, row_place, axis=1, keepdims=False)
-        for shift in range(1, row_count):
+        for shift in nearest_first(row_count):
             chunk = lax.dynamic_index_in_dim(
                 pieces, (row_place + shift) % row_count, axis=1, keepdims=False
             )
@@ -186,7 +192,7 @@
 
     if row_count <= PERMUTE_GROUP:
         middle = jnp.zeros((frames, all_rows, columns, out_channels), own_middle.dtype)
-        for shift in range(row_count):
+        for shift in [0] + nearest_first(row_count):
             block = own_middle if shift == 0 else shifted(
                 own_middle, ("rows",), (row_count,), (shift,)
             )

time: 58.1 us -> 58.3 us (level)
  waiting for transfers between devices: 19.4 us -> 24.7 us
  starting transfers between devices: 20.9 us -> 16 us
    ppermute x13 -> x10, waiting for transfers between devices: 18.7 us -> 24 us  [shifted(): return lax.ppermute(cells, axes, pairs)]
    ppermute x13 -> x10, starting transfers between devices: 20.7 us -> 15.8 us  [shifted(): return lax.ppermute(cells, axes, pairs)]
  transfers between devices with their start and end apart: 15 -> 12, of which waited for: 8 -> 10; matrix products, arithmetic and copies ran while one was open for 9% -> 9% of each run, Pallas kernels for 0% -> 0%
where the time goes in v8:
time: 58.3 us; the launch traced here: 58.1 us
  waiting for transfers between devices  24.7 us (42%)
  starting transfers between devices  16 us (27%)
  local copies, waits for them, and re-layouts  10.1 us (17%)
  matrix products  3.82 us (7%)
  other arithmetic  2.79 us (5%)
  between operations  0.67 us (1%)
    ppermute x10, waiting for transfers between devices, shifted(): return lax.ppermute(cells, axes, pairs)  24 us
    ppermute x10, starting transfers between devices, shifted(): return lax.ppermute(cells, axes, pairs)  15.8 us
    dynamic_slice x4, local copies, waits for them, and re-layouts, local(): lax.dynamic_slice(half, (tap // 9, tap // 3 % 3, tap % 3, 0), (frames, al...  3.7 us
    unnamed x52, local copies, waits for them, and re-layouts  1.71 us
    dot_general x6, matrix products, split_dot(): jnp.dot(half, half_rows(weight, shift, width), preferred_element_type=jnp...  1.58 us
    dot_general x2, matrix products, local(): term = jnp.dot(patches, block, preferred_element_type=jnp.float32)  1.42 us
  transfers between devices with their start and end apart: 12, of which 10 were waited for; matrix products, arithmetic and copies ran while one was open for 9% of the time, Pallas kernels for 0%

profile of v8, /device:TPU:0, one launch (start us, length us, event | category | flops | bytes accessed | tf_op | source)
XLA Modules:
  0.0 58.1 jit_solution(14731264539652871768)
XLA Ops:
  0.0 3.0 %collective-permute-start = (bf16[2,1,64,256]{3,2,1,0:T(8,128)(2,1)}, bf16[2,1,64,256]{3,2,1,0:T(8,128)(2,1)S(1)}, u32[]{:S(2)}, u32[]{:S(2)}) collective-permute-start(bf16[2,1,64,256]{3,2,1,0:T(8,128)(2,1)} %param.14), channel_id=1, source_target_pairs={{0,4},{4,8},{8,12},{12,0},{1,5},{5,9},{9,13},{13,1},{2,6},{6,10},{... | collective-permute-start | bytes 196616 | tf_op jit(solution)/shard_map/ppermute | solution.py:53
  3.0 2.1 %collective-permute-start.1 = (bf16[2,1,64,256]{3,2,1,0:T(8,128)(2,1)}, bf16[2,1,64,256]{3,2,1,0:T(8,128)(2,1)S(1)}, u32[]{:S(2)}, u32[]{:S(2)}) collective-permute-start(bf16[2,1,64,256]{3,2,1,0:T(8,128)(2,1)} %param.14), channel_id=1, source_target_pairs={{0,12},{4,0},{8,4},{12,8},{1,13},{5,1},{9,5},{13,9},{2,14},{6,2},{... | collective-permute-start | bytes 196616 | tf_op jit(solution)/shard_map/ppermute | solution.py:53
  5.1 0.9 %collective-permute-start.2 = (bf16[2,1,64,256]{3,2,1,0:T(8,128)(2,1)}, bf16[2,1,64,256]{3,2,1,0:T(8,128)(2,1)S(1)}, u32[]{:S(2)}, u32[]{:S(2)}) collective-permute-start(bf16[2,1,64,256]{3,2,1,0:T(8,128)(2,1)} %param.14), channel_id=1, source_target_pairs={{0,8},{4,12},{8,0},{12,4},{1,9},{5,13},{9,1},{13,5},{2,10},{6,14},... | collective-permute-start | bytes 196616 | tf_op jit(solution)/shard_map/ppermute | solution.py:53
  6.1 0.9 %constant_dynamic-update-slice_fusion.26 = bf16[2,4,64,256]{3,2,1,0:T(8,128)(2,1)S(1)} fusion(bf16[2,4,64,256]{3,2,1,0:T(8,128)(2,1)S(1)} %broadcast.147.clone, bf16[2,1,64,256]{3,2,1,0:T(8,128)(2,1)} %param.14, s32[]{:T(128)S(6)} %select_n.416), kind=kLoop, calls=%fused_computation.120 | loop fusion | bytes 131076 | tf_op jit(solution)/shard_map/dynamic_update_slice | solution.py:118
  7.0 0.1 broadcast_in_dim.17
  7.1 0.2 constant_dynamic-update-slice_fusion.20
  7.4 0.3 collective-permute-done
  7.7 0.5 collective-permute-done.1
  8.2 3.3 %collective-permute-done.2 = bf16[2,1,64,256]{3,2,1,0:T(8,128)(2,1)S(1)} collective-permute-done((bf16[2,1,64,256]{3,2,1,0:T(8,128)(2,1)}, bf16[2,1,64,256]{3,2,1,0:T(8,128)(2,1)S(1)}, u32[]{:S(2)}, u32[]{:S(2)}) %collective-permute-start.2) | collective-permute-done | bytes 65568 | tf_op jit(solution)/shard_map/ppermute | solution.py:53
  11.6 1.6 %collective-permute-start.3 = (bf16[2,4,64,256]{3,2,1,0:T(8,128)(2,1)S(1)}, bf16[2,4,64,256]{3,2,1,0:T(8,128)(2,1)S(1)}, u32[]{:S(2)}, u32[]{:S(2)}) collective-permute-start(bf16[2,4,64,256]{3,2,1,0:T(8,128)(2,1)S(1)} %constant_dynamic-update-slice_fusion.23), channel_id=1, source_target_pairs={{0,2},{2,0},{1,3},{3,1},{4,6},{6,4},{5,7},{7,5},{8,10},{10,8},{9,1... | collective-permute-start | bytes 786440 | tf_op jit(solution)/shard_map/ppermute | solution.py:53
  13.1 1.1 %constant_dynamic-slice_fusion.2 = (bf16[8,1,256,256]{3,2,1,0:T(8,128)(2,1)S(1)}, bf16[8,1,256,256]{3,2,1,0:T(8,128)(2,1)}) fusion(bf16[8,2,256,256]{3,2,1,0:T(8,128)(2,1)S(1)} %bitcast.68, s32[]{:T(128)S(6)} %select_n.491, s32[]{:T(128)S(6)} %select_n.489), kind=kLoop, calls=%fused_computation.96 | loop fusion | bytes 4194312 | tf_op jit(solution)/shard_map/jit(dynamic_index_in_dim)/dynamic_slice | solution.py:175
  14.3 5.2 %collective-permute-done.3 = bf16[2,4,64,256]{3,2,1,0:T(8,128)(2,1)S(1)} collective-permute-done((bf16[2,4,64,256]{3,2,1,0:T(8,128)(2,1)S(1)}, bf16[2,4,64,256]{3,2,1,0:T(8,128)(2,1)S(1)}, u32[]{:S(2)}, u32[]{:S(2)}) %collective-permute-start.3) | collective-permute-done | bytes 262176 | tf_op jit(solution)/shard_map/ppermute | solution.py:53
  19.5 0.2 convert_reduce_fusion
  19.7 0.1 reduce_sum.55
  19.8 0.1 reduce_sum.59
  20.0 0.1 sub.144
  20.1 0.2 fusion.14
  20.3 0.1 reduce_sum.61
  20.3 0.1 reduce_sum.62
  20.6 0.1 mul.91
  20.6 0.6 %gather_fusion = bf16[4,4,64,256]{3,2,1,0:T(8,128)(2,1)S(1)} fusion(bf16[4,4,64,256]{3,2,1,0:T(8,128)(2,1)S(1)} %constant_dynamic-update-slice_fusion.21, s32[1024]{0:T(1024)S(1)} %pad_clamp_fusion), kind=kCustom, calls=%fused_computation | custom fusion | bytes 1048592 | tf_op jit(solution)/shard_map/jit(_take)/gather | solution.py:141
  21.3 0.5 multiply_convert_fusion
  21.8 0.4 fusion.18
  22.1 0.4 copy.29
  22.5 0.2 constant_dynamic-slice_fusion.18
  22.9 1.1 %constant_dynamic-slice_fusion.12 = (bf16[2,4,64,256]{3,2,1,0:T(8,128)(2,1)S(1)}, bf16[2,4,64,256]{3,2,1,0:T(8,128)(2,1)S(1)}, bf16[2,4,64,256]{3,2,1,0:T(8,128)...) fusion(bf16[4,6,66,256]{3,2,1,0:T(8,128)(2,1)S(1)} %fusion.18, ...), kind=kLoop, calls=%fused_computation.107 | loop fusion | bytes 3145800 | tf_op jit(solution)/shard_map/dynamic_slice | solution.py:168
  24.2 1.0 %copy-done.2 = bf16[8,1,256,256]{3,2,1,0:T(8,128)(2,1)S(1)} copy-done((bf16[8,1,256,256]{3,2,1,0:T(8,128)(2,1)S(1)}, bf16[8,1,256,256]{3,2,1,0:T(8,128)(2,1)}, u32[]{:S(2)}) %copy-start.2) | copy-done | bytes 1048600
  25.2 0.7 %fusion.58 = f32[512,256]{1,0:T(8,128)S(1)} fusion(bf16[512,2048]{1,0:T(8,128)(2,1)S(1)} %constant_dynamic-update-slice_fusion, bf16[2048,256]{1,0:T(8,128)(2,1)S(1)} %bitcast.75), kind=kOutput, calls=%fused_computation.132 | convolution fusion | flops 536870912 | bytes 3670016 | tf_op jit(solution)/shard_map/dot_general | solution.py:178
  25.9 0.6 constant_dynamic-slice_fusion.9
  26.6 1.9 %constant_dynamic-slice_fusion.3 = (bf16[2,4,64,256]{3,0,2,1:T(2,128)(2,1)S(1)}, bf16[2,4,64,256]{3,0,2,1:T(2,128)(2,1)S(1)}, bf16[2,4,64,256]{3,0,2,1:T(2,128)(...) fusion(bf16[4,6,66,256]{3,0,2,1:T(4,128)(2,1)S(1)} %collective-, ...), kind=kLoop, calls=%fused_computation.97 | loop fusion | bytes 3145800 | tf_op jit(solution)/shard_map/dynamic_slice | solution.py:168
  29.0 0.7 %convolution_add_fusion.2 = f32[512,256]{1,0:T(8,128)S(1)} fusion(f32[512,256]{1,0:T(8,128)S(1)} %fusion.58, bf16[512,2048]{1,0:T(8,128)(2,1)S(1)} %constant_dynamic-update-slice_fusion.8, bf16[2048,256]{1,0:T(8,128)(2,1)S(1)} %bitcast.74), kind=kOutput, calls=%fused_computation.16 | convolution fusion | flops 537001984 | bytes 4194304 | tf_op jit(solution)/shard_map/dot_general | solution.py:178
  29.9 2.6 %collective-permute-start.6 = (f32[2,1,64,256]{3,2,1,0:T(8,128)S(1)}, f32[2,1,64,256]{3,2,1,0:T(8,128)S(1)}, u32[]{:S(2)}, u32[]{:S(2)}) collective-permute-start(f32[2,1,64,256]{3,2,1,0:T(8,128)S(1)} %get-tuple-element.27), channel_id=1, source_target_pairs={{0,12},{4,0},{8,4},{12,8},{1,13},{5,1},{9,5},{13,9},{2,14},{6,2},{... | collective-permute-start | bytes 393224 | tf_op jit(solution)/shard_map/ppermute | solution.py:53
  32.5 0.5 collective-permute-start.5
  33.0 6.7 %collective-permute-done.7 = f32[2,1,64,256]{3,2,1,0:T(8,128)S(1)} collective-permute-done((f32[2,1,64,256]{3,2,1,0:T(8,128)S(1)}, f32[2,1,64,256]{3,2,1,0:T(8,128)S(1)}, u32[]{:S(2)}, u32[]{:S(2)}) %collective-permute-start.7) | collective-permute-done | bytes 131104 | tf_op jit(solution)/shard_map/ppermute | solution.py:53
  39.7 2.8 %collective-permute-done.6 = f32[2,1,64,256]{3,2,1,0:T(8,128)S(1)} collective-permute-done((f32[2,1,64,256]{3,2,1,0:T(8,128)S(1)}, f32[2,1,64,256]{3,2,1,0:T(8,128)S(1)}, u32[]{:S(2)}, u32[]{:S(2)}) %collective-permute-start.6) | collective-permute-done | bytes 131104 | tf_op jit(solution)/shard_map/ppermute | solution.py:53
  42.6 3.2 %collective-permute-start.8 = (bf16[2,1,64,256]{3,2,1,0:T(8,128)(2,1)S(1)}, bf16[2,1,64,256]{3,2,1,0:T(8,128)(2,1)S(1)}, u32[]{:S(2)}, u32[]{:S(2)}) collective-permute-start(bf16[2,1,64,256]{3,2,1,0:T(8,128)(2,1)S(1)} %get-tuple-element.6), channel_id=1, source_target_pairs={{0,4},{4,8},{8,12},{12,0},{1,5},{5,9},{9,13},{13,1},{2,6},{6,10},{... | collective-permute-start | bytes 196616 | tf_op jit(solution)/shard_map/ppermute | solution.py:53
  45.8 0.1 dynamic_slice.129
  45.8 0.7 %collective-permute-start.9 = (bf16[2,1,64,256]{3,2,1,0:T(8,128)(2,1)S(1)}, bf16[2,1,64,256]{3,2,1,0:T(8,128)(2,1)S(1)}, u32[]{:S(2)}, u32[]{:S(2)}) collective-permute-start(bf16[2,1,64,256]{3,2,1,0:T(8,128)(2,1)S(1)} %get-tuple-element.6), channel_id=1, source_target_pairs={{0,12},{4,0},{8,4},{12,8},{1,13},{5,1},{9,5},{13,9},{2,14},{6,2},{... | collective-permute-start | bytes 196616 | tf_op jit(solution)/shard_map/ppermute | solution.py:53
  46.5 1.2 %collective-permute-start.10 = (bf16[2,1,64,256]{3,2,1,0:T(8,128)(2,1)S(1)}, bf16[2,1,64,256]{3,2,1,0:T(8,128)(2,1)S(1)}, u32[]{:S(2)}, u32[]{:S(2)}) collective-permute-start(bf16[2,1,64,256]{3,2,1,0:T(8,128)(2,1)S(1)} %get-tuple-element.6), channel_id=1, source_target_pairs={{0,8},{4,12},{8,0},{12,4},{1,9},{5,13},{9,1},{13,5},{2,10},{6,14},... | collective-permute-start | bytes 196616 | tf_op jit(solution)/shard_map/ppermute | solution.py:53
  47.7 1.6 %collective-permute-done.8 = bf16[2,1,64,256]{3,2,1,0:T(8,128)(2,1)S(1)} collective-permute-done((bf16[2,1,64,256]{3,2,1,0:T(8,128)(2,1)S(1)}, bf16[2,1,64,256]{3,2,1,0:T(8,128)(2,1)S(1)}, u32[]{:S(2)}, u32[]{:S(2)}) %collective-permute-start.8) | collective-permute-done | bytes 65568 | tf_op jit(solution)/shard_map/ppermute | solution.py:53
  49.3 1.3 %collective-permute-done.9 = bf16[2,1,64,256]{3,2,1,0:T(8,128)(2,1)S(1)} collective-permute-done((bf16[2,1,64,256]{3,2,1,0:T(8,128)(2,1)S(1)}, bf16[2,1,64,256]{3,2,1,0:T(8,128)(2,1)S(1)}, u32[]{:S(2)}, u32[]{:S(2)}) %collective-permute-start.9) | collective-permute-done | bytes 65568 | tf_op jit(solution)/shard_map/ppermute | solution.py:53
  50.7 2.2 %collective-permute-done.10 = bf16[2,1,64,256]{3,2,1,0:T(8,128)(2,1)S(1)} collective-permute-done((bf16[2,1,64,256]{3,2,1,0:T(8,128)(2,1)S(1)}, bf16[2,1,64,256]{3,2,1,0:T(8,128)(2,1)S(1)}, u32[]{:S(2)}, u32[]{:S(2)}) %collective-permute-start.10) | collective-permute-done | bytes 65568 | tf_op jit(solution)/shard_map/ppermute | solution.py:53
  53.0 0.1 reduce_sum.80
  53.1 0.1 reduce_sum.81
  53.2 0.1 sub.166
  53.2 0.1 sub.167
  53.3 0.1 fusion.23
  53.4 0.1 reduce_sum.83
  53.5 0.1 reduce_sum.84
  53.6 0.1 mul.99
  53.7 0.1 mul.100
  53.8 0.1 fusion.26
  54.0 0.3 fusion.29
  54.3 0.2 fusion.35
  54.5 0.3 fusion.32
  54.8 0.7 %collective-permute-done.11 = bf16[2,4,64,256]{3,2,1,0:T(8,128)(2,1)S(1)} collective-permute-done((bf16[2,4,64,256]{3,2,1,0:T(8,128)(2,1)S(1)}, bf16[2,4,64,256]{3,2,1,0:T(8,128)(2,1)S(1)}, u32[]{:S(2)}, u32[]{:S(2)}) %collective-permute-start.11) | collective-permute-done | bytes 262176 | tf_op jit(solution)/shard_map/ppermute | solution.py:68
  55.5 0.3 fusion.7
  55.8 0.3 fusion.8
  56.2 0.2 fusion.10
  56.4 0.4 fusion.57
  56.7 0.2 fusion.43
  56.9 0.3 fusion.11
  57.2 0.2 fusion.12
  57.4 0.6 %fusion.37 = bf16[2,1,64,256]{3,2,1,0:T(8,128)(2,1)} fusion(bf16[2,1,64,256]{3,2,1,0:T(8,128)(2,1)S(1)} %bitcast.97, bf16[2,1,64,256]{3,2,1,0:T(8,128)(2,1)S(1)} %get-tuple-element.6), kind=kLoop, calls=%fused_computation.53 | loop fusion | flops 131072 | bytes 196608 | tf_op jit(solution)/shard_map/convert_element_type | solution.py:253
  (84 shorter events, 1.6 us)
Async XLA Ops:
  0.0 54.5 %copy-start = (bf16[512,512]{1,0:T(8,128)(2,1)S(1)}, bf16[512,512]{1,0:T(8,128)(2,1)}, u32[]{:S(2)}) copy-start(bf16[512,512]{1,0:T(8,128)(2,1)} %param.23) | copy-start | bytes 1572868
  0.0 7.1 %copy-start.1 = (bf16[3456,256]{1,0:T(8,128)(2,1)S(1)}, bf16[3456,256]{1,0:T(8,128)(2,1)}, u32[]{:S(2)}) copy-start(bf16[3456,256]{1,0:T(8,128)(2,1)} %param.17) | copy-start | bytes 5308420
  0.0 7.7 %collective-permute-start = (bf16[2,1,64,256]{3,2,1,0:T(8,128)(2,1)}, bf16[2,1,64,256]{3,2,1,0:T(8,128)(2,1)S(1)}, u32[]{:S(2)}, u32[]{:S(2)}) collective-permute-start(bf16[2,1,64,256]{3,2,1,0:T(8,128)(2,1)} %param.14), channel_id=1, source_target_pairs={{0,4},{4,8},{8,12},{12,0},{1,5},{5,9},{9,13},{13,1},{2,6},{6,10},{... | collective-permute-start | bytes 196616 | tf_op jit(solution)/shard_map/ppermute | solution.py:53
  3.0 5.2 %collective-permute-start.1 = (bf16[2,1,64,256]{3,2,1,0:T(8,128)(2,1)}, bf16[2,1,64,256]{3,2,1,0:T(8,128)(2,1)S(1)}, u32[]{:S(2)}, u32[]{:S(2)}) collective-permute-start(bf16[2,1,64,256]{3,2,1,0:T(8,128)(2,1)} %param.14), channel_id=1, source_target_pairs={{0,12},{4,0},{8,4},{12,8},{1,13},{5,1},{9,5},{13,9},{2,14},{6,2},{... | collective-permute-start | bytes 196616 | tf_op jit(solution)/shard_map/ppermute | solution.py:53
  5.1 6.4 %collective-permute-start.2 = (bf16[2,1,64,256]{3,2,1,0:T(8,128)(2,1)}, bf16[2,1,64,256]{3,2,1,0:T(8,128)(2,1)S(1)}, u32[]{:S(2)}, u32[]{:S(2)}) collective-permute-start(bf16[2,1,64,256]{3,2,1,0:T(8,128)(2,1)} %param.14), channel_id=1, source_target_pairs={{0,8},{4,12},{8,0},{12,4},{1,9},{5,13},{9,1},{13,5},{2,10},{6,14},... | collective-permute-start | bytes 196616 | tf_op jit(solution)/shard_map/ppermute | solution.py:53
  11.6 7.9 %collective-permute-start.3 = (bf16[2,4,64,256]{3,2,1,0:T(8,128)(2,1)S(1)}, bf16[2,4,64,256]{3,2,1,0:T(8,128)(2,1)S(1)}, u32[]{:S(2)}, u32[]{:S(2)}) collective-permute-start(bf16[2,4,64,256]{3,2,1,0:T(8,128)(2,1)S(1)} %constant_dynamic-update-slice_fusion.23), channel_id=1, source_target_pairs={{0,2},{2,0},{1,3},{3,1},{4,6},{6,4},{5,7},{7,5},{8,10},{10,8},{9,1... | collective-permute-start | bytes 786440 | tf_op jit(solution)/shard_map/ppermute | solution.py:53
  14.3 7.0 %copy-start.12 = (f32[256]{0:T(256)S(1)}, f32[256]{0:T(256)}, u32[]{:S(2)}) copy-start(f32[256]{0:T(256)} %param.16) | copy-start | bytes 3076
  14.3 7.0 %copy-start.13 = (f32[256]{0:T(256)S(1)}, f32[256]{0:T(256)}, u32[]{:S(2)}) copy-start(f32[256]{0:T(256)} %param.15) | copy-start | bytes 3076
  22.8 3.1 %collective-permute-start.4 = (bf16[4,6,66,256]{3,0,2,1:T(4,128)(2,1)S(1)}, bf16[4,6,66,256]{3,0,2,1:T(4,128)(2,1)S(1)}, u32[]{:S(2)}, u32[]{:S(2)}) collective-permute-start(bf16[4,6,66,256]{3,0,2,1:T(4,128)(2,1)S(1)} %copy.29), channel_id=1, source_target_pairs={{0,1},{1,0},{2,3},{3,2},{4,5},{5,4},{6,7},{7,6},{8,9},{9,8},{10,11... | collective-permute-start | bytes 2433032 | tf_op jit(solution)/shard_map/ppermute | solution.py:68
  24.0 1.2 %copy-start.2 = (bf16[8,1,256,256]{3,2,1,0:T(8,128)(2,1)S(1)}, bf16[8,1,256,256]{3,2,1,0:T(8,128)(2,1)}, u32[]{:S(2)}) copy-start(bf16[8,1,256,256]{3,2,1,0:T(8,128)(2,1)} %get-tuple-element.8) | copy-start | bytes 3145732
  28.9 13.5 %copy-start.5 = (bf16[2,1,64,256]{3,2,1,0:T(8,128)(2,1)S(1)}, bf16[2,1,64,256]{3,2,1,0:T(8,128)(2,1)}, u32[]{:S(2)}) copy-start(bf16[2,1,64,256]{3,2,1,0:T(8,128)(2,1)} %param.14) | copy-start | bytes 196612
  29.0 13.5 %copy-start.9 = (f32[256]{0:T(256)S(1)}, f32[256]{0:T(256)}, u32[]{:S(2)}) copy-start(f32[256]{0:T(256)} %param.18) | copy-start | bytes 3076
  29.0 16.8 %copy-start.14 = (f32[512]{0:T(512)S(1)}, f32[512]{0:T(512)}, u32[]{:S(2)}) copy-start(f32[512]{0:T(512)} %param.27) | copy-start | bytes 6148
  29.7 24.1 %copy-start.10 = (f32[256]{0:T(256)S(1)}, f32[256]{0:T(256)}, u32[]{:S(2)}) copy-start(f32[256]{0:T(256)} %param.20) | copy-start | bytes 3076
  29.7 24.1 %copy-start.11 = (f32[256]{0:T(256)S(1)}, f32[256]{0:T(256)}, u32[]{:S(2)}) copy-start(f32[256]{0:T(256)} %param.19) | copy-start | bytes 3076
  29.7 24.3 %copy-start.4 = (bf16[512,512]{1,0:T(8,128)(2,1)S(1)}, bf16[512,512]{1,0:T(8,128)(2,1)}, u32[]{:S(2)}) copy-start(bf16[512,512]{1,0:T(8,128)(2,1)} %param.24) | copy-start | bytes 1572868
  29.8 9.9 %collective-permute-start.7 = (f32[2,1,64,256]{3,2,1,0:T(8,128)S(1)}, f32[2,1,64,256]{3,2,1,0:T(8,128)S(1)}, u32[]{:S(2)}, u32[]{:S(2)}) collective-permute-start(f32[2,1,64,256]{3,2,1,0:T(8,128)S(1)} %get-tuple-element.26), channel_id=1, source_target_pairs={{0,8},{4,12},{8,0},{12,4},{1,9},{5,13},{9,1},{13,5},{2,10},{6,14},... | collective-permute-start | bytes 393224 | tf_op jit(solution)/shard_map/ppermute | solution.py:53
  29.9 12.6 %collective-permute-start.6 = (f32[2,1,64,256]{3,2,1,0:T(8,128)S(1)}, f32[2,1,64,256]{3,2,1,0:T(8,128)S(1)}, u32[]{:S(2)}, u32[]{:S(2)}) collective-permute-start(f32[2,1,64,256]{3,2,1,0:T(8,128)S(1)} %get-tuple-element.27), channel_id=1, source_target_pairs={{0,12},{4,0},{8,4},{12,8},{1,13},{5,1},{9,5},{13,9},{2,14},{6,2},{... | collective-permute-start | bytes 393224 | tf_op jit(solution)/shard_map/ppermute | solution.py:53
  32.5 10.0 %collective-permute-start.5 = (f32[2,1,64,256]{3,2,1,0:T(8,128)S(1)}, f32[2,1,64,256]{3,2,1,0:T(8,128)S(1)}, u32[]{:S(2)}, u32[]{:S(2)}) collective-permute-start(f32[2,1,64,256]{3,2,1,0:T(8,128)S(1)} %get-tuple-element.25), channel_id=1, source_target_pairs={{0,4},{4,8},{8,12},{12,0},{1,5},{5,9},{9,13},{13,1},{2,6},{6,10},{... | collective-permute-start | bytes 393224 | tf_op jit(solution)/shard_map/ppermute | solution.py:53
  42.5 11.8 %copy-start.3 = (bf16[512,512]{1,0:T(8,128)(2,1)S(1)}, bf16[512,512]{1,0:T(8,128)(2,1)}, u32[]{:S(2)}) copy-start(bf16[512,512]{1,0:T(8,128)(2,1)} %param.21) | copy-start | bytes 1572868
  42.6 6.7 %collective-permute-start.8 = (bf16[2,1,64,256]{3,2,1,0:T(8,128)(2,1)S(1)}, bf16[2,1,64,256]{3,2,1,0:T(8,128)(2,1)S(1)}, u32[]{:S(2)}, u32[]{:S(2)}) collective-permute-start(bf16[2,1,64,256]{3,2,1,0:T(8,128)(2,1)S(1)} %get-tuple-element.6), channel_id=1, source_target_pairs={{0,4},{4,8},{8,12},{12,0},{1,5},{5,9},{9,13},{13,1},{2,6},{6,10},{... | collective-permute-start | bytes 196616 | tf_op jit(solution)/shard_map/ppermute | solution.py:53
  45.8 4.8 %collective-permute-start.9 = (bf16[2,1,64,256]{3,2,1,0:T(8,128)(2,1)S(1)}, bf16[2,1,64,256]{3,2,1,0:T(8,128)(2,1)S(1)}, u32[]{:S(2)}, u32[]{:S(2)}) collective-permute-start(bf16[2,1,64,256]{3,2,1,0:T(8,128)(2,1)S(1)} %get-tuple-element.6), channel_id=1, source_target_pairs={{0,12},{4,0},{8,4},{12,8},{1,13},{5,1},{9,5},{13,9},{2,14},{6,2},{... | collective-permute-start | bytes 196616 | tf_op jit(solution)/shard_map/ppermute | solution.py:53
  46.5 6.4 %collective-permute-start.10 = (bf16[2,1,64,256]{3,2,1,0:T(8,128)(2,1)S(1)}, bf16[2,1,64,256]{3,2,1,0:T(8,128)(2,1)S(1)}, u32[]{:S(2)}, u32[]{:S(2)}) collective-permute-start(bf16[2,1,64,256]{3,2,1,0:T(8,128)(2,1)S(1)} %get-tuple-element.6), channel_id=1, source_target_pairs={{0,8},{4,12},{8,0},{12,4},{1,9},{5,13},{9,1},{13,5},{2,10},{6,14},... | collective-permute-start | bytes 196616 | tf_op jit(solution)/shard_map/ppermute | solution.py:53
  53.9 1.6 %collective-permute-start.11 = (bf16[2,4,64,256]{3,2,1,0:T(8,128)(2,1)S(1)}, bf16[2,4,64,256]{3,2,1,0:T(8,128)(2,1)S(1)}, u32[]{:S(2)}, u32[]{:S(2)}) collective-permute-start(bf16[2,4,64,256]{3,2,1,0:T(8,128)(2,1)S(1)} %fusion.26), channel_id=1, source_target_pairs={{0,1},{1,0},{2,3},{3,2},{4,5},{5,4},{6,7},{7,6},{8,9},{9,8},{10,11... | collective-permute-start | bytes 786440 | tf_op jit(solution)/shard_map/ppermute | solution.py:68
  54.3 1.5 %copy-start.8 = (f32[512]{0:T(512)S(1)}, f32[512]{0:T(512)}, u32[]{:S(2)}) copy-start(f32[512]{0:T(512)} %param.25) | copy-start | bytes 6148
  55.5 0.7 %copy-start.7 = (f32[512]{0:T(512)S(1)}, f32[512]{0:T(512)}, u32[]{:S(2)}) copy-start(f32[512]{0:T(512)} %param.22) | copy-start | bytes 6148
  55.8 1.4 %copy-start.6 = (bf16[512,512]{1,0:T(8,128)(2,1)S(1)}, bf16[512,512]{1,0:T(8,128)(2,1)}, u32[]{:S(2)}) copy-start(bf16[512,512]{1,0:T(8,128)(2,1)} %param.26) | copy-start | bytes 1572868

commit v9 on v8

--- a/solution.py
+++ b/solution.py
@@ -158,35 +158,42 @@
         jnp.zeros((span * C, out_channels), conv_weight.dtype), conv_weight, (offset, 0)
     ).reshape(span, chan_count, channels, out_channels)
     taps = (block_rows * row_count) // C
-    partial = None
-    for shift, half in enumerate(padded_halves):
-        source = (chan_place - shift) % chan_count
-        windows = []
-        for step in range(span):
-            tap = jnp.minimum(first_tap + step, taps - 1)
-            windows.append(
-                lax.dynamic_slice(
-                    half,
-                    (tap // 9, (tap // 3) % 3, tap % 3, 0),
-                    (frames, all_rows, columns, channels),
-                ).reshape(-1, channels)
-            )
-        patches = jnp.concatenate(windows, axis=1)
-        block = lax.dynamic_index_in_dim(placed, source, axis=1, keepdims=False).reshape(
-            span * channels, out_channels
-        )
-        term = jnp.dot(patches, block, preferred_element_type=jnp.float32)
-        partial = term if partial is None else partial + term
-
-    pieces = partial.reshape(frames, row_count, rows_here, columns, out_channels)
+    blocks = [
+        lax.dynamic_index_in_dim(
+            placed, (chan_place - shift) % chan_count, axis=1, keepdims=False
+        ).reshape(span * channels, out_channels)
+        for shift in range(chan_count)
+    ]
+
+    def row_partial(row_block):
+        total = None
+        for half, block in zip(padded_halves, blocks):
+            windows = []
+            for step in range(span):
+                tap = jnp.minimum(first_tap + step, taps - 1)
+                windows.append(
+                    lax.dynamic_slice(
+                        half,
+                        (tap // 9, (tap // 3) % 3 + row_block * rows_here, tap % 3, 0),
+                        (frames, rows_here, columns, channels),
+                    ).reshape(-1, channels)
+                )
+            term = jnp.dot(
+                jnp.concatenate(windows, axis=1), block, preferred_element_type=jnp.float32
+            )
+            total = term if total is None else total + term
+        return total.reshape(frames, rows_here, columns, out_channels)
+
     if row_count <= PERMUTE_GROUP:
-        convolved = lax.dynamic_index_in_dim(pieces, row_place, axis=1, keepdims=False)
+        received = []
         for shift in nearest_first(row_count):
-            chunk = lax.dynamic_index_in_dim(
-                pieces, (row_place + shift) % row_count, axis=1, keepdims=False
-            )
-            convolved = convolved + shifted(chunk, ("rows",), (row_count,), (shift,))
+            chunk = row_partial((row_place + shift) % row_count)
+            received.append(shifted(chunk, ("rows",), (row_count,), (shift,)))
+        convolved = row_partial(row_place)
+        for piece in received:
+            convolved = convolved + piece
     else:
+        pieces = jnp.stack([row_partial(block) for block in range(row_count)], axis=1)
         convolved = jnp.sum(lax.all_to_all(pieces, "rows", 1, 1, tiled=True), axis=1)
     own_middle = (latent.astype(jnp.float32) + convolved + conv_bias).astype(jnp.bfloat16)
 

time: 58.3 us -> 58.1 us (level)
  local copies, waits for them, and re-layouts: 10.1 us -> 8.94 us
  matrix products: 3.82 us -> 4.94 us
  starting transfers between devices: 16 us -> 14.9 us
  other arithmetic: 2.79 us -> 3.84 us
  waiting for transfers between devices: 24.7 us -> 23.9 us
  between operations: 0.67 us -> 1.3 us
    dynamic_slice x5 -> x11, local copies, waits for them, and re-layouts: 4.81 us -> 3.35 us  [the longest x10 3.22 us: row_partial(): lax.dynamic_slice(half, (tap // 9, tap // 3 % 3 + row_block * rows_here,...]
    dot_general x2 -> x8, matrix products: 1.42 us -> 2.54 us  [row_partial(): jnp.dot(jnp.concatenate(windows, axis=1), block, preferred_element_type=j...]
    ppermute x10, starting transfers between devices: 15.8 us -> 14.8 us  [shifted(): return lax.ppermute(cells, axes, pairs)]
    convert_element_type x1, other arithmetic: 0.47 us -> 1.51 us  [local(): activated = jax.nn.silu(apply_norm(segment, mean1, var1, group_size) * no...]
    ppermute x10, waiting for transfers between devices: 24 us -> 23.2 us  [shifted(): return lax.ppermute(cells, axes, pairs)]
    gather x1, local copies, waits for them, and re-layouts: 0.6 us -> 1.39 us  [local(): segment = jnp.take(clip, frame_index, axis=0)]
    unnamed x52 -> x116, local copies, waits for them, and re-layouts: 1.71 us -> 1.15 us
  transfers between devices with their start and end apart: 12 -> 12, of which waited for: 10 -> 9; matrix products, arithmetic and copies ran while one was open for 9% -> 12% of each run, Pallas kernels for 0% -> 0%
where the time goes in v9:
time: 58.1 us; the launch traced here: 57.8 us
  waiting for transfers between devices  23.9 us (41%)
  starting transfers between devices  14.9 us (26%)
  local copies, waits for them, and re-layouts  8.94 us (15%)
  matrix products  4.94 us (9%)
  other arithmetic  3.84 us (7%)
  between operations  1.3 us (2%)
    ppermute x10, waiting for transfers between devices, shifted(): return lax.ppermute(cells, axes, pairs)  23.2 us
    ppermute x10, starting transfers between devices, shifted(): return lax.ppermute(cells, axes, pairs)  14.8 us
    dynamic_slice x10, local copies, waits for them, and re-layouts, row_partial(): lax.dynamic_slice(half, (tap // 9, tap // 3 % 3 + row_block * rows_here,...  3.22 us
    dot_general x8, matrix products, row_partial(): jnp.dot(jnp.concatenate(windows, axis=1), block, preferred_element_type=j...  2.54 us
    dot_general x6, matrix products, split_dot(): jnp.dot(half, half_rows(weight, shift, width), preferred_element_type=jnp...  1.57 us
    convert_element_type x1, other arithmetic, local(): activated = jax.nn.silu(apply_norm(segment, mean1, var1, group_size) * no...  1.51 us
    gather x1, local copies, waits for them, and re-layouts, local(): segment = jnp.take(clip, frame_index, axis=0)  1.39 us
  transfers between devices with their start and end apart: 12, of which 9 were waited for; matrix products, arithmetic and copies ran while one was open for 12% of the time, Pallas kernels for 0%

profile of v9, /device:TPU:0, one launch (start us, length us, event | category | flops | bytes accessed | tf_op | source)
XLA Modules:
  0.0 57.8 jit_solution(17034780529059173959)
XLA Ops:
  0.0 3.0 %collective-permute-start = (bf16[2,1,64,256]{3,2,1,0:T(8,128)(2,1)}, bf16[2,1,64,256]{3,2,1,0:T(8,128)(2,1)S(1)}, u32[]{:S(2)}, u32[]{:S(2)}) collective-permute-start(bf16[2,1,64,256]{3,2,1,0:T(8,128)(2,1)} %param.14), channel_id=1, source_target_pairs={{0,4},{4,8},{8,12},{12,0},{1,5},{5,9},{9,13},{13,1},{2,6},{6,10},{... | collective-permute-start | bytes 196616 | tf_op jit(solution)/shard_map/ppermute | solution.py:53
  3.0 2.1 %collective-permute-start.1 = (bf16[2,1,64,256]{3,2,1,0:T(8,128)(2,1)}, bf16[2,1,64,256]{3,2,1,0:T(8,128)(2,1)S(1)}, u32[]{:S(2)}, u32[]{:S(2)}) collective-permute-start(bf16[2,1,64,256]{3,2,1,0:T(8,128)(2,1)} %param.14), channel_id=1, source_target_pairs={{0,12},{4,0},{8,4},{12,8},{1,13},{5,1},{9,5},{13,9},{2,14},{6,2},{... | collective-permute-start | bytes 196616 | tf_op jit(solution)/shard_map/ppermute | solution.py:53
  5.1 1.0 %collective-permute-start.2 = (bf16[2,1,64,256]{3,2,1,0:T(8,128)(2,1)}, bf16[2,1,64,256]{3,2,1,0:T(8,128)(2,1)S(1)}, u32[]{:S(2)}, u32[]{:S(2)}) collective-permute-start(bf16[2,1,64,256]{3,2,1,0:T(8,128)(2,1)} %param.14), channel_id=1, source_target_pairs={{0,8},{4,12},{8,0},{12,4},{1,9},{5,13},{9,1},{13,5},{2,10},{6,14},... | collective-permute-start | bytes 196616 | tf_op jit(solution)/shard_map/ppermute | solution.py:53
  6.1 1.0 %constant_dynamic-update-slice_fusion.74 = bf16[2,4,64,256]{3,2,1,0:T(8,128)(2,1)S(1)} fusion(bf16[2,4,64,256]{3,2,1,0:T(8,128)(2,1)S(1)} %broadcast.147.clone, bf16[2,1,64,256]{3,2,1,0:T(8,128)(2,1)} %param.14, s32[]{:T(128)S(6)} %select_n.885), kind=kLoop, calls=%fused_computation.211 | loop fusion | bytes 131076 | tf_op jit(solution)/shard_map/dynamic_update_slice | solution.py:118
  7.1 0.1 broadcast_in_dim.17
  7.2 0.3 copy-done.1
  7.6 0.2 constant_dynamic-update-slice_fusion.68
  7.8 0.4 collective-permute-done.1
  8.2 3.3 %collective-permute-done.2 = bf16[2,1,64,256]{3,2,1,0:T(8,128)(2,1)S(1)} collective-permute-done((bf16[2,1,64,256]{3,2,1,0:T(8,128)(2,1)}, bf16[2,1,64,256]{3,2,1,0:T(8,128)(2,1)S(1)}, u32[]{:S(2)}, u32[]{:S(2)}) %collective-permute-start.2) | collective-permute-done | bytes 65568 | tf_op jit(solution)/shard_map/ppermute | solution.py:53
  11.6 1.6 %collective-permute-start.3 = (bf16[2,4,64,256]{3,2,1,0:T(8,128)(2,1)S(1)}, bf16[2,4,64,256]{3,2,1,0:T(8,128)(2,1)S(1)}, u32[]{:S(2)}, u32[]{:S(2)}) collective-permute-start(bf16[2,4,64,256]{3,2,1,0:T(8,128)(2,1)S(1)} %constant_dynamic-update-slice_fusion.71), channel_id=1, source_target_pairs={{0,2},{2,0},{1,3},{3,1},{4,6},{6,4},{5,7},{7,5},{8,10},{10,8},{9,1... | collective-permute-start | bytes 786440 | tf_op jit(solution)/shard_map/ppermute | solution.py:53
  13.1 0.1 constant_dynamic-slice_fusion.50
  13.4 6.1 %collective-permute-done.3 = bf16[2,4,64,256]{3,2,1,0:T(8,128)(2,1)S(1)} collective-permute-done((bf16[2,4,64,256]{3,2,1,0:T(8,128)(2,1)S(1)}, bf16[2,4,64,256]{3,2,1,0:T(8,128)(2,1)S(1)}, u32[]{:S(2)}, u32[]{:S(2)}) %collective-permute-start.3) | collective-permute-done | bytes 262176 | tf_op jit(solution)/shard_map/ppermute | solution.py:53
  19.5 0.2 convert_reduce_fusion
  19.8 0.1 reduce_sum.59
  20.1 0.2 fusion.14
  20.3 0.1 reduce_sum.62
  20.6 1.4 %gather_fusion = bf16[4,4,64,256]{3,2,1,0:T(8,128)(2,1)} fusion(bf16[4,4,64,256]{3,2,1,0:T(8,128)(2,1)S(1)} %constant_dynamic-update-slice_fusion.69, s32[1024]{0:T(1024)S(1)} %pad_clamp_fusion), kind=kCustom, calls=%fused_computation | custom fusion | bytes 1048592 | tf_op jit(solution)/shard_map/jit(_take)/gather | solution.py:141
  22.0 1.5 %multiply_convert_fusion = bf16[4,4,64,256]{3,2,1,0:T(8,128)(2,1)S(1)} fusion(f32[256]{0:T(256)S(1)} %copy-done.11, f32[256]{0:T(256)S(1)} %copy-done.12, f32[256]{0:T(256)S(1)} %mul.91, f32[256]{0:T(256)S(1)} %sub.240, bf16[4,4,64,256]{3,2,1,0:T(8,128)(2,1)} %gather_fusion, pred[4]{0:T(512)(128)(4,1)S(1)} %compare_and_fusion), kind=kLoop, calls=%fused_computation.30 | loop fusion | flops 2883584 | bytes 1052676 | tf_op jit(solution)/shard_map/convert_element_type | solution.py:144
  23.6 0.4 fusion.18
  23.9 0.4 copy.69
  24.4 0.2 constant_dynamic-slice_fusion.43
  24.6 0.2 constant_dynamic-slice_fusion.44
  24.8 0.2 constant_dynamic-slice_fusion.62
  25.0 0.2 constant_dynamic-slice_fusion.46
  25.2 0.2 constant_dynamic-slice_fusion.42
  25.4 0.3 fusion.55
  26.1 0.3 fusion.54
  26.4 0.3 fusion.52
  26.7 0.3 fusion.53
  27.1 0.6 constant_dynamic-slice_fusion.35
  27.7 0.4 constant_dynamic-slice_fusion.34
  28.2 0.3 constant_dynamic-slice_fusion.56
  28.7 0.3 convolution_add_fusion.4
  29.1 0.6 %constant_dynamic-slice_fusion.36 = (bf16[2,1,64,256]{3,0,2,1:T(2,128)(2,1)S(1)}, bf16[2,1,64,256]{3,0,2,1:T(2,128)(2,1)S(1)}, bf16[2,1,64,256]{3,0,2,1:T(2,128)...) fusion(bf16[4,6,66,256]{3,0,2,1:T(4,128)(2,1)S(1)} %collective-, ...), kind=kLoop, calls=%fused_computation.173 | loop fusion | bytes 1048648 | tf_op jit(solution)/shard_map/dynamic_slice | solution.py:175
  30.0 0.3 convolution_add_fusion.5
  30.3 2.6 %collective-permute-start.6 = (f32[2,1,64,256]{3,2,1,0:T(8,128)S(1)}, f32[2,1,64,256]{3,2,1,0:T(8,128)S(1)}, u32[]{:S(2)}, u32[]{:S(2)}) collective-permute-start(f32[2,1,64,256]{3,2,1,0:T(8,128)S(1)} %bitcast.205), channel_id=1, source_target_pairs={{0,12},{4,0},{8,4},{12,8},{1,13},{5,1},{9,5},{13,9},{2,14},{6,2},{... | collective-permute-start | bytes 393224 | tf_op jit(solution)/shard_map/ppermute | solution.py:53
  33.0 0.4 constant_dynamic-slice_fusion.41
  33.8 0.3 convolution_add_fusion.6
  34.1 0.6 %collective-permute-start.5 = (f32[2,1,64,256]{3,2,1,0:T(8,128)S(1)}, f32[2,1,64,256]{3,2,1,0:T(8,128)S(1)}, u32[]{:S(2)}, u32[]{:S(2)}) collective-permute-start(f32[2,1,64,256]{3,2,1,0:T(8,128)S(1)} %bitcast.206), channel_id=1, source_target_pairs={{0,4},{4,8},{8,12},{12,0},{1,5},{5,9},{9,13},{13,1},{2,6},{6,10},{... | collective-permute-start | bytes 393224 | tf_op jit(solution)/shard_map/ppermute | solution.py:53
  34.9 0.3 convolution_add_fusion.7
  35.2 3.5 %collective-permute-done.7 = f32[2,1,64,256]{3,2,1,0:T(8,128)S(1)} collective-permute-done((f32[2,1,64,256]{3,2,1,0:T(8,128)S(1)}, f32[2,1,64,256]{3,2,1,0:T(8,128)S(1)}, u32[]{:S(2)}, u32[]{:S(2)}) %collective-permute-start.7) | collective-permute-done | bytes 131104 | tf_op jit(solution)/shard_map/ppermute | solution.py:53
  38.7 4.2 %collective-permute-done.6 = f32[2,1,64,256]{3,2,1,0:T(8,128)S(1)} collective-permute-done((f32[2,1,64,256]{3,2,1,0:T(8,128)S(1)}, f32[2,1,64,256]{3,2,1,0:T(8,128)S(1)}, u32[]{:S(2)}, u32[]{:S(2)}) %collective-permute-start.6) | collective-permute-done | bytes 131104 | tf_op jit(solution)/shard_map/ppermute | solution.py:53
  42.9 2.0 %collective-permute-start.8 = (bf16[2,1,64,256]{3,2,1,0:T(8,128)(2,1)S(1)}, bf16[2,1,64,256]{3,2,1,0:T(8,128)(2,1)S(1)}, u32[]{:S(2)}, u32[]{:S(2)}) collective-permute-start(bf16[2,1,64,256]{3,2,1,0:T(8,128)(2,1)S(1)} %get-tuple-element.6), channel_id=1, source_target_pairs={{0,4},{4,8},{8,12},{12,0},{1,5},{5,9},{9,13},{13,1},{2,6},{6,10},{... | collective-permute-start | bytes 196616 | tf_op jit(solution)/shard_map/ppermute | solution.py:53
  45.0 1.9 %collective-permute-start.9 = (bf16[2,1,64,256]{3,2,1,0:T(8,128)(2,1)S(1)}, bf16[2,1,64,256]{3,2,1,0:T(8,128)(2,1)S(1)}, u32[]{:S(2)}, u32[]{:S(2)}) collective-permute-start(bf16[2,1,64,256]{3,2,1,0:T(8,128)(2,1)S(1)} %get-tuple-element.6), channel_id=1, source_target_pairs={{0,12},{4,0},{8,4},{12,8},{1,13},{5,1},{9,5},{13,9},{2,14},{6,2},{... | collective-permute-start | bytes 196616 | tf_op jit(solution)/shard_map/ppermute | solution.py:53
  46.9 2.5 %collective-permute-done.8 = bf16[2,1,64,256]{3,2,1,0:T(8,128)(2,1)S(1)} collective-permute-done((bf16[2,1,64,256]{3,2,1,0:T(8,128)(2,1)S(1)}, bf16[2,1,64,256]{3,2,1,0:T(8,128)(2,1)S(1)}, u32[]{:S(2)}, u32[]{:S(2)}) %collective-permute-start.8) | collective-permute-done | bytes 65568 | tf_op jit(solution)/shard_map/ppermute | solution.py:53
  49.4 0.6 %collective-permute-done.9 = bf16[2,1,64,256]{3,2,1,0:T(8,128)(2,1)S(1)} collective-permute-done((bf16[2,1,64,256]{3,2,1,0:T(8,128)(2,1)S(1)}, bf16[2,1,64,256]{3,2,1,0:T(8,128)(2,1)S(1)}, u32[]{:S(2)}, u32[]{:S(2)}) %collective-permute-start.9) | collective-permute-done | bytes 65568 | tf_op jit(solution)/shard_map/ppermute | solution.py:53
  50.0 2.7 %collective-permute-done.10 = bf16[2,1,64,256]{3,2,1,0:T(8,128)(2,1)S(1)} collective-permute-done((bf16[2,1,64,256]{3,2,1,0:T(8,128)(2,1)S(1)}, bf16[2,1,64,256]{3,2,1,0:T(8,128)(2,1)S(1)}, u32[]{:S(2)}, u32[]{:S(2)}) %collective-permute-start.10) | collective-permute-done | bytes 65568 | tf_op jit(solution)/shard_map/ppermute | solution.py:53
  52.8 0.1 reduce_sum.81
  53.1 0.1 fusion.23
  53.3 0.1 reduce_sum.84
  53.4 0.1 mul.100
  53.6 0.1 fusion.26
  53.8 0.3 fusion.29
  54.1 0.2 fusion.35
  54.3 0.3 fusion.32
  54.6 0.7 %collective-permute-done.11 = bf16[2,4,64,256]{3,2,1,0:T(8,128)(2,1)S(1)} collective-permute-done((bf16[2,4,64,256]{3,2,1,0:T(8,128)(2,1)S(1)}, bf16[2,4,64,256]{3,2,1,0:T(8,128)(2,1)S(1)}, u32[]{:S(2)}, u32[]{:S(2)}) %collective-permute-start.11) | collective-permute-done | bytes 262176 | tf_op jit(solution)/shard_map/ppermute | solution.py:68
  55.3 0.3 fusion.7
  55.6 0.3 fusion.8
  56.0 0.2 fusion.10
  56.1 0.4 fusion.51
  56.5 0.2 fusion.38
  56.7 0.3 fusion.11
  57.0 0.2 fusion.12
  57.2 0.6 %fusion.37 = bf16[2,1,64,256]{3,2,1,0:T(8,128)(2,1)} fusion(bf16[2,1,64,256]{3,2,1,0:T(8,128)(2,1)S(1)} %bitcast.198, bf16[2,1,64,256]{3,2,1,0:T(8,128)(2,1)S(1)} %get-tuple-element.6), kind=kLoop, calls=%fused_computation.120 | loop fusion | flops 131072 | bytes 196608 | tf_op jit(solution)/shard_map/convert_element_type | solution.py:260
  (165 shorter events, 2.4 us)
Async XLA Ops:
  0.0 54.3 %copy-start = (bf16[512,512]{1,0:T(8,128)(2,1)S(1)}, bf16[512,512]{1,0:T(8,128)(2,1)}, u32[]{:S(2)}) copy-start(bf16[512,512]{1,0:T(8,128)(2,1)} %param.23) | copy-start | bytes 1572868
  0.0 7.8 %collective-permute-start = (bf16[2,1,64,256]{3,2,1,0:T(8,128)(2,1)}, bf16[2,1,64,256]{3,2,1,0:T(8,128)(2,1)S(1)}, u32[]{:S(2)}, u32[]{:S(2)}) collective-permute-start(bf16[2,1,64,256]{3,2,1,0:T(8,128)(2,1)} %param.14), channel_id=1, source_target_pairs={{0,4},{4,8},{8,12},{12,0},{1,5},{5,9},{9,13},{13,1},{2,6},{6,10},{... | collective-permute-start | bytes 196616 | tf_op jit(solution)/shard_map/ppermute | solution.py:53
  3.0 5.2 %collective-permute-start.1 = (bf16[2,1,64,256]{3,2,1,0:T(8,128)(2,1)}, bf16[2,1,64,256]{3,2,1,0:T(8,128)(2,1)S(1)}, u32[]{:S(2)}, u32[]{:S(2)}) collective-permute-start(bf16[2,1,64,256]{3,2,1,0:T(8,128)(2,1)} %param.14), channel_id=1, source_target_pairs={{0,12},{4,0},{8,4},{12,8},{1,13},{5,1},{9,5},{13,9},{2,14},{6,2},{... | collective-permute-start | bytes 196616 | tf_op jit(solution)/shard_map/ppermute | solution.py:53
  5.1 6.5 %collective-permute-start.2 = (bf16[2,1,64,256]{3,2,1,0:T(8,128)(2,1)}, bf16[2,1,64,256]{3,2,1,0:T(8,128)(2,1)S(1)}, u32[]{:S(2)}, u32[]{:S(2)}) collective-permute-start(bf16[2,1,64,256]{3,2,1,0:T(8,128)(2,1)} %param.14), channel_id=1, source_target_pairs={{0,8},{4,12},{8,0},{12,4},{1,9},{5,13},{9,1},{13,5},{2,10},{6,14},... | collective-permute-start | bytes 196616 | tf_op jit(solution)/shard_map/ppermute | solution.py:53
  6.1 1.5 %copy-start.1 = (bf16[3456,256]{1,0:T(8,128)(2,1)S(1)}, bf16[3456,256]{1,0:T(8,128)(2,1)}, u32[]{:S(2)}) copy-start(bf16[3456,256]{1,0:T(8,128)(2,1)} %param.17) | copy-start | bytes 5308420
  11.6 7.9 %collective-permute-start.3 = (bf16[2,4,64,256]{3,2,1,0:T(8,128)(2,1)S(1)}, bf16[2,4,64,256]{3,2,1,0:T(8,128)(2,1)S(1)}, u32[]{:S(2)}, u32[]{:S(2)}) collective-permute-start(bf16[2,4,64,256]{3,2,1,0:T(8,128)(2,1)S(1)} %constant_dynamic-update-slice_fusion.71), channel_id=1, source_target_pairs={{0,2},{2,0},{1,3},{3,1},{4,6},{6,4},{5,7},{7,5},{8,10},{10,8},{9,1... | collective-permute-start | bytes 786440 | tf_op jit(solution)/shard_map/ppermute | solution.py:53
  13.3 8.7 %copy-start.11 = (f32[256]{0:T(256)S(1)}, f32[256]{0:T(256)}, u32[]{:S(2)}) copy-start(f32[256]{0:T(256)} %param.16) | copy-start | bytes 3076
  13.3 8.7 %copy-start.12 = (f32[256]{0:T(256)S(1)}, f32[256]{0:T(256)}, u32[]{:S(2)}) copy-start(f32[256]{0:T(256)} %param.15) | copy-start | bytes 3076
  24.5 2.5 %collective-permute-start.4 = (bf16[4,6,66,256]{3,0,2,1:T(4,128)(2,1)S(1)}, bf16[4,6,66,256]{3,0,2,1:T(4,128)(2,1)S(1)}, u32[]{:S(2)}, u32[]{:S(2)}) collective-permute-start(bf16[4,6,66,256]{3,0,2,1:T(4,128)(2,1)S(1)} %copy.69), channel_id=1, source_target_pairs={{0,1},{1,0},{2,3},{3,2},{4,5},{5,4},{6,7},{7,6},{8,9},{9,8},{10,11... | collective-permute-start | bytes 2433032 | tf_op jit(solution)/shard_map/ppermute | solution.py:68
  29.0 9.7 %collective-permute-start.7 = (f32[2,1,64,256]{3,2,1,0:T(8,128)S(1)}, f32[2,1,64,256]{3,2,1,0:T(8,128)S(1)}, u32[]{:S(2)}, u32[]{:S(2)}) collective-permute-start(f32[2,1,64,256]{3,2,1,0:T(8,128)S(1)} %bitcast.204), channel_id=1, source_target_pairs={{0,8},{4,12},{8,0},{12,4},{1,9},{5,13},{9,1},{13,5},{2,10},{6,14},... | collective-permute-start | bytes 393224 | tf_op jit(solution)/shard_map/ppermute | solution.py:53
  30.3 12.5 %collective-permute-start.6 = (f32[2,1,64,256]{3,2,1,0:T(8,128)S(1)}, f32[2,1,64,256]{3,2,1,0:T(8,128)S(1)}, u32[]{:S(2)}, u32[]{:S(2)}) collective-permute-start(f32[2,1,64,256]{3,2,1,0:T(8,128)S(1)} %bitcast.205), channel_id=1, source_target_pairs={{0,12},{4,0},{8,4},{12,8},{1,13},{5,1},{9,5},{13,9},{2,14},{6,2},{... | collective-permute-start | bytes 393224 | tf_op jit(solution)/shard_map/ppermute | solution.py:53
  34.1 8.8 %copy-start.4 = (bf16[2,1,64,256]{3,2,1,0:T(8,128)(2,1)S(1)}, bf16[2,1,64,256]{3,2,1,0:T(8,128)(2,1)}, u32[]{:S(2)}) copy-start(bf16[2,1,64,256]{3,2,1,0:T(8,128)(2,1)} %param.14) | copy-start | bytes 196612
  34.1 8.8 %copy-start.8 = (f32[256]{0:T(256)S(1)}, f32[256]{0:T(256)}, u32[]{:S(2)}) copy-start(f32[256]{0:T(256)} %param.18) | copy-start | bytes 3076
  34.1 8.7 %collective-permute-start.5 = (f32[2,1,64,256]{3,2,1,0:T(8,128)S(1)}, f32[2,1,64,256]{3,2,1,0:T(8,128)S(1)}, u32[]{:S(2)}, u32[]{:S(2)}) collective-permute-start(f32[2,1,64,256]{3,2,1,0:T(8,128)S(1)} %bitcast.206), channel_id=1, source_target_pairs={{0,4},{4,8},{8,12},{12,0},{1,5},{5,9},{9,13},{13,1},{2,6},{6,10},{... | collective-permute-start | bytes 393224 | tf_op jit(solution)/shard_map/ppermute | solution.py:53
  34.8 10.2 %copy-start.13 = (f32[512]{0:T(512)S(1)}, f32[512]{0:T(512)}, u32[]{:S(2)}) copy-start(f32[512]{0:T(512)} %param.27) | copy-start | bytes 6148
  34.8 18.7 %copy-start.9 = (f32[256]{0:T(256)S(1)}, f32[256]{0:T(256)}, u32[]{:S(2)}) copy-start(f32[256]{0:T(256)} %param.20) | copy-start | bytes 3076
  34.9 18.7 %copy-start.10 = (f32[256]{0:T(256)S(1)}, f32[256]{0:T(256)}, u32[]{:S(2)}) copy-start(f32[256]{0:T(256)} %param.19) | copy-start | bytes 3076
  35.2 18.6 %copy-start.3 = (bf16[512,512]{1,0:T(8,128)(2,1)S(1)}, bf16[512,512]{1,0:T(8,128)(2,1)}, u32[]{:S(2)}) copy-start(bf16[512,512]{1,0:T(8,128)(2,1)} %param.24) | copy-start | bytes 1572868
  42.9 11.2 %copy-start.2 = (bf16[512,512]{1,0:T(8,128)(2,1)S(1)}, bf16[512,512]{1,0:T(8,128)(2,1)}, u32[]{:S(2)}) copy-start(bf16[512,512]{1,0:T(8,128)(2,1)} %param.21) | copy-start | bytes 1572868
  42.9 6.5 %collective-permute-start.8 = (bf16[2,1,64,256]{3,2,1,0:T(8,128)(2,1)S(1)}, bf16[2,1,64,256]{3,2,1,0:T(8,128)(2,1)S(1)}, u32[]{:S(2)}, u32[]{:S(2)}) collective-permute-start(bf16[2,1,64,256]{3,2,1,0:T(8,128)(2,1)S(1)} %get-tuple-element.6), channel_id=1, source_target_pairs={{0,4},{4,8},{8,12},{12,0},{1,5},{5,9},{9,13},{13,1},{2,6},{6,10},{... | collective-permute-start | bytes 196616 | tf_op jit(solution)/shard_map/ppermute | solution.py:53
  45.0 5.0 %collective-permute-start.9 = (bf16[2,1,64,256]{3,2,1,0:T(8,128)(2,1)S(1)}, bf16[2,1,64,256]{3,2,1,0:T(8,128)(2,1)S(1)}, u32[]{:S(2)}, u32[]{:S(2)}) collective-permute-start(bf16[2,1,64,256]{3,2,1,0:T(8,128)(2,1)S(1)} %get-tuple-element.6), channel_id=1, source_target_pairs={{0,12},{4,0},{8,4},{12,8},{1,13},{5,1},{9,5},{13,9},{2,14},{6,2},{... | collective-permute-start | bytes 196616 | tf_op jit(solution)/shard_map/ppermute | solution.py:53
  46.9 5.8 %collective-permute-start.10 = (bf16[2,1,64,256]{3,2,1,0:T(8,128)(2,1)S(1)}, bf16[2,1,64,256]{3,2,1,0:T(8,128)(2,1)S(1)}, u32[]{:S(2)}, u32[]{:S(2)}) collective-permute-start(bf16[2,1,64,256]{3,2,1,0:T(8,128)(2,1)S(1)} %get-tuple-element.6), channel_id=1, source_target_pairs={{0,8},{4,12},{8,0},{12,4},{1,9},{5,13},{9,1},{13,5},{2,10},{6,14},... | collective-permute-start | bytes 196616 | tf_op jit(solution)/shard_map/ppermute | solution.py:53
  53.7 1.6 %collective-permute-start.11 = (bf16[2,4,64,256]{3,2,1,0:T(8,128)(2,1)S(1)}, bf16[2,4,64,256]{3,2,1,0:T(8,128)(2,1)S(1)}, u32[]{:S(2)}, u32[]{:S(2)}) collective-permute-start(bf16[2,4,64,256]{3,2,1,0:T(8,128)(2,1)S(1)} %fusion.26), channel_id=1, source_target_pairs={{0,1},{1,0},{2,3},{3,2},{4,5},{5,4},{6,7},{7,6},{8,9},{9,8},{10,11... | collective-permute-start | bytes 786440 | tf_op jit(solution)/shard_map/ppermute | solution.py:68
  54.3 1.3 %copy-start.7 = (f32[512]{0:T(512)S(1)}, f32[512]{0:T(512)}, u32[]{:S(2)}) copy-start(f32[512]{0:T(512)} %param.25) | copy-start | bytes 6148
  55.3 0.7 %copy-start.6 = (f32[512]{0:T(512)S(1)}, f32[512]{0:T(512)}, u32[]{:S(2)}) copy-start(f32[512]{0:T(512)} %param.22) | copy-start | bytes 6148
  55.9 1.1 %copy-start.5 = (bf16[512,512]{1,0:T(8,128)(2,1)S(1)}, bf16[512,512]{1,0:T(8,128)(2,1)}, u32[]{:S(2)}) copy-start(bf16[512,512]{1,0:T(8,128)(2,1)} %param.26) | copy-start | bytes 1572868

commit v10 on v8

--- a/solution.py
+++ b/solution.py
@@ -1,6 +1,8 @@
 import jax
 import jax.numpy as jnp
 from jax import lax
+from jax.experimental import pallas as pl
+from jax.experimental.pallas import tpu as pltpu
 from jax.sharding import PartitionSpec as P
 
 C = 512
@@ -32,6 +34,38 @@
     parts = [lax.slice_in_dim(cells, 0, 1, axis=dim)] * before + [cells]
     parts += [lax.slice_in_dim(cells, size - 1, size, axis=dim)] * after
     return jnp.concatenate(parts, axis=dim)
+
+
+def conv_taps_kernel(taps_ref, shifted_ref, weight_ref, init_ref, out_ref):
+    _, frames, rows, columns, channels = shifted_ref.shape
+    frames, rows = frames - 2, rows - 2
+    total = init_ref[...]
+    for step in range(weight_ref.shape[0]):
+        window = shifted_ref[
+            taps_ref[step, 2], pl.ds(taps_ref[step, 0], frames), pl.ds(taps_ref[step, 1], rows)
+        ]
+        total = total + jnp.dot(
+            window.reshape(frames * rows * columns, channels),
+            weight_ref[step],
+            preferred_element_type=jnp.float32,
+        )
+    out_ref[...] = total
+
+
+def conv_taps(taps, padded, weight, init):
+    columns = padded.shape[2] - 2
+    shifted = jnp.stack([padded[:, :, e : e + columns] for e in range(3)])
+    return pl.pallas_call(
+        conv_taps_kernel,
+        out_shape=jax.ShapeDtypeStruct(init.shape, jnp.float32),
+        in_specs=[
+            pl.BlockSpec(memory_space=pltpu.SMEM),
+            pl.BlockSpec(memory_space=pltpu.VMEM),
+            pl.BlockSpec(memory_space=pltpu.VMEM),
+            pl.BlockSpec(memory_space=pltpu.VMEM),
+        ],
+        out_specs=pl.BlockSpec(memory_space=pltpu.VMEM),
+    )(taps, shifted, weight, init)
 
 
 PERMUTE_GROUP = 8
@@ -158,25 +192,34 @@
         jnp.zeros((span * C, out_channels), conv_weight.dtype), conv_weight, (offset, 0)
     ).reshape(span, chan_count, channels, out_channels)
     taps = (block_rows * row_count) // C
-    partial = None
-    for shift, half in enumerate(padded_halves):
-        source = (chan_place - shift) % chan_count
-        windows = []
-        for step in range(span):
-            tap = jnp.minimum(first_tap + step, taps - 1)
-            windows.append(
-                lax.dynamic_slice(
-                    half,
-                    (tap // 9, (tap // 3) % 3, tap % 3, 0),
-                    (frames, all_rows, columns, channels),
-                ).reshape(-1, channels)
-            )
-        patches = jnp.concatenate(windows, axis=1)
-        block = lax.dynamic_index_in_dim(placed, source, axis=1, keepdims=False).reshape(
-            span * channels, out_channels
-        )
-        term = jnp.dot(patches, block, preferred_element_type=jnp.float32)
-        partial = term if partial is None else partial + term
+    if all_rows * columns * frames <= 1024:
+        steps = jnp.minimum(first_tap + jnp.arange(span), taps - 1)
+        tap_table = jnp.stack([steps // 9, (steps // 3) % 3, steps % 3], axis=1).astype(jnp.int32)
+        partial = jnp.zeros((frames * all_rows * columns, out_channels), jnp.float32)
+        for shift, half in enumerate(padded_halves):
+            source = (chan_place - shift) % chan_count
+            block = lax.dynamic_index_in_dim(placed, source, axis=1, keepdims=False)
+            partial = conv_taps(tap_table, half, block, partial)
+    else:
+        partial = None
+        for shift, half in enumerate(padded_halves):
+            source = (chan_place - shift) % chan_count
+            windows = []
+            for step in range(span):
+                tap = jnp.minimum(first_tap + step, taps - 1)
+                windows.append(
+                    lax.dynamic_slice(
+                        half,
+                        (tap // 9, (tap // 3) % 3, tap % 3, 0),
+                        (frames, all_rows, columns, channels),
+                    ).reshape(-1, channels)
+                )
+            patches = jnp.concatenate(windows, axis=1)
+            block = lax.dynamic_index_in_dim(placed, source, axis=1, keepdims=False).reshape(
+                span * channels, out_channels
+            )
+            term = jnp.dot(patches, block, preferred_element_type=jnp.float32)
+            partial = term if partial is None else partial + term
 
     pieces = partial.reshape(frames, row_count, rows_here, columns, out_channels)
     if row_count <= PERMUTE_GROUP:

time: 58.3 us -> 76.5 us (1.31)
  Pallas kernels: 0 us -> 7.2 us
  other arithmetic: 2.79 us -> 9.71 us
  local copies, waits for them, and re-layouts: 10.1 us -> 14.3 us
  waiting for transfers between devices: 24.7 us -> 26.5 us
  matrix products: 3.82 us -> 2.41 us
    pallas_call x0 -> x2, Pallas kernels: none -> 7.2 us  [conv_taps(): pl.pallas_call(conv_taps_kernel, out_shape=jax.ShapeDtypeStruct(init.shap...]
    dynamic_slice x5 -> x0, local copies, waits for them, and re-layouts: 4.81 us -> none  [the longest x4 3.7 us: local(): lax.dynamic_slice(half, (tap // 9, tap // 3 % 3, tap % 3, 0), (frames, al...]
    another operation x0 -> x4, other arithmetic: none -> 4.64 us  [the longest x3 3.97 us: conv_taps(): shifted = jnp.stack([padded[:, :, e:e + columns] for e in range(3)])]
    slice x0 -> x1, local copies, waits for them, and re-layouts: none -> 2.69 us  [conv_taps(): shifted = jnp.stack([padded[:, :, e:e + columns] for e in range(3)])]
    ppermute x10, waiting for transfers between devices: 24 us -> 25.9 us  [shifted(): return lax.ppermute(cells, axes, pairs)]
    squeeze x0 -> x1, local copies, waits for them, and re-layouts: none -> 1.46 us  [local(): block = lax.dynamic_index_in_dim(placed, source, axis=1, keepdims=False)]
    dot_general x2 -> x0, matrix products: 1.42 us -> none  [local(): term = jnp.dot(patches, block, preferred_element_type=jnp.float32)]
    squeeze x1, local copies, waits for them, and re-layouts: 0.04 us -> 1.1 us  [local(): lax.dynamic_index_in_dim(pieces, (row_place + shift) % row_count, axis=1,...]
  transfers between devices with their start and end apart: 12 -> 12, of which waited for: 10 -> 8; matrix products, arithmetic and copies ran while one was open for 9% -> 10% of each run, Pallas kernels for 0% -> 5%
where the time goes in v10:
time: 76.5 us; the launch traced here: 76.1 us
  waiting for transfers between devices  26.5 us (35%)
  starting transfers between devices  15.4 us (20%)
  local copies, waits for them, and re-layouts  14.3 us (19%)
  other arithmetic  9.71 us (13%)
  Pallas kernels  7.2 us (9%)
  matrix products  2.41 us (3%)
    ppermute x10, waiting for transfers between devices, shifted(): return lax.ppermute(cells, axes, pairs)  25.9 us
    ppermute x10, starting transfers between devices, shifted(): return lax.ppermute(cells, axes, pairs)  15.3 us
    pallas_call x2, Pallas kernels, conv_taps(): pl.pallas_call(conv_taps_kernel, out_shape=jax.ShapeDtypeStruct(init.shap...  7.2 us
    another operation x3, other arithmetic, conv_taps(): shifted = jnp.stack([padded[:, :, e:e + columns] for e in range(3)])  3.97 us
    slice x1, local copies, waits for them, and re-layouts, conv_taps(): shifted = jnp.stack([padded[:, :, e:e + columns] for e in range(3)])  2.69 us
    unnamed x29, local copies, waits for them, and re-layouts  1.8 us
    dot_general x6, matrix products, split_dot(): jnp.dot(half, half_rows(weight, shift, width), preferred_element_type=jnp...  1.59 us
  transfers between devices with their start and end apart: 12, of which 8 were waited for; matrix products, arithmetic and copies ran while one was open for 10% of the time, Pallas kernels for 5%

profile of v10, /device:TPU:0, one launch (start us, length us, event | category | flops | bytes accessed | tf_op | source)
XLA Modules:
  0.0 76.1 jit_solution(1646982261344434282)
XLA Ops:
  0.0 3.0 %collective-permute-start = (bf16[2,1,64,256]{3,2,1,0:T(8,128)(2,1)}, bf16[2,1,64,256]{3,2,1,0:T(8,128)(2,1)S(1)}, u32[]{:S(2)}, u32[]{:S(2)}) collective-permute-start(bf16[2,1,64,256]{3,2,1,0:T(8,128)(2,1)} %param.14), channel_id=1, source_target_pairs={{0,4},{4,8},{8,12},{12,0},{1,5},{5,9},{9,13},{13,1},{2,6},{6,10},{... | collective-permute-start | bytes 196616 | tf_op jit(solution)/shard_map/ppermute | solution.py:87
  3.0 2.1 %collective-permute-start.1 = (bf16[2,1,64,256]{3,2,1,0:T(8,128)(2,1)}, bf16[2,1,64,256]{3,2,1,0:T(8,128)(2,1)S(1)}, u32[]{:S(2)}, u32[]{:S(2)}) collective-permute-start(bf16[2,1,64,256]{3,2,1,0:T(8,128)(2,1)} %param.14), channel_id=1, source_target_pairs={{0,12},{4,0},{8,4},{12,8},{1,13},{5,1},{9,5},{13,9},{2,14},{6,2},{... | collective-permute-start | bytes 196616 | tf_op jit(solution)/shard_map/ppermute | solution.py:87
  5.1 1.0 %collective-permute-start.2 = (bf16[2,1,64,256]{3,2,1,0:T(8,128)(2,1)}, bf16[2,1,64,256]{3,2,1,0:T(8,128)(2,1)S(1)}, u32[]{:S(2)}, u32[]{:S(2)}) collective-permute-start(bf16[2,1,64,256]{3,2,1,0:T(8,128)(2,1)} %param.14), channel_id=1, source_target_pairs={{0,8},{4,12},{8,0},{12,4},{1,9},{5,13},{9,1},{13,5},{2,10},{6,14},... | collective-permute-start | bytes 196616 | tf_op jit(solution)/shard_map/ppermute | solution.py:87
  6.1 0.9 %constant_dynamic-update-slice_fusion.10 = bf16[2,4,64,256]{3,2,1,0:T(8,128)(2,1)S(1)} fusion(bf16[2,4,64,256]{3,2,1,0:T(8,128)(2,1)S(1)} %broadcast.312.clone, bf16[2,1,64,256]{3,2,1,0:T(8,128)(2,1)} %param.14, s32[]{:T(128)S(6)} %select_n.211), kind=kLoop, calls=%fused_computation.88 | loop fusion | bytes 131076 | tf_op jit(solution)/shard_map/dynamic_update_slice | solution.py:152
  6.9 0.1 broadcast_in_dim.19
  7.1 1.3 %copy-done.1 = bf16[3456,256]{1,0:T(8,128)(2,1)S(1)} copy-done((bf16[3456,256]{1,0:T(8,128)(2,1)S(1)}, bf16[3456,256]{1,0:T(8,128)(2,1)}, u32[]{:S(2)}) %copy-start.1) | copy-done | bytes 1769496
  8.4 0.2 constant_dynamic-update-slice_fusion.4
  8.7 2.9 %collective-permute-done.2 = bf16[2,1,64,256]{3,2,1,0:T(8,128)(2,1)S(1)} collective-permute-done((bf16[2,1,64,256]{3,2,1,0:T(8,128)(2,1)}, bf16[2,1,64,256]{3,2,1,0:T(8,128)(2,1)S(1)}, u32[]{:S(2)}, u32[]{:S(2)}) %collective-permute-start.2) | collective-permute-done | bytes 65568 | tf_op jit(solution)/shard_map/ppermute | solution.py:87
  11.6 1.6 %collective-permute-start.3 = (bf16[2,4,64,256]{3,2,1,0:T(8,128)(2,1)S(1)}, bf16[2,4,64,256]{3,2,1,0:T(8,128)(2,1)}, u32[]{:S(2)}, u32[]{:S(2)}) collective-permute-start(bf16[2,4,64,256]{3,2,1,0:T(8,128)(2,1)S(1)} %constant_dynamic-update-slice_fusion.7), channel_id=1, source_target_pairs={{0,2},{2,0},{1,3},{3,1},{4,6},{6,4},{5,7},{7,5},{8,10},{10,8},{9,1... | collective-permute-start | bytes 786440 | tf_op jit(solution)/shard_map/ppermute | solution.py:87
  13.3 6.3 %collective-permute-done.3 = bf16[2,4,64,256]{3,2,1,0:T(8,128)(2,1)} collective-permute-done((bf16[2,4,64,256]{3,2,1,0:T(8,128)(2,1)S(1)}, bf16[2,4,64,256]{3,2,1,0:T(8,128)(2,1)}, u32[]{:S(2)}, u32[]{:S(2)}) %collective-permute-start.3) | collective-permute-done | bytes 262176 | tf_op jit(solution)/shard_map/ppermute | solution.py:87
  19.6 1.0 %constant_dynamic-update-slice_fusion.5 = bf16[4,4,64,256]{3,2,1,0:T(8,128)(2,1)S(1)} fusion(bf16[4,4,64,256]{3,2,1,0:T(8,128)(2,1)S(1)} %constant_dynamic-update-slice_fusion.6, bf16[2,4,64,256]{3,2,1,0:T(8,128)(2,1)} %collective-permute-done.3, s32[]{:T(128)S(6)} %select_n.221), kind=kLoop, calls=%fused_computation.83 | loop fusion | bytes 524292 | tf_op jit(solution)/shard_map/dynamic_update_slice | solution.py:161
  20.6 0.2 convert_reduce_fusion
  20.7 1.4 %gather_fusion = bf16[4,4,64,256]{3,2,1,0:T(8,128)(2,1)} fusion(bf16[4,4,64,256]{3,2,1,0:T(8,128)(2,1)S(1)} %constant_dynamic-update-slice_fusion.5, s32[1024]{0:T(1024)S(1)} %pad_clamp_fusion), kind=kCustom, calls=%fused_computation | custom fusion | bytes 1048592 | tf_op jit(solution)/shard_map/jit(_take)/gather | solution.py:175
  22.2 0.1 reduce_sum.59
  22.4 0.1 sub.90
  22.5 0.2 fusion.8
  22.7 0.1 reduce_sum.61
  22.8 0.1 reduce_sum.62
  23.0 0.1 mul.92
  23.1 1.5 %multiply_convert_fusion = bf16[4,4,64,256]{3,2,1,0:T(8,128)(2,1)S(1)} fusion(f32[256]{0:T(256)S(1)} %copy-done.11, f32[256]{0:T(256)S(1)} %copy-done.12, f32[256]{0:T(256)S(1)} %mul.92, f32[256]{0:T(256)S(1)} %sub.90, bf16[4,4,64,256]{3,2,1,0:T(8,128)(2,1)} %gather_fusion, pred[4]{0:T(512)(128)(4,1)S(1)} %compare_and_fusion), kind=kLoop, calls=%fused_computation.22 | loop fusion | flops 2883584 | bytes 1052676 | tf_op jit(solution)/shard_map/convert_element_type | solution.py:178
  24.6 0.1 pad_maximum_fusion.9
  24.8 0.6 pad_maximum_fusion.2
  25.3 1.3 %copy.27 = bf16[4,6,66,256]{3,0,2,1:T(4,128)(2,1)} copy(bf16[4,6,66,256]{3,2,1,0:T(8,128)(2,1)S(1)} %pad_maximum_fusion.2) | data formatting | bytes 1622016 | tf_op jit(solution)/shard_map/concatenate | solution.py:36
  26.8 0.7 pad_add_fusion.taps_ref
  27.4 1.5 %dynamic-slice_bitcast_fusion = (bf16[8,256,256]{2,1,0:T(8,128)(2,1)}, bf16[8,256,256]{2,1,0:T(8,128)(2,1)}) fusion(bf16[8,2,256,256]{3,2,1,0:T(8,128)(2,1)S(1)} %bitcast.60, s32[]{:T(128)S(6)} %select_n.229, s32[]{:T(128)S(6)} %select_n.227), kind=kLoop, calls=%fused_computation.20 | loop fusion | bytes 4194312 | tf_op jit(solution)/shard_map/jit(dynamic_index_in_dim)/squeeze | solution.py:201
  28.9 0.6 fusion.10
  29.5 1.7 %pad_maximum_fusion.1.shifted_ref = bf16[3,4,6,64,256]{4,3,2,1,0:T(8,128)(2,1)} fusion(bf16[1,4,6,64,256]{4,3,2,1,0:T(8,128)(2,1)S(1)} %get-tuple-element.14, bf16[1,4,6,64,256]{4,3,2,1,0:T(8,128)(2,1)S(1)} %get-tuple-element.13, bf16[1,4,6,64,256]{4,3,2,1,0:T(8,128)(2,1)S(1)} %get-tuple-element.12), kind=kLoop, calls=%fused_computation.2 | loop fusion | flops 2359296 | bytes 4718592 | tf_op jit(solution)/shard_map/stack | solution.py:57
  31.2 0.8 %broadcast_in_dim.20.init_ref = f32[512,256]{1,0:T(8,128)} broadcast(f32[]{:T(128)} %constant.198.clone.1), dimensions={} | broadcast | bytes 524292 | tf_op jit(solution)/shard_map/broadcast_in_dim | solution.py:198
  32.0 3.6 %shard_map.136.init_ref = f32[512,256]{1,0:T(8,128)} custom-call(s32[8,3]{1,0:T(8,128)} %pad_add_fusion.taps_ref, bf16[3,4,6,64,256]{4,3,2,1,0:T(8,128)(2,1)} %pad_maximum_fusion.1.shifted_ref, bf16[8,256,256]{2,1,0:T(8,128)(2,1)} %get-tuple-element.7.weight_ref, f32[512,256]{1,0:T(8,128)} %broadcast_in_dim.20.init_ref), custom_call_target="tpu_custom_call" | custom-call | tf_op jit(solution)/shard_map/pallas_call | solution.py:58
  35.6 2.7 %fusion.53 = (bf16[4,6,64,256]{3,0,2,1:T(4,128)(2,1)S(1)}, bf16[4,6,64,256]{3,0,2,1:T(4,128)(2,1)S(1)}, bf16[4,6,64,256]{3,0,2,1:T(4,128)(2,1)S(1)}) fusion(bf16[4,6,66,256]{3,0,2,1:T(4,128)(2,1)} %collective-permute-done.4), kind=kLoop, calls=%fused_computation.113 | loop fusion | bytes 4718592 | tf_op jit(solution)/shard_map/slice | solution.py:57
  38.3 0.1 copy.37
  38.5 0.3 copy_bitcast_fusion
  38.7 1.7 %pad_maximum_fusion.shifted_ref = bf16[3,4,6,64,256]{4,3,2,1,0:T(8,128)(2,1)} fusion(bf16[1,4,6,64,256]{4,3,2,1,0:T(8,128)(2,1)S(1)} %get-tuple-element.26, bf16[1,4,6,64,256]{4,3,2,1,0:T(8,128)(2,1)S(1)} %get-tuple-element.27, bf16[1,4,6,64,256]{4,3,2,1,0:T(8,128)(2,1)S(1)} %bitcast.61), kind=kLoop, calls=%fused_computation.1 | loop fusion | flops 2359296 | bytes 4718592 | tf_op jit(solution)/shard_map/stack | solution.py:57
  40.4 3.6 %shard_map.137 = f32[512,256]{1,0:T(8,128)} custom-call(s32[8,3]{1,0:T(8,128)} %pad_add_fusion.taps_ref, bf16[3,4,6,64,256]{4,3,2,1,0:T(8,128)(2,1)} %pad_maximum_fusion.shifted_ref, bf16[8,256,256]{2,1,0:T(8,128)(2,1)} %get-tuple-element.8.weight_ref, f32[512,256]{1,0:T(8,128)} %shard_map.136.init_ref), custom_call_target="tpu_custom_call" | custom-call | tf_op jit(solution)/shard_map/pallas_call | solution.py:58
  44.0 1.1 %dynamic-slice_bitcast_fusion.4 = (f32[2,1,64,256]{3,2,1,0:T(8,128)S(1)}, f32[2,1,64,256]{3,2,1,0:T(8,128)S(1)}, f32[2,1,64,256]{3,2,1,0:T(8,128)S(1)}) fusion(f32[2,4,1,64,256]{4,3,1,0,2:T(8,128)} %bitcast.65, s32[]{:T(128)S(6)} %select_n.232, s32[]{:T(128)S(6)} %select_n.236, s32[]{:T(128)S(6)} %select_n.234), kind=kLoop, calls=%fused_computation.65 | loop fusion | bytes 786444 | tf_op jit(solution)/shard_map/jit(dynamic_index_in_dim)/squeeze | solution.py:228
  45.2 3.8 %collective-permute-start.6 = (f32[2,1,64,256]{3,2,1,0:T(8,128)S(1)}, f32[2,1,64,256]{3,2,1,0:T(8,128)S(1)}, u32[]{:S(2)}, u32[]{:S(2)}) collective-permute-start(f32[2,1,64,256]{3,2,1,0:T(8,128)S(1)} %get-tuple-element.19), channel_id=1, source_target_pairs={{0,12},{4,0},{8,4},{12,8},{1,13},{5,1},{9,5},{13,9},{2,14},{6,2},{... | collective-permute-start | bytes 393224 | tf_op jit(solution)/shard_map/ppermute | solution.py:87
  49.0 4.3 %collective-permute-done.5 = f32[2,1,64,256]{3,2,1,0:T(8,128)S(1)} collective-permute-done((f32[2,1,64,256]{3,2,1,0:T(8,128)S(1)}, f32[2,1,64,256]{3,2,1,0:T(8,128)S(1)}, u32[]{:S(2)}, u32[]{:S(2)}) %collective-permute-start.5) | collective-permute-done | bytes 131104 | tf_op jit(solution)/shard_map/ppermute | solution.py:87
  53.3 0.6 collective-permute-done.6
  54.0 6.6 %collective-permute-done.7 = f32[2,1,64,256]{3,2,1,0:T(8,128)S(1)} collective-permute-done((f32[2,1,64,256]{3,2,1,0:T(8,128)S(1)}, f32[2,1,64,256]{3,2,1,0:T(8,128)S(1)}, u32[]{:S(2)}, u32[]{:S(2)}) %collective-permute-start.7) | collective-permute-done | bytes 131104 | tf_op jit(solution)/shard_map/ppermute | solution.py:87
  60.6 1.0 %constant_dynamic-update-slice_fusion.3 = (bf16[2,4,64,256]{3,2,1,0:T(8,128)(2,1)S(1)}, bf16[2,1,64,256]{3,2,1,0:T(8,128)(2,1)S(1)}) fusion(bf16[2,4,64,256]{3,2,1,0:T(8,128)(2,1)S(1)} %broadcast.312, s32[]{:T(128)S(6)} %select_n.211, f32[256]{0:T(256)S(1)} %copy-done.8, f32[2,1,64,256]{3,2,1,0:T(8,128)S(1)} %collective-permute-done.7, ...), kind=kLoop, calls=%fused_computation.81 | loop fusion | flops 229376 | bytes 721928 | tf_op jit(solution)/shard_map/dynamic_update_slice | solution.py:243
  61.8 3.8 %collective-permute-start.9 = (bf16[2,1,64,256]{3,2,1,0:T(8,128)(2,1)S(1)}, bf16[2,1,64,256]{3,2,1,0:T(8,128)(2,1)S(1)}, u32[]{:S(2)}, u32[]{:S(2)}) collective-permute-start(bf16[2,1,64,256]{3,2,1,0:T(8,128)(2,1)S(1)} %get-tuple-element.6), channel_id=1, source_target_pairs={{0,12},{4,0},{8,4},{12,8},{1,13},{5,1},{9,5},{13,9},{2,14},{6,2},{... | collective-permute-start | bytes 196616 | tf_op jit(solution)/shard_map/ppermute | solution.py:87
  65.6 2.9 %collective-permute-done.8 = bf16[2,1,64,256]{3,2,1,0:T(8,128)(2,1)S(1)} collective-permute-done((bf16[2,1,64,256]{3,2,1,0:T(8,128)(2,1)S(1)}, bf16[2,1,64,256]{3,2,1,0:T(8,128)(2,1)S(1)}, u32[]{:S(2)}, u32[]{:S(2)}) %collective-permute-start.8) | collective-permute-done | bytes 65568 | tf_op jit(solution)/shard_map/ppermute | solution.py:87
  68.5 2.2 %collective-permute-done.10 = bf16[2,1,64,256]{3,2,1,0:T(8,128)(2,1)S(1)} collective-permute-done((bf16[2,1,64,256]{3,2,1,0:T(8,128)(2,1)S(1)}, bf16[2,1,64,256]{3,2,1,0:T(8,128)(2,1)S(1)}, u32[]{:S(2)}, u32[]{:S(2)}) %collective-permute-start.10) | collective-permute-done | bytes 65568 | tf_op jit(solution)/shard_map/ppermute | solution.py:87
  70.8 0.1 reduce_sum.80
  70.9 0.1 reduce_sum.81
  71.1 0.1 sub.96
  71.2 0.1 fusion.13
  71.3 0.1 reduce_sum.83
  71.3 0.1 reduce_sum.84
  71.5 0.1 mul.100
  71.6 0.1 fusion.16
  71.8 0.3 fusion.22
  72.1 0.2 fusion.25
  72.4 0.3 fusion.19
  72.7 0.7 collective-permute-done.11
  73.3 0.3 fusion.1
  73.7 0.2 fusion.4
  73.9 0.4 fusion.56
  74.2 0.2 fusion.33
  74.4 0.3 fusion.2
  74.8 0.3 fusion.5
  75.0 0.3 copy-done.5
  75.3 0.2 fusion.6
  75.5 0.6 fusion.27
  (66 shorter events, 1.1 us)
Async XLA Ops:
  0.0 71.8 %copy-start = (bf16[512,512]{1,0:T(8,128)(2,1)S(1)}, bf16[512,512]{1,0:T(8,128)(2,1)}, u32[]{:S(2)}) copy-start(bf16[512,512]{1,0:T(8,128)(2,1)} %param.23) | copy-start | bytes 1572868
  0.0 8.6 %collective-permute-start = (bf16[2,1,64,256]{3,2,1,0:T(8,128)(2,1)}, bf16[2,1,64,256]{3,2,1,0:T(8,128)(2,1)S(1)}, u32[]{:S(2)}, u32[]{:S(2)}) collective-permute-start(bf16[2,1,64,256]{3,2,1,0:T(8,128)(2,1)} %param.14), channel_id=1, source_target_pairs={{0,4},{4,8},{8,12},{12,0},{1,5},{5,9},{9,13},{13,1},{2,6},{6,10},{... | collective-permute-start | bytes 196616 | tf_op jit(solution)/shard_map/ppermute | solution.py:87
  3.0 5.7 %collective-permute-start.1 = (bf16[2,1,64,256]{3,2,1,0:T(8,128)(2,1)}, bf16[2,1,64,256]{3,2,1,0:T(8,128)(2,1)S(1)}, u32[]{:S(2)}, u32[]{:S(2)}) collective-permute-start(bf16[2,1,64,256]{3,2,1,0:T(8,128)(2,1)} %param.14), channel_id=1, source_target_pairs={{0,12},{4,0},{8,4},{12,8},{1,13},{5,1},{9,5},{13,9},{2,14},{6,2},{... | collective-permute-start | bytes 196616 | tf_op jit(solution)/shard_map/ppermute | solution.py:87
  5.1 6.5 %collective-permute-start.2 = (bf16[2,1,64,256]{3,2,1,0:T(8,128)(2,1)}, bf16[2,1,64,256]{3,2,1,0:T(8,128)(2,1)S(1)}, u32[]{:S(2)}, u32[]{:S(2)}) collective-permute-start(bf16[2,1,64,256]{3,2,1,0:T(8,128)(2,1)} %param.14), channel_id=1, source_target_pairs={{0,8},{4,12},{8,0},{12,4},{1,9},{5,13},{9,1},{13,5},{2,10},{6,14},... | collective-permute-start | bytes 196616 | tf_op jit(solution)/shard_map/ppermute | solution.py:87
  6.9 1.5 %copy-start.1 = (bf16[3456,256]{1,0:T(8,128)(2,1)S(1)}, bf16[3456,256]{1,0:T(8,128)(2,1)}, u32[]{:S(2)}) copy-start(bf16[3456,256]{1,0:T(8,128)(2,1)} %param.17) | copy-start | bytes 5308420
  11.6 8.0 %collective-permute-start.3 = (bf16[2,4,64,256]{3,2,1,0:T(8,128)(2,1)S(1)}, bf16[2,4,64,256]{3,2,1,0:T(8,128)(2,1)}, u32[]{:S(2)}, u32[]{:S(2)}) collective-permute-start(bf16[2,4,64,256]{3,2,1,0:T(8,128)(2,1)S(1)} %constant_dynamic-update-slice_fusion.7), channel_id=1, source_target_pairs={{0,2},{2,0},{1,3},{3,1},{4,6},{6,4},{5,7},{7,5},{8,10},{10,8},{9,1... | collective-permute-start | bytes 786440 | tf_op jit(solution)/shard_map/ppermute | solution.py:87
  13.2 9.8 %copy-start.11 = (f32[256]{0:T(256)S(1)}, f32[256]{0:T(256)}, u32[]{:S(2)}) copy-start(f32[256]{0:T(256)} %param.16) | copy-start | bytes 3076
  13.2 9.8 %copy-start.12 = (f32[256]{0:T(256)S(1)}, f32[256]{0:T(256)}, u32[]{:S(2)}) copy-start(f32[256]{0:T(256)} %param.15) | copy-start | bytes 3076
  26.6 9.0 %collective-permute-start.4 = (bf16[4,6,66,256]{3,0,2,1:T(4,128)(2,1)}, bf16[4,6,66,256]{3,0,2,1:T(4,128)(2,1)}, u32[]{:S(2)}, u32[]{:S(2)}) collective-permute-start(bf16[4,6,66,256]{3,0,2,1:T(4,128)(2,1)} %copy.27), channel_id=1, source_target_pairs={{0,1},{1,0},{2,3},{3,2},{4,5},{5,4},{6,7},{7,6},{8,9},{9,8},{10,11... | collective-permute-start | bytes 2433032 | tf_op jit(solution)/shard_map/ppermute | solution.py:102
  40.4 20.2 %copy-start.4 = (bf16[2,1,64,256]{3,2,1,0:T(8,128)(2,1)S(1)}, bf16[2,1,64,256]{3,2,1,0:T(8,128)(2,1)}, u32[]{:S(2)}) copy-start(bf16[2,1,64,256]{3,2,1,0:T(8,128)(2,1)} %param.14) | copy-start | bytes 196612
  40.4 20.2 %copy-start.8 = (f32[256]{0:T(256)S(1)}, f32[256]{0:T(256)}, u32[]{:S(2)}) copy-start(f32[256]{0:T(256)} %param.18) | copy-start | bytes 3076
  44.0 17.7 %copy-start.13 = (f32[512]{0:T(512)S(1)}, f32[512]{0:T(512)}, u32[]{:S(2)}) copy-start(f32[512]{0:T(512)} %param.27) | copy-start | bytes 6148
  44.0 27.6 %copy-start.9 = (f32[256]{0:T(256)S(1)}, f32[256]{0:T(256)}, u32[]{:S(2)}) copy-start(f32[256]{0:T(256)} %param.20) | copy-start | bytes 3076
  44.0 27.6 %copy-start.10 = (f32[256]{0:T(256)S(1)}, f32[256]{0:T(256)}, u32[]{:S(2)}) copy-start(f32[256]{0:T(256)} %param.19) | copy-start | bytes 3076
  45.1 8.2 %collective-permute-start.5 = (f32[2,1,64,256]{3,2,1,0:T(8,128)S(1)}, f32[2,1,64,256]{3,2,1,0:T(8,128)S(1)}, u32[]{:S(2)}, u32[]{:S(2)}) collective-permute-start(f32[2,1,64,256]{3,2,1,0:T(8,128)S(1)} %get-tuple-element.17), channel_id=1, source_target_pairs={{0,4},{4,8},{8,12},{12,0},{1,5},{5,9},{9,13},{13,1},{2,6},{6,10},{... | collective-permute-start | bytes 393224 | tf_op jit(solution)/shard_map/ppermute | solution.py:87
  45.2 8.8 %collective-permute-start.6 = (f32[2,1,64,256]{3,2,1,0:T(8,128)S(1)}, f32[2,1,64,256]{3,2,1,0:T(8,128)S(1)}, u32[]{:S(2)}, u32[]{:S(2)}) collective-permute-start(f32[2,1,64,256]{3,2,1,0:T(8,128)S(1)} %get-tuple-element.19), channel_id=1, source_target_pairs={{0,12},{4,0},{8,4},{12,8},{1,13},{5,1},{9,5},{13,9},{2,14},{6,2},{... | collective-permute-start | bytes 393224 | tf_op jit(solution)/shard_map/ppermute | solution.py:87
  49.0 11.6 %collective-permute-start.7 = (f32[2,1,64,256]{3,2,1,0:T(8,128)S(1)}, f32[2,1,64,256]{3,2,1,0:T(8,128)S(1)}, u32[]{:S(2)}, u32[]{:S(2)}) collective-permute-start(f32[2,1,64,256]{3,2,1,0:T(8,128)S(1)} %get-tuple-element.18), channel_id=1, source_target_pairs={{0,8},{4,12},{8,0},{12,4},{1,9},{5,13},{9,1},{13,5},{2,10},{6,14},... | collective-permute-start | bytes 393224 | tf_op jit(solution)/shard_map/ppermute | solution.py:87
  61.6 10.5 %copy-start.2 = (bf16[512,512]{1,0:T(8,128)(2,1)S(1)}, bf16[512,512]{1,0:T(8,128)(2,1)}, u32[]{:S(2)}) copy-start(bf16[512,512]{1,0:T(8,128)(2,1)} %param.21) | copy-start | bytes 1572868
  61.6 6.9 %collective-permute-start.8 = (bf16[2,1,64,256]{3,2,1,0:T(8,128)(2,1)S(1)}, bf16[2,1,64,256]{3,2,1,0:T(8,128)(2,1)S(1)}, u32[]{:S(2)}, u32[]{:S(2)}) collective-permute-start(bf16[2,1,64,256]{3,2,1,0:T(8,128)(2,1)S(1)} %get-tuple-element.6), channel_id=1, source_target_pairs={{0,4},{4,8},{8,12},{12,0},{1,5},{5,9},{9,13},{13,1},{2,6},{6,10},{... | collective-permute-start | bytes 196616 | tf_op jit(solution)/shard_map/ppermute | solution.py:87
  61.8 6.7 %collective-permute-start.9 = (bf16[2,1,64,256]{3,2,1,0:T(8,128)(2,1)S(1)}, bf16[2,1,64,256]{3,2,1,0:T(8,128)(2,1)S(1)}, u32[]{:S(2)}, u32[]{:S(2)}) collective-permute-start(bf16[2,1,64,256]{3,2,1,0:T(8,128)(2,1)S(1)} %get-tuple-element.6), channel_id=1, source_target_pairs={{0,12},{4,0},{8,4},{12,8},{1,13},{5,1},{9,5},{13,9},{2,14},{6,2},{... | collective-permute-start | bytes 196616 | tf_op jit(solution)/shard_map/ppermute | solution.py:87
  65.6 5.2 %collective-permute-start.10 = (bf16[2,1,64,256]{3,2,1,0:T(8,128)(2,1)S(1)}, bf16[2,1,64,256]{3,2,1,0:T(8,128)(2,1)S(1)}, u32[]{:S(2)}, u32[]{:S(2)}) collective-permute-start(bf16[2,1,64,256]{3,2,1,0:T(8,128)(2,1)S(1)} %get-tuple-element.6), channel_id=1, source_target_pairs={{0,8},{4,12},{8,0},{12,4},{1,9},{5,13},{9,1},{13,5},{2,10},{6,14},... | collective-permute-start | bytes 196616 | tf_op jit(solution)/shard_map/ppermute | solution.py:87
  70.8 1.6 %copy-start.3 = (bf16[512,512]{1,0:T(8,128)(2,1)S(1)}, bf16[512,512]{1,0:T(8,128)(2,1)}, u32[]{:S(2)}) copy-start(bf16[512,512]{1,0:T(8,128)(2,1)} %param.24) | copy-start | bytes 1572868
  71.7 1.6 %collective-permute-start.11 = (bf16[2,4,64,256]{3,2,1,0:T(8,128)(2,1)S(1)}, bf16[2,4,64,256]{3,2,1,0:T(8,128)(2,1)S(1)}, u32[]{:S(2)}, u32[]{:S(2)}) collective-permute-start(bf16[2,4,64,256]{3,2,1,0:T(8,128)(2,1)S(1)} %fusion.16), channel_id=1, source_target_pairs={{0,1},{1,0},{2,3},{3,2},{4,5},{5,4},{6,7},{7,6},{8,9},{9,8},{10,11... | collective-permute-start | bytes 786440 | tf_op jit(solution)/shard_map/ppermute | solution.py:102
  72.4 1.3 %copy-start.6 = (f32[512]{0:T(512)S(1)}, f32[512]{0:T(512)}, u32[]{:S(2)}) copy-start(f32[512]{0:T(512)} %param.22) | copy-start | bytes 6148
  73.3 1.1 %copy-start.7 = (f32[512]{0:T(512)S(1)}, f32[512]{0:T(512)}, u32[]{:S(2)}) copy-start(f32[512]{0:T(512)} %param.25) | copy-start | bytes 6148
  74.2 1.0 %copy-start.5 = (bf16[512,512]{1,0:T(8,128)(2,1)S(1)}, bf16[512,512]{1,0:T(8,128)(2,1)}, u32[]{:S(2)}) copy-start(bf16[512,512]{1,0:T(8,128)(2,1)} %param.26) | copy-start | bytes 1572868

commit v11 on v8

--- a/solution.py
+++ b/solution.py
@@ -142,8 +142,9 @@
     activated = jax.nn.silu(
         apply_norm(segment, mean1, var1, group_size) * norm1_gain + norm1_bias
     ).astype(jnp.bfloat16)
-    padded = edge_pad(edge_pad(activated, 1, 1, 1), 2, 1, 1)
-    padded_halves = chan_halves(padded)
+    padded_halves = [
+        edge_pad(edge_pad(half, 1, 1, 1), 2, 1, 1) for half in chan_halves(activated)
+    ]
 
     block_rows = conv_weight.shape[0]
     start = row_place * block_rows

time: 58.3 us -> 56.8 us (0.974)
  local copies, waits for them, and re-layouts: 10.1 us -> 8.31 us
    dynamic_slice x4, local copies, waits for them, and re-layouts: 3.7 us -> 2.55 us  [local(): lax.dynamic_slice(half, (tap // 9, tap // 3 % 3, tap % 3, 0), (frames, al...]
    unnamed x52 -> x44, local copies, waits for them, and re-layouts: 1.71 us -> 1.49 us
  transfers between devices with their start and end apart: 12 -> 12, of which waited for: 10 -> 10; matrix products, arithmetic and copies ran while one was open for 9% -> 10% of each run, Pallas kernels for 0% -> 0%
where the time goes in v11:
time: 56.8 us; the launch traced here: 56.6 us
  waiting for transfers between devices  24.7 us (43%)
  starting transfers between devices  16 us (28%)
  local copies, waits for them, and re-layouts  8.31 us (15%)
  matrix products  3.83 us (7%)
  other arithmetic  3.15 us (6%)
  between operations  0.6 us (1%)
    ppermute x10, waiting for transfers between devices, shifted(): return lax.ppermute(cells, axes, pairs)  24.1 us
    ppermute x10, starting transfers between devices, shifted(): return lax.ppermute(cells, axes, pairs)  15.8 us
    dynamic_slice x4, local copies, waits for them, and re-layouts, local(): lax.dynamic_slice(half, (tap // 9, tap // 3 % 3, tap % 3, 0), (frames, al...  2.55 us
    dot_general x6, matrix products, split_dot(): jnp.dot(half, half_rows(weight, shift, width), preferred_element_type=jnp...  1.56 us
    unnamed x44, local copies, waits for them, and re-layouts  1.49 us
    dot_general x2, matrix products, local(): term = jnp.dot(patches, block, preferred_element_type=jnp.float32)  1.45 us
  transfers between devices with their start and end apart: 12, of which 10 were waited for; matrix products, arithmetic and copies ran while one was open for 10% of the time, Pallas kernels for 0%

profile of v11, /device:TPU:0, one launch (start us, length us, event | category | flops | bytes accessed | tf_op | source)
XLA Modules:
  0.0 56.6 jit_solution(5398512639967054642)
XLA Ops:
  0.0 3.0 %collective-permute-start = (bf16[2,1,64,256]{3,2,1,0:T(8,128)(2,1)}, bf16[2,1,64,256]{3,2,1,0:T(8,128)(2,1)S(1)}, u32[]{:S(2)}, u32[]{:S(2)}) collective-permute-start(bf16[2,1,64,256]{3,2,1,0:T(8,128)(2,1)} %param.14), channel_id=1, source_target_pairs={{0,4},{4,8},{8,12},{12,0},{1,5},{5,9},{9,13},{13,1},{2,6},{6,10},{... | collective-permute-start | bytes 196616 | tf_op jit(solution)/shard_map/ppermute | solution.py:53
  3.0 2.1 %collective-permute-start.1 = (bf16[2,1,64,256]{3,2,1,0:T(8,128)(2,1)}, bf16[2,1,64,256]{3,2,1,0:T(8,128)(2,1)S(1)}, u32[]{:S(2)}, u32[]{:S(2)}) collective-permute-start(bf16[2,1,64,256]{3,2,1,0:T(8,128)(2,1)} %param.14), channel_id=1, source_target_pairs={{0,12},{4,0},{8,4},{12,8},{1,13},{5,1},{9,5},{13,9},{2,14},{6,2},{... | collective-permute-start | bytes 196616 | tf_op jit(solution)/shard_map/ppermute | solution.py:53
  5.1 0.9 %collective-permute-start.2 = (bf16[2,1,64,256]{3,2,1,0:T(8,128)(2,1)}, bf16[2,1,64,256]{3,2,1,0:T(8,128)(2,1)S(1)}, u32[]{:S(2)}, u32[]{:S(2)}) collective-permute-start(bf16[2,1,64,256]{3,2,1,0:T(8,128)(2,1)} %param.14), channel_id=1, source_target_pairs={{0,8},{4,12},{8,0},{12,4},{1,9},{5,13},{9,1},{13,5},{2,10},{6,14},... | collective-permute-start | bytes 196616 | tf_op jit(solution)/shard_map/ppermute | solution.py:53
  6.1 0.9 %constant_dynamic-update-slice_fusion.26 = bf16[2,4,64,256]{3,2,1,0:T(8,128)(2,1)S(1)} fusion(bf16[2,4,64,256]{3,2,1,0:T(8,128)(2,1)S(1)} %broadcast.147.clone, bf16[2,1,64,256]{3,2,1,0:T(8,128)(2,1)} %param.14, s32[]{:T(128)S(6)} %select_n.416), kind=kLoop, calls=%fused_computation.132 | loop fusion | bytes 131076 | tf_op jit(solution)/shard_map/dynamic_update_slice | solution.py:118
  7.0 0.1 broadcast_in_dim.17
  7.1 0.2 constant_dynamic-update-slice_fusion.20
  7.4 0.3 collective-permute-done
  7.7 0.5 collective-permute-done.1
  8.2 3.3 %collective-permute-done.2 = bf16[2,1,64,256]{3,2,1,0:T(8,128)(2,1)S(1)} collective-permute-done((bf16[2,1,64,256]{3,2,1,0:T(8,128)(2,1)}, bf16[2,1,64,256]{3,2,1,0:T(8,128)(2,1)S(1)}, u32[]{:S(2)}, u32[]{:S(2)}) %collective-permute-start.2) | collective-permute-done | bytes 65568 | tf_op jit(solution)/shard_map/ppermute | solution.py:53
  11.6 1.6 %collective-permute-start.3 = (bf16[2,4,64,256]{3,2,1,0:T(8,128)(2,1)S(1)}, bf16[2,4,64,256]{3,2,1,0:T(8,128)(2,1)S(1)}, u32[]{:S(2)}, u32[]{:S(2)}) collective-permute-start(bf16[2,4,64,256]{3,2,1,0:T(8,128)(2,1)S(1)} %constant_dynamic-update-slice_fusion.23), channel_id=1, source_target_pairs={{0,2},{2,0},{1,3},{3,1},{4,6},{6,4},{5,7},{7,5},{8,10},{10,8},{9,1... | collective-permute-start | bytes 786440 | tf_op jit(solution)/shard_map/ppermute | solution.py:53
  13.1 1.1 %constant_dynamic-slice_fusion.2 = (bf16[8,1,256,256]{3,2,1,0:T(8,128)(2,1)S(1)}, bf16[8,1,256,256]{3,2,1,0:T(8,128)(2,1)}) fusion(bf16[8,2,256,256]{3,2,1,0:T(8,128)(2,1)S(1)} %bitcast.68, s32[]{:T(128)S(6)} %select_n.491, s32[]{:T(128)S(6)} %select_n.489), kind=kLoop, calls=%fused_computation.108 | loop fusion | bytes 4194312 | tf_op jit(solution)/shard_map/jit(dynamic_index_in_dim)/dynamic_slice | solution.py:176
  14.3 5.2 %collective-permute-done.3 = bf16[2,4,64,256]{3,2,1,0:T(8,128)(2,1)S(1)} collective-permute-done((bf16[2,4,64,256]{3,2,1,0:T(8,128)(2,1)S(1)}, bf16[2,4,64,256]{3,2,1,0:T(8,128)(2,1)S(1)}, u32[]{:S(2)}, u32[]{:S(2)}) %collective-permute-start.3) | collective-permute-done | bytes 262176 | tf_op jit(solution)/shard_map/ppermute | solution.py:53
  19.5 0.2 convert_reduce_fusion
  19.7 0.1 reduce_sum.55
  19.8 0.1 reduce_sum.59
  20.0 0.1 sub.144
  20.1 0.2 fusion.20
  20.3 0.1 reduce_sum.61
  20.3 0.1 reduce_sum.62
  20.6 0.1 mul.91
  20.6 0.6 %gather_fusion = bf16[4,4,64,256]{3,2,1,0:T(8,128)(2,1)S(1)} fusion(bf16[4,4,64,256]{3,2,1,0:T(8,128)(2,1)S(1)} %constant_dynamic-update-slice_fusion.21, s32[1024]{0:T(1024)S(1)} %pad_clamp_fusion), kind=kCustom, calls=%fused_computation | custom fusion | bytes 1048592 | tf_op jit(solution)/shard_map/jit(_take)/gather | solution.py:141
  21.3 0.5 multiply_convert_fusion
  21.8 0.4 fusion.24
  22.2 0.2 constant_dynamic-slice_fusion.18
  22.5 1.1 %constant_dynamic-slice_fusion.12 = (bf16[2,4,64,256]{3,2,1,0:T(8,128)(2,1)S(1)}, bf16[2,4,64,256]{3,2,1,0:T(8,128)(2,1)S(1)}, bf16[2,4,64,256]{3,2,1,0:T(8,128)...) fusion(bf16[4,6,66,256]{3,2,1,0:T(8,128)(2,1)S(1)} %fusion.24, ...), kind=kLoop, calls=%fused_computation.119 | loop fusion | bytes 3145800 | tf_op jit(solution)/shard_map/dynamic_slice | solution.py:169
  23.8 1.0 %copy-done.2 = bf16[8,1,256,256]{3,2,1,0:T(8,128)(2,1)S(1)} copy-done((bf16[8,1,256,256]{3,2,1,0:T(8,128)(2,1)S(1)}, bf16[8,1,256,256]{3,2,1,0:T(8,128)(2,1)}, u32[]{:S(2)}) %copy-start.2) | copy-done | bytes 1048600
  24.8 0.7 %fusion.71 = f32[512,256]{1,0:T(8,128)S(1)} fusion(bf16[512,2048]{1,0:T(8,128)(2,1)S(1)} %constant_dynamic-update-slice_fusion, bf16[2048,256]{1,0:T(8,128)(2,1)S(1)} %bitcast.75), kind=kOutput, calls=%fused_computation.145 | convolution fusion | flops 536870912 | bytes 3670016 | tf_op jit(solution)/shard_map/dot_general | solution.py:179
  25.5 0.4 fusion.28
  25.9 0.2 constant_dynamic-slice_fusion.9
  26.1 1.1 %constant_dynamic-slice_fusion.3 = (bf16[2,4,64,256]{3,2,1,0:T(8,128)(2,1)S(1)}, bf16[2,4,64,256]{3,2,1,0:T(8,128)(2,1)S(1)}, bf16[2,4,64,256]{3,2,1,0:T(8,128)(...) fusion(bf16[4,6,66,256]{3,2,1,0:T(8,128)(2,1)S(1)} %fusion.28, ...), kind=kLoop, calls=%fused_computation.109 | loop fusion | bytes 3145800 | tf_op jit(solution)/shard_map/dynamic_slice | solution.py:169
  27.5 0.7 %convolution_add_fusion.2 = f32[512,256]{1,0:T(8,128)S(1)} fusion(f32[512,256]{1,0:T(8,128)S(1)} %fusion.71, bf16[512,2048]{1,0:T(8,128)(2,1)S(1)} %constant_dynamic-update-slice_fusion.8, bf16[2048,256]{1,0:T(8,128)(2,1)S(1)} %bitcast.74), kind=kOutput, calls=%fused_computation.22 | convolution fusion | flops 537001984 | bytes 4194304 | tf_op jit(solution)/shard_map/dot_general | solution.py:179
  28.4 2.6 %collective-permute-start.6 = (f32[2,1,64,256]{3,2,1,0:T(8,128)S(1)}, f32[2,1,64,256]{3,2,1,0:T(8,128)S(1)}, u32[]{:S(2)}, u32[]{:S(2)}) collective-permute-start(f32[2,1,64,256]{3,2,1,0:T(8,128)S(1)} %get-tuple-element.27), channel_id=1, source_target_pairs={{0,12},{4,0},{8,4},{12,8},{1,13},{5,1},{9,5},{13,9},{2,14},{6,2},{... | collective-permute-start | bytes 393224 | tf_op jit(solution)/shard_map/ppermute | solution.py:53
  31.0 0.5 collective-permute-start.5
  31.5 6.7 %collective-permute-done.7 = f32[2,1,64,256]{3,2,1,0:T(8,128)S(1)} collective-permute-done((f32[2,1,64,256]{3,2,1,0:T(8,128)S(1)}, f32[2,1,64,256]{3,2,1,0:T(8,128)S(1)}, u32[]{:S(2)}, u32[]{:S(2)}) %collective-permute-start.7) | collective-permute-done | bytes 131104 | tf_op jit(solution)/shard_map/ppermute | solution.py:53
  38.2 2.8 %collective-permute-done.6 = f32[2,1,64,256]{3,2,1,0:T(8,128)S(1)} collective-permute-done((f32[2,1,64,256]{3,2,1,0:T(8,128)S(1)}, f32[2,1,64,256]{3,2,1,0:T(8,128)S(1)}, u32[]{:S(2)}, u32[]{:S(2)}) %collective-permute-start.6) | collective-permute-done | bytes 131104 | tf_op jit(solution)/shard_map/ppermute | solution.py:53
  41.1 3.2 %collective-permute-start.8 = (bf16[2,1,64,256]{3,2,1,0:T(8,128)(2,1)S(1)}, bf16[2,1,64,256]{3,2,1,0:T(8,128)(2,1)S(1)}, u32[]{:S(2)}, u32[]{:S(2)}) collective-permute-start(bf16[2,1,64,256]{3,2,1,0:T(8,128)(2,1)S(1)} %get-tuple-element.6), channel_id=1, source_target_pairs={{0,4},{4,8},{8,12},{12,0},{1,5},{5,9},{9,13},{13,1},{2,6},{6,10},{... | collective-permute-start | bytes 196616 | tf_op jit(solution)/shard_map/ppermute | solution.py:53
  44.3 0.1 dynamic_slice.129
  44.4 0.7 %collective-permute-start.9 = (bf16[2,1,64,256]{3,2,1,0:T(8,128)(2,1)S(1)}, bf16[2,1,64,256]{3,2,1,0:T(8,128)(2,1)S(1)}, u32[]{:S(2)}, u32[]{:S(2)}) collective-permute-start(bf16[2,1,64,256]{3,2,1,0:T(8,128)(2,1)S(1)} %get-tuple-element.6), channel_id=1, source_target_pairs={{0,12},{4,0},{8,4},{12,8},{1,13},{5,1},{9,5},{13,9},{2,14},{6,2},{... | collective-permute-start | bytes 196616 | tf_op jit(solution)/shard_map/ppermute | solution.py:53
  45.1 1.2 %collective-permute-start.10 = (bf16[2,1,64,256]{3,2,1,0:T(8,128)(2,1)S(1)}, bf16[2,1,64,256]{3,2,1,0:T(8,128)(2,1)S(1)}, u32[]{:S(2)}, u32[]{:S(2)}) collective-permute-start(bf16[2,1,64,256]{3,2,1,0:T(8,128)(2,1)S(1)} %get-tuple-element.6), channel_id=1, source_target_pairs={{0,8},{4,12},{8,0},{12,4},{1,9},{5,13},{9,1},{13,5},{2,10},{6,14},... | collective-permute-start | bytes 196616 | tf_op jit(solution)/shard_map/ppermute | solution.py:53
  46.2 1.6 %collective-permute-done.8 = bf16[2,1,64,256]{3,2,1,0:T(8,128)(2,1)S(1)} collective-permute-done((bf16[2,1,64,256]{3,2,1,0:T(8,128)(2,1)S(1)}, bf16[2,1,64,256]{3,2,1,0:T(8,128)(2,1)S(1)}, u32[]{:S(2)}, u32[]{:S(2)}) %collective-permute-start.8) | collective-permute-done | bytes 65568 | tf_op jit(solution)/shard_map/ppermute | solution.py:53
  47.9 1.3 %collective-permute-done.9 = bf16[2,1,64,256]{3,2,1,0:T(8,128)(2,1)S(1)} collective-permute-done((bf16[2,1,64,256]{3,2,1,0:T(8,128)(2,1)S(1)}, bf16[2,1,64,256]{3,2,1,0:T(8,128)(2,1)S(1)}, u32[]{:S(2)}, u32[]{:S(2)}) %collective-permute-start.9) | collective-permute-done | bytes 65568 | tf_op jit(solution)/shard_map/ppermute | solution.py:53
  49.2 2.2 %collective-permute-done.10 = bf16[2,1,64,256]{3,2,1,0:T(8,128)(2,1)S(1)} collective-permute-done((bf16[2,1,64,256]{3,2,1,0:T(8,128)(2,1)S(1)}, bf16[2,1,64,256]{3,2,1,0:T(8,128)(2,1)S(1)}, u32[]{:S(2)}, u32[]{:S(2)}) %collective-permute-start.10) | collective-permute-done | bytes 65568 | tf_op jit(solution)/shard_map/ppermute | solution.py:53
  51.5 0.1 reduce_sum.80
  51.6 0.1 reduce_sum.81
  51.7 0.1 sub.166
  51.8 0.1 sub.167
  51.9 0.1 fusion.35
  52.0 0.1 reduce_sum.83
  52.0 0.1 reduce_sum.84
  52.1 0.1 mul.99
  52.2 0.1 mul.100
  52.3 0.1 fusion.38
  52.6 0.3 fusion.41
  52.9 0.2 fusion.47
  53.1 0.3 fusion.44
  53.4 0.7 %collective-permute-done.11 = bf16[2,4,64,256]{3,2,1,0:T(8,128)(2,1)S(1)} collective-permute-done((bf16[2,4,64,256]{3,2,1,0:T(8,128)(2,1)S(1)}, bf16[2,4,64,256]{3,2,1,0:T(8,128)(2,1)S(1)}, u32[]{:S(2)}, u32[]{:S(2)}) %collective-permute-start.11) | collective-permute-done | bytes 262176 | tf_op jit(solution)/shard_map/ppermute | solution.py:68
  54.0 0.3 fusion.13
  54.4 0.3 fusion.14
  54.7 0.2 fusion.16
  54.9 0.4 fusion.70
  55.3 0.2 fusion.55
  55.5 0.3 fusion.17
  55.7 0.2 fusion.18
  56.0 0.6 %fusion.49 = bf16[2,1,64,256]{3,2,1,0:T(8,128)(2,1)} fusion(bf16[2,1,64,256]{3,2,1,0:T(8,128)(2,1)S(1)} %bitcast.97, bf16[2,1,64,256]{3,2,1,0:T(8,128)(2,1)S(1)} %get-tuple-element.6), kind=kLoop, calls=%fused_computation.65 | loop fusion | flops 131072 | bytes 196608 | tf_op jit(solution)/shard_map/convert_element_type | solution.py:254
  (77 shorter events, 1.3 us)
Async XLA Ops:
  0.0 53.1 %copy-start = (bf16[512,512]{1,0:T(8,128)(2,1)S(1)}, bf16[512,512]{1,0:T(8,128)(2,1)}, u32[]{:S(2)}) copy-start(bf16[512,512]{1,0:T(8,128)(2,1)} %param.23) | copy-start | bytes 1572868
  0.0 7.1 %copy-start.1 = (bf16[3456,256]{1,0:T(8,128)(2,1)S(1)}, bf16[3456,256]{1,0:T(8,128)(2,1)}, u32[]{:S(2)}) copy-start(bf16[3456,256]{1,0:T(8,128)(2,1)} %param.17) | copy-start | bytes 5308420
  0.0 7.7 %collective-permute-start = (bf16[2,1,64,256]{3,2,1,0:T(8,128)(2,1)}, bf16[2,1,64,256]{3,2,1,0:T(8,128)(2,1)S(1)}, u32[]{:S(2)}, u32[]{:S(2)}) collective-permute-start(bf16[2,1,64,256]{3,2,1,0:T(8,128)(2,1)} %param.14), channel_id=1, source_target_pairs={{0,4},{4,8},{8,12},{12,0},{1,5},{5,9},{9,13},{13,1},{2,6},{6,10},{... | collective-permute-start | bytes 196616 | tf_op jit(solution)/shard_map/ppermute | solution.py:53
  3.0 5.2 %collective-permute-start.1 = (bf16[2,1,64,256]{3,2,1,0:T(8,128)(2,1)}, bf16[2,1,64,256]{3,2,1,0:T(8,128)(2,1)S(1)}, u32[]{:S(2)}, u32[]{:S(2)}) collective-permute-start(bf16[2,1,64,256]{3,2,1,0:T(8,128)(2,1)} %param.14), channel_id=1, source_target_pairs={{0,12},{4,0},{8,4},{12,8},{1,13},{5,1},{9,5},{13,9},{2,14},{6,2},{... | collective-permute-start | bytes 196616 | tf_op jit(solution)/shard_map/ppermute | solution.py:53
  5.1 6.4 %collective-permute-start.2 = (bf16[2,1,64,256]{3,2,1,0:T(8,128)(2,1)}, bf16[2,1,64,256]{3,2,1,0:T(8,128)(2,1)S(1)}, u32[]{:S(2)}, u32[]{:S(2)}) collective-permute-start(bf16[2,1,64,256]{3,2,1,0:T(8,128)(2,1)} %param.14), channel_id=1, source_target_pairs={{0,8},{4,12},{8,0},{12,4},{1,9},{5,13},{9,1},{13,5},{2,10},{6,14},... | collective-permute-start | bytes 196616 | tf_op jit(solution)/shard_map/ppermute | solution.py:53
  11.6 7.9 %collective-permute-start.3 = (bf16[2,4,64,256]{3,2,1,0:T(8,128)(2,1)S(1)}, bf16[2,4,64,256]{3,2,1,0:T(8,128)(2,1)S(1)}, u32[]{:S(2)}, u32[]{:S(2)}) collective-permute-start(bf16[2,4,64,256]{3,2,1,0:T(8,128)(2,1)S(1)} %constant_dynamic-update-slice_fusion.23), channel_id=1, source_target_pairs={{0,2},{2,0},{1,3},{3,1},{4,6},{6,4},{5,7},{7,5},{8,10},{10,8},{9,1... | collective-permute-start | bytes 786440 | tf_op jit(solution)/shard_map/ppermute | solution.py:53
  14.2 7.0 %copy-start.12 = (f32[256]{0:T(256)S(1)}, f32[256]{0:T(256)}, u32[]{:S(2)}) copy-start(f32[256]{0:T(256)} %param.16) | copy-start | bytes 3076
  14.2 7.0 %copy-start.13 = (f32[256]{0:T(256)S(1)}, f32[256]{0:T(256)}, u32[]{:S(2)}) copy-start(f32[256]{0:T(256)} %param.15) | copy-start | bytes 3076
  21.8 3.8 %collective-permute-start.4 = (bf16[4,4,64,256]{3,2,1,0:T(8,128)(2,1)S(1)}, bf16[4,4,64,256]{3,2,1,0:T(8,128)(2,1)S(1)}, u32[]{:S(2)}, u32[]{:S(2)}) collective-permute-start(bf16[4,4,64,256]{3,2,1,0:T(8,128)(2,1)S(1)} %multiply_convert_fusion), channel_id=1, source_target_pairs={{0,1},{1,0},{2,3},{3,2},{4,5},{5,4},{6,7},{7,6},{8,9},{9,8},{10,11... | collective-permute-start | bytes 1572872 | tf_op jit(solution)/shard_map/ppermute | solution.py:68
  23.6 1.2 %copy-start.2 = (bf16[8,1,256,256]{3,2,1,0:T(8,128)(2,1)S(1)}, bf16[8,1,256,256]{3,2,1,0:T(8,128)(2,1)}, u32[]{:S(2)}) copy-start(bf16[8,1,256,256]{3,2,1,0:T(8,128)(2,1)} %get-tuple-element.8) | copy-start | bytes 3145732
  27.5 13.5 %copy-start.5 = (bf16[2,1,64,256]{3,2,1,0:T(8,128)(2,1)S(1)}, bf16[2,1,64,256]{3,2,1,0:T(8,128)(2,1)}, u32[]{:S(2)}) copy-start(bf16[2,1,64,256]{3,2,1,0:T(8,128)(2,1)} %param.14) | copy-start | bytes 196612
  27.5 13.5 %copy-start.9 = (f32[256]{0:T(256)S(1)}, f32[256]{0:T(256)}, u32[]{:S(2)}) copy-start(f32[256]{0:T(256)} %param.18) | copy-start | bytes 3076
  27.5 16.8 %copy-start.14 = (f32[512]{0:T(512)S(1)}, f32[512]{0:T(512)}, u32[]{:S(2)}) copy-start(f32[512]{0:T(512)} %param.27) | copy-start | bytes 6148
  28.2 24.1 %copy-start.10 = (f32[256]{0:T(256)S(1)}, f32[256]{0:T(256)}, u32[]{:S(2)}) copy-start(f32[256]{0:T(256)} %param.20) | copy-start | bytes 3076
  28.3 24.1 %copy-start.11 = (f32[256]{0:T(256)S(1)}, f32[256]{0:T(256)}, u32[]{:S(2)}) copy-start(f32[256]{0:T(256)} %param.19) | copy-start | bytes 3076
  28.3 24.3 %copy-start.4 = (bf16[512,512]{1,0:T(8,128)(2,1)S(1)}, bf16[512,512]{1,0:T(8,128)(2,1)}, u32[]{:S(2)}) copy-start(bf16[512,512]{1,0:T(8,128)(2,1)} %param.24) | copy-start | bytes 1572868
  28.3 9.9 %collective-permute-start.7 = (f32[2,1,64,256]{3,2,1,0:T(8,128)S(1)}, f32[2,1,64,256]{3,2,1,0:T(8,128)S(1)}, u32[]{:S(2)}, u32[]{:S(2)}) collective-permute-start(f32[2,1,64,256]{3,2,1,0:T(8,128)S(1)} %get-tuple-element.26), channel_id=1, source_target_pairs={{0,8},{4,12},{8,0},{12,4},{1,9},{5,13},{9,1},{13,5},{2,10},{6,14},... | collective-permute-start | bytes 393224 | tf_op jit(solution)/shard_map/ppermute | solution.py:53
  28.4 12.6 %collective-permute-start.6 = (f32[2,1,64,256]{3,2,1,0:T(8,128)S(1)}, f32[2,1,64,256]{3,2,1,0:T(8,128)S(1)}, u32[]{:S(2)}, u32[]{:S(2)}) collective-permute-start(f32[2,1,64,256]{3,2,1,0:T(8,128)S(1)} %get-tuple-element.27), channel_id=1, source_target_pairs={{0,12},{4,0},{8,4},{12,8},{1,13},{5,1},{9,5},{13,9},{2,14},{6,2},{... | collective-permute-start | bytes 393224 | tf_op jit(solution)/shard_map/ppermute | solution.py:53
  31.0 10.0 %collective-permute-start.5 = (f32[2,1,64,256]{3,2,1,0:T(8,128)S(1)}, f32[2,1,64,256]{3,2,1,0:T(8,128)S(1)}, u32[]{:S(2)}, u32[]{:S(2)}) collective-permute-start(f32[2,1,64,256]{3,2,1,0:T(8,128)S(1)} %get-tuple-element.25), channel_id=1, source_target_pairs={{0,4},{4,8},{8,12},{12,0},{1,5},{5,9},{9,13},{13,1},{2,6},{6,10},{... | collective-permute-start | bytes 393224 | tf_op jit(solution)/shard_map/ppermute | solution.py:53
  41.0 11.8 %copy-start.3 = (bf16[512,512]{1,0:T(8,128)(2,1)S(1)}, bf16[512,512]{1,0:T(8,128)(2,1)}, u32[]{:S(2)}) copy-start(bf16[512,512]{1,0:T(8,128)(2,1)} %param.21) | copy-start | bytes 1572868
  41.1 6.8 %collective-permute-start.8 = (bf16[2,1,64,256]{3,2,1,0:T(8,128)(2,1)S(1)}, bf16[2,1,64,256]{3,2,1,0:T(8,128)(2,1)S(1)}, u32[]{:S(2)}, u32[]{:S(2)}) collective-permute-start(bf16[2,1,64,256]{3,2,1,0:T(8,128)(2,1)S(1)} %get-tuple-element.6), channel_id=1, source_target_pairs={{0,4},{4,8},{8,12},{12,0},{1,5},{5,9},{9,13},{13,1},{2,6},{6,10},{... | collective-permute-start | bytes 196616 | tf_op jit(solution)/shard_map/ppermute | solution.py:53
  44.4 4.8 %collective-permute-start.9 = (bf16[2,1,64,256]{3,2,1,0:T(8,128)(2,1)S(1)}, bf16[2,1,64,256]{3,2,1,0:T(8,128)(2,1)S(1)}, u32[]{:S(2)}, u32[]{:S(2)}) collective-permute-start(bf16[2,1,64,256]{3,2,1,0:T(8,128)(2,1)S(1)} %get-tuple-element.6), channel_id=1, source_target_pairs={{0,12},{4,0},{8,4},{12,8},{1,13},{5,1},{9,5},{13,9},{2,14},{6,2},{... | collective-permute-start | bytes 196616 | tf_op jit(solution)/shard_map/ppermute | solution.py:53
  45.1 6.4 %collective-permute-start.10 = (bf16[2,1,64,256]{3,2,1,0:T(8,128)(2,1)S(1)}, bf16[2,1,64,256]{3,2,1,0:T(8,128)(2,1)S(1)}, u32[]{:S(2)}, u32[]{:S(2)}) collective-permute-start(bf16[2,1,64,256]{3,2,1,0:T(8,128)(2,1)S(1)} %get-tuple-element.6), channel_id=1, source_target_pairs={{0,8},{4,12},{8,0},{12,4},{1,9},{5,13},{9,1},{13,5},{2,10},{6,14},... | collective-permute-start | bytes 196616 | tf_op jit(solution)/shard_map/ppermute | solution.py:53
  52.4 1.6 %collective-permute-start.11 = (bf16[2,4,64,256]{3,2,1,0:T(8,128)(2,1)S(1)}, bf16[2,4,64,256]{3,2,1,0:T(8,128)(2,1)S(1)}, u32[]{:S(2)}, u32[]{:S(2)}) collective-permute-start(bf16[2,4,64,256]{3,2,1,0:T(8,128)(2,1)S(1)} %fusion.38), channel_id=1, source_target_pairs={{0,1},{1,0},{2,3},{3,2},{4,5},{5,4},{6,7},{7,6},{8,9},{9,8},{10,11... | collective-permute-start | bytes 786440 | tf_op jit(solution)/shard_map/ppermute | solution.py:68
  52.9 1.5 %copy-start.8 = (f32[512]{0:T(512)S(1)}, f32[512]{0:T(512)}, u32[]{:S(2)}) copy-start(f32[512]{0:T(512)} %param.25) | copy-start | bytes 6148
  54.0 0.7 %copy-start.7 = (f32[512]{0:T(512)S(1)}, f32[512]{0:T(512)}, u32[]{:S(2)}) copy-start(f32[512]{0:T(512)} %param.22) | copy-start | bytes 6148
  54.4 1.4 %copy-start.6 = (bf16[512,512]{1,0:T(8,128)(2,1)S(1)}, bf16[512,512]{1,0:T(8,128)(2,1)}, u32[]{:S(2)}) copy-start(bf16[512,512]{1,0:T(8,128)(2,1)} %param.26) | copy-start | bytes 1572868

commit v12 on v11

--- a/solution.py
+++ b/solution.py
@@ -18,6 +18,12 @@
     centered = grouped - group_mean
     group_var = jnp.mean(centered * centered, axis=axes, keepdims=True)
     return group_mean, group_var
+
+
+def merged_stats(first, second):
+    (mean_a, var_a), (mean_b, var_b) = first, second
+    delta = mean_b - mean_a
+    return mean_a + 0.5 * delta, 0.5 * (var_a + var_b) + 0.25 * delta * delta
 
 
 def apply_norm(values, group_mean, group_var, group_size):
@@ -119,12 +125,20 @@
                 segment_rows, block, (0, source_row * rows_here, 0, 0)
             )
         clip = jnp.zeros((time_count * frames, all_rows, columns, channels), latent.dtype)
+        block_stats = []
         for shift in [0] + nearest_first(time_count):
             block = segment_rows if shift == 0 else shifted(
                 segment_rows, ("tm",), (time_count,), (shift,)
             )
+            block_stats.append(group_stats(block, group_size, (0, 1, 2, 4)))
             source_time = (time_place - shift) % time_count
             clip = lax.dynamic_update_slice(clip, block, (source_time * frames, 0, 0, 0))
+        while len(block_stats) > 1 and len(block_stats) % 2 == 0:
+            block_stats = [
+                merged_stats(block_stats[i], block_stats[i + 1])
+                for i in range(0, len(block_stats), 2)
+            ]
+        stats1 = block_stats[0] if len(block_stats) == 1 else None
     else:
         copies = jnp.broadcast_to(latent[None], (row_count * time_count,) + latent.shape)
         gathered = lax.all_to_all(copies, ("rows", "tm"), 0, 0, tiled=True).reshape(
@@ -133,8 +147,11 @@
         clip = jnp.transpose(gathered, (1, 2, 0, 3, 4, 5)).reshape(
             (time_count * frames, all_rows, columns, channels)
         )
-
-    mean1, var1 = group_stats(clip, group_size, (0, 1, 2, 4))
+        stats1 = None
+
+    if stats1 is None:
+        stats1 = group_stats(clip, group_size, (0, 1, 2, 4))
+    mean1, var1 = stats1
     frame_index = jnp.clip(
         time_place * frames - 2 + jnp.arange(frames + 2), 0, time_count * frames - 1
     )

time: 56.8 us -> 56.9 us (level)
  waiting for transfers between devices: 24.7 us -> 24 us
    ppermute x10, waiting for transfers between devices: 24.1 us -> 23.3 us  [shifted(): return lax.ppermute(cells, axes, pairs)]
  transfers between devices with their start and end apart: 12 -> 12, of which waited for: 10 -> 8; matrix products, arithmetic and copies ran while one was open for 10% -> 12% of each run, Pallas kernels for 0% -> 0%
where the time goes in v12:
time: 56.9 us; the launch traced here: 56.7 us
  waiting for transfers between devices  24 us (42%)
  starting transfers between devices  16 us (28%)
  local copies, waits for them, and re-layouts  8.84 us (16%)
  matrix products  3.82 us (7%)
  other arithmetic  3.45 us (6%)
  between operations  0.65 us (1%)
    ppermute x10, waiting for transfers between devices, shifted(): return lax.ppermute(cells, axes, pairs)  23.3 us
    ppermute x10, starting transfers between devices, shifted(): return lax.ppermute(cells, axes, pairs)  15.8 us
    dynamic_slice x4, local copies, waits for them, and re-layouts, local(): lax.dynamic_slice(half, (tap // 9, tap // 3 % 3, tap % 3, 0), (frames, al...  2.55 us
    dot_general x6, matrix products, split_dot(): jnp.dot(half, half_rows(weight, shift, width), preferred_element_type=jnp...  1.55 us
    unnamed x44, local copies, waits for them, and re-layouts  1.5 us
    dot_general x2, matrix products, local(): term = jnp.dot(patches, block, preferred_element_type=jnp.float32)  1.45 us
    dynamic_slice x1, local copies, waits for them, and re-layouts, local(): lax.dynamic_index_in_dim(placed, source, axis=1, keepdims=False)  1.14 us
  transfers between devices with their start and end apart: 12, of which 8 were waited for; matrix products, arithmetic and copies ran while one was open for 12% of the time, Pallas kernels for 0%

profile of v12, /device:TPU:0, one launch (start us, length us, event | category | flops | bytes accessed | tf_op | source)
XLA Modules:
  0.0 56.7 jit_solution(7191655150966037612)
XLA Ops:
  0.0 3.0 %collective-permute-start = (bf16[2,1,64,256]{3,2,1,0:T(8,128)(2,1)}, bf16[2,1,64,256]{3,2,1,0:T(8,128)(2,1)S(1)}, u32[]{:S(2)}, u32[]{:S(2)}) collective-permute-start(bf16[2,1,64,256]{3,2,1,0:T(8,128)(2,1)} %param.14), channel_id=1, source_target_pairs={{0,4},{4,8},{8,12},{12,0},{1,5},{5,9},{9,13},{13,1},{2,6},{6,10},{... | collective-permute-start | bytes 196616 | tf_op jit(solution)/shard_map/ppermute | solution.py:59
  3.0 2.1 %collective-permute-start.1 = (bf16[2,1,64,256]{3,2,1,0:T(8,128)(2,1)}, bf16[2,1,64,256]{3,2,1,0:T(8,128)(2,1)S(1)}, u32[]{:S(2)}, u32[]{:S(2)}) collective-permute-start(bf16[2,1,64,256]{3,2,1,0:T(8,128)(2,1)} %param.14), channel_id=1, source_target_pairs={{0,12},{4,0},{8,4},{12,8},{1,13},{5,1},{9,5},{13,9},{2,14},{6,2},{... | collective-permute-start | bytes 196616 | tf_op jit(solution)/shard_map/ppermute | solution.py:59
  5.1 0.9 %collective-permute-start.2 = (bf16[2,1,64,256]{3,2,1,0:T(8,128)(2,1)}, bf16[2,1,64,256]{3,2,1,0:T(8,128)(2,1)S(1)}, u32[]{:S(2)}, u32[]{:S(2)}) collective-permute-start(bf16[2,1,64,256]{3,2,1,0:T(8,128)(2,1)} %param.14), channel_id=1, source_target_pairs={{0,8},{4,12},{8,0},{12,4},{1,9},{5,13},{9,1},{13,5},{2,10},{6,14},... | collective-permute-start | bytes 196616 | tf_op jit(solution)/shard_map/ppermute | solution.py:59
  6.1 0.9 %constant_dynamic-update-slice_fusion.26 = bf16[2,4,64,256]{3,2,1,0:T(8,128)(2,1)S(1)} fusion(bf16[2,4,64,256]{3,2,1,0:T(8,128)(2,1)S(1)} %broadcast.189.clone, bf16[2,1,64,256]{3,2,1,0:T(8,128)(2,1)} %param.14, s32[]{:T(128)S(6)} %select_n.416), kind=kLoop, calls=%fused_computation.136 | loop fusion | bytes 131076 | tf_op jit(solution)/shard_map/dynamic_update_slice | solution.py:124
  7.0 0.1 broadcast_in_dim.17
  7.1 0.2 constant_dynamic-update-slice_fusion.20
  7.4 1.1 %constant_dynamic-slice_fusion.2 = (bf16[8,1,256,256]{3,2,1,0:T(8,128)(2,1)S(1)}, bf16[8,1,256,256]{3,2,1,0:T(8,128)(2,1)}) fusion(bf16[8,2,256,256]{3,2,1,0:T(8,128)(2,1)S(1)} %bitcast.68, s32[]{:T(128)S(6)} %select_n.491, s32[]{:T(128)S(6)} %select_n.489), kind=kLoop, calls=%fused_computation.112 | loop fusion | bytes 4194312 | tf_op jit(solution)/shard_map/jit(dynamic_index_in_dim)/dynamic_slice | solution.py:193
  8.6 3.0 %collective-permute-done.2 = bf16[2,1,64,256]{3,2,1,0:T(8,128)(2,1)S(1)} collective-permute-done((bf16[2,1,64,256]{3,2,1,0:T(8,128)(2,1)}, bf16[2,1,64,256]{3,2,1,0:T(8,128)(2,1)S(1)}, u32[]{:S(2)}, u32[]{:S(2)}) %collective-permute-start.2) | collective-permute-done | bytes 65568 | tf_op jit(solution)/shard_map/ppermute | solution.py:59
  11.6 0.1 convert_reduce_fusion.2
  11.7 1.5 %collective-permute-start.3 = (bf16[2,4,64,256]{3,2,1,0:T(8,128)(2,1)S(1)}, bf16[2,4,64,256]{3,2,1,0:T(8,128)(2,1)S(1)}, u32[]{:S(2)}, u32[]{:S(2)}) collective-permute-start(bf16[2,4,64,256]{3,2,1,0:T(8,128)(2,1)S(1)} %constant_dynamic-update-slice_fusion.23), channel_id=1, source_target_pairs={{0,2},{2,0},{1,3},{3,1},{4,6},{6,4},{5,7},{7,5},{8,10},{10,8},{9,1... | collective-permute-start | bytes 786440 | tf_op jit(solution)/shard_map/ppermute | solution.py:59
  13.3 0.1 reduce_sum.82
  13.5 0.1 sub.179
  13.6 0.1 fusion.38
  13.7 0.1 reduce_sum.90
  13.8 0.1 reduce_sum.91
  14.0 5.6 %collective-permute-done.3 = bf16[2,4,64,256]{3,2,1,0:T(8,128)(2,1)S(1)} collective-permute-done((bf16[2,4,64,256]{3,2,1,0:T(8,128)(2,1)S(1)}, bf16[2,4,64,256]{3,2,1,0:T(8,128)(2,1)S(1)}, u32[]{:S(2)}, u32[]{:S(2)}) %collective-permute-start.3) | collective-permute-done | bytes 262176 | tf_op jit(solution)/shard_map/ppermute | solution.py:59
  19.6 0.1 convert_reduce_fusion.1
  19.7 0.1 reduce_sum.84
  19.8 0.1 reduce_sum.85
  20.0 0.1 sub.183
  20.0 0.1 fusion.40
  20.2 0.1 reduce_sum.116
  20.4 0.1 mul.135
  20.6 0.1 sub.175
  20.7 0.6 %gather_fusion = bf16[4,4,64,256]{3,2,1,0:T(8,128)(2,1)S(1)} fusion(bf16[4,4,64,256]{3,2,1,0:T(8,128)(2,1)S(1)} %constant_dynamic-update-slice_fusion.21, s32[1024]{0:T(1024)S(1)} %pad_clamp_fusion), kind=kCustom, calls=%fused_computation | custom fusion | bytes 1048592 | tf_op jit(solution)/shard_map/jit(_take)/gather | solution.py:158
  21.3 0.5 multiply_convert_fusion
  21.9 0.4 fusion.22
  22.3 0.2 constant_dynamic-slice_fusion.18
  22.6 1.1 %constant_dynamic-slice_fusion.12 = (bf16[2,4,64,256]{3,2,1,0:T(8,128)(2,1)S(1)}, bf16[2,4,64,256]{3,2,1,0:T(8,128)(2,1)S(1)}, bf16[2,4,64,256]{3,2,1,0:T(8,128)...) fusion(bf16[4,6,66,256]{3,2,1,0:T(8,128)(2,1)S(1)} %fusion.22, ...), kind=kLoop, calls=%fused_computation.123 | loop fusion | bytes 3145800 | tf_op jit(solution)/shard_map/dynamic_slice | solution.py:186
  23.9 1.0 %copy-done.2 = bf16[8,1,256,256]{3,2,1,0:T(8,128)(2,1)S(1)} copy-done((bf16[8,1,256,256]{3,2,1,0:T(8,128)(2,1)S(1)}, bf16[8,1,256,256]{3,2,1,0:T(8,128)(2,1)}, u32[]{:S(2)}) %copy-start.2) | copy-done | bytes 1048600
  24.9 0.7 %fusion.74 = f32[512,256]{1,0:T(8,128)S(1)} fusion(bf16[512,2048]{1,0:T(8,128)(2,1)S(1)} %constant_dynamic-update-slice_fusion, bf16[2048,256]{1,0:T(8,128)(2,1)S(1)} %bitcast.75), kind=kOutput, calls=%fused_computation.153 | convolution fusion | flops 536870912 | bytes 3670016 | tf_op jit(solution)/shard_map/dot_general | solution.py:196
  25.6 0.4 fusion.26
  26.0 0.2 constant_dynamic-slice_fusion.9
  26.2 1.1 %constant_dynamic-slice_fusion.3 = (bf16[2,4,64,256]{3,2,1,0:T(8,128)(2,1)S(1)}, bf16[2,4,64,256]{3,2,1,0:T(8,128)(2,1)S(1)}, bf16[2,4,64,256]{3,2,1,0:T(8,128)(...) fusion(bf16[4,6,66,256]{3,2,1,0:T(8,128)(2,1)S(1)} %fusion.26, ...), kind=kLoop, calls=%fused_computation.113 | loop fusion | bytes 3145800 | tf_op jit(solution)/shard_map/dynamic_slice | solution.py:186
  27.6 0.7 %convolution_add_fusion.2 = f32[512,256]{1,0:T(8,128)S(1)} fusion(f32[512,256]{1,0:T(8,128)S(1)} %fusion.74, bf16[512,2048]{1,0:T(8,128)(2,1)S(1)} %constant_dynamic-update-slice_fusion.8, bf16[2048,256]{1,0:T(8,128)(2,1)S(1)} %bitcast.74), kind=kOutput, calls=%fused_computation.20 | convolution fusion | flops 537001984 | bytes 4194304 | tf_op jit(solution)/shard_map/dot_general | solution.py:196
  28.5 2.6 %collective-permute-start.6 = (f32[2,1,64,256]{3,2,1,0:T(8,128)S(1)}, f32[2,1,64,256]{3,2,1,0:T(8,128)S(1)}, u32[]{:S(2)}, u32[]{:S(2)}) collective-permute-start(f32[2,1,64,256]{3,2,1,0:T(8,128)S(1)} %get-tuple-element.27), channel_id=1, source_target_pairs={{0,12},{4,0},{8,4},{12,8},{1,13},{5,1},{9,5},{13,9},{2,14},{6,2},{... | collective-permute-start | bytes 393224 | tf_op jit(solution)/shard_map/ppermute | solution.py:59
  31.1 0.5 collective-permute-start.5
  31.6 6.7 %collective-permute-done.7 = f32[2,1,64,256]{3,2,1,0:T(8,128)S(1)} collective-permute-done((f32[2,1,64,256]{3,2,1,0:T(8,128)S(1)}, f32[2,1,64,256]{3,2,1,0:T(8,128)S(1)}, u32[]{:S(2)}, u32[]{:S(2)}) %collective-permute-start.7) | collective-permute-done | bytes 131104 | tf_op jit(solution)/shard_map/ppermute | solution.py:59
  38.3 2.8 %collective-permute-done.6 = f32[2,1,64,256]{3,2,1,0:T(8,128)S(1)} collective-permute-done((f32[2,1,64,256]{3,2,1,0:T(8,128)S(1)}, f32[2,1,64,256]{3,2,1,0:T(8,128)S(1)}, u32[]{:S(2)}, u32[]{:S(2)}) %collective-permute-start.6) | collective-permute-done | bytes 131104 | tf_op jit(solution)/shard_map/ppermute | solution.py:59
  41.2 3.2 %collective-permute-start.8 = (bf16[2,1,64,256]{3,2,1,0:T(8,128)(2,1)S(1)}, bf16[2,1,64,256]{3,2,1,0:T(8,128)(2,1)S(1)}, u32[]{:S(2)}, u32[]{:S(2)}) collective-permute-start(bf16[2,1,64,256]{3,2,1,0:T(8,128)(2,1)S(1)} %get-tuple-element.6), channel_id=1, source_target_pairs={{0,4},{4,8},{8,12},{12,0},{1,5},{5,9},{9,13},{13,1},{2,6},{6,10},{... | collective-permute-start | bytes 196616 | tf_op jit(solution)/shard_map/ppermute | solution.py:59
  44.5 0.7 %collective-permute-start.9 = (bf16[2,1,64,256]{3,2,1,0:T(8,128)(2,1)S(1)}, bf16[2,1,64,256]{3,2,1,0:T(8,128)(2,1)S(1)}, u32[]{:S(2)}, u32[]{:S(2)}) collective-permute-start(bf16[2,1,64,256]{3,2,1,0:T(8,128)(2,1)S(1)} %get-tuple-element.6), channel_id=1, source_target_pairs={{0,12},{4,0},{8,4},{12,8},{1,13},{5,1},{9,5},{13,9},{2,14},{6,2},{... | collective-permute-start | bytes 196616 | tf_op jit(solution)/shard_map/ppermute | solution.py:59
  45.1 1.2 %collective-permute-start.10 = (bf16[2,1,64,256]{3,2,1,0:T(8,128)(2,1)S(1)}, bf16[2,1,64,256]{3,2,1,0:T(8,128)(2,1)S(1)}, u32[]{:S(2)}, u32[]{:S(2)}) collective-permute-start(bf16[2,1,64,256]{3,2,1,0:T(8,128)(2,1)S(1)} %get-tuple-element.6), channel_id=1, source_target_pairs={{0,8},{4,12},{8,0},{12,4},{1,9},{5,13},{9,1},{13,5},{2,10},{6,14},... | collective-permute-start | bytes 196616 | tf_op jit(solution)/shard_map/ppermute | solution.py:59
  46.3 1.6 %collective-permute-done.8 = bf16[2,1,64,256]{3,2,1,0:T(8,128)(2,1)S(1)} collective-permute-done((bf16[2,1,64,256]{3,2,1,0:T(8,128)(2,1)S(1)}, bf16[2,1,64,256]{3,2,1,0:T(8,128)(2,1)S(1)}, u32[]{:S(2)}, u32[]{:S(2)}) %collective-permute-start.8) | collective-permute-done | bytes 65568 | tf_op jit(solution)/shard_map/ppermute | solution.py:59
  48.0 1.3 %collective-permute-done.9 = bf16[2,1,64,256]{3,2,1,0:T(8,128)(2,1)S(1)} collective-permute-done((bf16[2,1,64,256]{3,2,1,0:T(8,128)(2,1)S(1)}, bf16[2,1,64,256]{3,2,1,0:T(8,128)(2,1)S(1)}, u32[]{:S(2)}, u32[]{:S(2)}) %collective-permute-start.9) | collective-permute-done | bytes 65568 | tf_op jit(solution)/shard_map/ppermute | solution.py:59
  49.3 2.2 %collective-permute-done.10 = bf16[2,1,64,256]{3,2,1,0:T(8,128)(2,1)S(1)} collective-permute-done((bf16[2,1,64,256]{3,2,1,0:T(8,128)(2,1)S(1)}, bf16[2,1,64,256]{3,2,1,0:T(8,128)(2,1)S(1)}, u32[]{:S(2)}, u32[]{:S(2)}) %collective-permute-start.10) | collective-permute-done | bytes 65568 | tf_op jit(solution)/shard_map/ppermute | solution.py:59
  51.7 0.1 reduce_sum.119
  51.9 0.1 sub.205
  51.9 0.1 fusion.33
  52.0 0.1 reduce_sum.121
  52.1 0.1 reduce_sum.122
  52.3 0.1 mul.144
  52.4 0.1 fusion.36
  52.6 0.3 fusion.43
  52.9 0.2 fusion.49
  53.2 0.3 fusion.46
  53.5 0.7 %collective-permute-done.11 = bf16[2,4,64,256]{3,2,1,0:T(8,128)(2,1)S(1)} collective-permute-done((bf16[2,4,64,256]{3,2,1,0:T(8,128)(2,1)S(1)}, bf16[2,4,64,256]{3,2,1,0:T(8,128)(2,1)S(1)}, u32[]{:S(2)}, u32[]{:S(2)}) %collective-permute-start.11) | collective-permute-done | bytes 262176 | tf_op jit(solution)/shard_map/ppermute | solution.py:74
  54.1 0.3 fusion.13
  54.4 0.3 fusion.14
  54.8 0.2 fusion.16
  55.0 0.4 fusion.73
  55.4 0.2 fusion.57
  55.5 0.3 fusion.17
  55.8 0.2 fusion.18
  56.0 0.6 %fusion.51 = bf16[2,1,64,256]{3,2,1,0:T(8,128)(2,1)} fusion(bf16[2,1,64,256]{3,2,1,0:T(8,128)(2,1)S(1)} %bitcast.97, bf16[2,1,64,256]{3,2,1,0:T(8,128)(2,1)S(1)} %get-tuple-element.6), kind=kLoop, calls=%fused_computation.69 | loop fusion | flops 131072 | bytes 196608 | tf_op jit(solution)/shard_map/convert_element_type | solution.py:271
  (88 shorter events, 2.0 us)
Async XLA Ops:
  0.0 53.1 %copy-start = (bf16[512,512]{1,0:T(8,128)(2,1)S(1)}, bf16[512,512]{1,0:T(8,128)(2,1)}, u32[]{:S(2)}) copy-start(bf16[512,512]{1,0:T(8,128)(2,1)} %param.23) | copy-start | bytes 1572868
  0.0 7.1 %copy-start.1 = (bf16[3456,256]{1,0:T(8,128)(2,1)S(1)}, bf16[3456,256]{1,0:T(8,128)(2,1)}, u32[]{:S(2)}) copy-start(bf16[3456,256]{1,0:T(8,128)(2,1)} %param.17) | copy-start | bytes 5308420
  0.0 8.5 %collective-permute-start = (bf16[2,1,64,256]{3,2,1,0:T(8,128)(2,1)}, bf16[2,1,64,256]{3,2,1,0:T(8,128)(2,1)S(1)}, u32[]{:S(2)}, u32[]{:S(2)}) collective-permute-start(bf16[2,1,64,256]{3,2,1,0:T(8,128)(2,1)} %param.14), channel_id=1, source_target_pairs={{0,4},{4,8},{8,12},{12,0},{1,5},{5,9},{9,13},{13,1},{2,6},{6,10},{... | collective-permute-start | bytes 196616 | tf_op jit(solution)/shard_map/ppermute | solution.py:59
  3.0 5.5 %collective-permute-start.1 = (bf16[2,1,64,256]{3,2,1,0:T(8,128)(2,1)}, bf16[2,1,64,256]{3,2,1,0:T(8,128)(2,1)S(1)}, u32[]{:S(2)}, u32[]{:S(2)}) collective-permute-start(bf16[2,1,64,256]{3,2,1,0:T(8,128)(2,1)} %param.14), channel_id=1, source_target_pairs={{0,12},{4,0},{8,4},{12,8},{1,13},{5,1},{9,5},{13,9},{2,14},{6,2},{... | collective-permute-start | bytes 196616 | tf_op jit(solution)/shard_map/ppermute | solution.py:59
  5.1 6.4 %collective-permute-start.2 = (bf16[2,1,64,256]{3,2,1,0:T(8,128)(2,1)}, bf16[2,1,64,256]{3,2,1,0:T(8,128)(2,1)S(1)}, u32[]{:S(2)}, u32[]{:S(2)}) collective-permute-start(bf16[2,1,64,256]{3,2,1,0:T(8,128)(2,1)} %param.14), channel_id=1, source_target_pairs={{0,8},{4,12},{8,0},{12,4},{1,9},{5,13},{9,1},{13,5},{2,10},{6,14},... | collective-permute-start | bytes 196616 | tf_op jit(solution)/shard_map/ppermute | solution.py:59
  8.5 12.8 %copy-start.12 = (f32[256]{0:T(256)S(1)}, f32[256]{0:T(256)}, u32[]{:S(2)}) copy-start(f32[256]{0:T(256)} %param.16) | copy-start | bytes 3076
  8.5 12.8 %copy-start.13 = (f32[256]{0:T(256)S(1)}, f32[256]{0:T(256)}, u32[]{:S(2)}) copy-start(f32[256]{0:T(256)} %param.15) | copy-start | bytes 3076
  11.7 7.9 %collective-permute-start.3 = (bf16[2,4,64,256]{3,2,1,0:T(8,128)(2,1)S(1)}, bf16[2,4,64,256]{3,2,1,0:T(8,128)(2,1)S(1)}, u32[]{:S(2)}, u32[]{:S(2)}) collective-permute-start(bf16[2,4,64,256]{3,2,1,0:T(8,128)(2,1)S(1)} %constant_dynamic-update-slice_fusion.23), channel_id=1, source_target_pairs={{0,2},{2,0},{1,3},{3,1},{4,6},{6,4},{5,7},{7,5},{8,10},{10,8},{9,1... | collective-permute-start | bytes 786440 | tf_op jit(solution)/shard_map/ppermute | solution.py:59
  21.8 3.8 %collective-permute-start.4 = (bf16[4,4,64,256]{3,2,1,0:T(8,128)(2,1)S(1)}, bf16[4,4,64,256]{3,2,1,0:T(8,128)(2,1)S(1)}, u32[]{:S(2)}, u32[]{:S(2)}) collective-permute-start(bf16[4,4,64,256]{3,2,1,0:T(8,128)(2,1)S(1)} %multiply_convert_fusion), channel_id=1, source_target_pairs={{0,1},{1,0},{2,3},{3,2},{4,5},{5,4},{6,7},{7,6},{8,9},{9,8},{10,11... | collective-permute-start | bytes 1572872 | tf_op jit(solution)/shard_map/ppermute | solution.py:74
  23.6 1.2 %copy-start.2 = (bf16[8,1,256,256]{3,2,1,0:T(8,128)(2,1)S(1)}, bf16[8,1,256,256]{3,2,1,0:T(8,128)(2,1)}, u32[]{:S(2)}) copy-start(bf16[8,1,256,256]{3,2,1,0:T(8,128)(2,1)} %get-tuple-element.8) | copy-start | bytes 3145732
  27.6 13.5 %copy-start.5 = (bf16[2,1,64,256]{3,2,1,0:T(8,128)(2,1)S(1)}, bf16[2,1,64,256]{3,2,1,0:T(8,128)(2,1)}, u32[]{:S(2)}) copy-start(bf16[2,1,64,256]{3,2,1,0:T(8,128)(2,1)} %param.14) | copy-start | bytes 196612
  27.6 13.5 %copy-start.9 = (f32[256]{0:T(256)S(1)}, f32[256]{0:T(256)}, u32[]{:S(2)}) copy-start(f32[256]{0:T(256)} %param.18) | copy-start | bytes 3076
  27.6 16.8 %copy-start.14 = (f32[512]{0:T(512)S(1)}, f32[512]{0:T(512)}, u32[]{:S(2)}) copy-start(f32[512]{0:T(512)} %param.27) | copy-start | bytes 6148
  28.3 24.1 %copy-start.10 = (f32[256]{0:T(256)S(1)}, f32[256]{0:T(256)}, u32[]{:S(2)}) copy-start(f32[256]{0:T(256)} %param.20) | copy-start | bytes 3076
  28.3 24.1 %copy-start.11 = (f32[256]{0:T(256)S(1)}, f32[256]{0:T(256)}, u32[]{:S(2)}) copy-start(f32[256]{0:T(256)} %param.19) | copy-start | bytes 3076
  28.4 24.3 %copy-start.4 = (bf16[512,512]{1,0:T(8,128)(2,1)S(1)}, bf16[512,512]{1,0:T(8,128)(2,1)}, u32[]{:S(2)}) copy-start(bf16[512,512]{1,0:T(8,128)(2,1)} %param.24) | copy-start | bytes 1572868
  28.4 9.9 %collective-permute-start.7 = (f32[2,1,64,256]{3,2,1,0:T(8,128)S(1)}, f32[2,1,64,256]{3,2,1,0:T(8,128)S(1)}, u32[]{:S(2)}, u32[]{:S(2)}) collective-permute-start(f32[2,1,64,256]{3,2,1,0:T(8,128)S(1)} %get-tuple-element.26), channel_id=1, source_target_pairs={{0,8},{4,12},{8,0},{12,4},{1,9},{5,13},{9,1},{13,5},{2,10},{6,14},... | collective-permute-start | bytes 393224 | tf_op jit(solution)/shard_map/ppermute | solution.py:59
  28.5 12.6 %collective-permute-start.6 = (f32[2,1,64,256]{3,2,1,0:T(8,128)S(1)}, f32[2,1,64,256]{3,2,1,0:T(8,128)S(1)}, u32[]{:S(2)}, u32[]{:S(2)}) collective-permute-start(f32[2,1,64,256]{3,2,1,0:T(8,128)S(1)} %get-tuple-element.27), channel_id=1, source_target_pairs={{0,12},{4,0},{8,4},{12,8},{1,13},{5,1},{9,5},{13,9},{2,14},{6,2},{... | collective-permute-start | bytes 393224 | tf_op jit(solution)/shard_map/ppermute | solution.py:59
  31.1 10.0 %collective-permute-start.5 = (f32[2,1,64,256]{3,2,1,0:T(8,128)S(1)}, f32[2,1,64,256]{3,2,1,0:T(8,128)S(1)}, u32[]{:S(2)}, u32[]{:S(2)}) collective-permute-start(f32[2,1,64,256]{3,2,1,0:T(8,128)S(1)} %get-tuple-element.25), channel_id=1, source_target_pairs={{0,4},{4,8},{8,12},{12,0},{1,5},{5,9},{9,13},{13,1},{2,6},{6,10},{... | collective-permute-start | bytes 393224 | tf_op jit(solution)/shard_map/ppermute | solution.py:59
  41.1 11.8 %copy-start.3 = (bf16[512,512]{1,0:T(8,128)(2,1)S(1)}, bf16[512,512]{1,0:T(8,128)(2,1)}, u32[]{:S(2)}) copy-start(bf16[512,512]{1,0:T(8,128)(2,1)} %param.21) | copy-start | bytes 1572868
  41.2 6.8 %collective-permute-start.8 = (bf16[2,1,64,256]{3,2,1,0:T(8,128)(2,1)S(1)}, bf16[2,1,64,256]{3,2,1,0:T(8,128)(2,1)S(1)}, u32[]{:S(2)}, u32[]{:S(2)}) collective-permute-start(bf16[2,1,64,256]{3,2,1,0:T(8,128)(2,1)S(1)} %get-tuple-element.6), channel_id=1, source_target_pairs={{0,4},{4,8},{8,12},{12,0},{1,5},{5,9},{9,13},{13,1},{2,6},{6,10},{... | collective-permute-start | bytes 196616 | tf_op jit(solution)/shard_map/ppermute | solution.py:59
  44.5 4.8 %collective-permute-start.9 = (bf16[2,1,64,256]{3,2,1,0:T(8,128)(2,1)S(1)}, bf16[2,1,64,256]{3,2,1,0:T(8,128)(2,1)S(1)}, u32[]{:S(2)}, u32[]{:S(2)}) collective-permute-start(bf16[2,1,64,256]{3,2,1,0:T(8,128)(2,1)S(1)} %get-tuple-element.6), channel_id=1, source_target_pairs={{0,12},{4,0},{8,4},{12,8},{1,13},{5,1},{9,5},{13,9},{2,14},{6,2},{... | collective-permute-start | bytes 196616 | tf_op jit(solution)/shard_map/ppermute | solution.py:59
  45.1 6.4 %collective-permute-start.10 = (bf16[2,1,64,256]{3,2,1,0:T(8,128)(2,1)S(1)}, bf16[2,1,64,256]{3,2,1,0:T(8,128)(2,1)S(1)}, u32[]{:S(2)}, u32[]{:S(2)}) collective-permute-start(bf16[2,1,64,256]{3,2,1,0:T(8,128)(2,1)S(1)} %get-tuple-element.6), channel_id=1, source_target_pairs={{0,8},{4,12},{8,0},{12,4},{1,9},{5,13},{9,1},{13,5},{2,10},{6,14},... | collective-permute-start | bytes 196616 | tf_op jit(solution)/shard_map/ppermute | solution.py:59
  52.5 1.6 %collective-permute-start.11 = (bf16[2,4,64,256]{3,2,1,0:T(8,128)(2,1)S(1)}, bf16[2,4,64,256]{3,2,1,0:T(8,128)(2,1)S(1)}, u32[]{:S(2)}, u32[]{:S(2)}) collective-permute-start(bf16[2,4,64,256]{3,2,1,0:T(8,128)(2,1)S(1)} %fusion.36), channel_id=1, source_target_pairs={{0,1},{1,0},{2,3},{3,2},{4,5},{5,4},{6,7},{7,6},{8,9},{9,8},{10,11... | collective-permute-start | bytes 786440 | tf_op jit(solution)/shard_map/ppermute | solution.py:74
  52.9 1.5 %copy-start.8 = (f32[512]{0:T(512)S(1)}, f32[512]{0:T(512)}, u32[]{:S(2)}) copy-start(f32[512]{0:T(512)} %param.25) | copy-start | bytes 6148
  54.1 0.7 %copy-start.7 = (f32[512]{0:T(512)S(1)}, f32[512]{0:T(512)}, u32[]{:S(2)}) copy-start(f32[512]{0:T(512)} %param.22) | copy-start | bytes 6148
  54.4 1.4 %copy-start.6 = (bf16[512,512]{1,0:T(8,128)(2,1)S(1)}, bf16[512,512]{1,0:T(8,128)(2,1)}, u32[]{:S(2)}) copy-start(bf16[512,512]{1,0:T(8,128)(2,1)} %param.26) | copy-start | bytes 1572868

commit v13 on v11

--- a/solution.py
+++ b/solution.py
@@ -159,9 +159,8 @@
         jnp.zeros((span * C, out_channels), conv_weight.dtype), conv_weight, (offset, 0)
     ).reshape(span, chan_count, channels, out_channels)
     taps = (block_rows * row_count) // C
-    partial = None
-    for shift, half in enumerate(padded_halves):
-        source = (chan_place - shift) % chan_count
+    all_patches = []
+    for half in padded_halves:
         windows = []
         for step in range(span):
             tap = jnp.minimum(first_tap + step, taps - 1)
@@ -172,7 +171,11 @@
                     (frames, all_rows, columns, channels),
                 ).reshape(-1, channels)
             )
-        patches = jnp.concatenate(windows, axis=1)
+        all_patches.append(jnp.concatenate(windows, axis=1))
+    all_patches = lax.optimization_barrier(all_patches)
+    partial = None
+    for shift, patches in enumerate(all_patches):
+        source = (chan_place - shift) % chan_count
         block = lax.dynamic_index_in_dim(placed, source, axis=1, keepdims=False).reshape(
             span * channels, out_channels
         )

time: 56.8 us -> 58.3 us (1.026)
  waiting for transfers between devices: 24.7 us -> 26.7 us
    ppermute x10, waiting for transfers between devices: 24.1 us -> 26.1 us  [shifted(): return lax.ppermute(cells, axes, pairs)]
  transfers between devices with their start and end apart: 12 -> 12, of which waited for: 10 -> 10; matrix products, arithmetic and copies ran while one was open for 10% -> 9% of each run, Pallas kernels for 0% -> 0%
where the time goes in v13:
time: 58.3 us; the launch traced here: 58.1 us
  waiting for transfers between devices  26.7 us (46%)
  starting transfers between devices  15.5 us (27%)
  local copies, waits for them, and re-layouts  8.21 us (14%)
  matrix products  3.85 us (7%)
  other arithmetic  3.16 us (5%)
  between operations  0.65 us (1%)
    ppermute x10, waiting for transfers between devices, shifted(): return lax.ppermute(cells, axes, pairs)  26.1 us
    ppermute x10, starting transfers between devices, shifted(): return lax.ppermute(cells, axes, pairs)  15.3 us
    dynamic_slice x4, local copies, waits for them, and re-layouts, local(): lax.dynamic_slice(half, (tap // 9, tap // 3 % 3, tap % 3, 0), (frames, al...  2.55 us
    dot_general x6, matrix products, split_dot(): jnp.dot(half, half_rows(weight, shift, width), preferred_element_type=jnp...  1.59 us
    dot_general x2, matrix products, local(): term = jnp.dot(patches, block, preferred_element_type=jnp.float32)  1.45 us
    unnamed x44, local copies, waits for them, and re-layouts  1.39 us
  transfers between devices with their start and end apart: 12, of which 10 were waited for; matrix products, arithmetic and copies ran while one was open for 9% of the time, Pallas kernels for 0%

profile of v13, /device:TPU:0, one launch (start us, length us, event | category | flops | bytes accessed | tf_op | source)
XLA Modules:
  0.0 58.1 jit_solution(11112023992044061222)
XLA Ops:
  0.0 3.0 %collective-permute-start = (bf16[2,1,64,256]{3,2,1,0:T(8,128)(2,1)}, bf16[2,1,64,256]{3,2,1,0:T(8,128)(2,1)S(1)}, u32[]{:S(2)}, u32[]{:S(2)}) collective-permute-start(bf16[2,1,64,256]{3,2,1,0:T(8,128)(2,1)} %param.14), channel_id=1, source_target_pairs={{0,4},{4,8},{8,12},{12,0},{1,5},{5,9},{9,13},{13,1},{2,6},{6,10},{... | collective-permute-start | bytes 196616 | tf_op jit(solution)/shard_map/ppermute | solution.py:53
  3.0 2.1 %collective-permute-start.1 = (bf16[2,1,64,256]{3,2,1,0:T(8,128)(2,1)}, bf16[2,1,64,256]{3,2,1,0:T(8,128)(2,1)S(1)}, u32[]{:S(2)}, u32[]{:S(2)}) collective-permute-start(bf16[2,1,64,256]{3,2,1,0:T(8,128)(2,1)} %param.14), channel_id=1, source_target_pairs={{0,12},{4,0},{8,4},{12,8},{1,13},{5,1},{9,5},{13,9},{2,14},{6,2},{... | collective-permute-start | bytes 196616 | tf_op jit(solution)/shard_map/ppermute | solution.py:53
  5.1 0.9 %collective-permute-start.2 = (bf16[2,1,64,256]{3,2,1,0:T(8,128)(2,1)}, bf16[2,1,64,256]{3,2,1,0:T(8,128)(2,1)S(1)}, u32[]{:S(2)}, u32[]{:S(2)}) collective-permute-start(bf16[2,1,64,256]{3,2,1,0:T(8,128)(2,1)} %param.14), channel_id=1, source_target_pairs={{0,8},{4,12},{8,0},{12,4},{1,9},{5,13},{9,1},{13,5},{2,10},{6,14},... | collective-permute-start | bytes 196616 | tf_op jit(solution)/shard_map/ppermute | solution.py:53
  6.1 0.9 %constant_dynamic-update-slice_fusion.26 = bf16[2,4,64,256]{3,2,1,0:T(8,128)(2,1)S(1)} fusion(bf16[2,4,64,256]{3,2,1,0:T(8,128)(2,1)S(1)} %broadcast.147.clone, bf16[2,1,64,256]{3,2,1,0:T(8,128)(2,1)} %param.14, s32[]{:T(128)S(6)} %select_n.416), kind=kLoop, calls=%fused_computation.132 | loop fusion | bytes 131076 | tf_op jit(solution)/shard_map/dynamic_update_slice | solution.py:118
  7.0 0.1 broadcast_in_dim.17
  7.1 0.2 constant_dynamic-update-slice_fusion.20
  7.4 0.3 collective-permute-done
  7.7 0.5 collective-permute-done.1
  8.2 3.3 %collective-permute-done.2 = bf16[2,1,64,256]{3,2,1,0:T(8,128)(2,1)S(1)} collective-permute-done((bf16[2,1,64,256]{3,2,1,0:T(8,128)(2,1)}, bf16[2,1,64,256]{3,2,1,0:T(8,128)(2,1)S(1)}, u32[]{:S(2)}, u32[]{:S(2)}) %collective-permute-start.2) | collective-permute-done | bytes 65568 | tf_op jit(solution)/shard_map/ppermute | solution.py:53
  11.6 1.6 %collective-permute-start.3 = (bf16[2,4,64,256]{3,2,1,0:T(8,128)(2,1)S(1)}, bf16[2,4,64,256]{3,2,1,0:T(8,128)(2,1)S(1)}, u32[]{:S(2)}, u32[]{:S(2)}) collective-permute-start(bf16[2,4,64,256]{3,2,1,0:T(8,128)(2,1)S(1)} %constant_dynamic-update-slice_fusion.23), channel_id=1, source_target_pairs={{0,2},{2,0},{1,3},{3,1},{4,6},{6,4},{5,7},{7,5},{8,10},{10,8},{9,1... | collective-permute-start | bytes 786440 | tf_op jit(solution)/shard_map/ppermute | solution.py:53
  13.1 1.1 %constant_dynamic-slice_fusion.2 = (bf16[8,1,256,256]{3,2,1,0:T(8,128)(2,1)S(1)}, bf16[8,1,256,256]{3,2,1,0:T(8,128)(2,1)}) fusion(bf16[8,2,256,256]{3,2,1,0:T(8,128)(2,1)S(1)} %bitcast.68, s32[]{:T(128)S(6)} %select_n.491, s32[]{:T(128)S(6)} %select_n.489), kind=kLoop, calls=%fused_computation.108 | loop fusion | bytes 4194312 | tf_op jit(solution)/shard_map/jit(dynamic_index_in_dim)/dynamic_slice | solution.py:179
  14.3 5.2 %collective-permute-done.3 = bf16[2,4,64,256]{3,2,1,0:T(8,128)(2,1)S(1)} collective-permute-done((bf16[2,4,64,256]{3,2,1,0:T(8,128)(2,1)S(1)}, bf16[2,4,64,256]{3,2,1,0:T(8,128)(2,1)S(1)}, u32[]{:S(2)}, u32[]{:S(2)}) %collective-permute-start.3) | collective-permute-done | bytes 262176 | tf_op jit(solution)/shard_map/ppermute | solution.py:53
  19.5 0.2 convert_reduce_fusion
  19.7 0.6 gather_fusion
  20.3 0.1 reduce_sum.55
  20.4 0.1 reduce_sum.59
  20.5 0.1 sub.143
  20.6 0.1 sub.144
  20.6 0.2 fusion.20
  20.9 0.1 reduce_sum.61
  20.9 0.1 reduce_sum.62
  21.1 0.1 mul.91
  21.2 0.5 multiply_convert_fusion
  21.7 0.1 collective-permute-start.4
  21.8 0.4 fusion.24
  22.2 0.2 constant_dynamic-slice_fusion.18
  22.5 1.1 %constant_dynamic-slice_fusion.12 = (bf16[2,4,64,256]{3,2,1,0:T(8,128)(2,1)S(1)}, bf16[2,4,64,256]{3,2,1,0:T(8,128)(2,1)S(1)}, bf16[2,4,64,256]{3,2,1,0:T(8,128)...) fusion(bf16[4,6,66,256]{3,2,1,0:T(8,128)(2,1)S(1)} %fusion.24, ...), kind=kLoop, calls=%fused_computation.119 | loop fusion | bytes 3145800 | tf_op jit(solution)/shard_map/dynamic_slice | solution.py:168
  23.7 0.4 fusion.28
  24.1 1.1 %constant_dynamic-slice_fusion.4 = (bf16[2,4,64,256]{3,2,1,0:T(8,128)(2,1)S(1)}, bf16[2,4,64,256]{3,2,1,0:T(8,128)(2,1)S(1)}, bf16[2,4,64,256]{3,2,1,0:T(8,128)(...) fusion(bf16[4,6,66,256]{3,2,1,0:T(8,128)(2,1)S(1)} %fusion.28, ...), kind=kLoop, calls=%fused_computation.111 | loop fusion | bytes 3145800 | tf_op jit(solution)/shard_map/dynamic_slice | solution.py:168
  25.2 0.2 constant_dynamic-slice_fusion.10
  25.7 0.9 %copy-done.2 = bf16[8,1,256,256]{3,2,1,0:T(8,128)(2,1)S(1)} copy-done((bf16[8,1,256,256]{3,2,1,0:T(8,128)(2,1)S(1)}, bf16[8,1,256,256]{3,2,1,0:T(8,128)(2,1)}, u32[]{:S(2)}) %copy-start.2) | copy-done | bytes 1048600
  26.7 0.7 %fusion.71 = f32[512,256]{1,0:T(8,128)S(1)} fusion(bf16[512,2048]{1,0:T(8,128)(2,1)S(1)} %get-tuple-element.7, bf16[2048,256]{1,0:T(8,128)(2,1)S(1)} %bitcast.75), kind=kOutput, calls=%fused_computation.145 | convolution fusion | flops 536870912 | bytes 3670016 | tf_op jit(solution)/shard_map/dot_general | solution.py:182
  27.4 0.7 %convolution_add_fusion.2 = f32[512,256]{1,0:T(8,128)S(1)} fusion(f32[512,256]{1,0:T(8,128)S(1)} %fusion.71, bf16[512,2048]{1,0:T(8,128)(2,1)S(1)} %get-tuple-element.8, bf16[2048,256]{1,0:T(8,128)(2,1)S(1)} %bitcast.74), kind=kOutput, calls=%fused_computation.22 | convolution fusion | flops 537001984 | bytes 4194304 | tf_op jit(solution)/shard_map/dot_general | solution.py:182
  28.3 3.8 %collective-permute-start.6 = (f32[2,1,64,256]{3,2,1,0:T(8,128)S(1)}, f32[2,1,64,256]{3,2,1,0:T(8,128)S(1)}, u32[]{:S(2)}, u32[]{:S(2)}) collective-permute-start(f32[2,1,64,256]{3,2,1,0:T(8,128)S(1)} %get-tuple-element.31), channel_id=1, source_target_pairs={{0,12},{4,0},{8,4},{12,8},{1,13},{5,1},{9,5},{13,9},{2,14},{6,2},{... | collective-permute-start | bytes 393224 | tf_op jit(solution)/shard_map/ppermute | solution.py:53
  32.1 4.3 %collective-permute-done.5 = f32[2,1,64,256]{3,2,1,0:T(8,128)S(1)} collective-permute-done((f32[2,1,64,256]{3,2,1,0:T(8,128)S(1)}, f32[2,1,64,256]{3,2,1,0:T(8,128)S(1)}, u32[]{:S(2)}, u32[]{:S(2)}) %collective-permute-start.5) | collective-permute-done | bytes 131104 | tf_op jit(solution)/shard_map/ppermute | solution.py:53
  36.4 0.6 %collective-permute-done.6 = f32[2,1,64,256]{3,2,1,0:T(8,128)S(1)} collective-permute-done((f32[2,1,64,256]{3,2,1,0:T(8,128)S(1)}, f32[2,1,64,256]{3,2,1,0:T(8,128)S(1)}, u32[]{:S(2)}, u32[]{:S(2)}) %collective-permute-start.6) | collective-permute-done | bytes 131104 | tf_op jit(solution)/shard_map/ppermute | solution.py:53
  37.1 6.7 %collective-permute-done.7 = f32[2,1,64,256]{3,2,1,0:T(8,128)S(1)} collective-permute-done((f32[2,1,64,256]{3,2,1,0:T(8,128)S(1)}, f32[2,1,64,256]{3,2,1,0:T(8,128)S(1)}, u32[]{:S(2)}, u32[]{:S(2)}) %collective-permute-start.7) | collective-permute-done | bytes 131104 | tf_op jit(solution)/shard_map/ppermute | solution.py:53
  43.9 0.1 dynamic_slice.129
  44.0 3.8 %collective-permute-start.9 = (bf16[2,1,64,256]{3,2,1,0:T(8,128)(2,1)S(1)}, bf16[2,1,64,256]{3,2,1,0:T(8,128)(2,1)S(1)}, u32[]{:S(2)}, u32[]{:S(2)}) collective-permute-start(bf16[2,1,64,256]{3,2,1,0:T(8,128)(2,1)S(1)} %get-tuple-element.10), channel_id=1, source_target_pairs={{0,12},{4,0},{8,4},{12,8},{1,13},{5,1},{9,5},{13,9},{2,14},{6,2},{... | collective-permute-start | bytes 196616 | tf_op jit(solution)/shard_map/ppermute | solution.py:53
  47.8 2.9 %collective-permute-done.8 = bf16[2,1,64,256]{3,2,1,0:T(8,128)(2,1)S(1)} collective-permute-done((bf16[2,1,64,256]{3,2,1,0:T(8,128)(2,1)S(1)}, bf16[2,1,64,256]{3,2,1,0:T(8,128)(2,1)S(1)}, u32[]{:S(2)}, u32[]{:S(2)}) %collective-permute-start.8) | collective-permute-done | bytes 65568 | tf_op jit(solution)/shard_map/ppermute | solution.py:53
  50.7 2.2 %collective-permute-done.10 = bf16[2,1,64,256]{3,2,1,0:T(8,128)(2,1)S(1)} collective-permute-done((bf16[2,1,64,256]{3,2,1,0:T(8,128)(2,1)S(1)}, bf16[2,1,64,256]{3,2,1,0:T(8,128)(2,1)S(1)}, u32[]{:S(2)}, u32[]{:S(2)}) %collective-permute-start.10) | collective-permute-done | bytes 65568 | tf_op jit(solution)/shard_map/ppermute | solution.py:53
  53.0 0.1 reduce_sum.80
  53.1 0.1 reduce_sum.81
  53.2 0.1 sub.166
  53.3 0.1 sub.167
  53.4 0.1 fusion.35
  53.4 0.1 reduce_sum.83
  53.5 0.1 reduce_sum.84
  53.6 0.1 mul.99
  53.7 0.1 mul.100
  53.8 0.1 fusion.38
  53.9 0.1 collective-permute-start.11
  54.0 0.3 fusion.44
  54.4 0.2 fusion.47
  54.6 0.3 fusion.41
  54.9 0.6 %collective-permute-done.11 = bf16[2,4,64,256]{3,2,1,0:T(8,128)(2,1)S(1)} collective-permute-done((bf16[2,4,64,256]{3,2,1,0:T(8,128)(2,1)S(1)}, bf16[2,4,64,256]{3,2,1,0:T(8,128)(2,1)S(1)}, u32[]{:S(2)}, u32[]{:S(2)}) %collective-permute-start.11) | collective-permute-done | bytes 262176 | tf_op jit(solution)/shard_map/ppermute | solution.py:68
  55.5 0.3 fusion.13
  55.9 0.2 fusion.16
  56.1 0.4 fusion.70
  56.4 0.2 fusion.55
  56.6 0.3 fusion.14
  56.9 0.3 fusion.17
  57.2 0.2 fusion.18
  57.4 0.6 %fusion.49 = bf16[2,1,64,256]{3,2,1,0:T(8,128)(2,1)} fusion(bf16[2,1,64,256]{3,2,1,0:T(8,128)(2,1)S(1)} %bitcast.97, bf16[2,1,64,256]{3,2,1,0:T(8,128)(2,1)S(1)} %get-tuple-element.10), kind=kLoop, calls=%fused_computation.65 | loop fusion | flops 131072 | bytes 196608 | tf_op jit(solution)/shard_map/convert_element_type | solution.py:257
  (76 shorter events, 1.2 us)
Async XLA Ops:
  0.0 54.0 %copy-start = (bf16[512,512]{1,0:T(8,128)(2,1)S(1)}, bf16[512,512]{1,0:T(8,128)(2,1)}, u32[]{:S(2)}) copy-start(bf16[512,512]{1,0:T(8,128)(2,1)} %param.23) | copy-start | bytes 1572868
  0.0 7.1 %copy-start.1 = (bf16[3456,256]{1,0:T(8,128)(2,1)S(1)}, bf16[3456,256]{1,0:T(8,128)(2,1)}, u32[]{:S(2)}) copy-start(bf16[3456,256]{1,0:T(8,128)(2,1)} %param.17) | copy-start | bytes 5308420
  0.0 7.7 %collective-permute-start = (bf16[2,1,64,256]{3,2,1,0:T(8,128)(2,1)}, bf16[2,1,64,256]{3,2,1,0:T(8,128)(2,1)S(1)}, u32[]{:S(2)}, u32[]{:S(2)}) collective-permute-start(bf16[2,1,64,256]{3,2,1,0:T(8,128)(2,1)} %param.14), channel_id=1, source_target_pairs={{0,4},{4,8},{8,12},{12,0},{1,5},{5,9},{9,13},{13,1},{2,6},{6,10},{... | collective-permute-start | bytes 196616 | tf_op jit(solution)/shard_map/ppermute | solution.py:53
  3.0 5.2 %collective-permute-start.1 = (bf16[2,1,64,256]{3,2,1,0:T(8,128)(2,1)}, bf16[2,1,64,256]{3,2,1,0:T(8,128)(2,1)S(1)}, u32[]{:S(2)}, u32[]{:S(2)}) collective-permute-start(bf16[2,1,64,256]{3,2,1,0:T(8,128)(2,1)} %param.14), channel_id=1, source_target_pairs={{0,12},{4,0},{8,4},{12,8},{1,13},{5,1},{9,5},{13,9},{2,14},{6,2},{... | collective-permute-start | bytes 196616 | tf_op jit(solution)/shard_map/ppermute | solution.py:53
  5.1 6.4 %collective-permute-start.2 = (bf16[2,1,64,256]{3,2,1,0:T(8,128)(2,1)}, bf16[2,1,64,256]{3,2,1,0:T(8,128)(2,1)S(1)}, u32[]{:S(2)}, u32[]{:S(2)}) collective-permute-start(bf16[2,1,64,256]{3,2,1,0:T(8,128)(2,1)} %param.14), channel_id=1, source_target_pairs={{0,8},{4,12},{8,0},{12,4},{1,9},{5,13},{9,1},{13,5},{2,10},{6,14},... | collective-permute-start | bytes 196616 | tf_op jit(solution)/shard_map/ppermute | solution.py:53
  11.6 7.9 %collective-permute-start.3 = (bf16[2,4,64,256]{3,2,1,0:T(8,128)(2,1)S(1)}, bf16[2,4,64,256]{3,2,1,0:T(8,128)(2,1)S(1)}, u32[]{:S(2)}, u32[]{:S(2)}) collective-permute-start(bf16[2,4,64,256]{3,2,1,0:T(8,128)(2,1)S(1)} %constant_dynamic-update-slice_fusion.23), channel_id=1, source_target_pairs={{0,2},{2,0},{1,3},{3,1},{4,6},{6,4},{5,7},{7,5},{8,10},{10,8},{9,1... | collective-permute-start | bytes 786440 | tf_op jit(solution)/shard_map/ppermute | solution.py:53
  14.2 7.0 %copy-start.12 = (f32[256]{0:T(256)S(1)}, f32[256]{0:T(256)}, u32[]{:S(2)}) copy-start(f32[256]{0:T(256)} %param.16) | copy-start | bytes 3076
  14.2 7.0 %copy-start.13 = (f32[256]{0:T(256)S(1)}, f32[256]{0:T(256)}, u32[]{:S(2)}) copy-start(f32[256]{0:T(256)} %param.15) | copy-start | bytes 3076
  21.7 2.0 %collective-permute-start.4 = (bf16[4,4,64,256]{3,2,1,0:T(8,128)(2,1)S(1)}, bf16[4,4,64,256]{3,2,1,0:T(8,128)(2,1)S(1)}, u32[]{:S(2)}, u32[]{:S(2)}) collective-permute-start(bf16[4,4,64,256]{3,2,1,0:T(8,128)(2,1)S(1)} %multiply_convert_fusion), channel_id=1, source_target_pairs={{0,1},{1,0},{2,3},{3,2},{4,5},{5,4},{6,7},{7,6},{8,9},{9,8},{10,11... | collective-permute-start | bytes 1572872 | tf_op jit(solution)/shard_map/ppermute | solution.py:68
  25.4 1.2 %copy-start.2 = (bf16[8,1,256,256]{3,2,1,0:T(8,128)(2,1)S(1)}, bf16[8,1,256,256]{3,2,1,0:T(8,128)(2,1)}, u32[]{:S(2)}) copy-start(bf16[8,1,256,256]{3,2,1,0:T(8,128)(2,1)} %get-tuple-element.12) | copy-start | bytes 3145732
  27.4 16.3 %copy-start.5 = (bf16[2,1,64,256]{3,2,1,0:T(8,128)(2,1)S(1)}, bf16[2,1,64,256]{3,2,1,0:T(8,128)(2,1)}, u32[]{:S(2)}) copy-start(bf16[2,1,64,256]{3,2,1,0:T(8,128)(2,1)} %param.14) | copy-start | bytes 196612
  27.4 16.3 %copy-start.9 = (f32[256]{0:T(256)S(1)}, f32[256]{0:T(256)}, u32[]{:S(2)}) copy-start(f32[256]{0:T(256)} %param.18) | copy-start | bytes 3076
  27.4 16.5 %copy-start.14 = (f32[512]{0:T(512)S(1)}, f32[512]{0:T(512)}, u32[]{:S(2)}) copy-start(f32[512]{0:T(512)} %param.27) | copy-start | bytes 6148
  28.2 25.6 %copy-start.10 = (f32[256]{0:T(256)S(1)}, f32[256]{0:T(256)}, u32[]{:S(2)}) copy-start(f32[256]{0:T(256)} %param.20) | copy-start | bytes 3076
  28.2 25.6 %copy-start.11 = (f32[256]{0:T(256)S(1)}, f32[256]{0:T(256)}, u32[]{:S(2)}) copy-start(f32[256]{0:T(256)} %param.19) | copy-start | bytes 3076
  28.2 8.2 %collective-permute-start.5 = (f32[2,1,64,256]{3,2,1,0:T(8,128)S(1)}, f32[2,1,64,256]{3,2,1,0:T(8,128)S(1)}, u32[]{:S(2)}, u32[]{:S(2)}) collective-permute-start(f32[2,1,64,256]{3,2,1,0:T(8,128)S(1)} %get-tuple-element.29), channel_id=1, source_target_pairs={{0,4},{4,8},{8,12},{12,0},{1,5},{5,9},{9,13},{13,1},{2,6},{6,10},{... | collective-permute-start | bytes 393224 | tf_op jit(solution)/shard_map/ppermute | solution.py:53
  28.3 8.8 %collective-permute-start.6 = (f32[2,1,64,256]{3,2,1,0:T(8,128)S(1)}, f32[2,1,64,256]{3,2,1,0:T(8,128)S(1)}, u32[]{:S(2)}, u32[]{:S(2)}) collective-permute-start(f32[2,1,64,256]{3,2,1,0:T(8,128)S(1)} %get-tuple-element.31), channel_id=1, source_target_pairs={{0,12},{4,0},{8,4},{12,8},{1,13},{5,1},{9,5},{13,9},{2,14},{6,2},{... | collective-permute-start | bytes 393224 | tf_op jit(solution)/shard_map/ppermute | solution.py:53
  32.1 11.6 %collective-permute-start.7 = (f32[2,1,64,256]{3,2,1,0:T(8,128)S(1)}, f32[2,1,64,256]{3,2,1,0:T(8,128)S(1)}, u32[]{:S(2)}, u32[]{:S(2)}) collective-permute-start(f32[2,1,64,256]{3,2,1,0:T(8,128)S(1)} %get-tuple-element.30), channel_id=1, source_target_pairs={{0,8},{4,12},{8,0},{12,4},{1,9},{5,13},{9,1},{13,5},{2,10},{6,14},... | collective-permute-start | bytes 393224 | tf_op jit(solution)/shard_map/ppermute | solution.py:53
  43.7 10.6 %copy-start.3 = (bf16[512,512]{1,0:T(8,128)(2,1)S(1)}, bf16[512,512]{1,0:T(8,128)(2,1)}, u32[]{:S(2)}) copy-start(bf16[512,512]{1,0:T(8,128)(2,1)} %param.21) | copy-start | bytes 1572868
  43.8 10.7 %copy-start.4 = (bf16[512,512]{1,0:T(8,128)(2,1)S(1)}, bf16[512,512]{1,0:T(8,128)(2,1)}, u32[]{:S(2)}) copy-start(bf16[512,512]{1,0:T(8,128)(2,1)} %param.24) | copy-start | bytes 1572868
  43.8 6.9 %collective-permute-start.8 = (bf16[2,1,64,256]{3,2,1,0:T(8,128)(2,1)S(1)}, bf16[2,1,64,256]{3,2,1,0:T(8,128)(2,1)S(1)}, u32[]{:S(2)}, u32[]{:S(2)}) collective-permute-start(bf16[2,1,64,256]{3,2,1,0:T(8,128)(2,1)S(1)} %get-tuple-element.10), channel_id=1, source_target_pairs={{0,4},{4,8},{8,12},{12,0},{1,5},{5,9},{9,13},{13,1},{2,6},{6,10},{... | collective-permute-start | bytes 196616 | tf_op jit(solution)/shard_map/ppermute | solution.py:53
  44.0 6.7 %collective-permute-start.9 = (bf16[2,1,64,256]{3,2,1,0:T(8,128)(2,1)S(1)}, bf16[2,1,64,256]{3,2,1,0:T(8,128)(2,1)S(1)}, u32[]{:S(2)}, u32[]{:S(2)}) collective-permute-start(bf16[2,1,64,256]{3,2,1,0:T(8,128)(2,1)S(1)} %get-tuple-element.10), channel_id=1, source_target_pairs={{0,12},{4,0},{8,4},{12,8},{1,13},{5,1},{9,5},{13,9},{2,14},{6,2},{... | collective-permute-start | bytes 196616 | tf_op jit(solution)/shard_map/ppermute | solution.py:53
  47.8 5.2 %collective-permute-start.10 = (bf16[2,1,64,256]{3,2,1,0:T(8,128)(2,1)S(1)}, bf16[2,1,64,256]{3,2,1,0:T(8,128)(2,1)S(1)}, u32[]{:S(2)}, u32[]{:S(2)}) collective-permute-start(bf16[2,1,64,256]{3,2,1,0:T(8,128)(2,1)S(1)} %get-tuple-element.10), channel_id=1, source_target_pairs={{0,8},{4,12},{8,0},{12,4},{1,9},{5,13},{9,1},{13,5},{2,10},{6,14},... | collective-permute-start | bytes 196616 | tf_op jit(solution)/shard_map/ppermute | solution.py:53
  53.9 1.6 %collective-permute-start.11 = (bf16[2,4,64,256]{3,2,1,0:T(8,128)(2,1)S(1)}, bf16[2,4,64,256]{3,2,1,0:T(8,128)(2,1)S(1)}, u32[]{:S(2)}, u32[]{:S(2)}) collective-permute-start(bf16[2,4,64,256]{3,2,1,0:T(8,128)(2,1)S(1)} %fusion.38), channel_id=1, source_target_pairs={{0,1},{1,0},{2,3},{3,2},{4,5},{5,4},{6,7},{7,6},{8,9},{9,8},{10,11... | collective-permute-start | bytes 786440 | tf_op jit(solution)/shard_map/ppermute | solution.py:68
  54.3 1.5 %copy-start.7 = (f32[512]{0:T(512)S(1)}, f32[512]{0:T(512)}, u32[]{:S(2)}) copy-start(f32[512]{0:T(512)} %param.22) | copy-start | bytes 6148
  54.9 1.8 %copy-start.8 = (f32[512]{0:T(512)S(1)}, f32[512]{0:T(512)}, u32[]{:S(2)}) copy-start(f32[512]{0:T(512)} %param.25) | copy-start | bytes 6148
  56.1 1.1 %copy-start.6 = (bf16[512,512]{1,0:T(8,128)(2,1)S(1)}, bf16[512,512]{1,0:T(8,128)(2,1)}, u32[]{:S(2)}) copy-start(bf16[512,512]{1,0:T(8,128)(2,1)} %param.26) | copy-start | bytes 1572868

commit v14 on v12

--- a/solution.py
+++ b/solution.py
@@ -124,21 +124,27 @@
             segment_rows = lax.dynamic_update_slice(
                 segment_rows, block, (0, source_row * rows_here, 0, 0)
             )
-        clip = jnp.zeros((time_count * frames, all_rows, columns, channels), latent.dtype)
-        block_stats = []
-        for shift in [0] + nearest_first(time_count):
-            block = segment_rows if shift == 0 else shifted(
-                segment_rows, ("tm",), (time_count,), (shift,)
-            )
-            block_stats.append(group_stats(block, group_size, (0, 1, 2, 4)))
-            source_time = (time_place - shift) % time_count
-            clip = lax.dynamic_update_slice(clip, block, (source_time * frames, 0, 0, 0))
-        while len(block_stats) > 1 and len(block_stats) % 2 == 0:
-            block_stats = [
-                merged_stats(block_stats[i], block_stats[i + 1])
-                for i in range(0, len(block_stats), 2)
-            ]
-        stats1 = block_stats[0] if len(block_stats) == 1 else None
+        stats1 = None
+        if time_count == 2:
+            earlier = lax.ppermute(segment_rows, "tm", [(0, 1)])
+            own_stats = group_stats(segment_rows, group_size, (0, 1, 2, 4))
+            later_stats = lax.ppermute(own_stats, "tm", [(1, 0)])
+            earlier_stats = group_stats(earlier, group_size, (0, 1, 2, 4))
+            other_stats = tuple(
+                jnp.where(time_place == 0, late, early)
+                for late, early in zip(later_stats, earlier_stats)
+            )
+            stats1 = merged_stats(own_stats, other_stats)
+            first = jnp.where(time_place == 0, segment_rows, earlier)
+            clip = jnp.concatenate([first, segment_rows], axis=0)
+        else:
+            clip = jnp.zeros((time_count * frames, all_rows, columns, channels), latent.dtype)
+            for shift in [0] + nearest_first(time_count):
+                block = segment_rows if shift == 0 else shifted(
+                    segment_rows, ("tm",), (time_count,), (shift,)
+                )
+                source_time = (time_place - shift) % time_count
+                clip = lax.dynamic_update_slice(clip, block, (source_time * frames, 0, 0, 0))
     else:
         copies = jnp.broadcast_to(latent[None], (row_count * time_count,) + latent.shape)
         gathered = lax.all_to_all(copies, ("rows", "tm"), 0, 0, tiled=True).reshape(

time: 56.9 us -> 58.9 us (1.035)
  starting transfers between devices: 16 us -> 20.4 us
  waiting for transfers between devices: 24 us -> 21.5 us
    ppermute x0 -> x3, starting transfers between devices: none -> 5.99 us  [the longest x1 3.4 us: local(): earlier = lax.ppermute(segment_rows, 'tm', [(0, 1)])]
    ppermute x10 -> x9, waiting for transfers between devices: 23.3 us -> 17.4 us  [shifted(): return lax.ppermute(cells, axes, pairs)]
    ppermute x0 -> x3, waiting for transfers between devices: none -> 3.36 us  [the longest x1 1.99 us: local(): earlier = lax.ppermute(segment_rows, 'tm', [(0, 1)])]
    ppermute x10 -> x9, starting transfers between devices: 15.8 us -> 14.3 us  [shifted(): return lax.ppermute(cells, axes, pairs)]
  transfers between devices with their start and end apart: 12 -> 14, of which waited for: 8 -> 9; matrix products, arithmetic and copies ran while one was open for 12% -> 12% of each run, Pallas kernels for 0% -> 0%
where the time goes in v14:
time: 58.9 us; the launch traced here: 58.6 us
  waiting for transfers between devices  21.5 us (37%)
  starting transfers between devices  20.4 us (35%)
  local copies, waits for them, and re-layouts  8.72 us (15%)
  matrix products  3.85 us (7%)
  other arithmetic  3.53 us (6%)
  between operations  0.68 us (1%)
    ppermute x9, waiting for transfers between devices, shifted(): return lax.ppermute(cells, axes, pairs)  17.4 us
    ppermute x9, starting transfers between devices, shifted(): return lax.ppermute(cells, axes, pairs)  14.3 us
    ppermute x1, starting transfers between devices, local(): earlier = lax.ppermute(segment_rows, 'tm', [(0, 1)])  3.4 us
    ppermute x2, starting transfers between devices, local(): later_stats = lax.ppermute(own_stats, 'tm', [(1, 0)])  2.58 us
    dynamic_slice x4, local copies, waits for them, and re-layouts, local(): lax.dynamic_slice(half, (tap // 9, tap // 3 % 3, tap % 3, 0), (frames, al...  2.55 us
    ppermute x1, waiting for transfers between devices, local(): earlier = lax.ppermute(segment_rows, 'tm', [(0, 1)])  1.99 us
    dot_general x6, matrix products, split_dot(): jnp.dot(half, half_rows(weight, shift, width), preferred_element_type=jnp...  1.57 us
    unnamed x44, local copies, waits for them, and re-layouts  1.49 us
  transfers between devices with their start and end apart: 14, of which 9 were waited for; matrix products, arithmetic and copies ran while one was open for 12% of the time, Pallas kernels for 0%

profile of v14, /device:TPU:0, one launch (start us, length us, event | category | flops | bytes accessed | tf_op | source)
XLA Modules:
  0.0 58.6 jit_solution(6268857940354884459)
XLA Ops:
  0.0 3.0 %collective-permute-start = (bf16[2,1,64,256]{3,2,1,0:T(8,128)(2,1)}, bf16[2,1,64,256]{3,2,1,0:T(8,128)(2,1)S(1)}, u32[]{:S(2)}, u32[]{:S(2)}) collective-permute-start(bf16[2,1,64,256]{3,2,1,0:T(8,128)(2,1)} %param.14), channel_id=1, source_target_pairs={{0,4},{4,8},{8,12},{12,0},{1,5},{5,9},{9,13},{13,1},{2,6},{6,10},{... | collective-permute-start | bytes 196616 | tf_op jit(solution)/shard_map/ppermute | solution.py:59
  3.0 2.1 %collective-permute-start.1 = (bf16[2,1,64,256]{3,2,1,0:T(8,128)(2,1)}, bf16[2,1,64,256]{3,2,1,0:T(8,128)(2,1)S(1)}, u32[]{:S(2)}, u32[]{:S(2)}) collective-permute-start(bf16[2,1,64,256]{3,2,1,0:T(8,128)(2,1)} %param.14), channel_id=1, source_target_pairs={{0,12},{4,0},{8,4},{12,8},{1,13},{5,1},{9,5},{13,9},{2,14},{6,2},{... | collective-permute-start | bytes 196616 | tf_op jit(solution)/shard_map/ppermute | solution.py:59
  5.1 0.9 %collective-permute-start.2 = (bf16[2,1,64,256]{3,2,1,0:T(8,128)(2,1)}, bf16[2,1,64,256]{3,2,1,0:T(8,128)(2,1)S(1)}, u32[]{:S(2)}, u32[]{:S(2)}) collective-permute-start(bf16[2,1,64,256]{3,2,1,0:T(8,128)(2,1)} %param.14), channel_id=1, source_target_pairs={{0,8},{4,12},{8,0},{12,4},{1,9},{5,13},{9,1},{13,5},{2,10},{6,14},... | collective-permute-start | bytes 196616 | tf_op jit(solution)/shard_map/ppermute | solution.py:59
  6.1 0.9 %constant_dynamic-update-slice_fusion.24 = bf16[2,4,64,256]{3,2,1,0:T(8,128)(2,1)S(1)} fusion(bf16[2,4,64,256]{3,2,1,0:T(8,128)(2,1)S(1)} %broadcast.179.clone, bf16[2,1,64,256]{3,2,1,0:T(8,128)(2,1)} %param.14, s32[]{:T(128)S(6)} %select_n.423), kind=kLoop, calls=%fused_computation.136 | loop fusion | bytes 131076 | tf_op jit(solution)/shard_map/dynamic_update_slice | solution.py:124
  7.0 0.1 broadcast_in_dim.14
  7.1 0.2 constant_dynamic-update-slice_fusion.20
  7.4 1.1 %constant_dynamic-slice_fusion.2 = (bf16[8,1,256,256]{3,2,1,0:T(8,128)(2,1)S(1)}, bf16[8,1,256,256]{3,2,1,0:T(8,128)(2,1)}) fusion(bf16[8,2,256,256]{3,2,1,0:T(8,128)(2,1)S(1)} %bitcast.94, s32[]{:T(128)S(6)} %select_n.498, s32[]{:T(128)S(6)} %select_n.496), kind=kLoop, calls=%fused_computation.114 | loop fusion | bytes 4194312 | tf_op jit(solution)/shard_map/jit(dynamic_index_in_dim)/dynamic_slice | solution.py:199
  8.6 3.0 %collective-permute-done.2 = bf16[2,1,64,256]{3,2,1,0:T(8,128)(2,1)S(1)} collective-permute-done((bf16[2,1,64,256]{3,2,1,0:T(8,128)(2,1)}, bf16[2,1,64,256]{3,2,1,0:T(8,128)(2,1)S(1)}, u32[]{:S(2)}, u32[]{:S(2)}) %collective-permute-start.2) | collective-permute-done | bytes 65568 | tf_op jit(solution)/shard_map/ppermute | solution.py:59
  11.6 0.1 convert_reduce_fusion.2
  11.7 3.4 %collective-permute-start.3 = (bf16[2,4,64,256]{3,2,1,0:T(8,128)(2,1)S(1)}, bf16[2,4,64,256]{3,2,1,0:T(8,128)(2,1)S(1)}, u32[]{:S(2)}, u32[]{:S(2)}) collective-permute-start(bf16[2,4,64,256]{3,2,1,0:T(8,128)(2,1)S(1)} %constant_dynamic-update-slice_fusion.21), channel_id=1, source_target_pairs={{0,2},{1,3},{4,6},{5,7},{8,10},{9,11},{12,14},{13,15},{16,18},{17,... | collective-permute-start | bytes 786440 | tf_op jit(solution)/shard_map/ppermute | solution.py:129
  15.2 0.1 reduce_sum.82
  15.3 1.3 %collective-permute-start.4 = (f32[1,1,1,16,1]{3,4,2,1,0:T(1,128)S(1)}, f32[1,1,1,16,1]{3,4,2,1,0:T(1,128)S(1)}, u32[]{:S(2)}, u32[]{:S(2)}) collective-permute-start(f32[1,1,1,16,1]{3,4,2,1,0:T(1,128)S(1)} %get-tuple-element.34), channel_id=1, source_target_pairs={{2,0},{3,1},{6,4},{7,5},{10,8},{11,9},{14,12},{15,13},{18,16},{19,... | collective-permute-start | bytes 200 | tf_op jit(solution)/shard_map/ppermute | solution.py:131
  16.6 0.1 sub.170
  16.7 0.1 fusion.38
  16.9 0.1 reduce_sum.91
  17.1 1.3 %collective-permute-start.5 = (f32[1,1,1,16,1]{3,4,2,1,0:T(1,128)S(1)}, f32[1,1,1,16,1]{3,4,2,1,0:T(1,128)S(1)}, u32[]{:S(2)}, u32[]{:S(2)}) collective-permute-start(f32[1,1,1,16,1]{3,4,2,1,0:T(1,128)S(1)} %multiply_bitcast_fusion), channel_id=1, source_target_pairs={{2,0},{3,1},{6,4},{7,5},{10,8},{11,9},{14,12},{15,13},{18,16},{19,... | collective-permute-start | bytes 200 | tf_op jit(solution)/shard_map/ppermute | solution.py:131
  18.4 2.0 %collective-permute-done.3 = bf16[2,4,64,256]{3,2,1,0:T(8,128)(2,1)S(1)} collective-permute-done((bf16[2,4,64,256]{3,2,1,0:T(8,128)(2,1)S(1)}, bf16[2,4,64,256]{3,2,1,0:T(8,128)(2,1)S(1)}, u32[]{:S(2)}, u32[]{:S(2)}) %collective-permute-start.3) | collective-permute-done | bytes 262176 | tf_op jit(solution)/shard_map/ppermute | solution.py:129
  20.3 0.1 convert_reduce_fusion.1
  20.5 0.1 reduce_sum.85
  20.7 0.1 sub.174
  20.8 0.1 fusion.40
  21.0 0.1 reduce_sum.116
  21.1 1.4 %collective-permute-done.5 = f32[1,1,1,16,1]{3,4,2,1,0:T(1,128)S(1)} collective-permute-done((f32[1,1,1,16,1]{3,4,2,1,0:T(1,128)S(1)}, f32[1,1,1,16,1]{3,4,2,1,0:T(1,128)S(1)}, u32[]{:S(2)}, u32[]{:S(2)}) %collective-permute-start.5) | collective-permute-done | bytes 96 | tf_op jit(solution)/shard_map/ppermute | solution.py:131
  22.6 0.1 mul.107
  22.7 0.1 sub.166
  22.9 0.6 gather_fusion
  23.5 0.5 multiply_convert_fusion
  24.1 0.4 fusion.22
  24.5 0.2 constant_dynamic-slice_fusion.18
  24.8 1.1 %constant_dynamic-slice_fusion.12 = (bf16[2,4,64,256]{3,2,1,0:T(8,128)(2,1)S(1)}, bf16[2,4,64,256]{3,2,1,0:T(8,128)(2,1)S(1)}, bf16[2,4,64,256]{3,2,1,0:T(8,128)...) fusion(bf16[4,6,66,256]{3,2,1,0:T(8,128)(2,1)S(1)} %fusion.22, ...), kind=kLoop, calls=%fused_computation.125 | loop fusion | bytes 3145800 | tf_op jit(solution)/shard_map/dynamic_slice | solution.py:192
  26.0 1.0 %copy-done.2 = bf16[8,1,256,256]{3,2,1,0:T(8,128)(2,1)S(1)} copy-done((bf16[8,1,256,256]{3,2,1,0:T(8,128)(2,1)S(1)}, bf16[8,1,256,256]{3,2,1,0:T(8,128)(2,1)}, u32[]{:S(2)}) %copy-start.2) | copy-done | bytes 1048600
  27.0 0.7 %fusion.78 = f32[512,256]{1,0:T(8,128)S(1)} fusion(bf16[512,2048]{1,0:T(8,128)(2,1)S(1)} %constant_dynamic-update-slice_fusion, bf16[2048,256]{1,0:T(8,128)(2,1)S(1)} %bitcast.101), kind=kOutput, calls=%fused_computation.160 | convolution fusion | flops 536870912 | bytes 3670016 | tf_op jit(solution)/shard_map/dot_general | solution.py:202
  27.8 0.4 fusion.26
  28.2 0.2 constant_dynamic-slice_fusion.9
  28.4 1.1 %constant_dynamic-slice_fusion.3 = (bf16[2,4,64,256]{3,2,1,0:T(8,128)(2,1)S(1)}, bf16[2,4,64,256]{3,2,1,0:T(8,128)(2,1)S(1)}, bf16[2,4,64,256]{3,2,1,0:T(8,128)(...) fusion(bf16[4,6,66,256]{3,2,1,0:T(8,128)(2,1)S(1)} %fusion.26, ...), kind=kLoop, calls=%fused_computation.115 | loop fusion | bytes 3145800 | tf_op jit(solution)/shard_map/dynamic_slice | solution.py:192
  29.8 0.7 %convolution_add_fusion.2 = f32[512,256]{1,0:T(8,128)S(1)} fusion(f32[512,256]{1,0:T(8,128)S(1)} %fusion.78, bf16[512,2048]{1,0:T(8,128)(2,1)S(1)} %constant_dynamic-update-slice_fusion.8, bf16[2048,256]{1,0:T(8,128)(2,1)S(1)} %bitcast.100), kind=kOutput, calls=%fused_computation.20 | convolution fusion | flops 537001984 | bytes 4194304 | tf_op jit(solution)/shard_map/dot_general | solution.py:202
  30.7 2.3 %collective-permute-start.8 = (f32[2,1,64,256]{3,2,1,0:T(8,128)S(1)}, f32[2,1,64,256]{3,2,1,0:T(8,128)S(1)}, u32[]{:S(2)}, u32[]{:S(2)}) collective-permute-start(f32[2,1,64,256]{3,2,1,0:T(8,128)S(1)} %get-tuple-element.27), channel_id=1, source_target_pairs={{0,12},{4,0},{8,4},{12,8},{1,13},{5,1},{9,5},{13,9},{2,14},{6,2},{... | collective-permute-start | bytes 393224 | tf_op jit(solution)/shard_map/ppermute | solution.py:59
  32.9 0.5 collective-permute-start.7
  33.4 6.7 %collective-permute-done.9 = f32[2,1,64,256]{3,2,1,0:T(8,128)S(1)} collective-permute-done((f32[2,1,64,256]{3,2,1,0:T(8,128)S(1)}, f32[2,1,64,256]{3,2,1,0:T(8,128)S(1)}, u32[]{:S(2)}, u32[]{:S(2)}) %collective-permute-start.9) | collective-permute-done | bytes 131104 | tf_op jit(solution)/shard_map/ppermute | solution.py:59
  40.1 2.8 %collective-permute-done.8 = f32[2,1,64,256]{3,2,1,0:T(8,128)S(1)} collective-permute-done((f32[2,1,64,256]{3,2,1,0:T(8,128)S(1)}, f32[2,1,64,256]{3,2,1,0:T(8,128)S(1)}, u32[]{:S(2)}, u32[]{:S(2)}) %collective-permute-start.8) | collective-permute-done | bytes 131104 | tf_op jit(solution)/shard_map/ppermute | solution.py:59
  43.0 3.2 %collective-permute-start.10 = (bf16[2,1,64,256]{3,2,1,0:T(8,128)(2,1)S(1)}, bf16[2,1,64,256]{3,2,1,0:T(8,128)(2,1)S(1)}, u32[]{:S(2)}, u32[]{:S(2)}) collective-permute-start(bf16[2,1,64,256]{3,2,1,0:T(8,128)(2,1)S(1)} %get-tuple-element.6), channel_id=1, source_target_pairs={{0,4},{4,8},{8,12},{12,0},{1,5},{5,9},{9,13},{13,1},{2,6},{6,10},{... | collective-permute-start | bytes 196616 | tf_op jit(solution)/shard_map/ppermute | solution.py:59
  46.3 0.7 %collective-permute-start.11 = (bf16[2,1,64,256]{3,2,1,0:T(8,128)(2,1)S(1)}, bf16[2,1,64,256]{3,2,1,0:T(8,128)(2,1)S(1)}, u32[]{:S(2)}, u32[]{:S(2)}) collective-permute-start(bf16[2,1,64,256]{3,2,1,0:T(8,128)(2,1)S(1)} %get-tuple-element.6), channel_id=1, source_target_pairs={{0,12},{4,0},{8,4},{12,8},{1,13},{5,1},{9,5},{13,9},{2,14},{6,2},{... | collective-permute-start | bytes 196616 | tf_op jit(solution)/shard_map/ppermute | solution.py:59
  47.0 1.5 %collective-permute-start.12 = (bf16[2,1,64,256]{3,2,1,0:T(8,128)(2,1)S(1)}, bf16[2,1,64,256]{3,2,1,0:T(8,128)(2,1)S(1)}, u32[]{:S(2)}, u32[]{:S(2)}) collective-permute-start(bf16[2,1,64,256]{3,2,1,0:T(8,128)(2,1)S(1)} %get-tuple-element.6), channel_id=1, source_target_pairs={{0,8},{4,12},{8,0},{12,4},{1,9},{5,13},{9,1},{13,5},{2,10},{6,14},... | collective-permute-start | bytes 196616 | tf_op jit(solution)/shard_map/ppermute | solution.py:59
  48.5 1.2 %collective-permute-done.10 = bf16[2,1,64,256]{3,2,1,0:T(8,128)(2,1)S(1)} collective-permute-done((bf16[2,1,64,256]{3,2,1,0:T(8,128)(2,1)S(1)}, bf16[2,1,64,256]{3,2,1,0:T(8,128)(2,1)S(1)}, u32[]{:S(2)}, u32[]{:S(2)}) %collective-permute-start.10) | collective-permute-done | bytes 65568 | tf_op jit(solution)/shard_map/ppermute | solution.py:59
  49.7 1.4 %collective-permute-done.11 = bf16[2,1,64,256]{3,2,1,0:T(8,128)(2,1)S(1)} collective-permute-done((bf16[2,1,64,256]{3,2,1,0:T(8,128)(2,1)S(1)}, bf16[2,1,64,256]{3,2,1,0:T(8,128)(2,1)S(1)}, u32[]{:S(2)}, u32[]{:S(2)}) %collective-permute-start.11) | collective-permute-done | bytes 65568 | tf_op jit(solution)/shard_map/ppermute | solution.py:59
  51.1 2.4 %collective-permute-done.12 = bf16[2,1,64,256]{3,2,1,0:T(8,128)(2,1)S(1)} collective-permute-done((bf16[2,1,64,256]{3,2,1,0:T(8,128)(2,1)S(1)}, bf16[2,1,64,256]{3,2,1,0:T(8,128)(2,1)S(1)}, u32[]{:S(2)}, u32[]{:S(2)}) %collective-permute-start.12) | collective-permute-done | bytes 65568 | tf_op jit(solution)/shard_map/ppermute | solution.py:59
  53.6 0.1 reduce_sum.119
  53.8 0.1 sub.196
  53.9 0.1 fusion.33
  54.1 0.1 reduce_sum.122
  54.2 0.1 mul.116
  54.4 0.1 fusion.36
  54.6 0.3 fusion.43
  54.9 0.2 fusion.49
  55.1 0.3 fusion.46
  55.4 0.7 %collective-permute-done.13 = bf16[2,4,64,256]{3,2,1,0:T(8,128)(2,1)S(1)} collective-permute-done((bf16[2,4,64,256]{3,2,1,0:T(8,128)(2,1)S(1)}, bf16[2,4,64,256]{3,2,1,0:T(8,128)(2,1)S(1)}, u32[]{:S(2)}, u32[]{:S(2)}) %collective-permute-start.13) | collective-permute-done | bytes 262176 | tf_op jit(solution)/shard_map/ppermute | solution.py:74
  56.1 0.3 fusion.13
  56.4 0.3 fusion.14
  56.7 0.2 fusion.16
  56.9 0.4 fusion.77
  57.3 0.2 fusion.57
  57.5 0.3 fusion.17
  57.8 0.2 fusion.18
  58.0 0.6 %fusion.51 = bf16[2,1,64,256]{3,2,1,0:T(8,128)(2,1)} fusion(bf16[2,1,64,256]{3,2,1,0:T(8,128)(2,1)S(1)} %bitcast.123, bf16[2,1,64,256]{3,2,1,0:T(8,128)(2,1)S(1)} %get-tuple-element.6), kind=kLoop, calls=%fused_computation.71 | loop fusion | flops 131072 | bytes 196608 | tf_op jit(solution)/shard_map/convert_element_type | solution.py:277
  (92 shorter events, 2.2 us)
Async XLA Ops:
  0.0 55.1 %copy-start = (bf16[512,512]{1,0:T(8,128)(2,1)S(1)}, bf16[512,512]{1,0:T(8,128)(2,1)}, u32[]{:S(2)}) copy-start(bf16[512,512]{1,0:T(8,128)(2,1)} %param.23) | copy-start | bytes 1572868
  0.0 7.1 %copy-start.1 = (bf16[3456,256]{1,0:T(8,128)(2,1)S(1)}, bf16[3456,256]{1,0:T(8,128)(2,1)}, u32[]{:S(2)}) copy-start(bf16[3456,256]{1,0:T(8,128)(2,1)} %param.17) | copy-start | bytes 5308420
  0.0 8.5 %collective-permute-start = (bf16[2,1,64,256]{3,2,1,0:T(8,128)(2,1)}, bf16[2,1,64,256]{3,2,1,0:T(8,128)(2,1)S(1)}, u32[]{:S(2)}, u32[]{:S(2)}) collective-permute-start(bf16[2,1,64,256]{3,2,1,0:T(8,128)(2,1)} %param.14), channel_id=1, source_target_pairs={{0,4},{4,8},{8,12},{12,0},{1,5},{5,9},{9,13},{13,1},{2,6},{6,10},{... | collective-permute-start | bytes 196616 | tf_op jit(solution)/shard_map/ppermute | solution.py:59
  3.0 5.5 %collective-permute-start.1 = (bf16[2,1,64,256]{3,2,1,0:T(8,128)(2,1)}, bf16[2,1,64,256]{3,2,1,0:T(8,128)(2,1)S(1)}, u32[]{:S(2)}, u32[]{:S(2)}) collective-permute-start(bf16[2,1,64,256]{3,2,1,0:T(8,128)(2,1)} %param.14), channel_id=1, source_target_pairs={{0,12},{4,0},{8,4},{12,8},{1,13},{5,1},{9,5},{13,9},{2,14},{6,2},{... | collective-permute-start | bytes 196616 | tf_op jit(solution)/shard_map/ppermute | solution.py:59
  5.1 6.4 %collective-permute-start.2 = (bf16[2,1,64,256]{3,2,1,0:T(8,128)(2,1)}, bf16[2,1,64,256]{3,2,1,0:T(8,128)(2,1)S(1)}, u32[]{:S(2)}, u32[]{:S(2)}) collective-permute-start(bf16[2,1,64,256]{3,2,1,0:T(8,128)(2,1)} %param.14), channel_id=1, source_target_pairs={{0,8},{4,12},{8,0},{12,4},{1,9},{5,13},{9,1},{13,5},{2,10},{6,14},... | collective-permute-start | bytes 196616 | tf_op jit(solution)/shard_map/ppermute | solution.py:59
  8.6 14.9 %copy-start.12 = (f32[256]{0:T(256)S(1)}, f32[256]{0:T(256)}, u32[]{:S(2)}) copy-start(f32[256]{0:T(256)} %param.16) | copy-start | bytes 3076
  8.6 14.9 %copy-start.13 = (f32[256]{0:T(256)S(1)}, f32[256]{0:T(256)}, u32[]{:S(2)}) copy-start(f32[256]{0:T(256)} %param.15) | copy-start | bytes 3076
  11.7 8.7 %collective-permute-start.3 = (bf16[2,4,64,256]{3,2,1,0:T(8,128)(2,1)S(1)}, bf16[2,4,64,256]{3,2,1,0:T(8,128)(2,1)S(1)}, u32[]{:S(2)}, u32[]{:S(2)}) collective-permute-start(bf16[2,4,64,256]{3,2,1,0:T(8,128)(2,1)S(1)} %constant_dynamic-update-slice_fusion.21), channel_id=1, source_target_pairs={{0,2},{1,3},{4,6},{5,7},{8,10},{9,11},{12,14},{13,15},{16,18},{17,... | collective-permute-start | bytes 786440 | tf_op jit(solution)/shard_map/ppermute | solution.py:129
  15.3 5.8 %collective-permute-start.4 = (f32[1,1,1,16,1]{3,4,2,1,0:T(1,128)S(1)}, f32[1,1,1,16,1]{3,4,2,1,0:T(1,128)S(1)}, u32[]{:S(2)}, u32[]{:S(2)}) collective-permute-start(f32[1,1,1,16,1]{3,4,2,1,0:T(1,128)S(1)} %get-tuple-element.34), channel_id=1, source_target_pairs={{2,0},{3,1},{6,4},{7,5},{10,8},{11,9},{14,12},{15,13},{18,16},{19,... | collective-permute-start | bytes 200 | tf_op jit(solution)/shard_map/ppermute | solution.py:131
  17.1 5.4 %collective-permute-start.5 = (f32[1,1,1,16,1]{3,4,2,1,0:T(1,128)S(1)}, f32[1,1,1,16,1]{3,4,2,1,0:T(1,128)S(1)}, u32[]{:S(2)}, u32[]{:S(2)}) collective-permute-start(f32[1,1,1,16,1]{3,4,2,1,0:T(1,128)S(1)} %multiply_bitcast_fusion), channel_id=1, source_target_pairs={{2,0},{3,1},{6,4},{7,5},{10,8},{11,9},{14,12},{15,13},{18,16},{19,... | collective-permute-start | bytes 200 | tf_op jit(solution)/shard_map/ppermute | solution.py:131
  24.0 3.8 %collective-permute-start.6 = (bf16[4,4,64,256]{3,2,1,0:T(8,128)(2,1)S(1)}, bf16[4,4,64,256]{3,2,1,0:T(8,128)(2,1)S(1)}, u32[]{:S(2)}, u32[]{:S(2)}) collective-permute-start(bf16[4,4,64,256]{3,2,1,0:T(8,128)(2,1)S(1)} %multiply_convert_fusion), channel_id=1, source_target_pairs={{0,1},{1,0},{2,3},{3,2},{4,5},{5,4},{6,7},{7,6},{8,9},{9,8},{10,11... | collective-permute-start | bytes 1572872 | tf_op jit(solution)/shard_map/ppermute | solution.py:74
  25.8 1.2 %copy-start.2 = (bf16[8,1,256,256]{3,2,1,0:T(8,128)(2,1)S(1)}, bf16[8,1,256,256]{3,2,1,0:T(8,128)(2,1)}, u32[]{:S(2)}) copy-start(bf16[8,1,256,256]{3,2,1,0:T(8,128)(2,1)} %get-tuple-element.8) | copy-start | bytes 3145732
  29.7 13.2 %copy-start.5 = (bf16[2,1,64,256]{3,2,1,0:T(8,128)(2,1)S(1)}, bf16[2,1,64,256]{3,2,1,0:T(8,128)(2,1)}, u32[]{:S(2)}) copy-start(bf16[2,1,64,256]{3,2,1,0:T(8,128)(2,1)} %param.14) | copy-start | bytes 196612
  29.8 13.2 %copy-start.9 = (f32[256]{0:T(256)S(1)}, f32[256]{0:T(256)}, u32[]{:S(2)}) copy-start(f32[256]{0:T(256)} %param.18) | copy-start | bytes 3076
  29.8 16.5 %copy-start.14 = (f32[512]{0:T(512)S(1)}, f32[512]{0:T(512)}, u32[]{:S(2)}) copy-start(f32[512]{0:T(512)} %param.27) | copy-start | bytes 6148
  30.5 23.8 %copy-start.10 = (f32[256]{0:T(256)S(1)}, f32[256]{0:T(256)}, u32[]{:S(2)}) copy-start(f32[256]{0:T(256)} %param.20) | copy-start | bytes 3076
  30.5 23.8 %copy-start.11 = (f32[256]{0:T(256)S(1)}, f32[256]{0:T(256)}, u32[]{:S(2)}) copy-start(f32[256]{0:T(256)} %param.19) | copy-start | bytes 3076
  30.5 24.0 %copy-start.4 = (bf16[512,512]{1,0:T(8,128)(2,1)S(1)}, bf16[512,512]{1,0:T(8,128)(2,1)}, u32[]{:S(2)}) copy-start(bf16[512,512]{1,0:T(8,128)(2,1)} %param.24) | copy-start | bytes 1572868
  30.6 9.5 %collective-permute-start.9 = (f32[2,1,64,256]{3,2,1,0:T(8,128)S(1)}, f32[2,1,64,256]{3,2,1,0:T(8,128)S(1)}, u32[]{:S(2)}, u32[]{:S(2)}) collective-permute-start(f32[2,1,64,256]{3,2,1,0:T(8,128)S(1)} %get-tuple-element.26), channel_id=1, source_target_pairs={{0,8},{4,12},{8,0},{12,4},{1,9},{5,13},{9,1},{13,5},{2,10},{6,14},... | collective-permute-start | bytes 393224 | tf_op jit(solution)/shard_map/ppermute | solution.py:59
  30.7 12.2 %collective-permute-start.8 = (f32[2,1,64,256]{3,2,1,0:T(8,128)S(1)}, f32[2,1,64,256]{3,2,1,0:T(8,128)S(1)}, u32[]{:S(2)}, u32[]{:S(2)}) collective-permute-start(f32[2,1,64,256]{3,2,1,0:T(8,128)S(1)} %get-tuple-element.27), channel_id=1, source_target_pairs={{0,12},{4,0},{8,4},{12,8},{1,13},{5,1},{9,5},{13,9},{2,14},{6,2},{... | collective-permute-start | bytes 393224 | tf_op jit(solution)/shard_map/ppermute | solution.py:59
  32.9 10.0 %collective-permute-start.7 = (f32[2,1,64,256]{3,2,1,0:T(8,128)S(1)}, f32[2,1,64,256]{3,2,1,0:T(8,128)S(1)}, u32[]{:S(2)}, u32[]{:S(2)}) collective-permute-start(f32[2,1,64,256]{3,2,1,0:T(8,128)S(1)} %get-tuple-element.25), channel_id=1, source_target_pairs={{0,4},{4,8},{8,12},{12,0},{1,5},{5,9},{9,13},{13,1},{2,6},{6,10},{... | collective-permute-start | bytes 393224 | tf_op jit(solution)/shard_map/ppermute | solution.py:59
  43.0 11.9 %copy-start.3 = (bf16[512,512]{1,0:T(8,128)(2,1)S(1)}, bf16[512,512]{1,0:T(8,128)(2,1)}, u32[]{:S(2)}) copy-start(bf16[512,512]{1,0:T(8,128)(2,1)} %param.21) | copy-start | bytes 1572868
  43.0 6.7 %collective-permute-start.10 = (bf16[2,1,64,256]{3,2,1,0:T(8,128)(2,1)S(1)}, bf16[2,1,64,256]{3,2,1,0:T(8,128)(2,1)S(1)}, u32[]{:S(2)}, u32[]{:S(2)}) collective-permute-start(bf16[2,1,64,256]{3,2,1,0:T(8,128)(2,1)S(1)} %get-tuple-element.6), channel_id=1, source_target_pairs={{0,4},{4,8},{8,12},{12,0},{1,5},{5,9},{9,13},{13,1},{2,6},{6,10},{... | collective-permute-start | bytes 196616 | tf_op jit(solution)/shard_map/ppermute | solution.py:59
  46.3 4.8 %collective-permute-start.11 = (bf16[2,1,64,256]{3,2,1,0:T(8,128)(2,1)S(1)}, bf16[2,1,64,256]{3,2,1,0:T(8,128)(2,1)S(1)}, u32[]{:S(2)}, u32[]{:S(2)}) collective-permute-start(bf16[2,1,64,256]{3,2,1,0:T(8,128)(2,1)S(1)} %get-tuple-element.6), channel_id=1, source_target_pairs={{0,12},{4,0},{8,4},{12,8},{1,13},{5,1},{9,5},{13,9},{2,14},{6,2},{... | collective-permute-start | bytes 196616 | tf_op jit(solution)/shard_map/ppermute | solution.py:59
  47.0 6.5 %collective-permute-start.12 = (bf16[2,1,64,256]{3,2,1,0:T(8,128)(2,1)S(1)}, bf16[2,1,64,256]{3,2,1,0:T(8,128)(2,1)S(1)}, u32[]{:S(2)}, u32[]{:S(2)}) collective-permute-start(bf16[2,1,64,256]{3,2,1,0:T(8,128)(2,1)S(1)} %get-tuple-element.6), channel_id=1, source_target_pairs={{0,8},{4,12},{8,0},{12,4},{1,9},{5,13},{9,1},{13,5},{2,10},{6,14},... | collective-permute-start | bytes 196616 | tf_op jit(solution)/shard_map/ppermute | solution.py:59
  54.5 1.6 %collective-permute-start.13 = (bf16[2,4,64,256]{3,2,1,0:T(8,128)(2,1)S(1)}, bf16[2,4,64,256]{3,2,1,0:T(8,128)(2,1)S(1)}, u32[]{:S(2)}, u32[]{:S(2)}) collective-permute-start(bf16[2,4,64,256]{3,2,1,0:T(8,128)(2,1)S(1)} %fusion.36), channel_id=1, source_target_pairs={{0,1},{1,0},{2,3},{3,2},{4,5},{5,4},{6,7},{7,6},{8,9},{9,8},{10,11... | collective-permute-start | bytes 786440 | tf_op jit(solution)/shard_map/ppermute | solution.py:74
  54.9 1.5 %copy-start.8 = (f32[512]{0:T(512)S(1)}, f32[512]{0:T(512)}, u32[]{:S(2)}) copy-start(f32[512]{0:T(512)} %param.25) | copy-start | bytes 6148
  56.1 0.7 %copy-start.7 = (f32[512]{0:T(512)S(1)}, f32[512]{0:T(512)}, u32[]{:S(2)}) copy-start(f32[512]{0:T(512)} %param.22) | copy-start | bytes 6148
  56.4 1.4 %copy-start.6 = (bf16[512,512]{1,0:T(8,128)(2,1)S(1)}, bf16[512,512]{1,0:T(8,128)(2,1)}, u32[]{:S(2)}) copy-start(bf16[512,512]{1,0:T(8,128)(2,1)} %param.26) | copy-start | bytes 1572868

commit v15 on v11

--- a/solution.py
+++ b/solution.py
@@ -170,7 +170,9 @@
                     half,
                     (tap // 9, (tap // 3) % 3, tap % 3, 0),
                     (frames, all_rows, columns, channels),
-                ).reshape(-1, channels)
+                )
+                .transpose(1, 0, 2, 3)
+                .reshape(-1, channels)
             )
         patches = jnp.concatenate(windows, axis=1)
         block = lax.dynamic_index_in_dim(placed, source, axis=1, keepdims=False).reshape(
@@ -179,16 +181,17 @@
         term = jnp.dot(patches, block, preferred_element_type=jnp.float32)
         partial = term if partial is None else partial + term
 
-    pieces = partial.reshape(frames, row_count, rows_here, columns, out_channels)
+    pieces = partial.reshape(row_count, rows_here, frames, columns, out_channels)
     if row_count <= PERMUTE_GROUP:
-        convolved = lax.dynamic_index_in_dim(pieces, row_place, axis=1, keepdims=False)
+        convolved = lax.dynamic_index_in_dim(pieces, row_place, axis=0, keepdims=False)
         for shift in nearest_first(row_count):
             chunk = lax.dynamic_index_in_dim(
-                pieces, (row_place + shift) % row_count, axis=1, keepdims=False
+                pieces, (row_place + shift) % row_count, axis=0, keepdims=False
             )
             convolved = convolved + shifted(chunk, ("rows",), (row_count,), (shift,))
     else:
-        convolved = jnp.sum(lax.all_to_all(pieces, "rows", 1, 1, tiled=True), axis=1)
+        convolved = jnp.sum(lax.all_to_all(pieces, "rows", 0, 0, tiled=True), axis=0)
+    convolved = jnp.transpose(convolved, (1, 0, 2, 3))
     own_middle = (latent.astype(jnp.float32) + convolved + conv_bias).astype(jnp.bfloat16)
 
     if row_count <= PERMUTE_GROUP:

time: 56.8 us -> 57.2 us (level)
    transpose x0 -> x20, local copies, waits for them, and re-layouts: none -> 2.86 us  [local(): windows.append(lax.dynamic_slice(half, (tap // 9, tap // 3 % 3, tap % 3,...]
    dynamic_slice x4 -> x0, local copies, waits for them, and re-layouts: 2.55 us -> none  [local(): lax.dynamic_slice(half, (tap // 9, tap // 3 % 3, tap % 3, 0), (frames, al...]
  transfers between devices with their start and end apart: 12 -> 12, of which waited for: 10 -> 10; matrix products, arithmetic and copies ran while one was open for 10% -> 11% of each run, Pallas kernels for 0% -> 0%
where the time goes in v15:
time: 57.2 us; the launch traced here: 57 us
  waiting for transfers between devices  24.7 us (43%)
  starting transfers between devices  16 us (28%)
  local copies, waits for them, and re-layouts  8.54 us (15%)
  matrix products  3.86 us (7%)
  other arithmetic  3.15 us (6%)
  between operations  0.73 us (1%)
    ppermute x10, waiting for transfers between devices, shifted(): return lax.ppermute(cells, axes, pairs)  24.1 us
    ppermute x10, starting transfers between devices, shifted(): return lax.ppermute(cells, axes, pairs)  15.8 us
    transpose x20, local copies, waits for them, and re-layouts, local(): windows.append(lax.dynamic_slice(half, (tap // 9, tap // 3 % 3, tap % 3,...  2.86 us
    dot_general x6, matrix products, split_dot(): jnp.dot(half, half_rows(weight, shift, width), preferred_element_type=jnp...  1.59 us
    dot_general x2, matrix products, local(): term = jnp.dot(patches, block, preferred_element_type=jnp.float32)  1.45 us
    unnamed x44, local copies, waits for them, and re-layouts  1.41 us
  transfers between devices with their start and end apart: 12, of which 10 were waited for; matrix products, arithmetic and copies ran while one was open for 11% of the time, Pallas kernels for 0%

profile of v15, /device:TPU:0, one launch (start us, length us, event | category | flops | bytes accessed | tf_op | source)
XLA Modules:
  0.0 57.0 jit_solution(1336583195497498065)
XLA Ops:
  0.0 3.0 %collective-permute-start = (bf16[2,1,64,256]{3,2,1,0:T(8,128)(2,1)}, bf16[2,1,64,256]{3,2,1,0:T(8,128)(2,1)S(1)}, u32[]{:S(2)}, u32[]{:S(2)}) collective-permute-start(bf16[2,1,64,256]{3,2,1,0:T(8,128)(2,1)} %param.14), channel_id=1, source_target_pairs={{0,4},{4,8},{8,12},{12,0},{1,5},{5,9},{9,13},{13,1},{2,6},{6,10},{... | collective-permute-start | bytes 196616 | tf_op jit(solution)/shard_map/ppermute | solution.py:53
  3.0 2.1 %collective-permute-start.1 = (bf16[2,1,64,256]{3,2,1,0:T(8,128)(2,1)}, bf16[2,1,64,256]{3,2,1,0:T(8,128)(2,1)S(1)}, u32[]{:S(2)}, u32[]{:S(2)}) collective-permute-start(bf16[2,1,64,256]{3,2,1,0:T(8,128)(2,1)} %param.14), channel_id=1, source_target_pairs={{0,12},{4,0},{8,4},{12,8},{1,13},{5,1},{9,5},{13,9},{2,14},{6,2},{... | collective-permute-start | bytes 196616 | tf_op jit(solution)/shard_map/ppermute | solution.py:53
  5.1 0.9 %collective-permute-start.2 = (bf16[2,1,64,256]{3,2,1,0:T(8,128)(2,1)}, bf16[2,1,64,256]{3,2,1,0:T(8,128)(2,1)S(1)}, u32[]{:S(2)}, u32[]{:S(2)}) collective-permute-start(bf16[2,1,64,256]{3,2,1,0:T(8,128)(2,1)} %param.14), channel_id=1, source_target_pairs={{0,8},{4,12},{8,0},{12,4},{1,9},{5,13},{9,1},{13,5},{2,10},{6,14},... | collective-permute-start | bytes 196616 | tf_op jit(solution)/shard_map/ppermute | solution.py:53
  6.1 0.9 %constant_dynamic-update-slice_fusion.26 = bf16[2,4,64,256]{3,2,1,0:T(8,128)(2,1)S(1)} fusion(bf16[2,4,64,256]{3,2,1,0:T(8,128)(2,1)S(1)} %broadcast.147.clone, bf16[2,1,64,256]{3,2,1,0:T(8,128)(2,1)} %param.14, s32[]{:T(128)S(6)} %select_n.416), kind=kLoop, calls=%fused_computation.132 | loop fusion | bytes 131076 | tf_op jit(solution)/shard_map/dynamic_update_slice | solution.py:118
  7.0 0.1 broadcast_in_dim.17
  7.1 0.2 constant_dynamic-update-slice_fusion.20
  7.4 0.3 collective-permute-done
  7.7 0.5 collective-permute-done.1
  8.2 3.3 %collective-permute-done.2 = bf16[2,1,64,256]{3,2,1,0:T(8,128)(2,1)S(1)} collective-permute-done((bf16[2,1,64,256]{3,2,1,0:T(8,128)(2,1)}, bf16[2,1,64,256]{3,2,1,0:T(8,128)(2,1)S(1)}, u32[]{:S(2)}, u32[]{:S(2)}) %collective-permute-start.2) | collective-permute-done | bytes 65568 | tf_op jit(solution)/shard_map/ppermute | solution.py:53
  11.6 1.6 %collective-permute-start.3 = (bf16[2,4,64,256]{3,2,1,0:T(8,128)(2,1)S(1)}, bf16[2,4,64,256]{3,2,1,0:T(8,128)(2,1)S(1)}, u32[]{:S(2)}, u32[]{:S(2)}) collective-permute-start(bf16[2,4,64,256]{3,2,1,0:T(8,128)(2,1)S(1)} %constant_dynamic-update-slice_fusion.23), channel_id=1, source_target_pairs={{0,2},{2,0},{1,3},{3,1},{4,6},{6,4},{5,7},{7,5},{8,10},{10,8},{9,1... | collective-permute-start | bytes 786440 | tf_op jit(solution)/shard_map/ppermute | solution.py:53
  13.1 1.1 %constant_dynamic-slice_fusion.2 = (bf16[8,1,256,256]{3,2,1,0:T(8,128)(2,1)S(1)}, bf16[8,1,256,256]{3,2,1,0:T(8,128)(2,1)}) fusion(bf16[8,2,256,256]{3,2,1,0:T(8,128)(2,1)S(1)} %bitcast.103, s32[]{:T(128)S(6)} %select_n.491, s32[]{:T(128)S(6)} %select_n.489), kind=kLoop, calls=%fused_computation.124 | loop fusion | bytes 4194312 | tf_op jit(solution)/shard_map/jit(dynamic_index_in_dim)/dynamic_slice | solution.py:178
  14.3 5.2 %collective-permute-done.3 = bf16[2,4,64,256]{3,2,1,0:T(8,128)(2,1)S(1)} collective-permute-done((bf16[2,4,64,256]{3,2,1,0:T(8,128)(2,1)S(1)}, bf16[2,4,64,256]{3,2,1,0:T(8,128)(2,1)S(1)}, u32[]{:S(2)}, u32[]{:S(2)}) %collective-permute-start.3) | collective-permute-done | bytes 262176 | tf_op jit(solution)/shard_map/ppermute | solution.py:53
  19.5 0.2 convert_reduce_fusion
  19.7 0.1 reduce_sum.55
  19.8 0.1 reduce_sum.59
  20.0 0.1 sub.144
  20.1 0.2 fusion.20
  20.3 0.1 reduce_sum.61
  20.3 0.1 reduce_sum.62
  20.6 0.1 mul.91
  20.6 0.6 %gather_fusion = bf16[4,4,64,256]{3,2,1,0:T(8,128)(2,1)S(1)} fusion(bf16[4,4,64,256]{3,2,1,0:T(8,128)(2,1)S(1)} %constant_dynamic-update-slice_fusion.21, s32[1024]{0:T(1024)S(1)} %pad_clamp_fusion), kind=kCustom, calls=%fused_computation | custom fusion | bytes 1048592 | tf_op jit(solution)/shard_map/jit(_take)/gather | solution.py:141
  21.3 0.5 multiply_convert_fusion
  21.8 0.4 fusion.24
  22.2 0.2 dynamic-slice_bitcast_fusion.14
  22.5 1.1 %dynamic-slice_bitcast_fusion.8 = (bf16[4,2,64,256]{3,2,0,1:T(8,128)(2,1)S(1)}, bf16[4,2,64,256]{3,2,0,1:T(8,128)(2,1)S(1)}, bf16[4,2,64,256]{3,2,0,1:T(8,128)(2...) fusion(bf16[4,6,66,256]{3,2,1,0:T(8,128)(2,1)S(1)} %fusion.24, ...), kind=kLoop, calls=%fused_computation.72 | loop fusion | bytes 3145800 | tf_op jit(solution)/shard_map/transpose | solution.py:174
  24.0 0.9 %copy-done.2 = bf16[8,1,256,256]{3,2,1,0:T(8,128)(2,1)S(1)} copy-done((bf16[8,1,256,256]{3,2,1,0:T(8,128)(2,1)S(1)}, bf16[8,1,256,256]{3,2,1,0:T(8,128)(2,1)}, u32[]{:S(2)}) %copy-start.2) | copy-done | bytes 1048600
  24.9 0.7 %fusion.70 = f32[512,256]{1,0:T(8,128)S(1)} fusion(bf16[512,2048]{1,0:T(8,128)(2,1)S(1)} %constant_dynamic-update-slice_fusion, bf16[2048,256]{1,0:T(8,128)(2,1)S(1)} %bitcast.110), kind=kOutput, calls=%fused_computation.145 | convolution fusion | flops 536870912 | bytes 3670016 | tf_op jit(solution)/shard_map/dot_general | solution.py:181
  25.7 0.4 fusion.28
  26.1 0.2 dynamic-slice_bitcast_fusion.6
  26.3 1.1 %dynamic-slice_bitcast_fusion = (bf16[4,2,64,256]{3,2,0,1:T(8,128)(2,1)S(1)}, bf16[4,2,64,256]{3,2,0,1:T(8,128)(2,1)S(1)}, bf16[4,2,64,256]{3,2,0,1:T(8,128)(2,1...) fusion(bf16[4,6,66,256]{3,2,1,0:T(8,128)(2,1)S(1)} %fusion.28, ...), kind=kLoop, calls=%fused_computation.64 | loop fusion | bytes 3145800 | tf_op jit(solution)/shard_map/transpose | solution.py:174
  27.9 0.7 %convolution_add_fusion.2 = f32[512,256]{1,0:T(8,128)S(1)} fusion(f32[512,256]{1,0:T(8,128)S(1)} %fusion.70, bf16[512,2048]{1,0:T(8,128)(2,1)S(1)} %constant_dynamic-update-slice_fusion.8, bf16[2048,256]{1,0:T(8,128)(2,1)S(1)} %bitcast.109), kind=kOutput, calls=%fused_computation.22 | convolution fusion | flops 537001984 | bytes 4194304 | tf_op jit(solution)/shard_map/dot_general | solution.py:181
  28.8 2.6 %collective-permute-start.6 = (f32[1,2,64,256]{3,2,1,0:T(8,128)S(1)}, f32[1,2,64,256]{3,2,1,0:T(8,128)S(1)}, u32[]{:S(2)}, u32[]{:S(2)}) collective-permute-start(f32[1,2,64,256]{3,2,1,0:T(8,128)S(1)} %get-tuple-element.27), channel_id=1, source_target_pairs={{0,12},{4,0},{8,4},{12,8},{1,13},{5,1},{9,5},{13,9},{2,14},{6,2},{... | collective-permute-start | bytes 393224 | tf_op jit(solution)/shard_map/ppermute | solution.py:53
  31.4 0.5 collective-permute-start.5
  31.9 6.7 %collective-permute-done.7 = f32[1,2,64,256]{3,2,1,0:T(8,128)S(1)} collective-permute-done((f32[1,2,64,256]{3,2,1,0:T(8,128)S(1)}, f32[1,2,64,256]{3,2,1,0:T(8,128)S(1)}, u32[]{:S(2)}, u32[]{:S(2)}) %collective-permute-start.7) | collective-permute-done | bytes 131104 | tf_op jit(solution)/shard_map/ppermute | solution.py:53
  38.6 2.8 %collective-permute-done.6 = f32[1,2,64,256]{3,2,1,0:T(8,128)S(1)} collective-permute-done((f32[1,2,64,256]{3,2,1,0:T(8,128)S(1)}, f32[1,2,64,256]{3,2,1,0:T(8,128)S(1)}, u32[]{:S(2)}, u32[]{:S(2)}) %collective-permute-start.6) | collective-permute-done | bytes 131104 | tf_op jit(solution)/shard_map/ppermute | solution.py:53
  41.5 3.2 %collective-permute-start.8 = (bf16[2,1,64,256]{3,2,1,0:T(8,128)(2,1)S(1)}, bf16[2,1,64,256]{3,2,1,0:T(8,128)(2,1)S(1)}, u32[]{:S(2)}, u32[]{:S(2)}) collective-permute-start(bf16[2,1,64,256]{3,2,1,0:T(8,128)(2,1)S(1)} %get-tuple-element.6), channel_id=1, source_target_pairs={{0,4},{4,8},{8,12},{12,0},{1,5},{5,9},{9,13},{13,1},{2,6},{6,10},{... | collective-permute-start | bytes 196616 | tf_op jit(solution)/shard_map/ppermute | solution.py:53
  44.7 0.1 dynamic_slice.129
  44.8 0.7 %collective-permute-start.9 = (bf16[2,1,64,256]{3,2,1,0:T(8,128)(2,1)S(1)}, bf16[2,1,64,256]{3,2,1,0:T(8,128)(2,1)S(1)}, u32[]{:S(2)}, u32[]{:S(2)}) collective-permute-start(bf16[2,1,64,256]{3,2,1,0:T(8,128)(2,1)S(1)} %get-tuple-element.6), channel_id=1, source_target_pairs={{0,12},{4,0},{8,4},{12,8},{1,13},{5,1},{9,5},{13,9},{2,14},{6,2},{... | collective-permute-start | bytes 196616 | tf_op jit(solution)/shard_map/ppermute | solution.py:53
  45.4 1.2 %collective-permute-start.10 = (bf16[2,1,64,256]{3,2,1,0:T(8,128)(2,1)S(1)}, bf16[2,1,64,256]{3,2,1,0:T(8,128)(2,1)S(1)}, u32[]{:S(2)}, u32[]{:S(2)}) collective-permute-start(bf16[2,1,64,256]{3,2,1,0:T(8,128)(2,1)S(1)} %get-tuple-element.6), channel_id=1, source_target_pairs={{0,8},{4,12},{8,0},{12,4},{1,9},{5,13},{9,1},{13,5},{2,10},{6,14},... | collective-permute-start | bytes 196616 | tf_op jit(solution)/shard_map/ppermute | solution.py:53
  46.6 1.6 %collective-permute-done.8 = bf16[2,1,64,256]{3,2,1,0:T(8,128)(2,1)S(1)} collective-permute-done((bf16[2,1,64,256]{3,2,1,0:T(8,128)(2,1)S(1)}, bf16[2,1,64,256]{3,2,1,0:T(8,128)(2,1)S(1)}, u32[]{:S(2)}, u32[]{:S(2)}) %collective-permute-start.8) | collective-permute-done | bytes 65568 | tf_op jit(solution)/shard_map/ppermute | solution.py:53
  48.2 1.3 %collective-permute-done.9 = bf16[2,1,64,256]{3,2,1,0:T(8,128)(2,1)S(1)} collective-permute-done((bf16[2,1,64,256]{3,2,1,0:T(8,128)(2,1)S(1)}, bf16[2,1,64,256]{3,2,1,0:T(8,128)(2,1)S(1)}, u32[]{:S(2)}, u32[]{:S(2)}) %collective-permute-start.9) | collective-permute-done | bytes 65568 | tf_op jit(solution)/shard_map/ppermute | solution.py:53
  49.6 2.2 %collective-permute-done.10 = bf16[2,1,64,256]{3,2,1,0:T(8,128)(2,1)S(1)} collective-permute-done((bf16[2,1,64,256]{3,2,1,0:T(8,128)(2,1)S(1)}, bf16[2,1,64,256]{3,2,1,0:T(8,128)(2,1)S(1)}, u32[]{:S(2)}, u32[]{:S(2)}) %collective-permute-start.10) | collective-permute-done | bytes 65568 | tf_op jit(solution)/shard_map/ppermute | solution.py:53
  51.9 0.1 reduce_sum.80
  52.0 0.1 reduce_sum.81
  52.1 0.1 sub.166
  52.2 0.1 sub.167
  52.2 0.1 fusion.35
  52.3 0.1 reduce_sum.83
  52.4 0.1 reduce_sum.84
  52.5 0.1 mul.99
  52.6 0.1 mul.100
  52.7 0.1 fusion.38
  52.9 0.3 fusion.41
  53.2 0.2 fusion.47
  53.4 0.3 fusion.44
  53.8 0.7 %collective-permute-done.11 = bf16[2,4,64,256]{3,2,1,0:T(8,128)(2,1)S(1)} collective-permute-done((bf16[2,4,64,256]{3,2,1,0:T(8,128)(2,1)S(1)}, bf16[2,4,64,256]{3,2,1,0:T(8,128)(2,1)S(1)}, u32[]{:S(2)}, u32[]{:S(2)}) %collective-permute-start.11) | collective-permute-done | bytes 262176 | tf_op jit(solution)/shard_map/ppermute | solution.py:68
  54.4 0.3 fusion.13
  54.7 0.3 fusion.14
  55.1 0.2 fusion.16
  55.3 0.4 fusion.69
  55.7 0.2 fusion.54
  55.8 0.3 fusion.17
  56.1 0.2 fusion.18
  56.3 0.6 %fusion.49 = bf16[2,1,64,256]{3,2,1,0:T(8,128)(2,1)} fusion(bf16[2,1,64,256]{3,2,1,0:T(8,128)(2,1)S(1)} %bitcast.132, bf16[2,1,64,256]{3,2,1,0:T(8,128)(2,1)S(1)} %get-tuple-element.6), kind=kLoop, calls=%fused_computation.81 | loop fusion | flops 131072 | bytes 196608 | tf_op jit(solution)/shard_map/convert_element_type | solution.py:257
  (93 shorter events, 1.6 us)
Async XLA Ops:
  0.0 53.4 %copy-start = (bf16[512,512]{1,0:T(8,128)(2,1)S(1)}, bf16[512,512]{1,0:T(8,128)(2,1)}, u32[]{:S(2)}) copy-start(bf16[512,512]{1,0:T(8,128)(2,1)} %param.23) | copy-start | bytes 1572868
  0.0 7.1 %copy-start.1 = (bf16[3456,256]{1,0:T(8,128)(2,1)S(1)}, bf16[3456,256]{1,0:T(8,128)(2,1)}, u32[]{:S(2)}) copy-start(bf16[3456,256]{1,0:T(8,128)(2,1)} %param.17) | copy-start | bytes 5308420
  0.0 7.7 %collective-permute-start = (bf16[2,1,64,256]{3,2,1,0:T(8,128)(2,1)}, bf16[2,1,64,256]{3,2,1,0:T(8,128)(2,1)S(1)}, u32[]{:S(2)}, u32[]{:S(2)}) collective-permute-start(bf16[2,1,64,256]{3,2,1,0:T(8,128)(2,1)} %param.14), channel_id=1, source_target_pairs={{0,4},{4,8},{8,12},{12,0},{1,5},{5,9},{9,13},{13,1},{2,6},{6,10},{... | collective-permute-start | bytes 196616 | tf_op jit(solution)/shard_map/ppermute | solution.py:53
  3.0 5.2 %collective-permute-start.1 = (bf16[2,1,64,256]{3,2,1,0:T(8,128)(2,1)}, bf16[2,1,64,256]{3,2,1,0:T(8,128)(2,1)S(1)}, u32[]{:S(2)}, u32[]{:S(2)}) collective-permute-start(bf16[2,1,64,256]{3,2,1,0:T(8,128)(2,1)} %param.14), channel_id=1, source_target_pairs={{0,12},{4,0},{8,4},{12,8},{1,13},{5,1},{9,5},{13,9},{2,14},{6,2},{... | collective-permute-start | bytes 196616 | tf_op jit(solution)/shard_map/ppermute | solution.py:53
  5.1 6.4 %collective-permute-start.2 = (bf16[2,1,64,256]{3,2,1,0:T(8,128)(2,1)}, bf16[2,1,64,256]{3,2,1,0:T(8,128)(2,1)S(1)}, u32[]{:S(2)}, u32[]{:S(2)}) collective-permute-start(bf16[2,1,64,256]{3,2,1,0:T(8,128)(2,1)} %param.14), channel_id=1, source_target_pairs={{0,8},{4,12},{8,0},{12,4},{1,9},{5,13},{9,1},{13,5},{2,10},{6,14},... | collective-permute-start | bytes 196616 | tf_op jit(solution)/shard_map/ppermute | solution.py:53
  11.6 7.9 %collective-permute-start.3 = (bf16[2,4,64,256]{3,2,1,0:T(8,128)(2,1)S(1)}, bf16[2,4,64,256]{3,2,1,0:T(8,128)(2,1)S(1)}, u32[]{:S(2)}, u32[]{:S(2)}) collective-permute-start(bf16[2,4,64,256]{3,2,1,0:T(8,128)(2,1)S(1)} %constant_dynamic-update-slice_fusion.23), channel_id=1, source_target_pairs={{0,2},{2,0},{1,3},{3,1},{4,6},{6,4},{5,7},{7,5},{8,10},{10,8},{9,1... | collective-permute-start | bytes 786440 | tf_op jit(solution)/shard_map/ppermute | solution.py:53
  14.2 7.0 %copy-start.12 = (f32[256]{0:T(256)S(1)}, f32[256]{0:T(256)}, u32[]{:S(2)}) copy-start(f32[256]{0:T(256)} %param.16) | copy-start | bytes 3076
  14.2 7.0 %copy-start.13 = (f32[256]{0:T(256)S(1)}, f32[256]{0:T(256)}, u32[]{:S(2)}) copy-start(f32[256]{0:T(256)} %param.15) | copy-start | bytes 3076
  21.8 3.9 %collective-permute-start.4 = (bf16[4,4,64,256]{3,2,1,0:T(8,128)(2,1)S(1)}, bf16[4,4,64,256]{3,2,1,0:T(8,128)(2,1)S(1)}, u32[]{:S(2)}, u32[]{:S(2)}) collective-permute-start(bf16[4,4,64,256]{3,2,1,0:T(8,128)(2,1)S(1)} %multiply_convert_fusion), channel_id=1, source_target_pairs={{0,1},{1,0},{2,3},{3,2},{4,5},{5,4},{6,7},{7,6},{8,9},{9,8},{10,11... | collective-permute-start | bytes 1572872 | tf_op jit(solution)/shard_map/ppermute | solution.py:68
  23.7 1.2 %copy-start.2 = (bf16[8,1,256,256]{3,2,1,0:T(8,128)(2,1)S(1)}, bf16[8,1,256,256]{3,2,1,0:T(8,128)(2,1)}, u32[]{:S(2)}) copy-start(bf16[8,1,256,256]{3,2,1,0:T(8,128)(2,1)} %get-tuple-element.8) | copy-start | bytes 3145732
  27.8 13.5 %copy-start.5 = (bf16[2,1,64,256]{3,2,1,0:T(8,128)(2,1)S(1)}, bf16[2,1,64,256]{3,2,1,0:T(8,128)(2,1)}, u32[]{:S(2)}) copy-start(bf16[2,1,64,256]{3,2,1,0:T(8,128)(2,1)} %param.14) | copy-start | bytes 196612
  27.9 13.5 %copy-start.9 = (f32[256]{0:T(256)S(1)}, f32[256]{0:T(256)}, u32[]{:S(2)}) copy-start(f32[256]{0:T(256)} %param.18) | copy-start | bytes 3076
  27.9 16.8 %copy-start.14 = (f32[512]{0:T(512)S(1)}, f32[512]{0:T(512)}, u32[]{:S(2)}) copy-start(f32[512]{0:T(512)} %param.27) | copy-start | bytes 6148
  28.6 24.1 %copy-start.10 = (f32[256]{0:T(256)S(1)}, f32[256]{0:T(256)}, u32[]{:S(2)}) copy-start(f32[256]{0:T(256)} %param.20) | copy-start | bytes 3076
  28.6 24.1 %copy-start.11 = (f32[256]{0:T(256)S(1)}, f32[256]{0:T(256)}, u32[]{:S(2)}) copy-start(f32[256]{0:T(256)} %param.19) | copy-start | bytes 3076
  28.6 24.3 %copy-start.4 = (bf16[512,512]{1,0:T(8,128)(2,1)S(1)}, bf16[512,512]{1,0:T(8,128)(2,1)}, u32[]{:S(2)}) copy-start(bf16[512,512]{1,0:T(8,128)(2,1)} %param.24) | copy-start | bytes 1572868
  28.7 9.9 %collective-permute-start.7 = (f32[1,2,64,256]{3,2,1,0:T(8,128)S(1)}, f32[1,2,64,256]{3,2,1,0:T(8,128)S(1)}, u32[]{:S(2)}, u32[]{:S(2)}) collective-permute-start(f32[1,2,64,256]{3,2,1,0:T(8,128)S(1)} %get-tuple-element.26), channel_id=1, source_target_pairs={{0,8},{4,12},{8,0},{12,4},{1,9},{5,13},{9,1},{13,5},{2,10},{6,14},... | collective-permute-start | bytes 393224 | tf_op jit(solution)/shard_map/ppermute | solution.py:53
  28.8 12.6 %collective-permute-start.6 = (f32[1,2,64,256]{3,2,1,0:T(8,128)S(1)}, f32[1,2,64,256]{3,2,1,0:T(8,128)S(1)}, u32[]{:S(2)}, u32[]{:S(2)}) collective-permute-start(f32[1,2,64,256]{3,2,1,0:T(8,128)S(1)} %get-tuple-element.27), channel_id=1, source_target_pairs={{0,12},{4,0},{8,4},{12,8},{1,13},{5,1},{9,5},{13,9},{2,14},{6,2},{... | collective-permute-start | bytes 393224 | tf_op jit(solution)/shard_map/ppermute | solution.py:53
  31.4 10.0 %collective-permute-start.5 = (f32[1,2,64,256]{3,2,1,0:T(8,128)S(1)}, f32[1,2,64,256]{3,2,1,0:T(8,128)S(1)}, u32[]{:S(2)}, u32[]{:S(2)}) collective-permute-start(f32[1,2,64,256]{3,2,1,0:T(8,128)S(1)} %get-tuple-element.25), channel_id=1, source_target_pairs={{0,4},{4,8},{8,12},{12,0},{1,5},{5,9},{9,13},{13,1},{2,6},{6,10},{... | collective-permute-start | bytes 393224 | tf_op jit(solution)/shard_map/ppermute | solution.py:53
  41.4 11.8 %copy-start.3 = (bf16[512,512]{1,0:T(8,128)(2,1)S(1)}, bf16[512,512]{1,0:T(8,128)(2,1)}, u32[]{:S(2)}) copy-start(bf16[512,512]{1,0:T(8,128)(2,1)} %param.21) | copy-start | bytes 1572868
  41.5 6.8 %collective-permute-start.8 = (bf16[2,1,64,256]{3,2,1,0:T(8,128)(2,1)S(1)}, bf16[2,1,64,256]{3,2,1,0:T(8,128)(2,1)S(1)}, u32[]{:S(2)}, u32[]{:S(2)}) collective-permute-start(bf16[2,1,64,256]{3,2,1,0:T(8,128)(2,1)S(1)} %get-tuple-element.6), channel_id=1, source_target_pairs={{0,4},{4,8},{8,12},{12,0},{1,5},{5,9},{9,13},{13,1},{2,6},{6,10},{... | collective-permute-start | bytes 196616 | tf_op jit(solution)/shard_map/ppermute | solution.py:53
  44.8 4.8 %collective-permute-start.9 = (bf16[2,1,64,256]{3,2,1,0:T(8,128)(2,1)S(1)}, bf16[2,1,64,256]{3,2,1,0:T(8,128)(2,1)S(1)}, u32[]{:S(2)}, u32[]{:S(2)}) collective-permute-start(bf16[2,1,64,256]{3,2,1,0:T(8,128)(2,1)S(1)} %get-tuple-element.6), channel_id=1, source_target_pairs={{0,12},{4,0},{8,4},{12,8},{1,13},{5,1},{9,5},{13,9},{2,14},{6,2},{... | collective-permute-start | bytes 196616 | tf_op jit(solution)/shard_map/ppermute | solution.py:53
  45.4 6.4 %collective-permute-start.10 = (bf16[2,1,64,256]{3,2,1,0:T(8,128)(2,1)S(1)}, bf16[2,1,64,256]{3,2,1,0:T(8,128)(2,1)S(1)}, u32[]{:S(2)}, u32[]{:S(2)}) collective-permute-start(bf16[2,1,64,256]{3,2,1,0:T(8,128)(2,1)S(1)} %get-tuple-element.6), channel_id=1, source_target_pairs={{0,8},{4,12},{8,0},{12,4},{1,9},{5,13},{9,1},{13,5},{2,10},{6,14},... | collective-permute-start | bytes 196616 | tf_op jit(solution)/shard_map/ppermute | solution.py:53
  52.8 1.6 %collective-permute-start.11 = (bf16[2,4,64,256]{3,2,1,0:T(8,128)(2,1)S(1)}, bf16[2,4,64,256]{3,2,1,0:T(8,128)(2,1)S(1)}, u32[]{:S(2)}, u32[]{:S(2)}) collective-permute-start(bf16[2,4,64,256]{3,2,1,0:T(8,128)(2,1)S(1)} %fusion.38), channel_id=1, source_target_pairs={{0,1},{1,0},{2,3},{3,2},{4,5},{5,4},{6,7},{7,6},{8,9},{9,8},{10,11... | collective-permute-start | bytes 786440 | tf_op jit(solution)/shard_map/ppermute | solution.py:68
  53.2 1.5 %copy-start.8 = (f32[512]{0:T(512)S(1)}, f32[512]{0:T(512)}, u32[]{:S(2)}) copy-start(f32[512]{0:T(512)} %param.25) | copy-start | bytes 6148
  54.4 0.7 %copy-start.7 = (f32[512]{0:T(512)S(1)}, f32[512]{0:T(512)}, u32[]{:S(2)}) copy-start(f32[512]{0:T(512)} %param.22) | copy-start | bytes 6148
  54.7 1.4 %copy-start.6 = (bf16[512,512]{1,0:T(8,128)(2,1)S(1)}, bf16[512,512]{1,0:T(8,128)(2,1)}, u32[]{:S(2)}) copy-start(bf16[512,512]{1,0:T(8,128)(2,1)} %param.26) | copy-start | bytes 1572868

commit v16 on v11

--- a/solution.py
+++ b/solution.py
@@ -182,7 +182,7 @@
     pieces = partial.reshape(frames, row_count, rows_here, columns, out_channels)
     if row_count <= PERMUTE_GROUP:
         convolved = lax.dynamic_index_in_dim(pieces, row_place, axis=1, keepdims=False)
-        for shift in nearest_first(row_count):
+        for shift in nearest_first(row_count)[::-1]:
             chunk = lax.dynamic_index_in_dim(
                 pieces, (row_place + shift) % row_count, axis=1, keepdims=False
             )
@@ -193,7 +193,7 @@
 
     if row_count <= PERMUTE_GROUP:
         middle = jnp.zeros((frames, all_rows, columns, out_channels), own_middle.dtype)
-        for shift in [0] + nearest_first(row_count):
+        for shift in [0] + nearest_first(row_count)[::-1]:
             block = own_middle if shift == 0 else shifted(
                 own_middle, ("rows",), (row_count,), (shift,)
             )

time: 56.8 us -> 56.8 us (level)
  starting transfers between devices: 16 us -> 13.7 us
  waiting for transfers between devices: 24.7 us -> 26.9 us
    ppermute x10, starting transfers between devices: 15.8 us -> 13.6 us  [shifted(): return lax.ppermute(cells, axes, pairs)]
    ppermute x10, waiting for transfers between devices: 24.1 us -> 26.3 us  [shifted(): return lax.ppermute(cells, axes, pairs)]
where the time goes in v16:
time: 56.8 us; the launch traced here: 56.6 us
  waiting for transfers between devices  26.9 us (47%)
  starting transfers between devices  13.7 us (24%)
  local copies, waits for them, and re-layouts  8.32 us (15%)
  matrix products  3.84 us (7%)
  other arithmetic  3.15 us (6%)
  between operations  0.65 us (1%)
    ppermute x10, waiting for transfers between devices, shifted(): return lax.ppermute(cells, axes, pairs)  26.3 us
    ppermute x10, starting transfers between devices, shifted(): return lax.ppermute(cells, axes, pairs)  13.6 us
    dynamic_slice x4, local copies, waits for them, and re-layouts, local(): lax.dynamic_slice(half, (tap // 9, tap // 3 % 3, tap % 3, 0), (frames, al...  2.55 us
    dot_general x6, matrix products, split_dot(): jnp.dot(half, half_rows(weight, shift, width), preferred_element_type=jnp...  1.57 us
    unnamed x44, local copies, waits for them, and re-layouts  1.49 us
    dot_general x2, matrix products, local(): term = jnp.dot(patches, block, preferred_element_type=jnp.float32)  1.45 us
  transfers between devices with their start and end apart: 12, of which 10 were waited for; matrix products, arithmetic and copies ran while one was open for 10% of the time, Pallas kernels for 0%

profile of v16, /device:TPU:0, one launch (start us, length us, event | category | flops | bytes accessed | tf_op | source)
XLA Modules:
  0.0 56.6 jit_solution(14055397003032286817)
XLA Ops:
  0.0 3.0 %collective-permute-start = (bf16[2,1,64,256]{3,2,1,0:T(8,128)(2,1)}, bf16[2,1,64,256]{3,2,1,0:T(8,128)(2,1)S(1)}, u32[]{:S(2)}, u32[]{:S(2)}) collective-permute-start(bf16[2,1,64,256]{3,2,1,0:T(8,128)(2,1)} %param.14), channel_id=1, source_target_pairs={{0,4},{4,8},{8,12},{12,0},{1,5},{5,9},{9,13},{13,1},{2,6},{6,10},{... | collective-permute-start | bytes 196616 | tf_op jit(solution)/shard_map/ppermute | solution.py:53
  3.0 2.1 %collective-permute-start.1 = (bf16[2,1,64,256]{3,2,1,0:T(8,128)(2,1)}, bf16[2,1,64,256]{3,2,1,0:T(8,128)(2,1)S(1)}, u32[]{:S(2)}, u32[]{:S(2)}) collective-permute-start(bf16[2,1,64,256]{3,2,1,0:T(8,128)(2,1)} %param.14), channel_id=1, source_target_pairs={{0,12},{4,0},{8,4},{12,8},{1,13},{5,1},{9,5},{13,9},{2,14},{6,2},{... | collective-permute-start | bytes 196616 | tf_op jit(solution)/shard_map/ppermute | solution.py:53
  5.1 0.9 %collective-permute-start.2 = (bf16[2,1,64,256]{3,2,1,0:T(8,128)(2,1)}, bf16[2,1,64,256]{3,2,1,0:T(8,128)(2,1)S(1)}, u32[]{:S(2)}, u32[]{:S(2)}) collective-permute-start(bf16[2,1,64,256]{3,2,1,0:T(8,128)(2,1)} %param.14), channel_id=1, source_target_pairs={{0,8},{4,12},{8,0},{12,4},{1,9},{5,13},{9,1},{13,5},{2,10},{6,14},... | collective-permute-start | bytes 196616 | tf_op jit(solution)/shard_map/ppermute | solution.py:53
  6.1 0.9 %constant_dynamic-update-slice_fusion.26 = bf16[2,4,64,256]{3,2,1,0:T(8,128)(2,1)S(1)} fusion(bf16[2,4,64,256]{3,2,1,0:T(8,128)(2,1)S(1)} %broadcast.147.clone, bf16[2,1,64,256]{3,2,1,0:T(8,128)(2,1)} %param.14, s32[]{:T(128)S(6)} %select_n.416), kind=kLoop, calls=%fused_computation.132 | loop fusion | bytes 131076 | tf_op jit(solution)/shard_map/dynamic_update_slice | solution.py:118
  7.0 0.1 broadcast_in_dim.17
  7.1 0.2 constant_dynamic-update-slice_fusion.20
  7.4 0.3 collective-permute-done
  7.7 0.5 collective-permute-done.1
  8.2 3.3 %collective-permute-done.2 = bf16[2,1,64,256]{3,2,1,0:T(8,128)(2,1)S(1)} collective-permute-done((bf16[2,1,64,256]{3,2,1,0:T(8,128)(2,1)}, bf16[2,1,64,256]{3,2,1,0:T(8,128)(2,1)S(1)}, u32[]{:S(2)}, u32[]{:S(2)}) %collective-permute-start.2) | collective-permute-done | bytes 65568 | tf_op jit(solution)/shard_map/ppermute | solution.py:53
  11.6 1.6 %collective-permute-start.3 = (bf16[2,4,64,256]{3,2,1,0:T(8,128)(2,1)S(1)}, bf16[2,4,64,256]{3,2,1,0:T(8,128)(2,1)S(1)}, u32[]{:S(2)}, u32[]{:S(2)}) collective-permute-start(bf16[2,4,64,256]{3,2,1,0:T(8,128)(2,1)S(1)} %constant_dynamic-update-slice_fusion.23), channel_id=1, source_target_pairs={{0,2},{2,0},{1,3},{3,1},{4,6},{6,4},{5,7},{7,5},{8,10},{10,8},{9,1... | collective-permute-start | bytes 786440 | tf_op jit(solution)/shard_map/ppermute | solution.py:53
  13.1 1.1 %constant_dynamic-slice_fusion.2 = (bf16[8,1,256,256]{3,2,1,0:T(8,128)(2,1)S(1)}, bf16[8,1,256,256]{3,2,1,0:T(8,128)(2,1)}) fusion(bf16[8,2,256,256]{3,2,1,0:T(8,128)(2,1)S(1)} %bitcast.68, s32[]{:T(128)S(6)} %select_n.491, s32[]{:T(128)S(6)} %select_n.489), kind=kLoop, calls=%fused_computation.108 | loop fusion | bytes 4194312 | tf_op jit(solution)/shard_map/jit(dynamic_index_in_dim)/dynamic_slice | solution.py:176
  14.3 5.2 %collective-permute-done.3 = bf16[2,4,64,256]{3,2,1,0:T(8,128)(2,1)S(1)} collective-permute-done((bf16[2,4,64,256]{3,2,1,0:T(8,128)(2,1)S(1)}, bf16[2,4,64,256]{3,2,1,0:T(8,128)(2,1)S(1)}, u32[]{:S(2)}, u32[]{:S(2)}) %collective-permute-start.3) | collective-permute-done | bytes 262176 | tf_op jit(solution)/shard_map/ppermute | solution.py:53
  19.5 0.2 convert_reduce_fusion
  19.7 0.1 reduce_sum.55
  19.8 0.1 reduce_sum.59
  19.9 0.1 sub.143
  20.0 0.1 sub.144
  20.1 0.2 fusion.20
  20.3 0.1 reduce_sum.61
  20.3 0.1 reduce_sum.62
  20.6 0.1 mul.91
  20.6 0.6 %gather_fusion = bf16[4,4,64,256]{3,2,1,0:T(8,128)(2,1)S(1)} fusion(bf16[4,4,64,256]{3,2,1,0:T(8,128)(2,1)S(1)} %constant_dynamic-update-slice_fusion.21, s32[1024]{0:T(1024)S(1)} %pad_clamp_fusion), kind=kCustom, calls=%fused_computation | custom fusion | bytes 1048592 | tf_op jit(solution)/shard_map/jit(_take)/gather | solution.py:141
  21.3 0.5 multiply_convert_fusion
  21.8 0.1 collective-permute-start.4
  21.8 0.4 fusion.24
  22.2 0.2 constant_dynamic-slice_fusion.18
  22.5 1.1 %constant_dynamic-slice_fusion.12 = (bf16[2,4,64,256]{3,2,1,0:T(8,128)(2,1)S(1)}, bf16[2,4,64,256]{3,2,1,0:T(8,128)(2,1)S(1)}, bf16[2,4,64,256]{3,2,1,0:T(8,128)...) fusion(bf16[4,6,66,256]{3,2,1,0:T(8,128)(2,1)S(1)} %fusion.24, ...), kind=kLoop, calls=%fused_computation.119 | loop fusion | bytes 3145800 | tf_op jit(solution)/shard_map/dynamic_slice | solution.py:169
  23.8 1.0 %copy-done.2 = bf16[8,1,256,256]{3,2,1,0:T(8,128)(2,1)S(1)} copy-done((bf16[8,1,256,256]{3,2,1,0:T(8,128)(2,1)S(1)}, bf16[8,1,256,256]{3,2,1,0:T(8,128)(2,1)}, u32[]{:S(2)}) %copy-start.2) | copy-done | bytes 1048600
  24.8 0.7 %fusion.71 = f32[512,256]{1,0:T(8,128)S(1)} fusion(bf16[512,2048]{1,0:T(8,128)(2,1)S(1)} %constant_dynamic-update-slice_fusion, bf16[2048,256]{1,0:T(8,128)(2,1)S(1)} %bitcast.75), kind=kOutput, calls=%fused_computation.145 | convolution fusion | flops 536870912 | bytes 3670016 | tf_op jit(solution)/shard_map/dot_general | solution.py:179
  25.5 0.4 fusion.28
  25.9 0.2 constant_dynamic-slice_fusion.9
  26.1 1.1 %constant_dynamic-slice_fusion.3 = (bf16[2,4,64,256]{3,2,1,0:T(8,128)(2,1)S(1)}, bf16[2,4,64,256]{3,2,1,0:T(8,128)(2,1)S(1)}, bf16[2,4,64,256]{3,2,1,0:T(8,128)(...) fusion(bf16[4,6,66,256]{3,2,1,0:T(8,128)(2,1)S(1)} %fusion.28, ...), kind=kLoop, calls=%fused_computation.109 | loop fusion | bytes 3145800 | tf_op jit(solution)/shard_map/dynamic_slice | solution.py:169
  27.5 0.7 %convolution_add_fusion.2 = f32[512,256]{1,0:T(8,128)S(1)} fusion(f32[512,256]{1,0:T(8,128)S(1)} %fusion.71, bf16[512,2048]{1,0:T(8,128)(2,1)S(1)} %constant_dynamic-update-slice_fusion.8, bf16[2048,256]{1,0:T(8,128)(2,1)S(1)} %bitcast.74), kind=kOutput, calls=%fused_computation.22 | convolution fusion | flops 537001984 | bytes 4194304 | tf_op jit(solution)/shard_map/dot_general | solution.py:179
  28.4 3.8 %collective-permute-start.6 = (f32[2,1,64,256]{3,2,1,0:T(8,128)S(1)}, f32[2,1,64,256]{3,2,1,0:T(8,128)S(1)}, u32[]{:S(2)}, u32[]{:S(2)}) collective-permute-start(f32[2,1,64,256]{3,2,1,0:T(8,128)S(1)} %get-tuple-element.27), channel_id=1, source_target_pairs={{0,12},{4,0},{8,4},{12,8},{1,13},{5,1},{9,5},{13,9},{2,14},{6,2},{... | collective-permute-start | bytes 393224 | tf_op jit(solution)/shard_map/ppermute | solution.py:53
  32.2 4.3 %collective-permute-done.7 = f32[2,1,64,256]{3,2,1,0:T(8,128)S(1)} collective-permute-done((f32[2,1,64,256]{3,2,1,0:T(8,128)S(1)}, f32[2,1,64,256]{3,2,1,0:T(8,128)S(1)}, u32[]{:S(2)}, u32[]{:S(2)}) %collective-permute-start.7) | collective-permute-done | bytes 131104 | tf_op jit(solution)/shard_map/ppermute | solution.py:53
  36.5 0.6 %collective-permute-done.6 = f32[2,1,64,256]{3,2,1,0:T(8,128)S(1)} collective-permute-done((f32[2,1,64,256]{3,2,1,0:T(8,128)S(1)}, f32[2,1,64,256]{3,2,1,0:T(8,128)S(1)}, u32[]{:S(2)}, u32[]{:S(2)}) %collective-permute-start.6) | collective-permute-done | bytes 131104 | tf_op jit(solution)/shard_map/ppermute | solution.py:53
  37.2 6.7 %collective-permute-done.5 = f32[2,1,64,256]{3,2,1,0:T(8,128)S(1)} collective-permute-done((f32[2,1,64,256]{3,2,1,0:T(8,128)S(1)}, f32[2,1,64,256]{3,2,1,0:T(8,128)S(1)}, u32[]{:S(2)}, u32[]{:S(2)}) %collective-permute-start.5) | collective-permute-done | bytes 131104 | tf_op jit(solution)/shard_map/ppermute | solution.py:53
  44.0 0.1 dynamic_slice.129
  44.1 1.1 %collective-permute-start.9 = (bf16[2,1,64,256]{3,2,1,0:T(8,128)(2,1)S(1)}, bf16[2,1,64,256]{3,2,1,0:T(8,128)(2,1)S(1)}, u32[]{:S(2)}, u32[]{:S(2)}) collective-permute-start(bf16[2,1,64,256]{3,2,1,0:T(8,128)(2,1)S(1)} %get-tuple-element.6), channel_id=1, source_target_pairs={{0,12},{4,0},{8,4},{12,8},{1,13},{5,1},{9,5},{13,9},{2,14},{6,2},{... | collective-permute-start | bytes 196616 | tf_op jit(solution)/shard_map/ppermute | solution.py:53
  45.2 1.0 %collective-permute-start.10 = (bf16[2,1,64,256]{3,2,1,0:T(8,128)(2,1)S(1)}, bf16[2,1,64,256]{3,2,1,0:T(8,128)(2,1)S(1)}, u32[]{:S(2)}, u32[]{:S(2)}) collective-permute-start(bf16[2,1,64,256]{3,2,1,0:T(8,128)(2,1)S(1)} %get-tuple-element.6), channel_id=1, source_target_pairs={{0,4},{4,8},{8,12},{12,0},{1,5},{5,9},{9,13},{13,1},{2,6},{6,10},{... | collective-permute-start | bytes 196616 | tf_op jit(solution)/shard_map/ppermute | solution.py:53
  46.1 4.0 %collective-permute-done.8 = bf16[2,1,64,256]{3,2,1,0:T(8,128)(2,1)S(1)} collective-permute-done((bf16[2,1,64,256]{3,2,1,0:T(8,128)(2,1)S(1)}, bf16[2,1,64,256]{3,2,1,0:T(8,128)(2,1)S(1)}, u32[]{:S(2)}, u32[]{:S(2)}) %collective-permute-start.8) | collective-permute-done | bytes 65568 | tf_op jit(solution)/shard_map/ppermute | solution.py:53
  50.1 1.4 %collective-permute-done.10 = bf16[2,1,64,256]{3,2,1,0:T(8,128)(2,1)S(1)} collective-permute-done((bf16[2,1,64,256]{3,2,1,0:T(8,128)(2,1)S(1)}, bf16[2,1,64,256]{3,2,1,0:T(8,128)(2,1)S(1)}, u32[]{:S(2)}, u32[]{:S(2)}) %collective-permute-start.10) | collective-permute-done | bytes 65568 | tf_op jit(solution)/shard_map/ppermute | solution.py:53
  51.6 0.1 reduce_sum.80
  51.6 0.1 reduce_sum.81
  51.7 0.1 sub.166
  51.8 0.1 sub.167
  51.9 0.1 fusion.35
  52.0 0.1 reduce_sum.83
  52.1 0.1 reduce_sum.84
  52.2 0.1 mul.99
  52.2 0.1 mul.100
  52.4 0.1 fusion.38
  52.6 0.3 fusion.41
  52.9 0.2 fusion.47
  53.1 0.3 fusion.44
  53.4 0.7 %collective-permute-done.11 = bf16[2,4,64,256]{3,2,1,0:T(8,128)(2,1)S(1)} collective-permute-done((bf16[2,4,64,256]{3,2,1,0:T(8,128)(2,1)S(1)}, bf16[2,4,64,256]{3,2,1,0:T(8,128)(2,1)S(1)}, u32[]{:S(2)}, u32[]{:S(2)}) %collective-permute-start.11) | collective-permute-done | bytes 262176 | tf_op jit(solution)/shard_map/ppermute | solution.py:68
  54.1 0.3 fusion.13
  54.4 0.3 fusion.14
  54.8 0.2 fusion.16
  55.0 0.4 fusion.70
  55.3 0.2 fusion.55
  55.5 0.3 fusion.17
  55.8 0.2 fusion.18
  56.0 0.6 %fusion.49 = bf16[2,1,64,256]{3,2,1,0:T(8,128)(2,1)} fusion(bf16[2,1,64,256]{3,2,1,0:T(8,128)(2,1)S(1)} %bitcast.97, bf16[2,1,64,256]{3,2,1,0:T(8,128)(2,1)S(1)} %get-tuple-element.6), kind=kLoop, calls=%fused_computation.65 | loop fusion | flops 131072 | bytes 196608 | tf_op jit(solution)/shard_map/convert_element_type | solution.py:254
  (77 shorter events, 1.3 us)
Async XLA Ops:
  0.0 53.1 %copy-start = (bf16[512,512]{1,0:T(8,128)(2,1)S(1)}, bf16[512,512]{1,0:T(8,128)(2,1)}, u32[]{:S(2)}) copy-start(bf16[512,512]{1,0:T(8,128)(2,1)} %param.23) | copy-start | bytes 1572868
  0.0 7.1 %copy-start.1 = (bf16[3456,256]{1,0:T(8,128)(2,1)S(1)}, bf16[3456,256]{1,0:T(8,128)(2,1)}, u32[]{:S(2)}) copy-start(bf16[3456,256]{1,0:T(8,128)(2,1)} %param.17) | copy-start | bytes 5308420
  0.0 7.7 %collective-permute-start = (bf16[2,1,64,256]{3,2,1,0:T(8,128)(2,1)}, bf16[2,1,64,256]{3,2,1,0:T(8,128)(2,1)S(1)}, u32[]{:S(2)}, u32[]{:S(2)}) collective-permute-start(bf16[2,1,64,256]{3,2,1,0:T(8,128)(2,1)} %param.14), channel_id=1, source_target_pairs={{0,4},{4,8},{8,12},{12,0},{1,5},{5,9},{9,13},{13,1},{2,6},{6,10},{... | collective-permute-start | bytes 196616 | tf_op jit(solution)/shard_map/ppermute | solution.py:53
  3.0 5.2 %collective-permute-start.1 = (bf16[2,1,64,256]{3,2,1,0:T(8,128)(2,1)}, bf16[2,1,64,256]{3,2,1,0:T(8,128)(2,1)S(1)}, u32[]{:S(2)}, u32[]{:S(2)}) collective-permute-start(bf16[2,1,64,256]{3,2,1,0:T(8,128)(2,1)} %param.14), channel_id=1, source_target_pairs={{0,12},{4,0},{8,4},{12,8},{1,13},{5,1},{9,5},{13,9},{2,14},{6,2},{... | collective-permute-start | bytes 196616 | tf_op jit(solution)/shard_map/ppermute | solution.py:53
  5.1 6.4 %collective-permute-start.2 = (bf16[2,1,64,256]{3,2,1,0:T(8,128)(2,1)}, bf16[2,1,64,256]{3,2,1,0:T(8,128)(2,1)S(1)}, u32[]{:S(2)}, u32[]{:S(2)}) collective-permute-start(bf16[2,1,64,256]{3,2,1,0:T(8,128)(2,1)} %param.14), channel_id=1, source_target_pairs={{0,8},{4,12},{8,0},{12,4},{1,9},{5,13},{9,1},{13,5},{2,10},{6,14},... | collective-permute-start | bytes 196616 | tf_op jit(solution)/shard_map/ppermute | solution.py:53
  11.6 7.9 %collective-permute-start.3 = (bf16[2,4,64,256]{3,2,1,0:T(8,128)(2,1)S(1)}, bf16[2,4,64,256]{3,2,1,0:T(8,128)(2,1)S(1)}, u32[]{:S(2)}, u32[]{:S(2)}) collective-permute-start(bf16[2,4,64,256]{3,2,1,0:T(8,128)(2,1)S(1)} %constant_dynamic-update-slice_fusion.23), channel_id=1, source_target_pairs={{0,2},{2,0},{1,3},{3,1},{4,6},{6,4},{5,7},{7,5},{8,10},{10,8},{9,1... | collective-permute-start | bytes 786440 | tf_op jit(solution)/shard_map/ppermute | solution.py:53
  14.2 7.0 %copy-start.12 = (f32[256]{0:T(256)S(1)}, f32[256]{0:T(256)}, u32[]{:S(2)}) copy-start(f32[256]{0:T(256)} %param.16) | copy-start | bytes 3076
  14.2 7.0 %copy-start.13 = (f32[256]{0:T(256)S(1)}, f32[256]{0:T(256)}, u32[]{:S(2)}) copy-start(f32[256]{0:T(256)} %param.15) | copy-start | bytes 3076
  21.8 3.8 %collective-permute-start.4 = (bf16[4,4,64,256]{3,2,1,0:T(8,128)(2,1)S(1)}, bf16[4,4,64,256]{3,2,1,0:T(8,128)(2,1)S(1)}, u32[]{:S(2)}, u32[]{:S(2)}) collective-permute-start(bf16[4,4,64,256]{3,2,1,0:T(8,128)(2,1)S(1)} %multiply_convert_fusion), channel_id=1, source_target_pairs={{0,1},{1,0},{2,3},{3,2},{4,5},{5,4},{6,7},{7,6},{8,9},{9,8},{10,11... | collective-permute-start | bytes 1572872 | tf_op jit(solution)/shard_map/ppermute | solution.py:68
  23.6 1.2 %copy-start.2 = (bf16[8,1,256,256]{3,2,1,0:T(8,128)(2,1)S(1)}, bf16[8,1,256,256]{3,2,1,0:T(8,128)(2,1)}, u32[]{:S(2)}) copy-start(bf16[8,1,256,256]{3,2,1,0:T(8,128)(2,1)} %get-tuple-element.8) | copy-start | bytes 3145732
  27.5 16.4 %copy-start.5 = (bf16[2,1,64,256]{3,2,1,0:T(8,128)(2,1)S(1)}, bf16[2,1,64,256]{3,2,1,0:T(8,128)(2,1)}, u32[]{:S(2)}) copy-start(bf16[2,1,64,256]{3,2,1,0:T(8,128)(2,1)} %param.14) | copy-start | bytes 196612
  27.5 16.4 %copy-start.9 = (f32[256]{0:T(256)S(1)}, f32[256]{0:T(256)}, u32[]{:S(2)}) copy-start(f32[256]{0:T(256)} %param.18) | copy-start | bytes 3076
  27.5 16.5 %copy-start.14 = (f32[512]{0:T(512)S(1)}, f32[512]{0:T(512)}, u32[]{:S(2)}) copy-start(f32[512]{0:T(512)} %param.27) | copy-start | bytes 6148
  28.2 24.1 %copy-start.10 = (f32[256]{0:T(256)S(1)}, f32[256]{0:T(256)}, u32[]{:S(2)}) copy-start(f32[256]{0:T(256)} %param.20) | copy-start | bytes 3076
  28.3 24.1 %copy-start.11 = (f32[256]{0:T(256)S(1)}, f32[256]{0:T(256)}, u32[]{:S(2)}) copy-start(f32[256]{0:T(256)} %param.19) | copy-start | bytes 3076
  28.3 24.3 %copy-start.4 = (bf16[512,512]{1,0:T(8,128)(2,1)S(1)}, bf16[512,512]{1,0:T(8,128)(2,1)}, u32[]{:S(2)}) copy-start(bf16[512,512]{1,0:T(8,128)(2,1)} %param.24) | copy-start | bytes 1572868
  28.3 8.2 %collective-permute-start.7 = (f32[2,1,64,256]{3,2,1,0:T(8,128)S(1)}, f32[2,1,64,256]{3,2,1,0:T(8,128)S(1)}, u32[]{:S(2)}, u32[]{:S(2)}) collective-permute-start(f32[2,1,64,256]{3,2,1,0:T(8,128)S(1)} %get-tuple-element.26), channel_id=1, source_target_pairs={{0,4},{4,8},{8,12},{12,0},{1,5},{5,9},{9,13},{13,1},{2,6},{6,10},{... | collective-permute-start | bytes 393224 | tf_op jit(solution)/shard_map/ppermute | solution.py:53
  28.4 8.8 %collective-permute-start.6 = (f32[2,1,64,256]{3,2,1,0:T(8,128)S(1)}, f32[2,1,64,256]{3,2,1,0:T(8,128)S(1)}, u32[]{:S(2)}, u32[]{:S(2)}) collective-permute-start(f32[2,1,64,256]{3,2,1,0:T(8,128)S(1)} %get-tuple-element.27), channel_id=1, source_target_pairs={{0,12},{4,0},{8,4},{12,8},{1,13},{5,1},{9,5},{13,9},{2,14},{6,2},{... | collective-permute-start | bytes 393224 | tf_op jit(solution)/shard_map/ppermute | solution.py:53
  32.2 11.6 %collective-permute-start.5 = (f32[2,1,64,256]{3,2,1,0:T(8,128)S(1)}, f32[2,1,64,256]{3,2,1,0:T(8,128)S(1)}, u32[]{:S(2)}, u32[]{:S(2)}) collective-permute-start(f32[2,1,64,256]{3,2,1,0:T(8,128)S(1)} %get-tuple-element.25), channel_id=1, source_target_pairs={{0,8},{4,12},{8,0},{12,4},{1,9},{5,13},{9,1},{13,5},{2,10},{6,14},... | collective-permute-start | bytes 393224 | tf_op jit(solution)/shard_map/ppermute | solution.py:53
  43.9 9.0 %copy-start.3 = (bf16[512,512]{1,0:T(8,128)(2,1)S(1)}, bf16[512,512]{1,0:T(8,128)(2,1)}, u32[]{:S(2)}) copy-start(bf16[512,512]{1,0:T(8,128)(2,1)} %param.21) | copy-start | bytes 1572868
  43.9 6.2 %collective-permute-start.8 = (bf16[2,1,64,256]{3,2,1,0:T(8,128)(2,1)S(1)}, bf16[2,1,64,256]{3,2,1,0:T(8,128)(2,1)S(1)}, u32[]{:S(2)}, u32[]{:S(2)}) collective-permute-start(bf16[2,1,64,256]{3,2,1,0:T(8,128)(2,1)S(1)} %get-tuple-element.6), channel_id=1, source_target_pairs={{0,8},{4,12},{8,0},{12,4},{1,9},{5,13},{9,1},{13,5},{2,10},{6,14},... | collective-permute-start | bytes 196616 | tf_op jit(solution)/shard_map/ppermute | solution.py:53
  44.1 6.0 %collective-permute-start.9 = (bf16[2,1,64,256]{3,2,1,0:T(8,128)(2,1)S(1)}, bf16[2,1,64,256]{3,2,1,0:T(8,128)(2,1)S(1)}, u32[]{:S(2)}, u32[]{:S(2)}) collective-permute-start(bf16[2,1,64,256]{3,2,1,0:T(8,128)(2,1)S(1)} %get-tuple-element.6), channel_id=1, source_target_pairs={{0,12},{4,0},{8,4},{12,8},{1,13},{5,1},{9,5},{13,9},{2,14},{6,2},{... | collective-permute-start | bytes 196616 | tf_op jit(solution)/shard_map/ppermute | solution.py:53
  45.2 6.3 %collective-permute-start.10 = (bf16[2,1,64,256]{3,2,1,0:T(8,128)(2,1)S(1)}, bf16[2,1,64,256]{3,2,1,0:T(8,128)(2,1)S(1)}, u32[]{:S(2)}, u32[]{:S(2)}) collective-permute-start(bf16[2,1,64,256]{3,2,1,0:T(8,128)(2,1)S(1)} %get-tuple-element.6), channel_id=1, source_target_pairs={{0,4},{4,8},{8,12},{12,0},{1,5},{5,9},{9,13},{13,1},{2,6},{6,10},{... | collective-permute-start | bytes 196616 | tf_op jit(solution)/shard_map/ppermute | solution.py:53
  52.5 1.6 %collective-permute-start.11 = (bf16[2,4,64,256]{3,2,1,0:T(8,128)(2,1)S(1)}, bf16[2,4,64,256]{3,2,1,0:T(8,128)(2,1)S(1)}, u32[]{:S(2)}, u32[]{:S(2)}) collective-permute-start(bf16[2,4,64,256]{3,2,1,0:T(8,128)(2,1)S(1)} %fusion.38), channel_id=1, source_target_pairs={{0,1},{1,0},{2,3},{3,2},{4,5},{5,4},{6,7},{7,6},{8,9},{9,8},{10,11... | collective-permute-start | bytes 786440 | tf_op jit(solution)/shard_map/ppermute | solution.py:68
  52.9 1.5 %copy-start.8 = (f32[512]{0:T(512)S(1)}, f32[512]{0:T(512)}, u32[]{:S(2)}) copy-start(f32[512]{0:T(512)} %param.25) | copy-start | bytes 6148
  54.1 0.7 %copy-start.7 = (f32[512]{0:T(512)S(1)}, f32[512]{0:T(512)}, u32[]{:S(2)}) copy-start(f32[512]{0:T(512)} %param.22) | copy-start | bytes 6148
  54.4 1.4 %copy-start.6 = (bf16[512,512]{1,0:T(8,128)(2,1)S(1)}, bf16[512,512]{1,0:T(8,128)(2,1)}, u32[]{:S(2)}) copy-start(bf16[512,512]{1,0:T(8,128)(2,1)} %param.26) | copy-start | bytes 1572868

commit v17 on v11

--- a/solution.py
+++ b/solution.py
@@ -135,10 +135,7 @@
         )
 
     mean1, var1 = group_stats(clip, group_size, (0, 1, 2, 4))
-    frame_index = jnp.clip(
-        time_place * frames - 2 + jnp.arange(frames + 2), 0, time_count * frames - 1
-    )
-    segment = jnp.take(clip, frame_index, axis=0)
+    segment = lax.dynamic_slice_in_dim(edge_pad(clip, 0, 2, 0), time_place * frames, frames + 2)
     activated = jax.nn.silu(
         apply_norm(segment, mean1, var1, group_size) * norm1_gain + norm1_bias
     ).astype(jnp.bfloat16)

time: 56.8 us -> 55.2 us (0.972)
  local copies, waits for them, and re-layouts: 8.31 us -> 5.5 us
  waiting for transfers between devices: 24.7 us -> 26 us
    ppermute x10, waiting for transfers between devices: 24.1 us -> 25.3 us  [shifted(): return lax.ppermute(cells, axes, pairs)]
    dynamic_slice x1, local copies, waits for them, and re-layouts: 1.11 us -> 0.14 us  [local(): lax.dynamic_index_in_dim(placed, source, axis=1, keepdims=False)]
    dynamic_update_slice x4, local copies, waits for them, and re-layouts: 0.88 us -> 0.03 us  [local(): lax.dynamic_update_slice(segment_rows, block, (0, source_row * rows_here,...]
    gather x1 -> x0, local copies, waits for them, and re-layouts: 0.6 us -> none  [local(): segment = jnp.take(clip, frame_index, axis=0)]
    unnamed x44 -> x42, local copies, waits for them, and re-layouts: 1.49 us -> 1.08 us
  transfers between devices with their start and end apart: 12 -> 12, of which waited for: 10 -> 10; matrix products, arithmetic and copies ran while one was open for 10% -> 7% of each run, Pallas kernels for 0% -> 0%
where the time goes in v17:
time: 55.2 us; the launch traced here: 55 us
  waiting for transfers between devices  26 us (47%)
  starting transfers between devices  16 us (29%)
  local copies, waits for them, and re-layouts  5.5 us (10%)
  matrix products  3.83 us (7%)
  other arithmetic  3.17 us (6%)
  between operations  0.59 us (1%)
    ppermute x10, waiting for transfers between devices, shifted(): return lax.ppermute(cells, axes, pairs)  25.3 us
    ppermute x10, starting transfers between devices, shifted(): return lax.ppermute(cells, axes, pairs)  15.8 us
    dynamic_slice x4, local copies, waits for them, and re-layouts, local(): lax.dynamic_slice(half, (tap // 9, tap // 3 % 3, tap % 3, 0), (frames, al...  2.55 us
    dot_general x6, matrix products, split_dot(): jnp.dot(half, half_rows(weight, shift, width), preferred_element_type=jnp...  1.55 us
    dot_general x2, matrix products, local(): term = jnp.dot(patches, block, preferred_element_type=jnp.float32)  1.46 us
  transfers between devices with their start and end apart: 12, of which 10 were waited for; matrix products, arithmetic and copies ran while one was open for 7% of the time, Pallas kernels for 0%

profile of v17, /device:TPU:0, one launch (start us, length us, event | category | flops | bytes accessed | tf_op | source)
XLA Modules:
  0.0 55.0 jit_solution(4923274698427513232)
XLA Ops:
  0.0 3.0 %collective-permute-start = (bf16[2,1,64,256]{3,2,1,0:T(8,128)(2,1)}, bf16[2,1,64,256]{3,2,1,0:T(8,128)(2,1)S(1)}, u32[]{:S(2)}, u32[]{:S(2)}) collective-permute-start(bf16[2,1,64,256]{3,2,1,0:T(8,128)(2,1)} %param.14), channel_id=1, source_target_pairs={{0,4},{4,8},{8,12},{12,0},{1,5},{5,9},{9,13},{13,1},{2,6},{6,10},{... | collective-permute-start | bytes 196616 | tf_op jit(solution)/shard_map/ppermute | solution.py:53
  3.0 2.1 %collective-permute-start.1 = (bf16[2,1,64,256]{3,2,1,0:T(8,128)(2,1)}, bf16[2,1,64,256]{3,2,1,0:T(8,128)(2,1)S(1)}, u32[]{:S(2)}, u32[]{:S(2)}) collective-permute-start(bf16[2,1,64,256]{3,2,1,0:T(8,128)(2,1)} %param.14), channel_id=1, source_target_pairs={{0,12},{4,0},{8,4},{12,8},{1,13},{5,1},{9,5},{13,9},{2,14},{6,2},{... | collective-permute-start | bytes 196616 | tf_op jit(solution)/shard_map/ppermute | solution.py:53
  5.1 0.9 %collective-permute-start.2 = (bf16[2,1,64,256]{3,2,1,0:T(8,128)(2,1)}, bf16[2,1,64,256]{3,2,1,0:T(8,128)(2,1)S(1)}, u32[]{:S(2)}, u32[]{:S(2)}) collective-permute-start(bf16[2,1,64,256]{3,2,1,0:T(8,128)(2,1)} %param.14), channel_id=1, source_target_pairs={{0,8},{4,12},{8,0},{12,4},{1,9},{5,13},{9,1},{13,5},{2,10},{6,14},... | collective-permute-start | bytes 196616 | tf_op jit(solution)/shard_map/ppermute | solution.py:53
  6.1 0.1 broadcast_in_dim.5
  6.2 0.2 constant_dynamic-update-slice_fusion.20
  6.5 0.6 %copy-done.4 = bf16[2,1,64,256]{3,2,1,0:T(8,128)(2,1)S(1)} copy-done((bf16[2,1,64,256]{3,2,1,0:T(8,128)(2,1)S(1)}, bf16[2,1,64,256]{3,2,1,0:T(8,128)(2,1)}, u32[]{:S(2)}) %copy-start.4) | copy-done | bytes 65560
  7.1 0.6 %collective-permute-done = bf16[2,1,64,256]{3,2,1,0:T(8,128)(2,1)S(1)} collective-permute-done((bf16[2,1,64,256]{3,2,1,0:T(8,128)(2,1)}, bf16[2,1,64,256]{3,2,1,0:T(8,128)(2,1)S(1)}, u32[]{:S(2)}, u32[]{:S(2)}) %collective-permute-start) | collective-permute-done | bytes 65568 | tf_op jit(solution)/shard_map/ppermute | solution.py:53
  7.7 0.5 collective-permute-done.1
  8.2 3.3 %collective-permute-done.2 = bf16[2,1,64,256]{3,2,1,0:T(8,128)(2,1)S(1)} collective-permute-done((bf16[2,1,64,256]{3,2,1,0:T(8,128)(2,1)}, bf16[2,1,64,256]{3,2,1,0:T(8,128)(2,1)S(1)}, u32[]{:S(2)}, u32[]{:S(2)}) %collective-permute-start.2) | collective-permute-done | bytes 65568 | tf_op jit(solution)/shard_map/ppermute | solution.py:53
  11.6 1.6 %collective-permute-start.3 = (bf16[2,4,64,256]{3,2,1,0:T(8,128)(2,1)S(1)}, bf16[2,4,64,256]{3,2,1,0:T(8,128)(2,1)S(1)}, u32[]{:S(2)}, u32[]{:S(2)}) collective-permute-start(bf16[2,4,64,256]{3,2,1,0:T(8,128)(2,1)S(1)} %constant_dynamic-update-slice_fusion.23), channel_id=1, source_target_pairs={{0,2},{2,0},{1,3},{3,1},{4,6},{6,4},{5,7},{7,5},{8,10},{10,8},{9,1... | collective-permute-start | bytes 786440 | tf_op jit(solution)/shard_map/ppermute | solution.py:53
  13.1 0.1 constant_dynamic-slice_fusion.2
  13.4 6.1 %collective-permute-done.3 = bf16[2,4,64,256]{3,2,1,0:T(8,128)(2,1)S(1)} collective-permute-done((bf16[2,4,64,256]{3,2,1,0:T(8,128)(2,1)S(1)}, bf16[2,4,64,256]{3,2,1,0:T(8,128)(2,1)S(1)}, u32[]{:S(2)}, u32[]{:S(2)}) %collective-permute-start.3) | collective-permute-done | bytes 262176 | tf_op jit(solution)/shard_map/ppermute | solution.py:53
  19.6 0.2 convert_reduce_fusion
  19.7 0.1 reduce_sum.55
  19.8 0.1 reduce_sum.59
  19.9 0.1 sub.139
  20.0 0.1 sub.140
  20.1 0.2 fusion.20
  20.3 0.1 reduce_sum.61
  20.4 0.1 reduce_sum.62
  20.6 0.1 mul.91
  20.7 0.5 multiply_convert_fusion
  21.3 0.4 fusion.24
  21.7 0.2 constant_dynamic-slice_fusion.18
  22.0 1.1 %constant_dynamic-slice_fusion.12 = (bf16[2,4,64,256]{3,2,1,0:T(8,128)(2,1)S(1)}, bf16[2,4,64,256]{3,2,1,0:T(8,128)(2,1)S(1)}, bf16[2,4,64,256]{3,2,1,0:T(8,128)...) fusion(bf16[4,6,66,256]{3,2,1,0:T(8,128)(2,1)S(1)} %fusion.24, ...), kind=kLoop, calls=%fused_computation.123 | loop fusion | bytes 3145800 | tf_op jit(solution)/shard_map/dynamic_slice | solution.py:166
  23.2 0.7 %fusion.72 = f32[512,256]{1,0:T(8,128)S(1)} fusion(bf16[512,2048]{1,0:T(8,128)(2,1)S(1)} %constant_dynamic-update-slice_fusion, bf16[2048,256]{1,0:T(8,128)(2,1)S(1)} %bitcast.73), kind=kOutput, calls=%fused_computation.144 | convolution fusion | flops 536870912 | bytes 3670016 | tf_op jit(solution)/shard_map/dot_general | solution.py:176
  24.0 0.4 fusion.28
  24.4 0.2 constant_dynamic-slice_fusion.9
  24.6 1.1 %constant_dynamic-slice_fusion.3 = (bf16[2,4,64,256]{3,2,1,0:T(8,128)(2,1)S(1)}, bf16[2,4,64,256]{3,2,1,0:T(8,128)(2,1)S(1)}, bf16[2,4,64,256]{3,2,1,0:T(8,128)(...) fusion(bf16[4,6,66,256]{3,2,1,0:T(8,128)(2,1)S(1)} %fusion.28, ...), kind=kLoop, calls=%fused_computation.113 | loop fusion | bytes 3145800 | tf_op jit(solution)/shard_map/dynamic_slice | solution.py:166
  26.0 0.7 %convolution_add_fusion.2 = f32[512,256]{1,0:T(8,128)S(1)} fusion(f32[512,256]{1,0:T(8,128)S(1)} %fusion.72, bf16[512,2048]{1,0:T(8,128)(2,1)S(1)} %constant_dynamic-update-slice_fusion.8, bf16[2048,256]{1,0:T(8,128)(2,1)S(1)} %bitcast.72), kind=kOutput, calls=%fused_computation.21 | convolution fusion | flops 537001984 | bytes 4194304 | tf_op jit(solution)/shard_map/dot_general | solution.py:176
  26.8 0.1 collective-permute-start.7
  26.9 2.6 %collective-permute-start.6 = (f32[2,1,64,256]{3,2,1,0:T(8,128)S(1)}, f32[2,1,64,256]{3,2,1,0:T(8,128)S(1)}, u32[]{:S(2)}, u32[]{:S(2)}) collective-permute-start(f32[2,1,64,256]{3,2,1,0:T(8,128)S(1)} %get-tuple-element.27), channel_id=1, source_target_pairs={{0,12},{4,0},{8,4},{12,8},{1,13},{5,1},{9,5},{13,9},{2,14},{6,2},{... | collective-permute-start | bytes 393224 | tf_op jit(solution)/shard_map/ppermute | solution.py:53
  29.5 0.5 collective-permute-start.5
  30.0 6.7 %collective-permute-done.7 = f32[2,1,64,256]{3,2,1,0:T(8,128)S(1)} collective-permute-done((f32[2,1,64,256]{3,2,1,0:T(8,128)S(1)}, f32[2,1,64,256]{3,2,1,0:T(8,128)S(1)}, u32[]{:S(2)}, u32[]{:S(2)}) %collective-permute-start.7) | collective-permute-done | bytes 131104 | tf_op jit(solution)/shard_map/ppermute | solution.py:53
  36.7 2.8 %collective-permute-done.6 = f32[2,1,64,256]{3,2,1,0:T(8,128)S(1)} collective-permute-done((f32[2,1,64,256]{3,2,1,0:T(8,128)S(1)}, f32[2,1,64,256]{3,2,1,0:T(8,128)S(1)}, u32[]{:S(2)}, u32[]{:S(2)}) %collective-permute-start.6) | collective-permute-done | bytes 131104 | tf_op jit(solution)/shard_map/ppermute | solution.py:53
  39.5 3.2 %collective-permute-start.8 = (bf16[2,1,64,256]{3,2,1,0:T(8,128)(2,1)S(1)}, bf16[2,1,64,256]{3,2,1,0:T(8,128)(2,1)S(1)}, u32[]{:S(2)}, u32[]{:S(2)}) collective-permute-start(bf16[2,1,64,256]{3,2,1,0:T(8,128)(2,1)S(1)} %get-tuple-element.6), channel_id=1, source_target_pairs={{0,4},{4,8},{8,12},{12,0},{1,5},{5,9},{9,13},{13,1},{2,6},{6,10},{... | collective-permute-start | bytes 196616 | tf_op jit(solution)/shard_map/ppermute | solution.py:53
  42.8 0.1 dynamic_slice.133
  42.8 0.7 %collective-permute-start.9 = (bf16[2,1,64,256]{3,2,1,0:T(8,128)(2,1)S(1)}, bf16[2,1,64,256]{3,2,1,0:T(8,128)(2,1)S(1)}, u32[]{:S(2)}, u32[]{:S(2)}) collective-permute-start(bf16[2,1,64,256]{3,2,1,0:T(8,128)(2,1)S(1)} %get-tuple-element.6), channel_id=1, source_target_pairs={{0,12},{4,0},{8,4},{12,8},{1,13},{5,1},{9,5},{13,9},{2,14},{6,2},{... | collective-permute-start | bytes 196616 | tf_op jit(solution)/shard_map/ppermute | solution.py:53
  43.5 1.2 %collective-permute-start.10 = (bf16[2,1,64,256]{3,2,1,0:T(8,128)(2,1)S(1)}, bf16[2,1,64,256]{3,2,1,0:T(8,128)(2,1)S(1)}, u32[]{:S(2)}, u32[]{:S(2)}) collective-permute-start(bf16[2,1,64,256]{3,2,1,0:T(8,128)(2,1)S(1)} %get-tuple-element.6), channel_id=1, source_target_pairs={{0,8},{4,12},{8,0},{12,4},{1,9},{5,13},{9,1},{13,5},{2,10},{6,14},... | collective-permute-start | bytes 196616 | tf_op jit(solution)/shard_map/ppermute | solution.py:53
  44.7 1.6 %collective-permute-done.8 = bf16[2,1,64,256]{3,2,1,0:T(8,128)(2,1)S(1)} collective-permute-done((bf16[2,1,64,256]{3,2,1,0:T(8,128)(2,1)S(1)}, bf16[2,1,64,256]{3,2,1,0:T(8,128)(2,1)S(1)}, u32[]{:S(2)}, u32[]{:S(2)}) %collective-permute-start.8) | collective-permute-done | bytes 65568 | tf_op jit(solution)/shard_map/ppermute | solution.py:53
  46.3 1.3 %collective-permute-done.9 = bf16[2,1,64,256]{3,2,1,0:T(8,128)(2,1)S(1)} collective-permute-done((bf16[2,1,64,256]{3,2,1,0:T(8,128)(2,1)S(1)}, bf16[2,1,64,256]{3,2,1,0:T(8,128)(2,1)S(1)}, u32[]{:S(2)}, u32[]{:S(2)}) %collective-permute-start.9) | collective-permute-done | bytes 65568 | tf_op jit(solution)/shard_map/ppermute | solution.py:53
  47.7 2.2 %collective-permute-done.10 = bf16[2,1,64,256]{3,2,1,0:T(8,128)(2,1)S(1)} collective-permute-done((bf16[2,1,64,256]{3,2,1,0:T(8,128)(2,1)S(1)}, bf16[2,1,64,256]{3,2,1,0:T(8,128)(2,1)S(1)}, u32[]{:S(2)}, u32[]{:S(2)}) %collective-permute-start.10) | collective-permute-done | bytes 65568 | tf_op jit(solution)/shard_map/ppermute | solution.py:53
  50.0 0.1 reduce_sum.80
  50.1 0.1 reduce_sum.81
  50.1 0.1 sub.162
  50.2 0.1 sub.163
  50.3 0.1 fusion.35
  50.4 0.1 reduce_sum.83
  50.5 0.1 reduce_sum.84
  50.6 0.1 mul.99
  50.7 0.1 mul.100
  50.8 0.1 fusion.38
  51.0 0.3 fusion.43
  51.3 0.2 fusion.49
  51.5 0.3 fusion.46
  51.8 0.7 %collective-permute-done.11 = bf16[2,4,64,256]{3,2,1,0:T(8,128)(2,1)S(1)} collective-permute-done((bf16[2,4,64,256]{3,2,1,0:T(8,128)(2,1)S(1)}, bf16[2,4,64,256]{3,2,1,0:T(8,128)(2,1)S(1)}, u32[]{:S(2)}, u32[]{:S(2)}) %collective-permute-start.11) | collective-permute-done | bytes 262176 | tf_op jit(solution)/shard_map/ppermute | solution.py:68
  52.5 0.3 fusion.13
  52.8 0.3 fusion.14
  53.2 0.2 fusion.16
  53.4 0.4 fusion.71
  53.7 0.2 fusion.57
  53.9 0.3 fusion.17
  54.2 0.2 fusion.18
  54.4 0.6 %fusion.51 = bf16[2,1,64,256]{3,2,1,0:T(8,128)(2,1)} fusion(bf16[2,1,64,256]{3,2,1,0:T(8,128)(2,1)S(1)} %bitcast.95, bf16[2,1,64,256]{3,2,1,0:T(8,128)(2,1)S(1)} %get-tuple-element.6), kind=kLoop, calls=%fused_computation.69 | loop fusion | flops 131072 | bytes 196608 | tf_op jit(solution)/shard_map/convert_element_type | solution.py:251
  (72 shorter events, 1.2 us)
Async XLA Ops:
  0.0 51.5 %copy-start = (bf16[512,512]{1,0:T(8,128)(2,1)S(1)}, bf16[512,512]{1,0:T(8,128)(2,1)}, u32[]{:S(2)}) copy-start(bf16[512,512]{1,0:T(8,128)(2,1)} %param.23) | copy-start | bytes 1572868
  0.0 6.2 %copy-start.1 = (bf16[3456,256]{1,0:T(8,128)(2,1)S(1)}, bf16[3456,256]{1,0:T(8,128)(2,1)}, u32[]{:S(2)}) copy-start(bf16[3456,256]{1,0:T(8,128)(2,1)} %param.17) | copy-start | bytes 5308420
  0.0 7.7 %collective-permute-start = (bf16[2,1,64,256]{3,2,1,0:T(8,128)(2,1)}, bf16[2,1,64,256]{3,2,1,0:T(8,128)(2,1)S(1)}, u32[]{:S(2)}, u32[]{:S(2)}) collective-permute-start(bf16[2,1,64,256]{3,2,1,0:T(8,128)(2,1)} %param.14), channel_id=1, source_target_pairs={{0,4},{4,8},{8,12},{12,0},{1,5},{5,9},{9,13},{13,1},{2,6},{6,10},{... | collective-permute-start | bytes 196616 | tf_op jit(solution)/shard_map/ppermute | solution.py:53
  3.0 5.2 %collective-permute-start.1 = (bf16[2,1,64,256]{3,2,1,0:T(8,128)(2,1)}, bf16[2,1,64,256]{3,2,1,0:T(8,128)(2,1)S(1)}, u32[]{:S(2)}, u32[]{:S(2)}) collective-permute-start(bf16[2,1,64,256]{3,2,1,0:T(8,128)(2,1)} %param.14), channel_id=1, source_target_pairs={{0,12},{4,0},{8,4},{12,8},{1,13},{5,1},{9,5},{13,9},{2,14},{6,2},{... | collective-permute-start | bytes 196616 | tf_op jit(solution)/shard_map/ppermute | solution.py:53
  5.1 6.4 %collective-permute-start.2 = (bf16[2,1,64,256]{3,2,1,0:T(8,128)(2,1)}, bf16[2,1,64,256]{3,2,1,0:T(8,128)(2,1)S(1)}, u32[]{:S(2)}, u32[]{:S(2)}) collective-permute-start(bf16[2,1,64,256]{3,2,1,0:T(8,128)(2,1)} %param.14), channel_id=1, source_target_pairs={{0,8},{4,12},{8,0},{12,4},{1,9},{5,13},{9,1},{13,5},{2,10},{6,14},... | collective-permute-start | bytes 196616 | tf_op jit(solution)/shard_map/ppermute | solution.py:53
  6.2 0.8 %copy-start.4 = (bf16[2,1,64,256]{3,2,1,0:T(8,128)(2,1)S(1)}, bf16[2,1,64,256]{3,2,1,0:T(8,128)(2,1)}, u32[]{:S(2)}) copy-start(bf16[2,1,64,256]{3,2,1,0:T(8,128)(2,1)} %param.14) | copy-start | bytes 196612
  11.6 7.9 %collective-permute-start.3 = (bf16[2,4,64,256]{3,2,1,0:T(8,128)(2,1)S(1)}, bf16[2,4,64,256]{3,2,1,0:T(8,128)(2,1)S(1)}, u32[]{:S(2)}, u32[]{:S(2)}) collective-permute-start(bf16[2,4,64,256]{3,2,1,0:T(8,128)(2,1)S(1)} %constant_dynamic-update-slice_fusion.23), channel_id=1, source_target_pairs={{0,2},{2,0},{1,3},{3,1},{4,6},{6,4},{5,7},{7,5},{8,10},{10,8},{9,1... | collective-permute-start | bytes 786440 | tf_op jit(solution)/shard_map/ppermute | solution.py:53
  13.3 7.4 %copy-start.11 = (f32[256]{0:T(256)S(1)}, f32[256]{0:T(256)}, u32[]{:S(2)}) copy-start(f32[256]{0:T(256)} %param.16) | copy-start | bytes 3076
  13.3 7.4 %copy-start.12 = (f32[256]{0:T(256)S(1)}, f32[256]{0:T(256)}, u32[]{:S(2)}) copy-start(f32[256]{0:T(256)} %param.15) | copy-start | bytes 3076
  21.2 2.7 %collective-permute-start.4 = (bf16[4,4,64,256]{3,2,1,0:T(8,128)(2,1)S(1)}, bf16[4,4,64,256]{3,2,1,0:T(8,128)(2,1)S(1)}, u32[]{:S(2)}, u32[]{:S(2)}) collective-permute-start(bf16[4,4,64,256]{3,2,1,0:T(8,128)(2,1)S(1)} %multiply_convert_fusion), channel_id=1, source_target_pairs={{0,1},{1,0},{2,3},{3,2},{4,5},{5,4},{6,7},{7,6},{8,9},{9,8},{10,11... | collective-permute-start | bytes 1572872 | tf_op jit(solution)/shard_map/ppermute | solution.py:68
  25.9 13.5 %copy-start.8 = (f32[256]{0:T(256)S(1)}, f32[256]{0:T(256)}, u32[]{:S(2)}) copy-start(f32[256]{0:T(256)} %param.18) | copy-start | bytes 3076
  25.9 16.8 %copy-start.13 = (f32[512]{0:T(512)S(1)}, f32[512]{0:T(512)}, u32[]{:S(2)}) copy-start(f32[512]{0:T(512)} %param.27) | copy-start | bytes 6148
  26.7 24.1 %copy-start.9 = (f32[256]{0:T(256)S(1)}, f32[256]{0:T(256)}, u32[]{:S(2)}) copy-start(f32[256]{0:T(256)} %param.20) | copy-start | bytes 3076
  26.7 24.1 %copy-start.10 = (f32[256]{0:T(256)S(1)}, f32[256]{0:T(256)}, u32[]{:S(2)}) copy-start(f32[256]{0:T(256)} %param.19) | copy-start | bytes 3076
  26.7 24.3 %copy-start.3 = (bf16[512,512]{1,0:T(8,128)(2,1)S(1)}, bf16[512,512]{1,0:T(8,128)(2,1)}, u32[]{:S(2)}) copy-start(bf16[512,512]{1,0:T(8,128)(2,1)} %param.24) | copy-start | bytes 1572868
  26.8 9.9 %collective-permute-start.7 = (f32[2,1,64,256]{3,2,1,0:T(8,128)S(1)}, f32[2,1,64,256]{3,2,1,0:T(8,128)S(1)}, u32[]{:S(2)}, u32[]{:S(2)}) collective-permute-start(f32[2,1,64,256]{3,2,1,0:T(8,128)S(1)} %get-tuple-element.26), channel_id=1, source_target_pairs={{0,8},{4,12},{8,0},{12,4},{1,9},{5,13},{9,1},{13,5},{2,10},{6,14},... | collective-permute-start | bytes 393224 | tf_op jit(solution)/shard_map/ppermute | solution.py:53
  26.9 12.6 %collective-permute-start.6 = (f32[2,1,64,256]{3,2,1,0:T(8,128)S(1)}, f32[2,1,64,256]{3,2,1,0:T(8,128)S(1)}, u32[]{:S(2)}, u32[]{:S(2)}) collective-permute-start(f32[2,1,64,256]{3,2,1,0:T(8,128)S(1)} %get-tuple-element.27), channel_id=1, source_target_pairs={{0,12},{4,0},{8,4},{12,8},{1,13},{5,1},{9,5},{13,9},{2,14},{6,2},{... | collective-permute-start | bytes 393224 | tf_op jit(solution)/shard_map/ppermute | solution.py:53
  29.5 10.0 %collective-permute-start.5 = (f32[2,1,64,256]{3,2,1,0:T(8,128)S(1)}, f32[2,1,64,256]{3,2,1,0:T(8,128)S(1)}, u32[]{:S(2)}, u32[]{:S(2)}) collective-permute-start(f32[2,1,64,256]{3,2,1,0:T(8,128)S(1)} %get-tuple-element.25), channel_id=1, source_target_pairs={{0,4},{4,8},{8,12},{12,0},{1,5},{5,9},{9,13},{13,1},{2,6},{6,10},{... | collective-permute-start | bytes 393224 | tf_op jit(solution)/shard_map/ppermute | solution.py:53
  39.5 11.8 %copy-start.2 = (bf16[512,512]{1,0:T(8,128)(2,1)S(1)}, bf16[512,512]{1,0:T(8,128)(2,1)}, u32[]{:S(2)}) copy-start(bf16[512,512]{1,0:T(8,128)(2,1)} %param.21) | copy-start | bytes 1572868
  39.5 6.7 %collective-permute-start.8 = (bf16[2,1,64,256]{3,2,1,0:T(8,128)(2,1)S(1)}, bf16[2,1,64,256]{3,2,1,0:T(8,128)(2,1)S(1)}, u32[]{:S(2)}, u32[]{:S(2)}) collective-permute-start(bf16[2,1,64,256]{3,2,1,0:T(8,128)(2,1)S(1)} %get-tuple-element.6), channel_id=1, source_target_pairs={{0,4},{4,8},{8,12},{12,0},{1,5},{5,9},{9,13},{13,1},{2,6},{6,10},{... | collective-permute-start | bytes 196616 | tf_op jit(solution)/shard_map/ppermute | solution.py:53
  42.8 4.8 %collective-permute-start.9 = (bf16[2,1,64,256]{3,2,1,0:T(8,128)(2,1)S(1)}, bf16[2,1,64,256]{3,2,1,0:T(8,128)(2,1)S(1)}, u32[]{:S(2)}, u32[]{:S(2)}) collective-permute-start(bf16[2,1,64,256]{3,2,1,0:T(8,128)(2,1)S(1)} %get-tuple-element.6), channel_id=1, source_target_pairs={{0,12},{4,0},{8,4},{12,8},{1,13},{5,1},{9,5},{13,9},{2,14},{6,2},{... | collective-permute-start | bytes 196616 | tf_op jit(solution)/shard_map/ppermute | solution.py:53
  43.5 6.4 %collective-permute-start.10 = (bf16[2,1,64,256]{3,2,1,0:T(8,128)(2,1)S(1)}, bf16[2,1,64,256]{3,2,1,0:T(8,128)(2,1)S(1)}, u32[]{:S(2)}, u32[]{:S(2)}) collective-permute-start(bf16[2,1,64,256]{3,2,1,0:T(8,128)(2,1)S(1)} %get-tuple-element.6), channel_id=1, source_target_pairs={{0,8},{4,12},{8,0},{12,4},{1,9},{5,13},{9,1},{13,5},{2,10},{6,14},... | collective-permute-start | bytes 196616 | tf_op jit(solution)/shard_map/ppermute | solution.py:53
  50.9 1.6 %collective-permute-start.11 = (bf16[2,4,64,256]{3,2,1,0:T(8,128)(2,1)S(1)}, bf16[2,4,64,256]{3,2,1,0:T(8,128)(2,1)S(1)}, u32[]{:S(2)}, u32[]{:S(2)}) collective-permute-start(bf16[2,4,64,256]{3,2,1,0:T(8,128)(2,1)S(1)} %fusion.38), channel_id=1, source_target_pairs={{0,1},{1,0},{2,3},{3,2},{4,5},{5,4},{6,7},{7,6},{8,9},{9,8},{10,11... | collective-permute-start | bytes 786440 | tf_op jit(solution)/shard_map/ppermute | solution.py:68
  51.3 1.5 %copy-start.7 = (f32[512]{0:T(512)S(1)}, f32[512]{0:T(512)}, u32[]{:S(2)}) copy-start(f32[512]{0:T(512)} %param.25) | copy-start | bytes 6148
  52.5 0.7 %copy-start.6 = (f32[512]{0:T(512)S(1)}, f32[512]{0:T(512)}, u32[]{:S(2)}) copy-start(f32[512]{0:T(512)} %param.22) | copy-start | bytes 6148
  52.8 1.4 %copy-start.5 = (bf16[512,512]{1,0:T(8,128)(2,1)S(1)}, bf16[512,512]{1,0:T(8,128)(2,1)}, u32[]{:S(2)}) copy-start(bf16[512,512]{1,0:T(8,128)(2,1)} %param.26) | copy-start | bytes 1572868

commit v18 on v17

--- a/solution.py
+++ b/solution.py
@@ -136,11 +136,14 @@
 
     mean1, var1 = group_stats(clip, group_size, (0, 1, 2, 4))
     segment = lax.dynamic_slice_in_dim(edge_pad(clip, 0, 2, 0), time_place * frames, frames + 2)
-    activated = jax.nn.silu(
-        apply_norm(segment, mean1, var1, group_size) * norm1_gain + norm1_bias
+    own_padded = jax.nn.silu(
+        apply_norm(edge_pad(edge_pad(segment, 1, 1, 1), 2, 1, 1), mean1, var1, group_size)
+        * norm1_gain
+        + norm1_bias
     ).astype(jnp.bfloat16)
-    padded_halves = [
-        edge_pad(edge_pad(half, 1, 1, 1), 2, 1, 1) for half in chan_halves(activated)
+    activated = own_padded[:, 1:-1, 1:-1]
+    padded_halves = [own_padded] + [
+        edge_pad(edge_pad(half, 1, 1, 1), 2, 1, 1) for half in chan_halves(activated)[1:]
     ]
 
     block_rows = conv_weight.shape[0]

time: 55.2 us -> 56.7 us (1.027)
  local copies, waits for them, and re-layouts: 5.5 us -> 7.63 us
  waiting for transfers between devices: 26 us -> 25 us
    unnamed x42 -> x44, local copies, waits for them, and re-layouts: 1.08 us -> 2.06 us
    dynamic_slice x1, local copies, waits for them, and re-layouts: 0.14 us -> 1.11 us  [local(): lax.dynamic_index_in_dim(placed, source, axis=1, keepdims=False)]
    ppermute x10, waiting for transfers between devices: 25.3 us -> 24.3 us  [shifted(): return lax.ppermute(cells, axes, pairs)]
  transfers between devices with their start and end apart: 12 -> 12, of which waited for: 10 -> 10; matrix products, arithmetic and copies ran while one was open for 7% -> 8% of each run, Pallas kernels for 0% -> 0%
where the time goes in v18:
time: 56.7 us; the launch traced here: 56.5 us
  waiting for transfers between devices  25 us (44%)
  starting transfers between devices  16 us (28%)
  local copies, waits for them, and re-layouts  7.63 us (13%)
  matrix products  3.84 us (7%)
  other arithmetic  3.44 us (6%)
  between operations  0.6 us (1%)
    ppermute x10, waiting for transfers between devices, shifted(): return lax.ppermute(cells, axes, pairs)  24.3 us
    ppermute x10, starting transfers between devices, shifted(): return lax.ppermute(cells, axes, pairs)  15.8 us
    dynamic_slice x4, local copies, waits for them, and re-layouts, local(): lax.dynamic_slice(half, (tap // 9, tap // 3 % 3, tap % 3, 0), (frames, al...  2.55 us
    unnamed x44, local copies, waits for them, and re-layouts  2.06 us
    dot_general x6, matrix products, split_dot(): jnp.dot(half, half_rows(weight, shift, width), preferred_element_type=jnp...  1.56 us
    dot_general x2, matrix products, local(): term = jnp.dot(patches, block, preferred_element_type=jnp.float32)  1.45 us
  transfers between devices with their start and end apart: 12, of which 10 were waited for; matrix products, arithmetic and copies ran while one was open for 8% of the time, Pallas kernels for 0%

profile of v18, /device:TPU:0, one launch (start us, length us, event | category | flops | bytes accessed | tf_op | source)
XLA Modules:
  0.0 56.5 jit_solution(8896097568581650876)
XLA Ops:
  0.0 3.0 %collective-permute-start = (bf16[2,1,64,256]{3,2,1,0:T(8,128)(2,1)}, bf16[2,1,64,256]{3,2,1,0:T(8,128)(2,1)S(1)}, u32[]{:S(2)}, u32[]{:S(2)}) collective-permute-start(bf16[2,1,64,256]{3,2,1,0:T(8,128)(2,1)} %param.14), channel_id=1, source_target_pairs={{0,4},{4,8},{8,12},{12,0},{1,5},{5,9},{9,13},{13,1},{2,6},{6,10},{... | collective-permute-start | bytes 196616 | tf_op jit(solution)/shard_map/ppermute | solution.py:53
  3.0 2.1 %collective-permute-start.1 = (bf16[2,1,64,256]{3,2,1,0:T(8,128)(2,1)}, bf16[2,1,64,256]{3,2,1,0:T(8,128)(2,1)S(1)}, u32[]{:S(2)}, u32[]{:S(2)}) collective-permute-start(bf16[2,1,64,256]{3,2,1,0:T(8,128)(2,1)} %param.14), channel_id=1, source_target_pairs={{0,12},{4,0},{8,4},{12,8},{1,13},{5,1},{9,5},{13,9},{2,14},{6,2},{... | collective-permute-start | bytes 196616 | tf_op jit(solution)/shard_map/ppermute | solution.py:53
  5.1 0.9 %collective-permute-start.2 = (bf16[2,1,64,256]{3,2,1,0:T(8,128)(2,1)}, bf16[2,1,64,256]{3,2,1,0:T(8,128)(2,1)S(1)}, u32[]{:S(2)}, u32[]{:S(2)}) collective-permute-start(bf16[2,1,64,256]{3,2,1,0:T(8,128)(2,1)} %param.14), channel_id=1, source_target_pairs={{0,8},{4,12},{8,0},{12,4},{1,9},{5,13},{9,1},{13,5},{2,10},{6,14},... | collective-permute-start | bytes 196616 | tf_op jit(solution)/shard_map/ppermute | solution.py:53
  6.1 0.1 broadcast_in_dim.5
  6.2 0.2 constant_dynamic-update-slice_fusion.20
  6.5 0.6 %copy-done.5 = bf16[2,1,64,256]{3,2,1,0:T(8,128)(2,1)S(1)} copy-done((bf16[2,1,64,256]{3,2,1,0:T(8,128)(2,1)S(1)}, bf16[2,1,64,256]{3,2,1,0:T(8,128)(2,1)}, u32[]{:S(2)}) %copy-start.5) | copy-done | bytes 65560
  7.1 0.6 %collective-permute-done = bf16[2,1,64,256]{3,2,1,0:T(8,128)(2,1)S(1)} collective-permute-done((bf16[2,1,64,256]{3,2,1,0:T(8,128)(2,1)}, bf16[2,1,64,256]{3,2,1,0:T(8,128)(2,1)S(1)}, u32[]{:S(2)}, u32[]{:S(2)}) %collective-permute-start) | collective-permute-done | bytes 65568 | tf_op jit(solution)/shard_map/ppermute | solution.py:53
  7.7 0.5 collective-permute-done.1
  8.2 3.3 %collective-permute-done.2 = bf16[2,1,64,256]{3,2,1,0:T(8,128)(2,1)S(1)} collective-permute-done((bf16[2,1,64,256]{3,2,1,0:T(8,128)(2,1)}, bf16[2,1,64,256]{3,2,1,0:T(8,128)(2,1)S(1)}, u32[]{:S(2)}, u32[]{:S(2)}) %collective-permute-start.2) | collective-permute-done | bytes 65568 | tf_op jit(solution)/shard_map/ppermute | solution.py:53
  11.6 1.6 %collective-permute-start.3 = (bf16[2,4,64,256]{3,2,1,0:T(8,128)(2,1)S(1)}, bf16[2,4,64,256]{3,2,1,0:T(8,128)(2,1)S(1)}, u32[]{:S(2)}, u32[]{:S(2)}) collective-permute-start(bf16[2,4,64,256]{3,2,1,0:T(8,128)(2,1)S(1)} %constant_dynamic-update-slice_fusion.23), channel_id=1, source_target_pairs={{0,2},{2,0},{1,3},{3,1},{4,6},{6,4},{5,7},{7,5},{8,10},{10,8},{9,1... | collective-permute-start | bytes 786440 | tf_op jit(solution)/shard_map/ppermute | solution.py:53
  13.1 1.1 %constant_dynamic-slice_fusion.2 = (bf16[8,1,256,256]{3,2,1,0:T(8,128)(2,1)S(1)}, bf16[8,1,256,256]{3,2,1,0:T(8,128)(2,1)}) fusion(bf16[8,2,256,256]{3,2,1,0:T(8,128)(2,1)S(1)} %bitcast.66, s32[]{:T(128)S(6)} %select_n.470, s32[]{:T(128)S(6)} %select_n.468), kind=kLoop, calls=%fused_computation.112 | loop fusion | bytes 4194312 | tf_op jit(solution)/shard_map/jit(dynamic_index_in_dim)/dynamic_slice | solution.py:176
  14.4 5.2 %collective-permute-done.3 = bf16[2,4,64,256]{3,2,1,0:T(8,128)(2,1)S(1)} collective-permute-done((bf16[2,4,64,256]{3,2,1,0:T(8,128)(2,1)S(1)}, bf16[2,4,64,256]{3,2,1,0:T(8,128)(2,1)S(1)}, u32[]{:S(2)}, u32[]{:S(2)}) %collective-permute-start.3) | collective-permute-done | bytes 262176 | tf_op jit(solution)/shard_map/ppermute | solution.py:53
  19.6 0.2 convert_reduce_fusion
  19.7 0.2 fusion.40
  19.9 0.1 reduce_sum.55
  20.0 0.1 reduce_sum.59
  20.2 0.1 sub.142
  20.3 0.2 fusion.20
  20.5 0.1 reduce_sum.61
  20.6 0.1 reduce_sum.62
  20.8 0.1 mul.91
  20.9 1.0 %multiply_convert_fusion = bf16[4,6,66,256]{3,2,1,0:T(8,128)(2,1)S(1)} fusion(bf16[4,1,64,256]{3,2,1,0:T(8,128)(2,1)S(1)} %get-tuple-element.31, bf16[4,4,64,256]{3,2,1,0:T(8,128)(2,1)S(1)} %fusion.40, bf16[4,1,64,256]{3,2,1,0:T(8,128)(2,1)S(1)} %get-tuple-element.30, f32[256]{0:T(256)S(1)} %copy-done.9, f32[256]{0:T(256)S(1)} %copy-done.10, ...), kind=kLoop, calls=%fused_computation.14 | loop fusion | flops 14192640 | bytes 1601536 | tf_op jit(solution)/shard_map/convert_element_type | solution.py:143
  21.9 0.2 slice.43
  22.0 0.2 constant_dynamic-slice_fusion.18
  22.4 1.1 %constant_dynamic-slice_fusion.12 = (bf16[2,4,64,256]{3,2,1,0:T(8,128)(2,1)S(1)}, bf16[2,4,64,256]{3,2,1,0:T(8,128)(2,1)S(1)}, bf16[2,4,64,256]{3,2,1,0:T(8,128)...) fusion(bf16[4,6,66,256]{3,2,1,0:T(8,128)(2,1)S(1)} %multiply_co, ...), kind=kLoop, calls=%fused_computation.123 | loop fusion | bytes 3145800 | tf_op jit(solution)/shard_map/dynamic_slice | solution.py:169
  23.7 1.0 %copy-done.2 = bf16[8,1,256,256]{3,2,1,0:T(8,128)(2,1)S(1)} copy-done((bf16[8,1,256,256]{3,2,1,0:T(8,128)(2,1)S(1)}, bf16[8,1,256,256]{3,2,1,0:T(8,128)(2,1)}, u32[]{:S(2)}) %copy-start.2) | copy-done | bytes 1048600
  24.7 0.7 %fusion.72 = f32[512,256]{1,0:T(8,128)S(1)} fusion(bf16[512,2048]{1,0:T(8,128)(2,1)S(1)} %constant_dynamic-update-slice_fusion, bf16[2048,256]{1,0:T(8,128)(2,1)S(1)} %bitcast.73), kind=kOutput, calls=%fused_computation.144 | convolution fusion | flops 536870912 | bytes 3670016 | tf_op jit(solution)/shard_map/dot_general | solution.py:179
  25.5 0.4 fusion.28
  25.8 0.2 constant_dynamic-slice_fusion.9
  26.0 1.1 %constant_dynamic-slice_fusion.3 = (bf16[2,4,64,256]{3,2,1,0:T(8,128)(2,1)S(1)}, bf16[2,4,64,256]{3,2,1,0:T(8,128)(2,1)S(1)}, bf16[2,4,64,256]{3,2,1,0:T(8,128)(...) fusion(bf16[4,6,66,256]{3,2,1,0:T(8,128)(2,1)S(1)} %fusion.28, ...), kind=kLoop, calls=%fused_computation.113 | loop fusion | bytes 3145800 | tf_op jit(solution)/shard_map/dynamic_slice | solution.py:169
  27.4 0.7 %convolution_add_fusion.2 = f32[512,256]{1,0:T(8,128)S(1)} fusion(f32[512,256]{1,0:T(8,128)S(1)} %fusion.72, bf16[512,2048]{1,0:T(8,128)(2,1)S(1)} %constant_dynamic-update-slice_fusion.8, bf16[2048,256]{1,0:T(8,128)(2,1)S(1)} %bitcast.72), kind=kOutput, calls=%fused_computation.22 | convolution fusion | flops 537001984 | bytes 4194304 | tf_op jit(solution)/shard_map/dot_general | solution.py:179
  28.3 2.6 %collective-permute-start.6 = (f32[2,1,64,256]{3,2,1,0:T(8,128)S(1)}, f32[2,1,64,256]{3,2,1,0:T(8,128)S(1)}, u32[]{:S(2)}, u32[]{:S(2)}) collective-permute-start(f32[2,1,64,256]{3,2,1,0:T(8,128)S(1)} %get-tuple-element.27), channel_id=1, source_target_pairs={{0,12},{4,0},{8,4},{12,8},{1,13},{5,1},{9,5},{13,9},{2,14},{6,2},{... | collective-permute-start | bytes 393224 | tf_op jit(solution)/shard_map/ppermute | solution.py:53
  30.9 0.5 collective-permute-start.5
  31.4 6.7 %collective-permute-done.7 = f32[2,1,64,256]{3,2,1,0:T(8,128)S(1)} collective-permute-done((f32[2,1,64,256]{3,2,1,0:T(8,128)S(1)}, f32[2,1,64,256]{3,2,1,0:T(8,128)S(1)}, u32[]{:S(2)}, u32[]{:S(2)}) %collective-permute-start.7) | collective-permute-done | bytes 131104 | tf_op jit(solution)/shard_map/ppermute | solution.py:53
  38.1 2.8 %collective-permute-done.6 = f32[2,1,64,256]{3,2,1,0:T(8,128)S(1)} collective-permute-done((f32[2,1,64,256]{3,2,1,0:T(8,128)S(1)}, f32[2,1,64,256]{3,2,1,0:T(8,128)S(1)}, u32[]{:S(2)}, u32[]{:S(2)}) %collective-permute-start.6) | collective-permute-done | bytes 131104 | tf_op jit(solution)/shard_map/ppermute | solution.py:53
  41.0 3.2 %collective-permute-start.8 = (bf16[2,1,64,256]{3,2,1,0:T(8,128)(2,1)S(1)}, bf16[2,1,64,256]{3,2,1,0:T(8,128)(2,1)S(1)}, u32[]{:S(2)}, u32[]{:S(2)}) collective-permute-start(bf16[2,1,64,256]{3,2,1,0:T(8,128)(2,1)S(1)} %get-tuple-element.6), channel_id=1, source_target_pairs={{0,4},{4,8},{8,12},{12,0},{1,5},{5,9},{9,13},{13,1},{2,6},{6,10},{... | collective-permute-start | bytes 196616 | tf_op jit(solution)/shard_map/ppermute | solution.py:53
  44.2 0.1 dynamic_slice.133
  44.3 0.7 %collective-permute-start.9 = (bf16[2,1,64,256]{3,2,1,0:T(8,128)(2,1)S(1)}, bf16[2,1,64,256]{3,2,1,0:T(8,128)(2,1)S(1)}, u32[]{:S(2)}, u32[]{:S(2)}) collective-permute-start(bf16[2,1,64,256]{3,2,1,0:T(8,128)(2,1)S(1)} %get-tuple-element.6), channel_id=1, source_target_pairs={{0,12},{4,0},{8,4},{12,8},{1,13},{5,1},{9,5},{13,9},{2,14},{6,2},{... | collective-permute-start | bytes 196616 | tf_op jit(solution)/shard_map/ppermute | solution.py:53
  44.9 1.2 %collective-permute-start.10 = (bf16[2,1,64,256]{3,2,1,0:T(8,128)(2,1)S(1)}, bf16[2,1,64,256]{3,2,1,0:T(8,128)(2,1)S(1)}, u32[]{:S(2)}, u32[]{:S(2)}) collective-permute-start(bf16[2,1,64,256]{3,2,1,0:T(8,128)(2,1)S(1)} %get-tuple-element.6), channel_id=1, source_target_pairs={{0,8},{4,12},{8,0},{12,4},{1,9},{5,13},{9,1},{13,5},{2,10},{6,14},... | collective-permute-start | bytes 196616 | tf_op jit(solution)/shard_map/ppermute | solution.py:53
  46.1 1.6 %collective-permute-done.8 = bf16[2,1,64,256]{3,2,1,0:T(8,128)(2,1)S(1)} collective-permute-done((bf16[2,1,64,256]{3,2,1,0:T(8,128)(2,1)S(1)}, bf16[2,1,64,256]{3,2,1,0:T(8,128)(2,1)S(1)}, u32[]{:S(2)}, u32[]{:S(2)}) %collective-permute-start.8) | collective-permute-done | bytes 65568 | tf_op jit(solution)/shard_map/ppermute | solution.py:53
  47.8 1.3 %collective-permute-done.9 = bf16[2,1,64,256]{3,2,1,0:T(8,128)(2,1)S(1)} collective-permute-done((bf16[2,1,64,256]{3,2,1,0:T(8,128)(2,1)S(1)}, bf16[2,1,64,256]{3,2,1,0:T(8,128)(2,1)S(1)}, u32[]{:S(2)}, u32[]{:S(2)}) %collective-permute-start.9) | collective-permute-done | bytes 65568 | tf_op jit(solution)/shard_map/ppermute | solution.py:53
  49.1 2.2 %collective-permute-done.10 = bf16[2,1,64,256]{3,2,1,0:T(8,128)(2,1)S(1)} collective-permute-done((bf16[2,1,64,256]{3,2,1,0:T(8,128)(2,1)S(1)}, bf16[2,1,64,256]{3,2,1,0:T(8,128)(2,1)S(1)}, u32[]{:S(2)}, u32[]{:S(2)}) %collective-permute-start.10) | collective-permute-done | bytes 65568 | tf_op jit(solution)/shard_map/ppermute | solution.py:53
  51.4 0.1 reduce_sum.80
  51.5 0.1 reduce_sum.81
  51.6 0.1 sub.165
  51.7 0.1 sub.166
  51.8 0.1 fusion.35
  51.9 0.1 reduce_sum.83
  51.9 0.1 reduce_sum.84
  52.0 0.1 mul.99
  52.1 0.1 mul.100
  52.2 0.1 fusion.38
  52.4 0.3 fusion.43
  52.8 0.2 fusion.49
  53.0 0.3 fusion.46
  53.3 0.7 %collective-permute-done.11 = bf16[2,4,64,256]{3,2,1,0:T(8,128)(2,1)S(1)} collective-permute-done((bf16[2,4,64,256]{3,2,1,0:T(8,128)(2,1)S(1)}, bf16[2,4,64,256]{3,2,1,0:T(8,128)(2,1)S(1)}, u32[]{:S(2)}, u32[]{:S(2)}) %collective-permute-start.11) | collective-permute-done | bytes 262176 | tf_op jit(solution)/shard_map/ppermute | solution.py:68
  53.9 0.3 fusion.13
  54.3 0.3 fusion.14
  54.6 0.2 fusion.16
  54.8 0.4 fusion.71
  55.2 0.2 fusion.57
  55.4 0.3 fusion.17
  55.6 0.2 fusion.18
  55.8 0.6 %fusion.51 = bf16[2,1,64,256]{3,2,1,0:T(8,128)(2,1)} fusion(bf16[2,1,64,256]{3,2,1,0:T(8,128)(2,1)S(1)} %bitcast.95, bf16[2,1,64,256]{3,2,1,0:T(8,128)(2,1)S(1)} %get-tuple-element.6), kind=kLoop, calls=%fused_computation.69 | loop fusion | flops 131072 | bytes 196608 | tf_op jit(solution)/shard_map/convert_element_type | solution.py:254
  (75 shorter events, 1.3 us)
Async XLA Ops:
  0.0 53.0 %copy-start = (bf16[512,512]{1,0:T(8,128)(2,1)S(1)}, bf16[512,512]{1,0:T(8,128)(2,1)}, u32[]{:S(2)}) copy-start(bf16[512,512]{1,0:T(8,128)(2,1)} %param.23) | copy-start | bytes 1572868
  0.0 6.2 %copy-start.1 = (bf16[3456,256]{1,0:T(8,128)(2,1)S(1)}, bf16[3456,256]{1,0:T(8,128)(2,1)}, u32[]{:S(2)}) copy-start(bf16[3456,256]{1,0:T(8,128)(2,1)} %param.17) | copy-start | bytes 5308420
  0.0 7.7 %collective-permute-start = (bf16[2,1,64,256]{3,2,1,0:T(8,128)(2,1)}, bf16[2,1,64,256]{3,2,1,0:T(8,128)(2,1)S(1)}, u32[]{:S(2)}, u32[]{:S(2)}) collective-permute-start(bf16[2,1,64,256]{3,2,1,0:T(8,128)(2,1)} %param.14), channel_id=1, source_target_pairs={{0,4},{4,8},{8,12},{12,0},{1,5},{5,9},{9,13},{13,1},{2,6},{6,10},{... | collective-permute-start | bytes 196616 | tf_op jit(solution)/shard_map/ppermute | solution.py:53
  3.0 5.2 %collective-permute-start.1 = (bf16[2,1,64,256]{3,2,1,0:T(8,128)(2,1)}, bf16[2,1,64,256]{3,2,1,0:T(8,128)(2,1)S(1)}, u32[]{:S(2)}, u32[]{:S(2)}) collective-permute-start(bf16[2,1,64,256]{3,2,1,0:T(8,128)(2,1)} %param.14), channel_id=1, source_target_pairs={{0,12},{4,0},{8,4},{12,8},{1,13},{5,1},{9,5},{13,9},{2,14},{6,2},{... | collective-permute-start | bytes 196616 | tf_op jit(solution)/shard_map/ppermute | solution.py:53
  5.1 6.4 %collective-permute-start.2 = (bf16[2,1,64,256]{3,2,1,0:T(8,128)(2,1)}, bf16[2,1,64,256]{3,2,1,0:T(8,128)(2,1)S(1)}, u32[]{:S(2)}, u32[]{:S(2)}) collective-permute-start(bf16[2,1,64,256]{3,2,1,0:T(8,128)(2,1)} %param.14), channel_id=1, source_target_pairs={{0,8},{4,12},{8,0},{12,4},{1,9},{5,13},{9,1},{13,5},{2,10},{6,14},... | collective-permute-start | bytes 196616 | tf_op jit(solution)/shard_map/ppermute | solution.py:53
  6.2 0.8 %copy-start.5 = (bf16[2,1,64,256]{3,2,1,0:T(8,128)(2,1)S(1)}, bf16[2,1,64,256]{3,2,1,0:T(8,128)(2,1)}, u32[]{:S(2)}) copy-start(bf16[2,1,64,256]{3,2,1,0:T(8,128)(2,1)} %param.14) | copy-start | bytes 196612
  11.6 7.9 %collective-permute-start.3 = (bf16[2,4,64,256]{3,2,1,0:T(8,128)(2,1)S(1)}, bf16[2,4,64,256]{3,2,1,0:T(8,128)(2,1)S(1)}, u32[]{:S(2)}, u32[]{:S(2)}) collective-permute-start(bf16[2,4,64,256]{3,2,1,0:T(8,128)(2,1)S(1)} %constant_dynamic-update-slice_fusion.23), channel_id=1, source_target_pairs={{0,2},{2,0},{1,3},{3,1},{4,6},{6,4},{5,7},{7,5},{8,10},{10,8},{9,1... | collective-permute-start | bytes 786440 | tf_op jit(solution)/shard_map/ppermute | solution.py:53
  14.3 6.6 %copy-start.9 = (f32[256]{0:T(256)S(1)}, f32[256]{0:T(256)}, u32[]{:S(2)}) copy-start(f32[256]{0:T(256)} %param.16) | copy-start | bytes 3076
  14.3 6.6 %copy-start.10 = (f32[256]{0:T(256)S(1)}, f32[256]{0:T(256)}, u32[]{:S(2)}) copy-start(f32[256]{0:T(256)} %param.15) | copy-start | bytes 3076
  22.3 3.1 %collective-permute-start.4 = (bf16[4,4,64,256]{3,2,1,0:T(8,128)(2,1)S(1)}, bf16[4,4,64,256]{3,2,1,0:T(8,128)(2,1)S(1)}, u32[]{:S(2)}, u32[]{:S(2)}) collective-permute-start(bf16[4,4,64,256]{3,2,1,0:T(8,128)(2,1)S(1)} %slice.43), channel_id=1, source_target_pairs={{0,1},{1,0},{2,3},{3,2},{4,5},{5,4},{6,7},{7,6},{8,9},{9,8},{10,11... | collective-permute-start | bytes 1572872 | tf_op jit(solution)/shard_map/ppermute | solution.py:68
  23.5 1.2 %copy-start.2 = (bf16[8,1,256,256]{3,2,1,0:T(8,128)(2,1)S(1)}, bf16[8,1,256,256]{3,2,1,0:T(8,128)(2,1)}, u32[]{:S(2)}) copy-start(bf16[8,1,256,256]{3,2,1,0:T(8,128)(2,1)} %get-tuple-element.8) | copy-start | bytes 3145732
  27.4 13.5 %copy-start.11 = (f32[256]{0:T(256)S(1)}, f32[256]{0:T(256)}, u32[]{:S(2)}) copy-start(f32[256]{0:T(256)} %param.18) | copy-start | bytes 3076
  27.4 16.8 %copy-start.14 = (f32[512]{0:T(512)S(1)}, f32[512]{0:T(512)}, u32[]{:S(2)}) copy-start(f32[512]{0:T(512)} %param.27) | copy-start | bytes 6148
  28.1 24.1 %copy-start.12 = (f32[256]{0:T(256)S(1)}, f32[256]{0:T(256)}, u32[]{:S(2)}) copy-start(f32[256]{0:T(256)} %param.20) | copy-start | bytes 3076
  28.2 24.1 %copy-start.13 = (f32[256]{0:T(256)S(1)}, f32[256]{0:T(256)}, u32[]{:S(2)}) copy-start(f32[256]{0:T(256)} %param.19) | copy-start | bytes 3076
  28.2 24.3 %copy-start.4 = (bf16[512,512]{1,0:T(8,128)(2,1)S(1)}, bf16[512,512]{1,0:T(8,128)(2,1)}, u32[]{:S(2)}) copy-start(bf16[512,512]{1,0:T(8,128)(2,1)} %param.24) | copy-start | bytes 1572868
  28.2 9.9 %collective-permute-start.7 = (f32[2,1,64,256]{3,2,1,0:T(8,128)S(1)}, f32[2,1,64,256]{3,2,1,0:T(8,128)S(1)}, u32[]{:S(2)}, u32[]{:S(2)}) collective-permute-start(f32[2,1,64,256]{3,2,1,0:T(8,128)S(1)} %get-tuple-element.26), channel_id=1, source_target_pairs={{0,8},{4,12},{8,0},{12,4},{1,9},{5,13},{9,1},{13,5},{2,10},{6,14},... | collective-permute-start | bytes 393224 | tf_op jit(solution)/shard_map/ppermute | solution.py:53
  28.3 12.6 %collective-permute-start.6 = (f32[2,1,64,256]{3,2,1,0:T(8,128)S(1)}, f32[2,1,64,256]{3,2,1,0:T(8,128)S(1)}, u32[]{:S(2)}, u32[]{:S(2)}) collective-permute-start(f32[2,1,64,256]{3,2,1,0:T(8,128)S(1)} %get-tuple-element.27), channel_id=1, source_target_pairs={{0,12},{4,0},{8,4},{12,8},{1,13},{5,1},{9,5},{13,9},{2,14},{6,2},{... | collective-permute-start | bytes 393224 | tf_op jit(solution)/shard_map/ppermute | solution.py:53
  30.9 10.0 %collective-permute-start.5 = (f32[2,1,64,256]{3,2,1,0:T(8,128)S(1)}, f32[2,1,64,256]{3,2,1,0:T(8,128)S(1)}, u32[]{:S(2)}, u32[]{:S(2)}) collective-permute-start(f32[2,1,64,256]{3,2,1,0:T(8,128)S(1)} %get-tuple-element.25), channel_id=1, source_target_pairs={{0,4},{4,8},{8,12},{12,0},{1,5},{5,9},{9,13},{13,1},{2,6},{6,10},{... | collective-permute-start | bytes 393224 | tf_op jit(solution)/shard_map/ppermute | solution.py:53
  40.9 11.8 %copy-start.3 = (bf16[512,512]{1,0:T(8,128)(2,1)S(1)}, bf16[512,512]{1,0:T(8,128)(2,1)}, u32[]{:S(2)}) copy-start(bf16[512,512]{1,0:T(8,128)(2,1)} %param.21) | copy-start | bytes 1572868
  41.0 6.7 %collective-permute-start.8 = (bf16[2,1,64,256]{3,2,1,0:T(8,128)(2,1)S(1)}, bf16[2,1,64,256]{3,2,1,0:T(8,128)(2,1)S(1)}, u32[]{:S(2)}, u32[]{:S(2)}) collective-permute-start(bf16[2,1,64,256]{3,2,1,0:T(8,128)(2,1)S(1)} %get-tuple-element.6), channel_id=1, source_target_pairs={{0,4},{4,8},{8,12},{12,0},{1,5},{5,9},{9,13},{13,1},{2,6},{6,10},{... | collective-permute-start | bytes 196616 | tf_op jit(solution)/shard_map/ppermute | solution.py:53
  44.3 4.8 %collective-permute-start.9 = (bf16[2,1,64,256]{3,2,1,0:T(8,128)(2,1)S(1)}, bf16[2,1,64,256]{3,2,1,0:T(8,128)(2,1)S(1)}, u32[]{:S(2)}, u32[]{:S(2)}) collective-permute-start(bf16[2,1,64,256]{3,2,1,0:T(8,128)(2,1)S(1)} %get-tuple-element.6), channel_id=1, source_target_pairs={{0,12},{4,0},{8,4},{12,8},{1,13},{5,1},{9,5},{13,9},{2,14},{6,2},{... | collective-permute-start | bytes 196616 | tf_op jit(solution)/shard_map/ppermute | solution.py:53
  44.9 6.4 %collective-permute-start.10 = (bf16[2,1,64,256]{3,2,1,0:T(8,128)(2,1)S(1)}, bf16[2,1,64,256]{3,2,1,0:T(8,128)(2,1)S(1)}, u32[]{:S(2)}, u32[]{:S(2)}) collective-permute-start(bf16[2,1,64,256]{3,2,1,0:T(8,128)(2,1)S(1)} %get-tuple-element.6), channel_id=1, source_target_pairs={{0,8},{4,12},{8,0},{12,4},{1,9},{5,13},{9,1},{13,5},{2,10},{6,14},... | collective-permute-start | bytes 196616 | tf_op jit(solution)/shard_map/ppermute | solution.py:53
  52.3 1.6 %collective-permute-start.11 = (bf16[2,4,64,256]{3,2,1,0:T(8,128)(2,1)S(1)}, bf16[2,4,64,256]{3,2,1,0:T(8,128)(2,1)S(1)}, u32[]{:S(2)}, u32[]{:S(2)}) collective-permute-start(bf16[2,4,64,256]{3,2,1,0:T(8,128)(2,1)S(1)} %fusion.38), channel_id=1, source_target_pairs={{0,1},{1,0},{2,3},{3,2},{4,5},{5,4},{6,7},{7,6},{8,9},{9,8},{10,11... | collective-permute-start | bytes 786440 | tf_op jit(solution)/shard_map/ppermute | solution.py:68
  52.7 1.5 %copy-start.8 = (f32[512]{0:T(512)S(1)}, f32[512]{0:T(512)}, u32[]{:S(2)}) copy-start(f32[512]{0:T(512)} %param.25) | copy-start | bytes 6148
  53.9 0.7 %copy-start.7 = (f32[512]{0:T(512)S(1)}, f32[512]{0:T(512)}, u32[]{:S(2)}) copy-start(f32[512]{0:T(512)} %param.22) | copy-start | bytes 6148
  54.2 1.4 %copy-start.6 = (bf16[512,512]{1,0:T(8,128)(2,1)S(1)}, bf16[512,512]{1,0:T(8,128)(2,1)}, u32[]{:S(2)}) copy-start(bf16[512,512]{1,0:T(8,128)(2,1)} %param.26) | copy-start | bytes 1572868

commit v19 on v17

--- a/solution.py
+++ b/solution.py
@@ -189,14 +189,17 @@
     own_middle = (latent.astype(jnp.float32) + convolved + conv_bias).astype(jnp.bfloat16)
 
     if row_count <= PERMUTE_GROUP:
-        middle = jnp.zeros((frames, all_rows, columns, out_channels), own_middle.dtype)
-        for shift in [0] + nearest_first(row_count):
-            block = own_middle if shift == 0 else shifted(
-                own_middle, ("rows",), (row_count,), (shift,)
-            )
-            source_row = (row_place - shift) % row_count
-            middle = lax.dynamic_update_slice(middle, block, (0, source_row * rows_here, 0, 0))
+        middle = jnp.concatenate(
+            [own_middle]
+            + [
+                shifted(own_middle, ("rows",), (row_count,), (shift,))
+                for shift in nearest_first(row_count)
+            ],
+            axis=1,
+        )
+        query_row = 0
     else:
+        query_row = row_place * rows_here
         middle = lax.all_to_all(
             jnp.tile(own_middle, (1, row_count, 1, 1)), "rows", 1, 1, tiled=True
         )
@@ -209,7 +212,7 @@
     tokens = all_rows * columns
     local_tokens = rows_here * columns
     own_rows = [
-        lax.dynamic_slice_in_dim(half, row_place * rows_here, rows_here, axis=1).reshape(
+        lax.dynamic_slice_in_dim(half, query_row, rows_here, axis=1).reshape(
             -1, channels
         )
         for half in normed_halves

time: 55.2 us -> 77.1 us (1.40)
  waiting for transfers between devices: 26 us -> 37.2 us
  local copies, waits for them, and re-layouts: 5.5 us -> 10.9 us
  starting transfers between devices: 16 us -> 19.2 us
  matrix products: 3.83 us -> 4.83 us
  other arithmetic: 3.17 us -> 4.02 us
    ppermute x10, waiting for transfers between devices: 25.3 us -> 37.2 us  [shifted(): return lax.ppermute(cells, axes, pairs)]
    ppermute x10, starting transfers between devices: 15.8 us -> 19.1 us  [shifted(): return lax.ppermute(cells, axes, pairs)]
    dynamic_slice x2 -> x9, local copies, waits for them, and re-layouts: 0.03 us -> 2.56 us  [the longest x4 2.02 us: local(): lax.dynamic_slice_in_dim(half, query_row, rows_here, axis=1)]
    ppermute x0 -> x1, local copies, waits for them, and re-layouts: none -> 1.23 us  [chan_halves(): lax.ppermute(cells, 'chan', [(i, (i + shift) % count) for i in range(coun...]
    convert_element_type x1 -> x2, other arithmetic: 0.1 us -> 1.16 us  [local(): (apply_norm(middle, mean2, var2, group_size) * norm2_gain + norm2_bias).a...]
    dot_general x6, matrix products: 1.55 us -> 2.56 us  [split_dot(): jnp.dot(half, half_rows(weight, shift, width), preferred_element_type=jnp...]
    convert_element_type x0 -> x2, local copies, waits for them, and re-layouts: none -> 0.83 us  [the longest x1 0.73 us: local(): (own_middle.astype(jnp.float32) + branch.astype(jnp.float32)).astype(jnp....]
    unnamed x42 -> x45, local copies, waits for them, and re-layouts: 1.08 us -> 1.85 us
  transfers between devices with their start and end apart: 12 -> 12, of which waited for: 10 -> 8; matrix products, arithmetic and copies ran while one was open for 7% -> 9% of each run, Pallas kernels for 0% -> 0%
where the time goes in v19:
time: 77.1 us; the launch traced here: 76.8 us
  waiting for transfers between devices  37.2 us (48%)
  starting transfers between devices  19.2 us (25%)
  local copies, waits for them, and re-layouts  10.9 us (14%)
  matrix products  4.83 us (6%)
  other arithmetic  4.02 us (5%)
    ppermute x10, waiting for transfers between devices, shifted(): return lax.ppermute(cells, axes, pairs)  37.2 us
    ppermute x10, starting transfers between devices, shifted(): return lax.ppermute(cells, axes, pairs)  19.1 us
    dot_general x6, matrix products, split_dot(): jnp.dot(half, half_rows(weight, shift, width), preferred_element_type=jnp...  2.56 us
    dynamic_slice x4, local copies, waits for them, and re-layouts, local(): lax.dynamic_slice(half, (tap // 9, tap // 3 % 3, tap % 3, 0), (frames, al...  2.55 us
    dynamic_slice x4, local copies, waits for them, and re-layouts, local(): lax.dynamic_slice_in_dim(half, query_row, rows_here, axis=1)  2.02 us
    unnamed x45, local copies, waits for them, and re-layouts  1.85 us
  transfers between devices with their start and end apart: 12, of which 8 were waited for; matrix products, arithmetic and copies ran while one was open for 9% of the time, Pallas kernels for 0%

profile of v19, /device:TPU:0, one launch (start us, length us, event | category | flops | bytes accessed | tf_op | source)
XLA Modules:
  0.0 76.8 jit_solution(8402268833518946812)
XLA Ops:
  0.0 3.0 %collective-permute-start = (bf16[2,1,64,256]{3,2,1,0:T(8,128)(2,1)}, bf16[2,1,64,256]{3,2,1,0:T(8,128)(2,1)S(1)}, u32[]{:S(2)}, u32[]{:S(2)}) collective-permute-start(bf16[2,1,64,256]{3,2,1,0:T(8,128)(2,1)} %param.14), channel_id=1, source_target_pairs={{0,4},{4,8},{8,12},{12,0},{1,5},{5,9},{9,13},{13,1},{2,6},{6,10},{... | collective-permute-start | bytes 196616 | tf_op jit(solution)/shard_map/ppermute | solution.py:53
  3.0 2.1 %collective-permute-start.1 = (bf16[2,1,64,256]{3,2,1,0:T(8,128)(2,1)}, bf16[2,1,64,256]{3,2,1,0:T(8,128)(2,1)S(1)}, u32[]{:S(2)}, u32[]{:S(2)}) collective-permute-start(bf16[2,1,64,256]{3,2,1,0:T(8,128)(2,1)} %param.14), channel_id=1, source_target_pairs={{0,12},{4,0},{8,4},{12,8},{1,13},{5,1},{9,5},{13,9},{2,14},{6,2},{... | collective-permute-start | bytes 196616 | tf_op jit(solution)/shard_map/ppermute | solution.py:53
  5.1 0.9 %collective-permute-start.2 = (bf16[2,1,64,256]{3,2,1,0:T(8,128)(2,1)}, bf16[2,1,64,256]{3,2,1,0:T(8,128)(2,1)S(1)}, u32[]{:S(2)}, u32[]{:S(2)}) collective-permute-start(bf16[2,1,64,256]{3,2,1,0:T(8,128)(2,1)} %param.14), channel_id=1, source_target_pairs={{0,8},{4,12},{8,0},{12,4},{1,9},{5,13},{9,1},{13,5},{2,10},{6,14},... | collective-permute-start | bytes 196616 | tf_op jit(solution)/shard_map/ppermute | solution.py:53
  6.1 0.1 broadcast_in_dim.8
  6.2 0.2 constant_dynamic-update-slice_fusion.16
  6.5 0.6 copy-done.5
  7.1 0.6 collective-permute-done
  7.7 0.5 collective-permute-done.1
  8.2 3.3 %collective-permute-done.2 = bf16[2,1,64,256]{3,2,1,0:T(8,128)(2,1)S(1)} collective-permute-done((bf16[2,1,64,256]{3,2,1,0:T(8,128)(2,1)}, bf16[2,1,64,256]{3,2,1,0:T(8,128)(2,1)S(1)}, u32[]{:S(2)}, u32[]{:S(2)}) %collective-permute-start.2) | collective-permute-done | bytes 65568 | tf_op jit(solution)/shard_map/ppermute | solution.py:53
  11.6 1.6 %collective-permute-start.3 = (bf16[2,4,64,256]{3,2,1,0:T(8,128)(2,1)S(1)}, bf16[2,4,64,256]{3,2,1,0:T(8,128)(2,1)S(1)}, u32[]{:S(2)}, u32[]{:S(2)}) collective-permute-start(bf16[2,4,64,256]{3,2,1,0:T(8,128)(2,1)S(1)} %constant_dynamic-update-slice_fusion.19), channel_id=1, source_target_pairs={{0,2},{2,0},{1,3},{3,1},{4,6},{6,4},{5,7},{7,5},{8,10},{10,8},{9,1... | collective-permute-start | bytes 786440 | tf_op jit(solution)/shard_map/ppermute | solution.py:53
  13.1 0.1 constant_dynamic-slice_fusion.4
  13.4 6.1 %collective-permute-done.3 = bf16[2,4,64,256]{3,2,1,0:T(8,128)(2,1)S(1)} collective-permute-done((bf16[2,4,64,256]{3,2,1,0:T(8,128)(2,1)S(1)}, bf16[2,4,64,256]{3,2,1,0:T(8,128)(2,1)S(1)}, u32[]{:S(2)}, u32[]{:S(2)}) %collective-permute-start.3) | collective-permute-done | bytes 262176 | tf_op jit(solution)/shard_map/ppermute | solution.py:53
  19.6 0.2 convert_reduce_fusion.1
  19.8 0.1 reduce_sum.61
  20.0 0.1 sub.142
  20.1 0.2 fusion.20
  20.4 0.1 reduce_sum.64
  20.7 0.5 multiply_convert_fusion
  21.3 0.4 fusion.26
  21.7 0.2 constant_dynamic-slice_fusion.20
  22.0 1.1 %constant_dynamic-slice_fusion.14 = (bf16[2,4,64,256]{3,2,1,0:T(8,128)(2,1)S(1)}, bf16[2,4,64,256]{3,2,1,0:T(8,128)(2,1)S(1)}, bf16[2,4,64,256]{3,2,1,0:T(8,128)...) fusion(bf16[4,6,66,256]{3,2,1,0:T(8,128)(2,1)S(1)} %fusion.26, ...), kind=kLoop, calls=%fused_computation.119 | loop fusion | bytes 3145800 | tf_op jit(solution)/shard_map/dynamic_slice | solution.py:166
  23.2 0.7 fusion.68
  24.0 0.4 fusion.30
  24.4 0.2 constant_dynamic-slice_fusion.11
  24.6 1.1 %constant_dynamic-slice_fusion.5 = (bf16[2,4,64,256]{3,2,1,0:T(8,128)(2,1)S(1)}, bf16[2,4,64,256]{3,2,1,0:T(8,128)(2,1)S(1)}, bf16[2,4,64,256]{3,2,1,0:T(8,128)(...) fusion(bf16[4,6,66,256]{3,2,1,0:T(8,128)(2,1)S(1)} %fusion.30, ...), kind=kLoop, calls=%fused_computation.109 | loop fusion | bytes 3145800 | tf_op jit(solution)/shard_map/dynamic_slice | solution.py:166
  25.9 0.7 convolution_add_fusion.2
  26.8 0.1 copy.38
  27.0 0.1 copy.37
  27.1 2.6 %collective-permute-start.6 = (f32[2,1,64,256]{2,3,0,1:T(8,128)S(1)}, f32[2,1,64,256]{2,3,0,1:T(8,128)S(1)}, u32[]{:S(2)}, u32[]{:S(2)}) collective-permute-start(f32[2,1,64,256]{2,3,0,1:T(8,128)S(1)} %bitcast.103), channel_id=1, source_target_pairs={{0,12},{4,0},{8,4},{12,8},{1,13},{5,1},{9,5},{13,9},{2,14},{6,2},{... | collective-permute-start | bytes 393224 | tf_op jit(solution)/shard_map/ppermute | solution.py:53
  29.7 0.1 copy.36
  29.9 0.6 collective-permute-start.5
  30.5 0.1 copy.34
  30.6 0.1 copy.35
  30.7 11.7 %collective-permute-done.7 = f32[2,1,64,256]{2,3,0,1:T(8,128)S(1)} collective-permute-done((f32[2,1,64,256]{2,3,0,1:T(8,128)S(1)}, f32[2,1,64,256]{2,3,0,1:T(8,128)S(1)}, u32[]{:S(2)}, u32[]{:S(2)}) %collective-permute-start.7) | collective-permute-done | bytes 131104 | tf_op jit(solution)/shard_map/ppermute | solution.py:53
  42.4 5.7 %collective-permute-done.6 = f32[2,1,64,256]{2,3,0,1:T(8,128)S(1)} collective-permute-done((f32[2,1,64,256]{2,3,0,1:T(8,128)S(1)}, f32[2,1,64,256]{2,3,0,1:T(8,128)S(1)}, u32[]{:S(2)}, u32[]{:S(2)}) %collective-permute-start.6) | collective-permute-done | bytes 131104 | tf_op jit(solution)/shard_map/ppermute | solution.py:53
  48.2 0.1 fusion.43
  48.3 5.7 %collective-permute-start.10 = (bf16[2,1,64,256]{2,3,0,1:T(8,128)(2,1)S(1)}, bf16[2,1,64,256]{2,3,0,1:T(8,128)(2,1)S(1)}, u32[]{:S(2)}, u32[]{:S(2)}) collective-permute-start(bf16[2,1,64,256]{2,3,0,1:T(8,128)(2,1)S(1)} %fusion.43), channel_id=1, source_target_pairs={{0,8},{4,12},{8,0},{12,4},{1,9},{5,13},{9,1},{13,5},{2,10},{6,14},... | collective-permute-start | bytes 196616 | tf_op jit(solution)/shard_map/ppermute | solution.py:53
  53.9 2.6 %collective-permute-start.9 = (bf16[2,1,64,256]{2,3,0,1:T(8,128)(2,1)S(1)}, bf16[2,1,64,256]{2,3,0,1:T(8,128)(2,1)S(1)}, u32[]{:S(2)}, u32[]{:S(2)}) collective-permute-start(bf16[2,1,64,256]{2,3,0,1:T(8,128)(2,1)S(1)} %fusion.43), channel_id=1, source_target_pairs={{0,12},{4,0},{8,4},{12,8},{1,13},{5,1},{9,5},{13,9},{2,14},{6,2},{... | collective-permute-start | bytes 196616 | tf_op jit(solution)/shard_map/ppermute | solution.py:53
  56.6 4.5 %collective-permute-done.10 = bf16[2,1,64,256]{2,3,0,1:T(8,128)(2,1)S(1)} collective-permute-done((bf16[2,1,64,256]{2,3,0,1:T(8,128)(2,1)S(1)}, bf16[2,1,64,256]{2,3,0,1:T(8,128)(2,1)S(1)}, u32[]{:S(2)}, u32[]{:S(2)}) %collective-permute-start.10) | collective-permute-done | bytes 65568 | tf_op jit(solution)/shard_map/ppermute | solution.py:53
  61.0 4.7 %collective-permute-done.8 = bf16[2,1,64,256]{2,3,0,1:T(8,128)(2,1)S(1)} collective-permute-done((bf16[2,1,64,256]{2,3,0,1:T(8,128)(2,1)S(1)}, bf16[2,1,64,256]{2,3,0,1:T(8,128)(2,1)S(1)}, u32[]{:S(2)}, u32[]{:S(2)}) %collective-permute-start.8) | collective-permute-done | bytes 65568 | tf_op jit(solution)/shard_map/ppermute | solution.py:53
  65.7 0.3 convert_reduce_fusion
  66.0 0.4 fusion.22
  66.5 0.1 mul.108
  66.7 0.1 sub.165
  66.8 1.1 %add_convert_fusion = (bf16[2,4,64,256]{2,3,0,1:T(8,128)(2,1)}, f32[2,4,64,256]{2,3,0,1:T(8,128)S(1)}) fusion(f32[256]{0:T(256)S(1)} %copy-done.7, f32[256]{0:T(256)S(1)} %copy-done.8, f32[2,256]{1,0:T(2,128)S(1)} %mul.108, f32[2,256]{1,0:T(2,128)S(1)} %sub.165, bf16[2,1,64,256]{2,3,0,1:T(8,128)(2,1)S(1)} %collective-permute-done.10, ...), kind=kLoop, calls=%fused_computation.36 | loop fusion | flops 1179648 | bytes 1054720 | tf_op jit(solution)/shard_map/convert_element_type | solution.py:207
  67.9 0.9 %dynamic_slice.137 = bf16[2,1,64,256]{2,3,0,1:T(8,128)(2,1)S(1)} slice(bf16[2,4,64,256]{2,3,0,1:T(8,128)(2,1)} %get-tuple-element.23), slice={[0:2], [0:1], [0:64], [0:256]} | slice | bytes 131072 | tf_op jit(solution)/shard_map/dynamic_slice | solution.py:215
  68.8 0.3 copy.41
  69.2 0.1 copy.39
  69.3 1.3 %fusion.46 = f32[512,512]{1,0:T(8,128)S(1)} fusion(bf16[512,256]{1,0:T(8,128)(2,1)S(1)} %fusion.38, bf16[512,512]{1,0:T(8,128)(2,1)} %param.24, s32[]{:T(128)S(6)} %select_n.464), kind=kOutput, calls=%fused_computation.69 | convolution fusion | flops 134217728 | bytes 1572868 | tf_op jit(solution)/shard_map/dot_general | solution.py:82
  70.6 0.2 fusion.52
  70.8 0.3 fusion.49
  71.1 0.9 %dynamic_slice.138 = bf16[2,1,64,256]{2,3,0,1:T(8,128)(2,1)S(1)} slice(bf16[2,4,64,256]{2,3,0,1:T(8,128)(2,1)} %collective-permute-done.11), slice={[0:2], [0:1], [0:64], [0:256]} | slice | bytes 131072 | tf_op jit(solution)/shard_map/dynamic_slice | solution.py:215
  72.0 0.1 copy.40
  72.1 1.2 %copy.42 = bf16[2,4,64,256]{3,2,1,0:T(8,128)(2,1)S(1)} copy(bf16[2,4,64,256]{2,3,0,1:T(8,128)(2,1)} %collective-permute-done.11) | data formatting | bytes 524288 | tf_op jit(solution)/shard_map/ppermute | solution.py:68
  73.4 0.3 fusion.13
  73.7 0.7 copy-done.4
  74.4 0.3 fusion.14
  74.7 0.2 fusion.16
  74.9 0.4 fusion.67
  75.3 0.2 fusion.54
  75.5 0.3 fusion.17
  75.7 0.2 fusion.18
  76.0 0.1 copy.43
  76.1 0.7 copy.44
  (78 shorter events, 1.6 us)
Async XLA Ops:
  0.0 70.8 %copy-start = (bf16[512,512]{1,0:T(8,128)(2,1)S(1)}, bf16[512,512]{1,0:T(8,128)(2,1)}, u32[]{:S(2)}) copy-start(bf16[512,512]{1,0:T(8,128)(2,1)} %param.23) | copy-start | bytes 1572868
  0.0 6.2 %copy-start.1 = (bf16[3456,256]{1,0:T(8,128)(2,1)S(1)}, bf16[3456,256]{1,0:T(8,128)(2,1)}, u32[]{:S(2)}) copy-start(bf16[3456,256]{1,0:T(8,128)(2,1)} %param.17) | copy-start | bytes 5308420
  0.0 7.7 %collective-permute-start = (bf16[2,1,64,256]{3,2,1,0:T(8,128)(2,1)}, bf16[2,1,64,256]{3,2,1,0:T(8,128)(2,1)S(1)}, u32[]{:S(2)}, u32[]{:S(2)}) collective-permute-start(bf16[2,1,64,256]{3,2,1,0:T(8,128)(2,1)} %param.14), channel_id=1, source_target_pairs={{0,4},{4,8},{8,12},{12,0},{1,5},{5,9},{9,13},{13,1},{2,6},{6,10},{... | collective-permute-start | bytes 196616 | tf_op jit(solution)/shard_map/ppermute | solution.py:53
  3.0 5.2 %collective-permute-start.1 = (bf16[2,1,64,256]{3,2,1,0:T(8,128)(2,1)}, bf16[2,1,64,256]{3,2,1,0:T(8,128)(2,1)S(1)}, u32[]{:S(2)}, u32[]{:S(2)}) collective-permute-start(bf16[2,1,64,256]{3,2,1,0:T(8,128)(2,1)} %param.14), channel_id=1, source_target_pairs={{0,12},{4,0},{8,4},{12,8},{1,13},{5,1},{9,5},{13,9},{2,14},{6,2},{... | collective-permute-start | bytes 196616 | tf_op jit(solution)/shard_map/ppermute | solution.py:53
  5.1 6.4 %collective-permute-start.2 = (bf16[2,1,64,256]{3,2,1,0:T(8,128)(2,1)}, bf16[2,1,64,256]{3,2,1,0:T(8,128)(2,1)S(1)}, u32[]{:S(2)}, u32[]{:S(2)}) collective-permute-start(bf16[2,1,64,256]{3,2,1,0:T(8,128)(2,1)} %param.14), channel_id=1, source_target_pairs={{0,8},{4,12},{8,0},{12,4},{1,9},{5,13},{9,1},{13,5},{2,10},{6,14},... | collective-permute-start | bytes 196616 | tf_op jit(solution)/shard_map/ppermute | solution.py:53
  6.2 0.8 %copy-start.5 = (bf16[2,1,64,256]{3,2,1,0:T(8,128)(2,1)S(1)}, bf16[2,1,64,256]{3,2,1,0:T(8,128)(2,1)}, u32[]{:S(2)}) copy-start(bf16[2,1,64,256]{3,2,1,0:T(8,128)(2,1)} %param.14) | copy-start | bytes 196612
  11.6 7.9 %collective-permute-start.3 = (bf16[2,4,64,256]{3,2,1,0:T(8,128)(2,1)S(1)}, bf16[2,4,64,256]{3,2,1,0:T(8,128)(2,1)S(1)}, u32[]{:S(2)}, u32[]{:S(2)}) collective-permute-start(bf16[2,4,64,256]{3,2,1,0:T(8,128)(2,1)S(1)} %constant_dynamic-update-slice_fusion.19), channel_id=1, source_target_pairs={{0,2},{2,0},{1,3},{3,1},{4,6},{6,4},{5,7},{7,5},{8,10},{10,8},{9,1... | collective-permute-start | bytes 786440 | tf_op jit(solution)/shard_map/ppermute | solution.py:53
  13.3 7.4 %copy-start.11 = (f32[256]{0:T(256)S(1)}, f32[256]{0:T(256)}, u32[]{:S(2)}) copy-start(f32[256]{0:T(256)} %param.16) | copy-start | bytes 3076
  13.3 7.4 %copy-start.12 = (f32[256]{0:T(256)S(1)}, f32[256]{0:T(256)}, u32[]{:S(2)}) copy-start(f32[256]{0:T(256)} %param.15) | copy-start | bytes 3076
  21.2 2.7 %collective-permute-start.4 = (bf16[4,4,64,256]{3,2,1,0:T(8,128)(2,1)S(1)}, bf16[4,4,64,256]{3,2,1,0:T(8,128)(2,1)S(1)}, u32[]{:S(2)}, u32[]{:S(2)}) collective-permute-start(bf16[4,4,64,256]{3,2,1,0:T(8,128)(2,1)S(1)} %multiply_convert_fusion), channel_id=1, source_target_pairs={{0,1},{1,0},{2,3},{3,2},{4,5},{5,4},{6,7},{7,6},{8,9},{9,8},{10,11... | collective-permute-start | bytes 1572872 | tf_op jit(solution)/shard_map/ppermute | solution.py:68
  26.7 21.5 %copy-start.13 = (f32[256]{0:T(256)S(1)}, f32[256]{0:T(256)}, u32[]{:S(2)}) copy-start(f32[256]{0:T(256)} %param.18) | copy-start | bytes 3076
  26.7 29.8 %copy-start.14 = (f32[512]{0:T(512)S(1)}, f32[512]{0:T(512)}, u32[]{:S(2)}) copy-start(f32[512]{0:T(512)} %param.27) | copy-start | bytes 6148
  26.8 40.0 %copy-start.7 = (f32[256]{0:T(256)S(1)}, f32[256]{0:T(256)}, u32[]{:S(2)}) copy-start(f32[256]{0:T(256)} %param.20) | copy-start | bytes 3076
  26.8 40.0 %copy-start.8 = (f32[256]{0:T(256)S(1)}, f32[256]{0:T(256)}, u32[]{:S(2)}) copy-start(f32[256]{0:T(256)} %param.19) | copy-start | bytes 3076
  26.9 15.5 %collective-permute-start.7 = (f32[2,1,64,256]{2,3,0,1:T(8,128)S(1)}, f32[2,1,64,256]{2,3,0,1:T(8,128)S(1)}, u32[]{:S(2)}, u32[]{:S(2)}) collective-permute-start(f32[2,1,64,256]{2,3,0,1:T(8,128)S(1)} %bitcast.102), channel_id=1, source_target_pairs={{0,8},{4,12},{8,0},{12,4},{1,9},{5,13},{9,1},{13,5},{2,10},{6,14},... | collective-permute-start | bytes 393224 | tf_op jit(solution)/shard_map/ppermute | solution.py:53
  27.1 21.1 %collective-permute-start.6 = (f32[2,1,64,256]{2,3,0,1:T(8,128)S(1)}, f32[2,1,64,256]{2,3,0,1:T(8,128)S(1)}, u32[]{:S(2)}, u32[]{:S(2)}) collective-permute-start(f32[2,1,64,256]{2,3,0,1:T(8,128)S(1)} %bitcast.103), channel_id=1, source_target_pairs={{0,12},{4,0},{8,4},{12,8},{1,13},{5,1},{9,5},{13,9},{2,14},{6,2},{... | collective-permute-start | bytes 393224 | tf_op jit(solution)/shard_map/ppermute | solution.py:53
  29.9 18.3 %collective-permute-start.5 = (f32[2,1,64,256]{2,3,0,1:T(8,128)S(1)}, f32[2,1,64,256]{2,3,0,1:T(8,128)S(1)}, u32[]{:S(2)}, u32[]{:S(2)}) collective-permute-start(f32[2,1,64,256]{2,3,0,1:T(8,128)S(1)} %bitcast.104), channel_id=1, source_target_pairs={{0,4},{4,8},{8,12},{12,0},{1,5},{5,9},{9,13},{13,1},{2,6},{6,10},{... | collective-permute-start | bytes 393224 | tf_op jit(solution)/shard_map/ppermute | solution.py:53
  48.3 12.8 %collective-permute-start.10 = (bf16[2,1,64,256]{2,3,0,1:T(8,128)(2,1)S(1)}, bf16[2,1,64,256]{2,3,0,1:T(8,128)(2,1)S(1)}, u32[]{:S(2)}, u32[]{:S(2)}) collective-permute-start(bf16[2,1,64,256]{2,3,0,1:T(8,128)(2,1)S(1)} %fusion.43), channel_id=1, source_target_pairs={{0,8},{4,12},{8,0},{12,4},{1,9},{5,13},{9,1},{13,5},{2,10},{6,14},... | collective-permute-start | bytes 196616 | tf_op jit(solution)/shard_map/ppermute | solution.py:53
  53.9 7.1 %collective-permute-start.9 = (bf16[2,1,64,256]{2,3,0,1:T(8,128)(2,1)S(1)}, bf16[2,1,64,256]{2,3,0,1:T(8,128)(2,1)S(1)}, u32[]{:S(2)}, u32[]{:S(2)}) collective-permute-start(bf16[2,1,64,256]{2,3,0,1:T(8,128)(2,1)S(1)} %fusion.43), channel_id=1, source_target_pairs={{0,12},{4,0},{8,4},{12,8},{1,13},{5,1},{9,5},{13,9},{2,14},{6,2},{... | collective-permute-start | bytes 196616 | tf_op jit(solution)/shard_map/ppermute | solution.py:53
  56.5 9.2 %collective-permute-start.8 = (bf16[2,1,64,256]{2,3,0,1:T(8,128)(2,1)S(1)}, bf16[2,1,64,256]{2,3,0,1:T(8,128)(2,1)S(1)}, u32[]{:S(2)}, u32[]{:S(2)}) collective-permute-start(bf16[2,1,64,256]{2,3,0,1:T(8,128)(2,1)S(1)} %fusion.43), channel_id=1, source_target_pairs={{0,4},{4,8},{8,12},{12,0},{1,5},{5,9},{9,13},{13,1},{2,6},{6,10},{... | collective-permute-start | bytes 196616 | tf_op jit(solution)/shard_map/ppermute | solution.py:53
  67.9 3.2 %collective-permute-start.11 = (bf16[2,4,64,256]{2,3,0,1:T(8,128)(2,1)}, bf16[2,4,64,256]{2,3,0,1:T(8,128)(2,1)}, u32[]{:S(2)}, u32[]{:S(2)}) collective-permute-start(bf16[2,4,64,256]{2,3,0,1:T(8,128)(2,1)} %get-tuple-element.23), channel_id=1, source_target_pairs={{0,1},{1,0},{2,3},{3,2},{4,5},{5,4},{6,7},{7,6},{8,9},{9,8},{10,11... | collective-permute-start | bytes 786440 | tf_op jit(solution)/shard_map/ppermute | solution.py:68
  68.8 1.8 %copy-start.2 = (bf16[512,512]{1,0:T(8,128)(2,1)S(1)}, bf16[512,512]{1,0:T(8,128)(2,1)}, u32[]{:S(2)}) copy-start(bf16[512,512]{1,0:T(8,128)(2,1)} %param.21) | copy-start | bytes 1572868
  70.8 2.9 %copy-start.10 = (f32[512]{0:T(512)S(1)}, f32[512]{0:T(512)}, u32[]{:S(2)}) copy-start(f32[512]{0:T(512)} %param.25) | copy-start | bytes 6148
  73.3 1.0 %copy-start.4 = (bf16[512,512]{1,0:T(8,128)(2,1)S(1)}, bf16[512,512]{1,0:T(8,128)(2,1)}, u32[]{:S(2)}) copy-start(bf16[512,512]{1,0:T(8,128)(2,1)} %param.24) | copy-start | bytes 1572868
  73.4 1.3 %copy-start.3 = (bf16[512,512]{1,0:T(8,128)(2,1)S(1)}, bf16[512,512]{1,0:T(8,128)(2,1)}, u32[]{:S(2)}) copy-start(bf16[512,512]{1,0:T(8,128)(2,1)} %param.21) | copy-start | bytes 1572868
  73.4 1.3 %copy-start.9 = (f32[512]{0:T(512)S(1)}, f32[512]{0:T(512)}, u32[]{:S(2)}) copy-start(f32[512]{0:T(512)} %param.22) | copy-start | bytes 6148
  74.4 1.3 %copy-start.6 = (bf16[512,512]{1,0:T(8,128)(2,1)S(1)}, bf16[512,512]{1,0:T(8,128)(2,1)}, u32[]{:S(2)}) copy-start(bf16[512,512]{1,0:T(8,128)(2,1)} %param.26) | copy-start | bytes 1572868

commit v20 on v17

--- a/solution.py
+++ b/solution.py
@@ -118,13 +118,21 @@
             segment_rows = lax.dynamic_update_slice(
                 segment_rows, block, (0, source_row * rows_here, 0, 0)
             )
-        clip = jnp.zeros((time_count * frames, all_rows, columns, channels), latent.dtype)
-        for shift in [0] + nearest_first(time_count):
-            block = segment_rows if shift == 0 else shifted(
-                segment_rows, ("tm",), (time_count,), (shift,)
-            )
-            source_time = (time_place - shift) % time_count
-            clip = lax.dynamic_update_slice(clip, block, (source_time * frames, 0, 0, 0))
+        if time_count == 2:
+            other = shifted(segment_rows, ("tm",), (2,), (1,))
+            first = time_place == 0
+            clip = jnp.concatenate(
+                [jnp.where(first, segment_rows, other), jnp.where(first, other, segment_rows)],
+                axis=0,
+            )
+        else:
+            clip = jnp.zeros((time_count * frames, all_rows, columns, channels), latent.dtype)
+            for shift in [0] + nearest_first(time_count):
+                block = segment_rows if shift == 0 else shifted(
+                    segment_rows, ("tm",), (time_count,), (shift,)
+                )
+                source_time = (time_place - shift) % time_count
+                clip = lax.dynamic_update_slice(clip, block, (source_time * frames, 0, 0, 0))
     else:
         copies = jnp.broadcast_to(latent[None], (row_count * time_count,) + latent.shape)
         gathered = lax.all_to_all(copies, ("rows", "tm"), 0, 0, tiled=True).reshape(

time: 55.2 us -> 58.1 us (1.053)
  local copies, waits for them, and re-layouts: 5.5 us -> 9.45 us
  waiting for transfers between devices: 26 us -> 23.6 us
  between operations: 0.59 us -> 1.34 us
    ppermute x10, waiting for transfers between devices: 25.3 us -> 22.9 us  [shifted(): return lax.ppermute(cells, axes, pairs)]
    dynamic_slice x1, local copies, waits for them, and re-layouts: 0.14 us -> 1.49 us  [local(): lax.dynamic_index_in_dim(placed, source, axis=1, keepdims=False)]
    unnamed x42 -> x46, local copies, waits for them, and re-layouts: 1.08 us -> 2.41 us
    dynamic_update_slice x4, local copies, waits for them, and re-layouts: 0.03 us -> 1 us  [local(): lax.dynamic_update_slice(segment_rows, block, (0, source_row * rows_here,...]
  transfers between devices with their start and end apart: 12 -> 12, of which waited for: 10 -> 10; matrix products, arithmetic and copies ran while one was open for 7% -> 11% of each run, Pallas kernels for 0% -> 0%
where the time goes in v20:
time: 58.1 us; the launch traced here: 57.9 us
  waiting for transfers between devices  23.6 us (41%)
  starting transfers between devices  16 us (28%)
  local copies, waits for them, and re-layouts  9.45 us (16%)
  matrix products  3.84 us (7%)
  other arithmetic  3.7 us (6%)
  between operations  1.34 us (2%)
    ppermute x10, waiting for transfers between devices, shifted(): return lax.ppermute(cells, axes, pairs)  22.9 us
    ppermute x10, starting transfers between devices, shifted(): return lax.ppermute(cells, axes, pairs)  15.8 us
    dynamic_slice x4, local copies, waits for them, and re-layouts, local(): lax.dynamic_slice(half, (tap // 9, tap // 3 % 3, tap % 3, 0), (frames, al...  2.55 us
    unnamed x46, local copies, waits for them, and re-layouts  2.41 us
    dot_general x6, matrix products, split_dot(): jnp.dot(half, half_rows(weight, shift, width), preferred_element_type=jnp...  1.58 us
    dynamic_slice x1, local copies, waits for them, and re-layouts, local(): lax.dynamic_index_in_dim(placed, source, axis=1, keepdims=False)  1.49 us
    dot_general x2, matrix products, local(): term = jnp.dot(patches, block, preferred_element_type=jnp.float32)  1.45 us
  transfers between devices with their start and end apart: 12, of which 10 were waited for; matrix products, arithmetic and copies ran while one was open for 11% of the time, Pallas kernels for 0%

profile of v20, /device:TPU:0, one launch (start us, length us, event | category | flops | bytes accessed | tf_op | source)
XLA Modules:
  0.0 57.9 jit_solution(16871219324577033281)
XLA Ops:
  0.0 3.0 %collective-permute-start = (bf16[2,1,64,256]{3,2,1,0:T(8,128)(2,1)}, bf16[2,1,64,256]{3,2,1,0:T(8,128)(2,1)S(1)}, u32[]{:S(2)}, u32[]{:S(2)}) collective-permute-start(bf16[2,1,64,256]{3,2,1,0:T(8,128)(2,1)} %param.14), channel_id=1, source_target_pairs={{0,4},{4,8},{8,12},{12,0},{1,5},{5,9},{9,13},{13,1},{2,6},{6,10},{... | collective-permute-start | bytes 196616 | tf_op jit(solution)/shard_map/ppermute | solution.py:53
  3.0 2.1 %collective-permute-start.1 = (bf16[2,1,64,256]{3,2,1,0:T(8,128)(2,1)}, bf16[2,1,64,256]{3,2,1,0:T(8,128)(2,1)S(1)}, u32[]{:S(2)}, u32[]{:S(2)}) collective-permute-start(bf16[2,1,64,256]{3,2,1,0:T(8,128)(2,1)} %param.14), channel_id=1, source_target_pairs={{0,12},{4,0},{8,4},{12,8},{1,13},{5,1},{9,5},{13,9},{2,14},{6,2},{... | collective-permute-start | bytes 196616 | tf_op jit(solution)/shard_map/ppermute | solution.py:53
  5.1 1.0 %collective-permute-start.2 = (bf16[2,1,64,256]{3,2,1,0:T(8,128)(2,1)}, bf16[2,1,64,256]{3,2,1,0:T(8,128)(2,1)S(1)}, u32[]{:S(2)}, u32[]{:S(2)}) collective-permute-start(bf16[2,1,64,256]{3,2,1,0:T(8,128)(2,1)} %param.14), channel_id=1, source_target_pairs={{0,8},{4,12},{8,0},{12,4},{1,9},{5,13},{9,1},{13,5},{2,10},{6,14},... | collective-permute-start | bytes 196616 | tf_op jit(solution)/shard_map/ppermute | solution.py:53
  6.1 1.0 %constant_dynamic-update-slice_fusion.24 = bf16[2,4,64,256]{3,2,1,0:T(8,128)(2,1)S(1)} fusion(bf16[2,4,64,256]{3,2,1,0:T(8,128)(2,1)S(1)} %broadcast.80.clone, bf16[2,1,64,256]{3,2,1,0:T(8,128)(2,1)} %param.14, s32[]{:T(128)S(6)} %select_n.395), kind=kLoop, calls=%fused_computation.139 | loop fusion | bytes 131076 | tf_op jit(solution)/shard_map/dynamic_update_slice | solution.py:118
  7.1 0.6 %collective-permute-done = bf16[2,1,64,256]{3,2,1,0:T(8,128)(2,1)S(1)} collective-permute-done((bf16[2,1,64,256]{3,2,1,0:T(8,128)(2,1)}, bf16[2,1,64,256]{3,2,1,0:T(8,128)(2,1)S(1)}, u32[]{:S(2)}, u32[]{:S(2)}) %collective-permute-start) | collective-permute-done | bytes 65568 | tf_op jit(solution)/shard_map/ppermute | solution.py:53
  7.7 0.5 collective-permute-done.1
  8.2 3.3 %collective-permute-done.2 = bf16[2,1,64,256]{3,2,1,0:T(8,128)(2,1)S(1)} collective-permute-done((bf16[2,1,64,256]{3,2,1,0:T(8,128)(2,1)}, bf16[2,1,64,256]{3,2,1,0:T(8,128)(2,1)S(1)}, u32[]{:S(2)}, u32[]{:S(2)}) %collective-permute-start.2) | collective-permute-done | bytes 65568 | tf_op jit(solution)/shard_map/ppermute | solution.py:53
  11.6 1.6 %collective-permute-start.3 = (bf16[2,4,64,256]{3,2,1,0:T(8,128)(2,1)S(1)}, bf16[2,4,64,256]{3,2,1,0:T(8,128)(2,1)S(1)}, u32[]{:S(2)}, u32[]{:S(2)}) collective-permute-start(bf16[2,4,64,256]{3,2,1,0:T(8,128)(2,1)S(1)} %constant_dynamic-update-slice_fusion.21), channel_id=1, source_target_pairs={{0,2},{2,0},{1,3},{3,1},{4,6},{6,4},{5,7},{7,5},{8,10},{10,8},{9,1... | collective-permute-start | bytes 786440 | tf_op jit(solution)/shard_map/ppermute | solution.py:53
  13.1 0.1 broadcast_in_dim.2
  13.3 0.2 constant_dynamic-update-slice_fusion.20
  14.3 1.5 %constant_dynamic-slice_fusion.2 = (bf16[8,1,256,256]{3,2,1,0:T(8,128)(2,1)}, bf16[8,1,256,256]{3,2,1,0:T(8,128)(2,1)}) fusion(bf16[8,2,256,256]{3,2,1,0:T(8,128)(2,1)S(1)} %bitcast.73, s32[]{:T(128)S(6)} %select_n.467, s32[]{:T(128)S(6)} %select_n.465), kind=kLoop, calls=%fused_computation.117 | loop fusion | bytes 4194312 | tf_op jit(solution)/shard_map/jit(dynamic_index_in_dim)/dynamic_slice | solution.py:181
  15.8 3.8 %collective-permute-done.3 = bf16[2,4,64,256]{3,2,1,0:T(8,128)(2,1)S(1)} collective-permute-done((bf16[2,4,64,256]{3,2,1,0:T(8,128)(2,1)S(1)}, bf16[2,4,64,256]{3,2,1,0:T(8,128)(2,1)S(1)}, u32[]{:S(2)}, u32[]{:S(2)}) %collective-permute-start.3) | collective-permute-done | bytes 262176 | tf_op jit(solution)/shard_map/ppermute | solution.py:53
  19.6 0.3 copy.106
  19.9 0.3 copy.107
  20.2 0.4 convert_reduce_fusion
  20.6 0.6 fusion.1
  21.2 0.1 mul.81
  21.2 0.1 mul.82
  21.4 0.1 sub.137
  21.5 0.6 %multiply_convert_fusion = bf16[4,4,64,256]{3,2,1,0:T(8,128)(2,1)S(1)} fusion(s32[]{:T(128)S(6)} %select_n.404, bf16[1,4,64,256]{3,2,1,0:T(8,128)(2,1)S(1)} %slice.36, bf16[2,4,64,256]{3,2,1,0:T(8,128)(2,1)S(1)} %get-tuple-element.33, bf16[2,4,64,256]{3,2,1,0:T(8,128)(2,1)S(1)} %get-tuple-element.32, f32[256]{0:T(256)S(1)} %copy-done.13, ...), kind=kLoop, calls=%fused_computation.33 | loop fusion | flops 3407872 | bytes 1183748 | tf_op jit(solution)/shard_map/convert_element_type | solution.py:149
  22.1 0.1 collective-permute-start.4
  22.2 0.4 fusion.24
  22.6 0.2 constant_dynamic-slice_fusion.18
  22.9 1.1 %constant_dynamic-slice_fusion.12 = (bf16[2,4,64,256]{3,2,1,0:T(8,128)(2,1)S(1)}, bf16[2,4,64,256]{3,2,1,0:T(8,128)(2,1)S(1)}, bf16[2,4,64,256]{3,2,1,0:T(8,128)...) fusion(bf16[4,6,66,256]{3,2,1,0:T(8,128)(2,1)S(1)} %fusion.24, ...), kind=kLoop, calls=%fused_computation.128 | loop fusion | bytes 3145800 | tf_op jit(solution)/shard_map/dynamic_slice | solution.py:174
  24.2 1.0 %copy-done.3 = bf16[8,1,256,256]{3,2,1,0:T(8,128)(2,1)S(1)} copy-done((bf16[8,1,256,256]{3,2,1,0:T(8,128)(2,1)S(1)}, bf16[8,1,256,256]{3,2,1,0:T(8,128)(2,1)}, u32[]{:S(2)}) %copy-start.3) | copy-done | bytes 1048600
  25.2 0.7 %fusion.73 = f32[512,256]{1,0:T(8,128)S(1)} fusion(bf16[512,2048]{1,0:T(8,128)(2,1)S(1)} %constant_dynamic-update-slice_fusion, bf16[2048,256]{1,0:T(8,128)(2,1)S(1)} %bitcast.84), kind=kOutput, calls=%fused_computation.147 | convolution fusion | flops 536870912 | bytes 3670016 | tf_op jit(solution)/shard_map/dot_general | solution.py:184
  25.9 0.4 fusion.28
  26.3 0.2 constant_dynamic-slice_fusion.9
  26.5 1.1 %constant_dynamic-slice_fusion.3 = (bf16[2,4,64,256]{3,2,1,0:T(8,128)(2,1)S(1)}, bf16[2,4,64,256]{3,2,1,0:T(8,128)(2,1)S(1)}, bf16[2,4,64,256]{3,2,1,0:T(8,128)(...) fusion(bf16[4,6,66,256]{3,2,1,0:T(8,128)(2,1)S(1)} %fusion.28, ...), kind=kLoop, calls=%fused_computation.118 | loop fusion | bytes 3145800 | tf_op jit(solution)/shard_map/dynamic_slice | solution.py:174
  27.9 0.9 %copy-done.2 = bf16[8,1,256,256]{3,2,1,0:T(8,128)(2,1)S(1)} copy-done((bf16[8,1,256,256]{3,2,1,0:T(8,128)(2,1)S(1)}, bf16[8,1,256,256]{3,2,1,0:T(8,128)(2,1)}, u32[]{:S(2)}) %copy-start.2) | copy-done | bytes 1048600
  28.8 0.7 %convolution_add_fusion.2 = f32[512,256]{1,0:T(8,128)S(1)} fusion(f32[512,256]{1,0:T(8,128)S(1)} %fusion.73, bf16[512,2048]{1,0:T(8,128)(2,1)S(1)} %constant_dynamic-update-slice_fusion.8, bf16[2048,256]{1,0:T(8,128)(2,1)S(1)} %bitcast.83), kind=kOutput, calls=%fused_computation.23 | convolution fusion | flops 537001984 | bytes 4194304 | tf_op jit(solution)/shard_map/dot_general | solution.py:184
  29.7 2.6 %collective-permute-start.6 = (f32[2,1,64,256]{3,2,1,0:T(8,128)S(1)}, f32[2,1,64,256]{3,2,1,0:T(8,128)S(1)}, u32[]{:S(2)}, u32[]{:S(2)}) collective-permute-start(f32[2,1,64,256]{3,2,1,0:T(8,128)S(1)} %get-tuple-element.26), channel_id=1, source_target_pairs={{0,12},{4,0},{8,4},{12,8},{1,13},{5,1},{9,5},{13,9},{2,14},{6,2},{... | collective-permute-start | bytes 393224 | tf_op jit(solution)/shard_map/ppermute | solution.py:53
  32.3 0.5 collective-permute-start.5
  32.8 6.7 %collective-permute-done.7 = f32[2,1,64,256]{3,2,1,0:T(8,128)S(1)} collective-permute-done((f32[2,1,64,256]{3,2,1,0:T(8,128)S(1)}, f32[2,1,64,256]{3,2,1,0:T(8,128)S(1)}, u32[]{:S(2)}, u32[]{:S(2)}) %collective-permute-start.7) | collective-permute-done | bytes 131104 | tf_op jit(solution)/shard_map/ppermute | solution.py:53
  39.5 2.8 %collective-permute-done.6 = f32[2,1,64,256]{3,2,1,0:T(8,128)S(1)} collective-permute-done((f32[2,1,64,256]{3,2,1,0:T(8,128)S(1)}, f32[2,1,64,256]{3,2,1,0:T(8,128)S(1)}, u32[]{:S(2)}, u32[]{:S(2)}) %collective-permute-start.6) | collective-permute-done | bytes 131104 | tf_op jit(solution)/shard_map/ppermute | solution.py:53
  42.4 3.2 %collective-permute-start.8 = (bf16[2,1,64,256]{3,2,1,0:T(8,128)(2,1)S(1)}, bf16[2,1,64,256]{3,2,1,0:T(8,128)(2,1)S(1)}, u32[]{:S(2)}, u32[]{:S(2)}) collective-permute-start(bf16[2,1,64,256]{3,2,1,0:T(8,128)(2,1)S(1)} %get-tuple-element.6), channel_id=1, source_target_pairs={{0,4},{4,8},{8,12},{12,0},{1,5},{5,9},{9,13},{13,1},{2,6},{6,10},{... | collective-permute-start | bytes 196616 | tf_op jit(solution)/shard_map/ppermute | solution.py:53
  45.6 0.1 dynamic_slice.133
  45.7 0.7 %collective-permute-start.9 = (bf16[2,1,64,256]{3,2,1,0:T(8,128)(2,1)S(1)}, bf16[2,1,64,256]{3,2,1,0:T(8,128)(2,1)S(1)}, u32[]{:S(2)}, u32[]{:S(2)}) collective-permute-start(bf16[2,1,64,256]{3,2,1,0:T(8,128)(2,1)S(1)} %get-tuple-element.6), channel_id=1, source_target_pairs={{0,12},{4,0},{8,4},{12,8},{1,13},{5,1},{9,5},{13,9},{2,14},{6,2},{... | collective-permute-start | bytes 196616 | tf_op jit(solution)/shard_map/ppermute | solution.py:53
  46.4 1.2 %collective-permute-start.10 = (bf16[2,1,64,256]{3,2,1,0:T(8,128)(2,1)S(1)}, bf16[2,1,64,256]{3,2,1,0:T(8,128)(2,1)S(1)}, u32[]{:S(2)}, u32[]{:S(2)}) collective-permute-start(bf16[2,1,64,256]{3,2,1,0:T(8,128)(2,1)S(1)} %get-tuple-element.6), channel_id=1, source_target_pairs={{0,8},{4,12},{8,0},{12,4},{1,9},{5,13},{9,1},{13,5},{2,10},{6,14},... | collective-permute-start | bytes 196616 | tf_op jit(solution)/shard_map/ppermute | solution.py:53
  47.5 1.6 %collective-permute-done.8 = bf16[2,1,64,256]{3,2,1,0:T(8,128)(2,1)S(1)} collective-permute-done((bf16[2,1,64,256]{3,2,1,0:T(8,128)(2,1)S(1)}, bf16[2,1,64,256]{3,2,1,0:T(8,128)(2,1)S(1)}, u32[]{:S(2)}, u32[]{:S(2)}) %collective-permute-start.8) | collective-permute-done | bytes 65568 | tf_op jit(solution)/shard_map/ppermute | solution.py:53
  49.2 1.3 %collective-permute-done.9 = bf16[2,1,64,256]{3,2,1,0:T(8,128)(2,1)S(1)} collective-permute-done((bf16[2,1,64,256]{3,2,1,0:T(8,128)(2,1)S(1)}, bf16[2,1,64,256]{3,2,1,0:T(8,128)(2,1)S(1)}, u32[]{:S(2)}, u32[]{:S(2)}) %collective-permute-start.9) | collective-permute-done | bytes 65568 | tf_op jit(solution)/shard_map/ppermute | solution.py:53
  50.5 2.2 %collective-permute-done.10 = bf16[2,1,64,256]{3,2,1,0:T(8,128)(2,1)S(1)} collective-permute-done((bf16[2,1,64,256]{3,2,1,0:T(8,128)(2,1)S(1)}, bf16[2,1,64,256]{3,2,1,0:T(8,128)(2,1)S(1)}, u32[]{:S(2)}, u32[]{:S(2)}) %collective-permute-start.10) | collective-permute-done | bytes 65568 | tf_op jit(solution)/shard_map/ppermute | solution.py:53
  52.8 0.1 reduce_sum.62
  52.9 0.1 reduce_sum.63
  53.0 0.1 sub.160
  53.1 0.1 sub.161
  53.2 0.1 fusion.35
  53.3 0.1 reduce_sum.65
  53.3 0.1 reduce_sum.66
  53.4 0.1 mul.90
  53.5 0.1 mul.91
  53.6 0.1 fusion.38
  53.9 0.3 fusion.44
  54.2 0.2 fusion.50
  54.4 0.3 fusion.47
  54.7 0.7 %collective-permute-done.11 = bf16[2,4,64,256]{3,2,1,0:T(8,128)(2,1)S(1)} collective-permute-done((bf16[2,4,64,256]{3,2,1,0:T(8,128)(2,1)S(1)}, bf16[2,4,64,256]{3,2,1,0:T(8,128)(2,1)S(1)}, u32[]{:S(2)}, u32[]{:S(2)}) %collective-permute-start.11) | collective-permute-done | bytes 262176 | tf_op jit(solution)/shard_map/ppermute | solution.py:68
  55.3 0.3 fusion.15
  55.7 0.3 fusion.16
  56.0 0.2 fusion.18
  56.2 0.4 fusion.72
  56.6 0.2 fusion.58
  56.8 0.3 fusion.19
  57.0 0.2 fusion.20
  57.3 0.6 %fusion.57 = bf16[2,1,64,256]{3,2,1,0:T(8,128)(2,1)} fusion(bf16[2,1,64,256]{3,2,1,0:T(8,128)(2,1)S(1)} %bitcast.106, bf16[2,1,64,256]{3,2,1,0:T(8,128)(2,1)S(1)} %get-tuple-element.6), kind=kLoop, calls=%fused_computation.80 | loop fusion | flops 131072 | bytes 196608 | tf_op jit(solution)/shard_map/convert_element_type | solution.py:259
  (72 shorter events, 1.1 us)
Async XLA Ops:
  0.0 54.4 %copy-start = (bf16[512,512]{1,0:T(8,128)(2,1)S(1)}, bf16[512,512]{1,0:T(8,128)(2,1)}, u32[]{:S(2)}) copy-start(bf16[512,512]{1,0:T(8,128)(2,1)} %param.23) | copy-start | bytes 1572868
  0.0 7.7 %collective-permute-start = (bf16[2,1,64,256]{3,2,1,0:T(8,128)(2,1)}, bf16[2,1,64,256]{3,2,1,0:T(8,128)(2,1)S(1)}, u32[]{:S(2)}, u32[]{:S(2)}) collective-permute-start(bf16[2,1,64,256]{3,2,1,0:T(8,128)(2,1)} %param.14), channel_id=1, source_target_pairs={{0,4},{4,8},{8,12},{12,0},{1,5},{5,9},{9,13},{13,1},{2,6},{6,10},{... | collective-permute-start | bytes 196616 | tf_op jit(solution)/shard_map/ppermute | solution.py:53
  3.0 5.2 %collective-permute-start.1 = (bf16[2,1,64,256]{3,2,1,0:T(8,128)(2,1)}, bf16[2,1,64,256]{3,2,1,0:T(8,128)(2,1)S(1)}, u32[]{:S(2)}, u32[]{:S(2)}) collective-permute-start(bf16[2,1,64,256]{3,2,1,0:T(8,128)(2,1)} %param.14), channel_id=1, source_target_pairs={{0,12},{4,0},{8,4},{12,8},{1,13},{5,1},{9,5},{13,9},{2,14},{6,2},{... | collective-permute-start | bytes 196616 | tf_op jit(solution)/shard_map/ppermute | solution.py:53
  5.1 6.5 %collective-permute-start.2 = (bf16[2,1,64,256]{3,2,1,0:T(8,128)(2,1)}, bf16[2,1,64,256]{3,2,1,0:T(8,128)(2,1)S(1)}, u32[]{:S(2)}, u32[]{:S(2)}) collective-permute-start(bf16[2,1,64,256]{3,2,1,0:T(8,128)(2,1)} %param.14), channel_id=1, source_target_pairs={{0,8},{4,12},{8,0},{12,4},{1,9},{5,13},{9,1},{13,5},{2,10},{6,14},... | collective-permute-start | bytes 196616 | tf_op jit(solution)/shard_map/ppermute | solution.py:53
  6.1 7.2 %copy-start.1 = (bf16[3456,256]{1,0:T(8,128)(2,1)S(1)}, bf16[3456,256]{1,0:T(8,128)(2,1)}, u32[]{:S(2)}) copy-start(bf16[3456,256]{1,0:T(8,128)(2,1)} %param.17) | copy-start | bytes 5308420
  11.6 7.9 %collective-permute-start.3 = (bf16[2,4,64,256]{3,2,1,0:T(8,128)(2,1)S(1)}, bf16[2,4,64,256]{3,2,1,0:T(8,128)(2,1)S(1)}, u32[]{:S(2)}, u32[]{:S(2)}) collective-permute-start(bf16[2,4,64,256]{3,2,1,0:T(8,128)(2,1)S(1)} %constant_dynamic-update-slice_fusion.21), channel_id=1, source_target_pairs={{0,2},{2,0},{1,3},{3,1},{4,6},{6,4},{5,7},{7,5},{8,10},{10,8},{9,1... | collective-permute-start | bytes 786440 | tf_op jit(solution)/shard_map/ppermute | solution.py:53
  19.6 1.9 %copy-start.13 = (f32[256]{0:T(256)S(1)}, f32[256]{0:T(256)}, u32[]{:S(2)}) copy-start(f32[256]{0:T(256)} %param.16) | copy-start | bytes 3076
  19.6 1.9 %copy-start.14 = (f32[256]{0:T(256)S(1)}, f32[256]{0:T(256)}, u32[]{:S(2)}) copy-start(f32[256]{0:T(256)} %param.15) | copy-start | bytes 3076
  22.1 3.8 %collective-permute-start.4 = (bf16[4,4,64,256]{3,2,1,0:T(8,128)(2,1)S(1)}, bf16[4,4,64,256]{3,2,1,0:T(8,128)(2,1)S(1)}, u32[]{:S(2)}, u32[]{:S(2)}) collective-permute-start(bf16[4,4,64,256]{3,2,1,0:T(8,128)(2,1)S(1)} %multiply_convert_fusion), channel_id=1, source_target_pairs={{0,1},{1,0},{2,3},{3,2},{4,5},{5,4},{6,7},{7,6},{8,9},{9,8},{10,11... | collective-permute-start | bytes 1572872 | tf_op jit(solution)/shard_map/ppermute | solution.py:68
  23.9 1.2 %copy-start.3 = (bf16[8,1,256,256]{3,2,1,0:T(8,128)(2,1)S(1)}, bf16[8,1,256,256]{3,2,1,0:T(8,128)(2,1)}, u32[]{:S(2)}) copy-start(bf16[8,1,256,256]{3,2,1,0:T(8,128)(2,1)} %get-tuple-element.8) | copy-start | bytes 3145732
  27.6 1.2 %copy-start.2 = (bf16[8,1,256,256]{3,2,1,0:T(8,128)(2,1)S(1)}, bf16[8,1,256,256]{3,2,1,0:T(8,128)(2,1)}, u32[]{:S(2)}) copy-start(bf16[8,1,256,256]{3,2,1,0:T(8,128)(2,1)} %get-tuple-element.7) | copy-start | bytes 3145732
  28.8 13.5 %copy-start.6 = (bf16[2,1,64,256]{3,2,1,0:T(8,128)(2,1)S(1)}, bf16[2,1,64,256]{3,2,1,0:T(8,128)(2,1)}, u32[]{:S(2)}) copy-start(bf16[2,1,64,256]{3,2,1,0:T(8,128)(2,1)} %param.14) | copy-start | bytes 196612
  28.8 13.5 %copy-start.10 = (f32[256]{0:T(256)S(1)}, f32[256]{0:T(256)}, u32[]{:S(2)}) copy-start(f32[256]{0:T(256)} %param.18) | copy-start | bytes 3076
  28.8 16.8 %copy-start.15 = (f32[512]{0:T(512)S(1)}, f32[512]{0:T(512)}, u32[]{:S(2)}) copy-start(f32[512]{0:T(512)} %param.27) | copy-start | bytes 6148
  29.5 24.1 %copy-start.11 = (f32[256]{0:T(256)S(1)}, f32[256]{0:T(256)}, u32[]{:S(2)}) copy-start(f32[256]{0:T(256)} %param.20) | copy-start | bytes 3076
  29.6 24.1 %copy-start.12 = (f32[256]{0:T(256)S(1)}, f32[256]{0:T(256)}, u32[]{:S(2)}) copy-start(f32[256]{0:T(256)} %param.19) | copy-start | bytes 3076
  29.6 24.3 %copy-start.5 = (bf16[512,512]{1,0:T(8,128)(2,1)S(1)}, bf16[512,512]{1,0:T(8,128)(2,1)}, u32[]{:S(2)}) copy-start(bf16[512,512]{1,0:T(8,128)(2,1)} %param.24) | copy-start | bytes 1572868
  29.6 9.9 %collective-permute-start.7 = (f32[2,1,64,256]{3,2,1,0:T(8,128)S(1)}, f32[2,1,64,256]{3,2,1,0:T(8,128)S(1)}, u32[]{:S(2)}, u32[]{:S(2)}) collective-permute-start(f32[2,1,64,256]{3,2,1,0:T(8,128)S(1)} %get-tuple-element.27), channel_id=1, source_target_pairs={{0,8},{4,12},{8,0},{12,4},{1,9},{5,13},{9,1},{13,5},{2,10},{6,14},... | collective-permute-start | bytes 393224 | tf_op jit(solution)/shard_map/ppermute | solution.py:53
  29.7 12.6 %collective-permute-start.6 = (f32[2,1,64,256]{3,2,1,0:T(8,128)S(1)}, f32[2,1,64,256]{3,2,1,0:T(8,128)S(1)}, u32[]{:S(2)}, u32[]{:S(2)}) collective-permute-start(f32[2,1,64,256]{3,2,1,0:T(8,128)S(1)} %get-tuple-element.26), channel_id=1, source_target_pairs={{0,12},{4,0},{8,4},{12,8},{1,13},{5,1},{9,5},{13,9},{2,14},{6,2},{... | collective-permute-start | bytes 393224 | tf_op jit(solution)/shard_map/ppermute | solution.py:53
  32.3 10.0 %collective-permute-start.5 = (f32[2,1,64,256]{3,2,1,0:T(8,128)S(1)}, f32[2,1,64,256]{3,2,1,0:T(8,128)S(1)}, u32[]{:S(2)}, u32[]{:S(2)}) collective-permute-start(f32[2,1,64,256]{3,2,1,0:T(8,128)S(1)} %get-tuple-element.25), channel_id=1, source_target_pairs={{0,4},{4,8},{8,12},{12,0},{1,5},{5,9},{9,13},{13,1},{2,6},{6,10},{... | collective-permute-start | bytes 393224 | tf_op jit(solution)/shard_map/ppermute | solution.py:53
  42.3 11.8 %copy-start.4 = (bf16[512,512]{1,0:T(8,128)(2,1)S(1)}, bf16[512,512]{1,0:T(8,128)(2,1)}, u32[]{:S(2)}) copy-start(bf16[512,512]{1,0:T(8,128)(2,1)} %param.21) | copy-start | bytes 1572868
  42.4 6.8 %collective-permute-start.8 = (bf16[2,1,64,256]{3,2,1,0:T(8,128)(2,1)S(1)}, bf16[2,1,64,256]{3,2,1,0:T(8,128)(2,1)S(1)}, u32[]{:S(2)}, u32[]{:S(2)}) collective-permute-start(bf16[2,1,64,256]{3,2,1,0:T(8,128)(2,1)S(1)} %get-tuple-element.6), channel_id=1, source_target_pairs={{0,4},{4,8},{8,12},{12,0},{1,5},{5,9},{9,13},{13,1},{2,6},{6,10},{... | collective-permute-start | bytes 196616 | tf_op jit(solution)/shard_map/ppermute | solution.py:53
  45.7 4.8 %collective-permute-start.9 = (bf16[2,1,64,256]{3,2,1,0:T(8,128)(2,1)S(1)}, bf16[2,1,64,256]{3,2,1,0:T(8,128)(2,1)S(1)}, u32[]{:S(2)}, u32[]{:S(2)}) collective-permute-start(bf16[2,1,64,256]{3,2,1,0:T(8,128)(2,1)S(1)} %get-tuple-element.6), channel_id=1, source_target_pairs={{0,12},{4,0},{8,4},{12,8},{1,13},{5,1},{9,5},{13,9},{2,14},{6,2},{... | collective-permute-start | bytes 196616 | tf_op jit(solution)/shard_map/ppermute | solution.py:53
  46.4 6.4 %collective-permute-start.10 = (bf16[2,1,64,256]{3,2,1,0:T(8,128)(2,1)S(1)}, bf16[2,1,64,256]{3,2,1,0:T(8,128)(2,1)S(1)}, u32[]{:S(2)}, u32[]{:S(2)}) collective-permute-start(bf16[2,1,64,256]{3,2,1,0:T(8,128)(2,1)S(1)} %get-tuple-element.6), channel_id=1, source_target_pairs={{0,8},{4,12},{8,0},{12,4},{1,9},{5,13},{9,1},{13,5},{2,10},{6,14},... | collective-permute-start | bytes 196616 | tf_op jit(solution)/shard_map/ppermute | solution.py:53
  53.7 1.6 %collective-permute-start.11 = (bf16[2,4,64,256]{3,2,1,0:T(8,128)(2,1)S(1)}, bf16[2,4,64,256]{3,2,1,0:T(8,128)(2,1)S(1)}, u32[]{:S(2)}, u32[]{:S(2)}) collective-permute-start(bf16[2,4,64,256]{3,2,1,0:T(8,128)(2,1)S(1)} %fusion.38), channel_id=1, source_target_pairs={{0,1},{1,0},{2,3},{3,2},{4,5},{5,4},{6,7},{7,6},{8,9},{9,8},{10,11... | collective-permute-start | bytes 786440 | tf_op jit(solution)/shard_map/ppermute | solution.py:68
  54.2 1.5 %copy-start.9 = (f32[512]{0:T(512)S(1)}, f32[512]{0:T(512)}, u32[]{:S(2)}) copy-start(f32[512]{0:T(512)} %param.25) | copy-start | bytes 6148
  55.3 0.7 %copy-start.8 = (f32[512]{0:T(512)S(1)}, f32[512]{0:T(512)}, u32[]{:S(2)}) copy-start(f32[512]{0:T(512)} %param.22) | copy-start | bytes 6148
  55.7 1.4 %copy-start.7 = (bf16[512,512]{1,0:T(8,128)(2,1)S(1)}, bf16[512,512]{1,0:T(8,128)(2,1)}, u32[]{:S(2)}) copy-start(bf16[512,512]{1,0:T(8,128)(2,1)} %param.26) | copy-start | bytes 1572868
